TPU v7x, 32 devices: a whole 2x2x4 slice. The times are simulated.
32 devices in a mesh: sec: 2 (over x), seq: 8 (over z, core), mp: 2 (over y).
Axes of the slice: x: 2, y: 2, z: 4, core: 2. Of those that a mesh axis runs over, the one named last changes fastest.
Arguments:
- heads_in: bfloat16 [2, 2, 3072, 2048], P('sec', None, 'seq', 'mp'), may hold values from -8 to 8
- doc_units: int32 [12], replicated, may hold values from 1 to 3, 24 in all
Outputs:
- results: bfloat16 [2, 2, 3072, 2048], P('sec', None, 'seq', 'mp')
Inputs may be any that keep to these rules, and one draw needn't show every extreme that they name: `doc_units`: lengths of 12 packed documents in steps of 128 tokens, summing to 24; the longest is exactly 3 steps.
All inputs are finite; a program needn't handle non-finite values.
Results may differ from a plain program's by a relative error of at most 0.0084.
Values may be sent and summed in bfloat16 or wider, within the bound.
No kernel may reach another device: no remote copies, remote signals or barrier semaphores. Data moves between devices by JAX's collectives and lax.ppermute only.
A program may use at most 128 MiB of HBM per device.

v0:
```python
import jax
import jax.numpy as jnp
from jax import lax
from jax.sharding import PartitionSpec as P

UNIT = 128
HEADS = 32
DH = 64
MAX_DOC_UNITS = 3


epsilon = 1e-06


def seq_shift(value, steps):
    count = lax.axis_size("seq")
    initial, last = (max(0, -steps), min(count, count - steps))
    return lax.ppermute(value, "seq", [(source, source + steps) for source in range(initial, last)])


def sec_swap(value):
    return lax.ppermute(value, "sec", [(0, 1), (1, 0)])


def window_plan(doc_units, seq_place, unit_count, halo_units):
    ends = jnp.cumsum(doc_units).astype(jnp.int32)
    first_unit = seq_place * unit_count
    query_units = first_unit + jnp.arange(unit_count, dtype=jnp.int32)

    def unit_doc(units):
        counted = jnp.sum((ends[None, :] <= units[:, None]).astype(jnp.int32), axis=1)
        return jnp.where(units < 0, jnp.int32(-1), counted)

    starts = jnp.max(
        jnp.where(ends[None, :] <= query_units[:, None], ends[None, :], 0), axis=1
    ).astype(jnp.int32)
    key_units = starts[:, None] + jnp.arange(MAX_DOC_UNITS, dtype=jnp.int32)[None, :]
    allowed = unit_doc(key_units.reshape(-1)).reshape(key_units.shape) == unit_doc(query_units)[:, None]
    return starts - (first_unit - halo_units), allowed


def attention_grads(queries, cotangent, near_keys, near_values, rel_starts, allowed, total_fn, total_cols):
    rows, head_cols = queries.shape
    heads = head_cols // DH
    unit_count = rows // UNIT
    window = MAX_DOC_UNITS * UNIT
    score_scale = DH ** (-0.5)

    def windows(near):
        pieces = [
            lax.dynamic_slice_in_dim(near, rel_starts[j] * UNIT, window, 0) for j in range(unit_count)
        ]
        return jnp.stack(pieces).reshape(unit_count, window, heads, DH)

    keys_w = windows(near_keys)
    values_w = windows(near_values)
    q4 = queries.reshape(unit_count, UNIT, heads, DH)
    cot_float = cotangent.astype(jnp.float32)

    mask = jnp.repeat(allowed, UNIT, axis=1)[:, None, None, :]
    scores = (
        jnp.einsum("jqhd,jkhd->jhqk", q4, keys_w, preferred_element_type=jnp.float32) * score_scale
    )
    scores = jnp.where(mask, scores, -jnp.inf)
    row_max = jnp.max(scores, axis=3, keepdims=True)
    expven = jnp.exp(scores - row_max)
    weights = expven / jnp.sum(expven, axis=3, keepdims=True)
    rounded = weights.astype(jnp.bfloat16)
    attended4 = jnp.einsum("jhqk,jkhd->jqhd", rounded, values_w, preferred_element_type=jnp.float32)
    attended = attended4.reshape(rows, head_cols)

    squares, crosses = total_fn(
        (jnp.sum(attended * attended, axis=1), jnp.sum(cot_float * attended, axis=1))
    )
    spread = jnp.sqrt(squares / total_cols + epsilon)
    normed = attended / spread[:, None]
    shared = crosses / total_cols / spread
    upstream = ((cot_float - normed * shared[:, None]) / spread[:, None]).astype(jnp.bfloat16)
    up4 = upstream.reshape(unit_count, UNIT, heads, DH)

    delta = jnp.sum(up4.astype(jnp.float32) * attended4, axis=3)
    delta = jnp.transpose(delta, (0, 2, 1))[..., None]
    dprobs = jnp.einsum("jqhd,jkhd->jhqk", up4, values_w, preferred_element_type=jnp.float32)
    dscores = (weights * (dprobs - delta) * score_scale).astype(jnp.bfloat16)
    grad_q = jnp.einsum("jhqk,jkhd->jqhd", dscores, keys_w, preferred_element_type=jnp.float32)
    grad_kw = jnp.einsum("jhqk,jqhd->jkhd", dscores, q4, preferred_element_type=jnp.float32)
    grad_vw = jnp.einsum("jhqk,jqhd->jkhd", rounded, up4, preferred_element_type=jnp.float32)
    grad_kvw = jnp.concatenate(
        [grad_kw.reshape(unit_count, window, head_cols), grad_vw.reshape(unit_count, window, head_cols)],
        axis=2,
    )
    near_rows = near_keys.shape[0]
    total = jnp.zeros((near_rows, 2 * head_cols), jnp.float32)
    for j in range(unit_count):
        start = rel_starts[j] * UNIT
        total = lax.dynamic_update_slice_in_dim(
            total, lax.dynamic_slice_in_dim(total, start, window, 0) + grad_kvw[j], start, 0
        )
    return grad_q.reshape(rows, head_cols), normed, total


def per_device(heads_in, doc_units):
    section = lax.axis_index("sec")
    seq_place = lax.axis_index("seq")
    is_first = section == 0
    local_heads = heads_in[0]
    _, rows, cols = local_heads.shape
    half = cols // 2
    unit_count = rows // UNIT
    halo_units = MAX_DOC_UNITS - 1
    halo = halo_units * UNIT
    total_cols = cols * lax.axis_size("mp")

    keep_offset = section * half
    send_offset = (1 - section) * half
    sent = lax.dynamic_slice_in_dim(local_heads, send_offset, half, 2)
    kept = lax.dynamic_slice_in_dim(local_heads, keep_offset, half, 2)
    arrived = sec_swap(sent)
    key_value = jnp.where(is_first, kept, arrived)
    query_cot = jnp.where(is_first, arrived, kept)

    joined = jnp.concatenate([key_value[0], key_value[1]], axis=1)
    low = seq_shift(joined[rows - halo :], 1)
    high = seq_shift(joined[:halo], -1)
    near = jnp.concatenate([low, joined, high], axis=0)

    rel_starts, allowed = window_plan(doc_units, seq_place, unit_count, halo_units)

    def row_total(sums_pair):
        return lax.psum(sums_pair, ("sec", "mp"))

    grad_q, normed, total = attention_grads(
        query_cot[0],
        query_cot[1],
        near[:, :half],
        near[:, half:],
        rel_starts,
        allowed,
        row_total,
        total_cols,
    )
    from_left = seq_shift(total[near.shape[0] - halo :], 1)
    from_right = seq_shift(total[:halo], -1)
    own = total[halo : halo + rows]
    own = own.at[:halo].add(from_left)
    own = own.at[rows - halo :].add(from_right)
    grad_k = own[:, :half].astype(jnp.bfloat16)
    grad_v = own[:, half:].astype(jnp.bfloat16)

    kv_pair = jnp.stack([grad_k, grad_v])
    qn_pair = jnp.stack([grad_q.astype(jnp.bfloat16), normed.astype(jnp.bfloat16)])
    keep_pair = jnp.where(is_first, kv_pair, qn_pair)
    back = sec_swap(jnp.where(is_first, qn_pair, kv_pair))
    result = jnp.where(
        is_first,
        jnp.concatenate([keep_pair, back], axis=2),
        jnp.concatenate([back, keep_pair], axis=2),
    )
    return result[None]


def solution(mesh):
    return jax.shard_map(
        per_device,
        mesh=mesh,
        in_specs=(P("sec", None, "seq", "mp"), P()),
        out_specs=P("sec", None, "seq", "mp"),
        check_vma=False,
    )
```

profile of v0, /device:TPU:18, one launch (start us, length us, event | category | flops | bytes accessed | tf_op | source)
XLA Modules:
  0.0 104.4 jit_solution(9215667205354717378)
XLA Ops:
  0.0 1.5 %constant_dynamic-slice_fusion.6 = (bf16[1,2,384,512]{3,2,1,0:T(8,128)(2,1)S(1)}, bf16[1,2,384,512]{3,2,1,0:T(8,128)(2,1)S(1)}) fusion(bf16[1,2,384,1024]{3,2,1,0:T(8,128)(2,1)} %param.6, s32[]{:T(128)S(6)} %select_n.91, s32[]{:T(128)S(6)} %select_n.90), kind=kLoop, calls=%fused_computation.68 | loop fusion | bytes 3145736 | tf_op jit(solution)/shard_map/dynamic_slice | solution.py:117
  1.5 0.4 copy.20
  1.9 0.6 collective-permute-start
  2.5 0.2 reduce-window.8
  2.6 0.2 fusion.25
  2.8 0.4 copy.21
  3.4 0.2 convert_reduce_fusion
  3.7 17.5 %collective-permute-done = bf16[2,384,512]{1,2,0:T(8,128)(2,1)S(1)} collective-permute-done((bf16[2,384,512]{1,2,0:T(8,128)(2,1)S(1)}, bf16[2,384,512]{1,2,0:T(8,128)(2,1)S(1)}, u32[]{:S(2)}, u32[]{:S(2)}) %collective-permute-start) | collective-permute-done | bytes 786464 | tf_op jit(solution)/shard_map/ppermute | solution.py:22
  21.2 0.1 bitcast_select_fusion.1
  21.4 1.1 %fusion.19 = (bf16[256,1024]{0,1:T(8,128)(2,1)}, bf16[256,1024]{0,1:T(8,128)(2,1)}) fusion(bf16[384,512]{0,1:T(8,128)(2,1)S(1)} %get-tuple-element.59, bf16[384,512]{0,1:T(8,128)(2,1)S(1)} %get-tuple-element.60), kind=kLoop, calls=%fused_computation.49 | loop fusion | flops 2097152 | bytes 1835008 | tf_op jit(solution)/shard_map/concatenate | solution.py:122
  22.5 1.9 %collective-permute-start.2 = (bf16[256,1024]{0,1:T(8,128)(2,1)}, bf16[256,1024]{0,1:T(8,128)(2,1)S(1)}, u32[]{:S(2)}, u32[]{:S(2)}) collective-permute-start(bf16[256,1024]{0,1:T(8,128)(2,1)} %get-tuple-element.58), channel_id=1, source_target_pairs={{2,0},{4,2},{6,4},{8,6},{10,8},{12,10},{14,12},{3,1},{5,3},{7,5},{... | collective-permute-start | bytes 1572872 | tf_op jit(solution)/shard_map/ppermute | solution.py:18
  24.4 2.4 %collective-permute-start.1 = (bf16[256,1024]{0,1:T(8,128)(2,1)}, bf16[256,1024]{0,1:T(8,128)(2,1)}, u32[]{:S(2)}, u32[]{:S(2)}) collective-permute-start(bf16[256,1024]{0,1:T(8,128)(2,1)} %get-tuple-element.57), channel_id=1, source_target_pairs={{0,2},{2,4},{4,6},{6,8},{8,10},{10,12},{12,14},{1,3},{3,5},{5,7},{... | collective-permute-start | bytes 1572872 | tf_op jit(solution)/shard_map/ppermute | solution.py:18
  26.8 0.7 fusion.36
  29.7 0.3 reshape.316
  30.1 1.3 %collective-permute-done.2 = bf16[256,1024]{0,1:T(8,128)(2,1)S(1)} collective-permute-done((bf16[256,1024]{0,1:T(8,128)(2,1)}, bf16[256,1024]{0,1:T(8,128)(2,1)S(1)}, u32[]{:S(2)}, u32[]{:S(2)}) %collective-permute-start.2) | collective-permute-done | bytes 524320 | tf_op jit(solution)/shard_map/ppermute | solution.py:18
  31.4 3.8 %collective-permute-done.1 = bf16[256,1024]{0,1:T(8,128)(2,1)} collective-permute-done((bf16[256,1024]{0,1:T(8,128)(2,1)}, bf16[256,1024]{0,1:T(8,128)(2,1)}, u32[]{:S(2)}, u32[]{:S(2)}) %collective-permute-start.1) | collective-permute-done | bytes 524320 | tf_op jit(solution)/shard_map/ppermute | solution.py:18
  35.2 1.2 %pad_maximum_fusion = bf16[896,1024]{0,1:T(8,128)(2,1)S(1)} fusion(bf16[256,1024]{0,1:T(8,128)(2,1)S(1)} %collective-permute-done.2, bf16[384,512]{0,1:T(8,128)(2,1)S(1)} %get-tuple-element.60, bf16[384,512]{0,1:T(8,128)(2,1)S(1)} %get-tuple-element.59, bf16[256,1024]{0,1:T(8,128)(2,1)} %collective-permute-done.1), kind=kLoop, calls=%fused_computation.14 | loop fusion | flops 7340032 | bytes 3670016 | tf_op jit(solution)/shard_map/concatenate | solution.py:125
  37.0 0.8 fusion.20
  37.8 1.7 %fusion.37 = (f32[3,8,128]{2,1,0:T(8,128)S(1)}, f32[3,8,128,384]{3,2,1,0:T(8,128)S(1)}) fusion(f32[3,8,128,384]{3,2,1,0:T(8,128)S(1)} %fusion.20, pred[3,384]{1,0:T(4,128)(4,1)S(1)} %bitcast.101), kind=kOutput, calls=%fused_computation.93 | output fusion | flops 7078271 | bytes 9450624 | tf_op jit(solution)/shard_map/sub | solution.py:66
  39.6 0.6 fusion.5
  40.2 1.5 %copy-done.1 = f32[3,8,128,384]{3,2,1,0:T(8,128)} copy-done((f32[3,8,128,384]{3,2,1,0:T(8,128)}, f32[3,8,128,384]{3,2,1,0:T(8,128)S(1)}, u32[]{:S(2)}) %copy-start.1) | copy-done | bytes 4718616
  41.7 2.1 %multiply_reduce_fusion.1 = (f32[3,128]{1,0:T(4,128)S(1)}, f32[3,128]{1,0:T(4,128)S(1)}, f32[3,128,8,64]{1,3,2,0:T(8,128)}) fusion(f32[3,128,8,64]{1,0,3,2:T(4,128)S(1)} %reshape.316, bf16[3,8,128,384]{3,2,1,0:T(8,128)(2,1)S(1)} %fusion.5, bf16[1,384,8,64]{1,3,2,0:T(8,128)(2,1)S(1)} %bitcast.94, bf16[1,384,8,64]{1,3,2,0:T(8,128)(2,1)S(1)} %bitcast.96, ...), kind=kOutput, calls=%fused_computation.46 | convolution fusion | flops 152960256 | bytes 5114880 | tf_op jit(solution)/shard_map/jhqk,jkhd->jqhd/dot_general | solution.py:69
  43.8 8.9 %all-reduce = (f32[384]{0:T(512)S(1)}, f32[384]{0:T(512)S(1)}) all-reduce(f32[384]{0:T(512)S(1)} %bitcast.100, f32[384]{0:T(512)S(1)} %bitcast.99), channel_id=1, replica_groups=mesh['sec'=2,'seq'=8,'mp'=2] {'sec','mp'}, use_global_device_ids=true, to_apply=%region_7.8 | all-reduce | flops 768 | bytes 6144 | tf_op jit(solution)/shard_map/psum | solution.py:130
  52.8 1.4 %multiply_reduce_fusion = (f32[3,128,8]{1,2,0:T(8,128)S(1)}, bf16[3,128,8,64]{1,3,2,0:T(8,128)(2,1)S(1)}) fusion(f32[3,128,8,64]{1,3,2,0:T(8,128)} %get-tuple-element.69, f32[3,128]{1,0:T(4,128)S(1)} %get-tuple-element.62, f32[3,128]{1,0:T(4,128)S(1)} %get-tuple-element.61, f32[3,128,8,64]{1,0,3,2:T(4,128)S(1)} %reshape.316), kind=kLoop, calls=%fused_computation.44 | loop fusion | flops 1569792 | bytes 1981440 | tf_op jit(solution)/shard_map/reduce_sum | solution.py:81
  54.2 0.6 fusion.38
  54.7 1.7 %copy-done.2 = f32[3,8,128,384]{3,2,1,0:T(8,128)S(1)} copy-done((f32[3,8,128,384]{3,2,1,0:T(8,128)S(1)}, f32[3,8,128,384]{3,2,1,0:T(8,128)}, u32[]{:S(2)}) %copy-start.2) | copy-done | bytes 4718616
  56.8 1.9 %multiply_convert_fusion = bf16[3,8,128,384]{3,2,1,0:T(8,128)(2,1)S(1)} fusion(f32[3,8,128]{2,1,0:T(8,128)S(1)} %bitcast.98, bf16[3,128,8,64]{1,3,2,0:T(8,128)(2,1)S(1)} %get-tuple-element.36, f32[3,8,128,384]{3,2,1,0:T(8,128)S(1)} %copy-done.2, f32[3,8,128]{2,1,0:T(8,128)S(1)} %get-tuple-element.67, bf16[1,384,8,64]{1,3,2,0:T(8,128)(2,1)S(1)} %bitcast.95, ...), kind=kOutput, calls=%fused_computation.5 | convolution fusion | flops 158072832 | bytes 8675328 | tf_op jit(solution)/shard_map/jqhd,jkhd->jhqk/dot_general | solution.py:83
  58.7 0.6 fusion.22
  59.2 0.8 copy-done.3
  60.1 0.2 broadcast_in_dim.36
  60.4 0.3 fusion.9
  60.8 0.3 fusion.15
  61.1 1.6 %fusion.34 = (f32[256,1024]{0,1:T(8,128)}, f32[256,1024]{0,1:T(8,128)}) fusion(f32[896,1024]{0,1:T(8,128)S(1)} %fusion.15), kind=kLoop, calls=%fused_computation.90 | loop fusion | bytes 4194304 | tf_op jit(solution)/shard_map/slice | solution.py:143
  62.7 1.9 %collective-permute-start.3 = (f32[256,1024]{0,1:T(8,128)}, f32[256,1024]{0,1:T(8,128)}, u32[]{:S(2)}, u32[]{:S(2)}) collective-permute-start(f32[256,1024]{0,1:T(8,128)} %get-tuple-element.38), channel_id=1, source_target_pairs={{0,2},{2,4},{4,6},{6,8},{8,10},{10,12},{12,14},{1,3},{3,5},{5,7},{... | collective-permute-start | bytes 3145736 | tf_op jit(solution)/shard_map/ppermute | solution.py:18
  64.6 3.8 %collective-permute-start.4 = (f32[256,1024]{0,1:T(8,128)}, f32[256,1024]{0,1:T(8,128)}, u32[]{:S(2)}, u32[]{:S(2)}) collective-permute-start(f32[256,1024]{0,1:T(8,128)} %get-tuple-element.37), channel_id=1, source_target_pairs={{2,0},{4,2},{6,4},{8,6},{10,8},{12,10},{14,12},{3,1},{5,3},{7,5},{... | collective-permute-start | bytes 3145736 | tf_op jit(solution)/shard_map/ppermute | solution.py:18
  68.4 0.5 copy.27
  69.1 0.4 reshape.315
  69.5 3.2 %fusion.16 = bf16[3,128,8,64]{1,3,2,0:T(8,128)(2,1)S(1)} fusion(bf16[3,8,128,384]{3,2,1,0:T(8,128)(2,1)} %copy-done.3, bf16[1,384,8,64]{1,3,2,0:T(8,128)(2,1)} %bitcast.87, bf16[1,384,8,64]{1,3,2,0:T(8,128)(2,1)} %bitcast.89, bf16[1,384,8,64]{1,3,2,0:T(8,128)(2,1)} %bitcast.85), kind=kOutput, calls=%fused_computation.29 | convolution fusion | flops 152371200 | bytes 3932160 | tf_op jit(solution)/shard_map/jhqk,jkhd->jqhd/dot_general | solution.py:85
  72.7 0.3 copy.26
  73.1 0.3 convert_element_type.65
  73.5 5.6 %collective-permute-done.3 = f32[256,1024]{0,1:T(8,128)} collective-permute-done((f32[256,1024]{0,1:T(8,128)}, f32[256,1024]{0,1:T(8,128)}, u32[]{:S(2)}, u32[]{:S(2)}) %collective-permute-start.3) | collective-permute-done | bytes 1048608 | tf_op jit(solution)/shard_map/ppermute | solution.py:18
  79.1 1.7 %fusion.18 = f32[384,1024]{0,1:T(8,128)S(1)} fusion(f32[384,1024]{0,1:T(8,128)S(1)} %slice.137, f32[256,1024]{0,1:T(8,128)} %collective-permute-done.3, f32[896,1024]{0,1:T(8,128)} %copy-done), kind=kLoop, calls=%fused_computation.35 | loop fusion | flops 262144 | bytes 3145728 | tf_op jit(solution)/shard_map/scatter-add | solution.py:145
  80.8 1.4 %fusion.17 = f32[384,1024]{0,1:T(8,128)S(1)} fusion(f32[384,1024]{0,1:T(8,128)S(1)} %fusion.18, f32[256,1024]{0,1:T(8,128)} %collective-permute-done.4), kind=kLoop, calls=%fused_computation.33 | loop fusion | flops 262144 | bytes 3145728 | tf_op jit(solution)/shard_map/scatter-add | solution.py:146
  82.5 0.2 select_bitcast_fusion
  82.7 1.5 %collective-permute-start.5 = (bf16[2,384,512]{1,2,0:T(8,128)(2,1)S(1)}, bf16[2,384,512]{1,2,0:T(8,128)(2,1)S(1)}, u32[]{:S(2)}, u32[]{:S(2)}) collective-permute-start(bf16[2,384,512]{1,2,0:T(8,128)(2,1)S(1)} %get-tuple-element.42), channel_id=1, source_target_pairs={{0,16},{16,0},{1,17},{17,1},{2,18},{18,2},{3,19},{19,3},{4,20},{20... | collective-permute-start | bytes 2359304 | tf_op jit(solution)/shard_map/ppermute | solution.py:22
  84.2 18.2 %collective-permute-done.5 = bf16[2,384,512]{1,2,0:T(8,128)(2,1)S(1)} collective-permute-done((bf16[2,384,512]{1,2,0:T(8,128)(2,1)S(1)}, bf16[2,384,512]{1,2,0:T(8,128)(2,1)S(1)}, u32[]{:S(2)}, u32[]{:S(2)}) %collective-permute-start.5) | collective-permute-done | bytes 786464 | tf_op jit(solution)/shard_map/ppermute | solution.py:22
  102.3 0.4 maximum_select_fusion
  102.8 1.6 %copy.28 = bf16[1,2,384,1024]{3,2,1,0:T(8,128)(2,1)} copy(bf16[1,2,384,1024]{2,3,1,0:T(8,128)(2,1)S(1)} %maximum_select_fusion) | data formatting | bytes 3145728 | tf_op jit(solution)/shard_map/jit(_where)/select_n | solution.py:154
  (52 shorter events, 2.0 us)
Async XLA Ops:
  0.0 2.5 %copy-start.16 = (s32[12]{0:T(128)S(1)}, s32[12]{0:T(128)}, u32[]{:S(2)}) copy-start(s32[12]{0:T(128)} %param.7) | copy-start | bytes 148
  1.9 19.3 %collective-permute-start = (bf16[2,384,512]{1,2,0:T(8,128)(2,1)S(1)}, bf16[2,384,512]{1,2,0:T(8,128)(2,1)S(1)}, u32[]{:S(2)}, u32[]{:S(2)}) collective-permute-start(bf16[2,384,512]{1,2,0:T(8,128)(2,1)S(1)} %bitcast.90), channel_id=1, source_target_pairs={{0,16},{16,0},{1,17},{17,1},{2,18},{18,2},{3,19},{19,3},{4,20},{20... | collective-permute-start | bytes 2359304 | tf_op jit(solution)/shard_map/ppermute | solution.py:22
  22.5 8.9 %collective-permute-start.2 = (bf16[256,1024]{0,1:T(8,128)(2,1)}, bf16[256,1024]{0,1:T(8,128)(2,1)S(1)}, u32[]{:S(2)}, u32[]{:S(2)}) collective-permute-start(bf16[256,1024]{0,1:T(8,128)(2,1)} %get-tuple-element.58), channel_id=1, source_target_pairs={{2,0},{4,2},{6,4},{8,6},{10,8},{12,10},{14,12},{3,1},{5,3},{7,5},{... | collective-permute-start | bytes 1572872 | tf_op jit(solution)/shard_map/ppermute | solution.py:18
  24.4 10.8 %collective-permute-start.1 = (bf16[256,1024]{0,1:T(8,128)(2,1)}, bf16[256,1024]{0,1:T(8,128)(2,1)}, u32[]{:S(2)}, u32[]{:S(2)}) collective-permute-start(bf16[256,1024]{0,1:T(8,128)(2,1)} %get-tuple-element.57), channel_id=1, source_target_pairs={{0,2},{2,4},{4,6},{6,8},{8,10},{10,12},{12,14},{1,3},{3,5},{5,7},{... | collective-permute-start | bytes 1572872 | tf_op jit(solution)/shard_map/ppermute | solution.py:18
  30.1 6.8 %copy-start.4 = (bf16[3,128,8,64]{1,0,3,2:T(4,128)(2,1)}, bf16[3,128,8,64]{1,0,3,2:T(4,128)(2,1)S(1)}, u32[]{:S(2)}) copy-start(bf16[3,128,8,64]{1,0,3,2:T(4,128)(2,1)S(1)} %reshape_squeeze.3) | copy-start | bytes 1179652
  36.7 1.0 copy-start.7
  36.8 1.0 copy-start.8
  36.8 1.0 copy-start.9
  36.9 4.8 %copy-start.10 = (bf16[384,512]{0,1:T(8,128)(2,1)}, bf16[384,512]{0,1:T(8,128)(2,1)S(1)}, u32[]{:S(2)}) copy-start(bf16[384,512]{0,1:T(8,128)(2,1)S(1)} %get-tuple-element.47) | copy-start | bytes 1179652
  36.9 4.8 %copy-start.12 = (bf16[384,512]{0,1:T(8,128)(2,1)}, bf16[384,512]{0,1:T(8,128)(2,1)S(1)}, u32[]{:S(2)}) copy-start(bf16[384,512]{0,1:T(8,128)(2,1)S(1)} %get-tuple-element.48) | copy-start | bytes 1179652
  36.9 4.8 %copy-start.14 = (bf16[384,512]{0,1:T(8,128)(2,1)}, bf16[384,512]{0,1:T(8,128)(2,1)S(1)}, u32[]{:S(2)}) copy-start(bf16[384,512]{0,1:T(8,128)(2,1)S(1)} %get-tuple-element.49) | copy-start | bytes 1179652
  39.5 2.1 %copy-start.1 = (f32[3,8,128,384]{3,2,1,0:T(8,128)}, f32[3,8,128,384]{3,2,1,0:T(8,128)S(1)}, u32[]{:S(2)}) copy-start(f32[3,8,128,384]{3,2,1,0:T(8,128)S(1)} %get-tuple-element.68) | copy-start | bytes 14155780
  54.1 2.3 %copy-start.2 = (f32[3,8,128,384]{3,2,1,0:T(8,128)S(1)}, f32[3,8,128,384]{3,2,1,0:T(8,128)}, u32[]{:S(2)}) copy-start(f32[3,8,128,384]{3,2,1,0:T(8,128)} %copy-done.1) | copy-start | bytes 14155780
  54.1 2.4 %copy-start.11 = (bf16[384,512]{0,1:T(8,128)(2,1)S(1)}, bf16[384,512]{0,1:T(8,128)(2,1)}, u32[]{:S(2)}) copy-start(bf16[384,512]{0,1:T(8,128)(2,1)} %copy-done.10) | copy-start | bytes 1179652
  54.2 2.5 %copy-start.13 = (bf16[384,512]{0,1:T(8,128)(2,1)S(1)}, bf16[384,512]{0,1:T(8,128)(2,1)}, u32[]{:S(2)}) copy-start(bf16[384,512]{0,1:T(8,128)(2,1)} %copy-done.12) | copy-start | bytes 1179652
  54.2 2.6 %copy-start.15 = (bf16[384,512]{0,1:T(8,128)(2,1)S(1)}, bf16[384,512]{0,1:T(8,128)(2,1)}, u32[]{:S(2)}) copy-start(bf16[384,512]{0,1:T(8,128)(2,1)} %copy-done.14) | copy-start | bytes 1179652
  56.8 1.9 %copy-start.5 = (bf16[3,128,8,64]{1,0,3,2:T(4,128)(2,1)S(1)}, bf16[3,128,8,64]{1,0,3,2:T(4,128)(2,1)}, u32[]{:S(2)}) copy-start(bf16[3,128,8,64]{1,0,3,2:T(4,128)(2,1)} %copy-done.4) | copy-start | bytes 1179652
  58.7 1.4 %copy-start.3 = (bf16[3,8,128,384]{3,2,1,0:T(8,128)(2,1)}, bf16[3,8,128,384]{3,2,1,0:T(8,128)(2,1)S(1)}, u32[]{:S(2)}) copy-start(bf16[3,8,128,384]{3,2,1,0:T(8,128)(2,1)S(1)} %multiply_convert_fusion) | copy-start | bytes 7077892
  61.1 7.9 %copy-start = (f32[896,1024]{0,1:T(8,128)}, f32[896,1024]{0,1:T(8,128)S(1)}, u32[]{:S(2)}) copy-start(f32[896,1024]{0,1:T(8,128)S(1)} %fusion.15) | copy-start | bytes 11010052
  61.1 7.3 %copy-start.6 = (f32[3,128,8,64]{1,3,2,0:T(8,128)S(1)}, f32[3,128,8,64]{1,3,2,0:T(8,128)}, u32[]{:S(2)}) copy-start(f32[3,128,8,64]{1,3,2,0:T(8,128)} %get-tuple-element.69) | copy-start | bytes 2359300
  62.7 16.4 %collective-permute-start.3 = (f32[256,1024]{0,1:T(8,128)}, f32[256,1024]{0,1:T(8,128)}, u32[]{:S(2)}, u32[]{:S(2)}) collective-permute-start(f32[256,1024]{0,1:T(8,128)} %get-tuple-element.38), channel_id=1, source_target_pairs={{0,2},{2,4},{4,6},{6,8},{8,10},{10,12},{12,14},{1,3},{3,5},{5,7},{... | collective-permute-start | bytes 3145736 | tf_op jit(solution)/shard_map/ppermute | solution.py:18
  64.6 16.3 %collective-permute-start.4 = (f32[256,1024]{0,1:T(8,128)}, f32[256,1024]{0,1:T(8,128)}, u32[]{:S(2)}, u32[]{:S(2)}) collective-permute-start(f32[256,1024]{0,1:T(8,128)} %get-tuple-element.37), channel_id=1, source_target_pairs={{2,0},{4,2},{6,4},{8,6},{10,8},{12,10},{14,12},{3,1},{5,3},{7,5},{... | collective-permute-start | bytes 3145736 | tf_op jit(solution)/shard_map/ppermute | solution.py:18
  82.7 19.6 %collective-permute-start.5 = (bf16[2,384,512]{1,2,0:T(8,128)(2,1)S(1)}, bf16[2,384,512]{1,2,0:T(8,128)(2,1)S(1)}, u32[]{:S(2)}, u32[]{:S(2)}) collective-permute-start(bf16[2,384,512]{1,2,0:T(8,128)(2,1)S(1)} %get-tuple-element.42), channel_id=1, source_target_pairs={{0,16},{16,0},{1,17},{17,1},{2,18},{18,2},{3,19},{19,3},{4,20},{20... | collective-permute-start | bytes 2359304 | tf_op jit(solution)/shard_map/ppermute | solution.py:22
where the time goes:
time: 107 us; the launch traced here: 104 us
  waiting for transfers between devices  46.4 us (43%)
  local copies, waits for them, and re-layouts  13.7 us (13%)
  starting transfers between devices  12.1 us (11%)
  other arithmetic  11.6 us (11%)
  matrix products  9.11 us (9%)
  blocking collectives  8.95 us (8%)
  between operations  2.46 us (2%)
    ppermute x2, waiting for transfers between devices, sec_swap(): return lax.ppermute(value, 'sec', [(0, 1), (1, 0)])  35.6 us
    ppermute x4, waiting for transfers between devices, seq_shift(): lax.ppermute(value, 'seq', [(source, source + steps) for source in range(...  10.8 us
    ppermute x4, starting transfers between devices, seq_shift(): lax.ppermute(value, 'seq', [(source, source + steps) for source in range(...  10 us
    psum x1, blocking collectives, row_total(): return lax.psum(sums_pair, ('sec', 'mp'))  8.95 us
    unnamed x36, local copies, waits for them, and re-layouts  4.54 us
    dot_general x1, matrix products, attention_grads(): jnp.einsum('jhqk,jkhd->jqhd', dscores, keys_w, preferred_element_type=jnp...  3.2 us
  transfers between devices with their start and end apart: 6, of which 6 were waited for; matrix products, arithmetic and copies ran while one was open for 9% of the time, Pallas kernels for 0%

commit v1 on v0

--- a/solution.py
+++ b/solution.py
@@ -39,7 +39,7 @@
     return starts - (first_unit - halo_units), allowed
 
 
-def attention_grads(queries, cotangent, near_keys, near_values, rel_starts, allowed, total_fn, total_cols):
+def chunk_forward(queries, cotangent, near_keys, near_values, rel_starts, allowed):
     rows, head_cols = queries.shape
     heads = head_cols // DH
     unit_count = rows // UNIT
@@ -56,7 +56,6 @@
     values_w = windows(near_values)
     q4 = queries.reshape(unit_count, UNIT, heads, DH)
     cot_float = cotangent.astype(jnp.float32)
-
     mask = jnp.repeat(allowed, UNIT, axis=1)[:, None, None, :]
     scores = (
         jnp.einsum("jqhd,jkhd->jhqk", q4, keys_w, preferred_element_type=jnp.float32) * score_scale
@@ -68,16 +67,20 @@
     rounded = weights.astype(jnp.bfloat16)
     attended4 = jnp.einsum("jhqk,jkhd->jqhd", rounded, values_w, preferred_element_type=jnp.float32)
     attended = attended4.reshape(rows, head_cols)
+    sums = jnp.stack([jnp.sum(attended * attended, axis=1), jnp.sum(cot_float * attended, axis=1)])
+    return (q4, keys_w, values_w, cot_float, weights, rounded, attended4, attended), sums
 
-    squares, crosses = total_fn(
-        (jnp.sum(attended * attended, axis=1), jnp.sum(cot_float * attended, axis=1))
-    )
-    spread = jnp.sqrt(squares / total_cols + epsilon)
+
+def chunk_backward(saved, spread, shared, rel_starts, near_rows):
+    q4, keys_w, values_w, cot_float, weights, rounded, attended4, attended = saved
+    unit_count, _, heads, _ = q4.shape
+    rows = unit_count * UNIT
+    head_cols = heads * DH
+    window = MAX_DOC_UNITS * UNIT
+    score_scale = DH ** (-0.5)
     normed = attended / spread[:, None]
-    shared = crosses / total_cols / spread
     upstream = ((cot_float - normed * shared[:, None]) / spread[:, None]).astype(jnp.bfloat16)
     up4 = upstream.reshape(unit_count, UNIT, heads, DH)
-
     delta = jnp.sum(up4.astype(jnp.float32) * attended4, axis=3)
     delta = jnp.transpose(delta, (0, 2, 1))[..., None]
     dprobs = jnp.einsum("jqhd,jkhd->jhqk", up4, values_w, preferred_element_type=jnp.float32)
@@ -89,7 +92,6 @@
         [grad_kw.reshape(unit_count, window, head_cols), grad_vw.reshape(unit_count, window, head_cols)],
         axis=2,
     )
-    near_rows = near_keys.shape[0]
     total = jnp.zeros((near_rows, 2 * head_cols), jnp.float32)
     for j in range(unit_count):
         start = rel_starts[j] * UNIT
@@ -110,47 +112,69 @@
     halo_units = MAX_DOC_UNITS - 1
     halo = halo_units * UNIT
     total_cols = cols * lax.axis_size("mp")
+    chunks = 2 if (half // DH) % 2 == 0 else 1
+    width = half // chunks
 
     keep_offset = section * half
     send_offset = (1 - section) * half
-    sent = lax.dynamic_slice_in_dim(local_heads, send_offset, half, 2)
-    kept = lax.dynamic_slice_in_dim(local_heads, keep_offset, half, 2)
-    arrived = sec_swap(sent)
-    key_value = jnp.where(is_first, kept, arrived)
-    query_cot = jnp.where(is_first, arrived, kept)
-
-    joined = jnp.concatenate([key_value[0], key_value[1]], axis=1)
-    low = seq_shift(joined[rows - halo :], 1)
-    high = seq_shift(joined[:halo], -1)
-    near = jnp.concatenate([low, joined, high], axis=0)
-
     rel_starts, allowed = window_plan(doc_units, seq_place, unit_count, halo_units)
 
-    def row_total(sums_pair):
-        return lax.psum(sums_pair, ("sec", "mp"))
+    saved, partial = [], []
+    for c in range(chunks):
+        sent = lax.dynamic_slice_in_dim(local_heads, send_offset + c * width, width, 2)
+        kept = lax.dynamic_slice_in_dim(local_heads, keep_offset + c * width, width, 2)
+        arrived = sec_swap(sent)
+        if partial:
+            arrived, partial[-1] = lax.optimization_barrier((arrived, partial[-1]))
+        key_value = jnp.where(is_first, kept, arrived)
+        query_cot = jnp.where(is_first, arrived, kept)
+        joined = jnp.concatenate([key_value[0], key_value[1]], axis=1)
+        low = seq_shift(joined[rows - halo :], 1)
+        high = seq_shift(joined[:halo], -1)
+        near = jnp.concatenate([low, joined, high], axis=0)
+        state, sums = chunk_forward(
+            query_cot[0], query_cot[1], near[:, :width], near[:, width:], rel_starts, allowed
+        )
+        saved.append(state)
+        partial.append(sums)
+    sums = partial[0]
+    for more in partial[1:]:
+        sums = sums + more
+    sums = sums + sec_swap(sums)
+    sums = sums + lax.ppermute(sums, "mp", [(0, 1), (1, 0)])
+    squares, crosses = sums[0], sums[1]
+    spread = jnp.sqrt(squares / total_cols + epsilon)
+    shared = crosses / total_cols / spread
 
-    grad_q, normed, total = attention_grads(
-        query_cot[0],
-        query_cot[1],
-        near[:, :half],
-        near[:, half:],
-        rel_starts,
-        allowed,
-        row_total,
-        total_cols,
-    )
-    from_left = seq_shift(total[near.shape[0] - halo :], 1)
-    from_right = seq_shift(total[:halo], -1)
-    own = total[halo : halo + rows]
-    own = own.at[:halo].add(from_left)
-    own = own.at[rows - halo :].add(from_right)
-    grad_k = own[:, :half].astype(jnp.bfloat16)
-    grad_v = own[:, half:].astype(jnp.bfloat16)
-
-    kv_pair = jnp.stack([grad_k, grad_v])
-    qn_pair = jnp.stack([grad_q.astype(jnp.bfloat16), normed.astype(jnp.bfloat16)])
-    keep_pair = jnp.where(is_first, kv_pair, qn_pair)
-    back = sec_swap(jnp.where(is_first, qn_pair, kv_pair))
+    near_rows = rows + 2 * halo
+    keep_parts, back_parts = [], []
+    pending = None
+    previous_total = None
+    for c in range(chunks + 1):
+        if c < chunks:
+            state = saved[c]
+            if previous_total is not None:
+                state, previous_total = lax.optimization_barrier((state, previous_total))
+                pending = (previous_total,) + pending[1:]
+            grad_q, normed, total = chunk_backward(state, spread, shared, rel_starts, near_rows)
+            from_left = seq_shift(total[near_rows - halo :], 1)
+            from_right = seq_shift(total[:halo], -1)
+        if pending is not None:
+            p_total, p_left, p_right, p_grad_q, p_normed = pending
+            if c < chunks:
+                p_left, p_right, total = lax.optimization_barrier((p_left, p_right, total))
+            own = p_total[halo : halo + rows]
+            own = own.at[:halo].add(p_left)
+            own = own.at[rows - halo :].add(p_right)
+            kv_pair = jnp.stack([own[:, :width], own[:, width:]]).astype(jnp.bfloat16)
+            qn_pair = jnp.stack([p_grad_q.astype(jnp.bfloat16), p_normed.astype(jnp.bfloat16)])
+            keep_parts.append(jnp.where(is_first, kv_pair, qn_pair))
+            back_parts.append(sec_swap(jnp.where(is_first, qn_pair, kv_pair)))
+        if c < chunks:
+            pending = (total, from_left, from_right, grad_q, normed)
+            previous_total = total
+    keep_pair = jnp.concatenate(keep_parts, axis=2)
+    back = jnp.concatenate(back_parts, axis=2)
     result = jnp.where(
         is_first,
         jnp.concatenate([keep_pair, back], axis=2),

time: 107 us -> 119 us (1.11)
  waiting for transfers between devices: 46.4 us -> 26.5 us
  starting transfers between devices: 12.1 us -> 29.2 us
  other arithmetic: 11.6 us -> 23.9 us
  local copies, waits for them, and re-layouts: 13.7 us -> 23.8 us
  blocking collectives: 8.95 us -> 0 us
  matrix products: 9.11 us -> 11.3 us
    ppermute x4 -> x8, starting transfers between devices: 10 us -> 22.8 us  [seq_shift(): lax.ppermute(value, 'seq', [(source, source + steps) for source in range(...]
    ppermute x2 -> x5, waiting for transfers between devices: 35.6 us -> 24.7 us  [sec_swap(): return lax.ppermute(value, 'sec', [(0, 1), (1, 0)])]
    ppermute x4 -> x8, waiting for transfers between devices: 10.8 us -> 0.94 us  [seq_shift(): lax.ppermute(value, 'seq', [(source, source + steps) for source in range(...]
    psum x1 -> x0, blocking collectives: 8.95 us -> none  [row_total(): return lax.psum(sums_pair, ('sec', 'mp'))]
    convert_element_type x3 -> x6, other arithmetic: 0.77 us -> 7.23 us  [the longest x2 5.46 us: chunk_forward(): rounded = weights.astype(jnp.bfloat16)]
    sub x0 -> x2, matrix products: none -> 4.79 us  [chunk_forward(): expven = jnp.exp(scores - row_max)]
    convert_element_type x3 -> x6, local copies, waits for them, and re-layouts: 1 us -> 4.85 us  [the longest x4 3.74 us: per_device(): p_grad_q.astype(jnp.bfloat16)]
    scatter-add x2 -> x4, other arithmetic: 3.12 us -> 6.46 us  [the longest x2 3.3 us: per_device(): own = own.at[rows - halo:].add(p_right)]
  transfers between devices with their start and end apart: 6 -> 14, of which waited for: 6 -> 7; matrix products, arithmetic and copies ran while one was open for 9% -> 29% of each run, Pallas kernels for 0% -> 0%
where the time goes in v1:
time: 119 us; the launch traced here: 118 us
  starting transfers between devices  29.2 us (25%)
  waiting for transfers between devices  26.5 us (22%)
  other arithmetic  23.9 us (20%)
  local copies, waits for them, and re-layouts  23.8 us (20%)
  matrix products  11.3 us (9%)
  between operations  2.79 us (2%)
    ppermute x5, waiting for transfers between devices, sec_swap(): return lax.ppermute(value, 'sec', [(0, 1), (1, 0)])  24.7 us
    ppermute x8, starting transfers between devices, seq_shift(): lax.ppermute(value, 'seq', [(source, source + steps) for source in range(...  22.8 us
    convert_element_type x2, other arithmetic, chunk_forward(): rounded = weights.astype(jnp.bfloat16)  5.46 us
    unnamed x87, local copies, waits for them, and re-layouts  5.02 us
    ppermute x5, starting transfers between devices, sec_swap(): return lax.ppermute(value, 'sec', [(0, 1), (1, 0)])  4.84 us
    sub x2, matrix products, chunk_forward(): expven = jnp.exp(scores - row_max)  4.79 us
    convert_element_type x4, local copies, waits for them, and re-layouts, per_device(): p_grad_q.astype(jnp.bfloat16)  3.74 us
    scatter-add x2, other arithmetic, per_device(): own = own.at[rows - halo:].add(p_right)  3.3 us
  transfers between devices with their start and end apart: 14, of which 7 were waited for; matrix products, arithmetic and copies ran while one was open for 29% of the time, Pallas kernels for 0%

profile of v1, /device:TPU:18, one launch (start us, length us, event | category | flops | bytes accessed | tf_op | source)
XLA Modules:
  0.0 117.6 jit_solution(2211200785746610713)
XLA Ops:
  0.0 1.5 %constant_dynamic-slice_fusion.6 = (bf16[1,2,384,256]{3,2,1,0:T(8,128)(2,1)S(1)}, bf16[1,2,384,256]{3,2,1,0:T(8,128)(2,1)S(1)}, bf16[1,2,384,256]{3,2,1,0:T(8,128)(2,1)S(1)}, bf16[1,2,384,256]{3,2,1,0:T(8,128)(2,1)S(1)}) fusion(bf16[1,2,384,1024]{3,2,1,0:T(8,128)(2,1)} %param.10, s32[]{:T(128)S(6)} %select_n.147, s32[]{:T(128)S(6)} %select_n.136, ...), kind=kLoop, calls=%fused_computation.133 | loop fusion | bytes 3145744 | tf_op jit(solution)/shard_map/dynamic_slice | solution.py:125
  2.3 0.9 copy.38
  3.2 1.5 %collective-permute-start = (bf16[2,384,256]{1,2,0:T(8,128)(2,1)}, bf16[2,384,256]{1,2,0:T(8,128)(2,1)}, u32[]{:S(2)}, u32[]{:S(2)}) collective-permute-start(bf16[2,384,256]{1,2,0:T(8,128)(2,1)} %bitcast), channel_id=1, source_target_pairs={{0,16},{16,0},{1,17},{17,1},{2,18},{18,2},{3,19},{19,3},{4,20},{20... | collective-permute-start | bytes 1179656 | tf_op jit(solution)/shard_map/ppermute | solution.py:22
  5.9 7.9 %collective-permute-done.1 = bf16[2,384,256]{1,2,0:T(8,128)(2,1)S(1)} collective-permute-done((bf16[2,384,256]{1,2,0:T(8,128)(2,1)S(1)}, bf16[2,384,256]{1,2,0:T(8,128)(2,1)S(1)}, u32[]{:S(2)}, u32[]{:S(2)}) %collective-permute-start.1) | collective-permute-done | bytes 393248 | tf_op jit(solution)/shard_map/ppermute | solution.py:22
  14.7 1.9 %collective-permute-start.2 = (bf16[256,512]{0,1:T(8,128)(2,1)}, bf16[256,512]{0,1:T(8,128)(2,1)S(1)}, u32[]{:S(2)}, u32[]{:S(2)}) collective-permute-start(bf16[256,512]{0,1:T(8,128)(2,1)} %get-tuple-element.140), channel_id=1, source_target_pairs={{0,2},{2,4},{4,6},{6,8},{8,10},{10,12},{12,14},{1,3},{3,5},{5,7},{... | collective-permute-start | bytes 786440 | tf_op jit(solution)/shard_map/ppermute | solution.py:18
  16.6 3.6 %collective-permute-start.3 = (bf16[256,512]{0,1:T(8,128)(2,1)S(1)}, bf16[256,512]{0,1:T(8,128)(2,1)}, u32[]{:S(2)}, u32[]{:S(2)}) collective-permute-start(bf16[256,512]{0,1:T(8,128)(2,1)S(1)} %get-tuple-element.141), channel_id=1, source_target_pairs={{2,0},{4,2},{6,4},{8,6},{10,8},{12,10},{14,12},{3,1},{5,3},{7,5},{... | collective-permute-start | bytes 786440 | tf_op jit(solution)/shard_map/ppermute | solution.py:18
  24.1 1.0 pad_maximum_fusion
  25.3 2.4 %fusion.81 = (f32[3,4,128]{2,1,0:T(4,128)S(1)}, f32[3,4,128,384]{3,2,1,0:T(8,128)}) fusion(pred[3,384]{1,0:T(4,128)(4,1)S(1)} %bitcast.222, bf16[1,384,4,64]{1,3,2,0:T(8,128)(2,1)S(1)} %bitcast.198, bf16[1,384,4,64]{1,3,2,0:T(8,128)(2,1)S(1)} %bitcast.200, bf16[1,384,4,64]{1,3,2,0:T(8,128)(2,1)S(1)} %bitcast.196, ...), kind=kOutput, calls=%fused_computation.181 | convolution fusion | flops 78446976 | bytes 3153024 | tf_op jit(solution)/shard_map/sub | solution.py:65
  27.7 1.9 %fusion.12 = bf16[3,4,128,384]{3,2,1,0:T(8,128)(2,1)S(1)} fusion(f32[3,4,128,384]{3,2,1,0:T(8,128)} %get-tuple-element.148, f32[3,4,128]{2,1,0:T(4,128)S(1)} %get-tuple-element.147), kind=kLoop, calls=%fused_computation.33 | loop fusion | flops 1179648 | bytes 3545088 | tf_op jit(solution)/shard_map/convert_element_type | solution.py:67
  30.5 1.1 bitcast_select_fusion
  31.7 0.9 fusion.36
  32.5 3.9 %collective-permute-start.4 = (bf16[256,512]{0,1:T(8,128)(2,1)}, bf16[256,512]{0,1:T(8,128)(2,1)}, u32[]{:S(2)}, u32[]{:S(2)}) collective-permute-start(bf16[256,512]{0,1:T(8,128)(2,1)} %get-tuple-element.134), channel_id=1, source_target_pairs={{0,2},{2,4},{4,6},{6,8},{8,10},{10,12},{12,14},{1,3},{3,5},{5,7},{... | collective-permute-start | bytes 786440 | tf_op jit(solution)/shard_map/ppermute | solution.py:18
  36.4 2.0 %collective-permute-start.5 = (bf16[256,512]{0,1:T(8,128)(2,1)}, bf16[256,512]{0,1:T(8,128)(2,1)}, u32[]{:S(2)}, u32[]{:S(2)}) collective-permute-start(bf16[256,512]{0,1:T(8,128)(2,1)} %get-tuple-element.135), channel_id=1, source_target_pairs={{2,0},{4,2},{6,4},{8,6},{10,8},{12,10},{14,12},{3,1},{5,3},{7,5},{... | collective-permute-start | bytes 786440 | tf_op jit(solution)/shard_map/ppermute | solution.py:18
  38.4 0.9 slice_convert_fusion
  39.3 1.0 reshape_squeeze.7
  40.3 0.9 reshape.575
  41.5 1.0 reshape.572
  42.6 1.1 pad_maximum_fusion.1
  43.9 1.0 constant_dynamic-slice_fusion.2
  44.8 2.4 %fusion.84 = (f32[3,4,128]{2,1,0:T(4,128)S(1)}, f32[3,4,128,384]{3,2,1,0:T(8,128)}) fusion(pred[3,384]{1,0:T(4,128)(4,1)S(1)} %bitcast.223, bf16[3,128,4,64]{1,0,3,2:T(4,128)(2,1)S(1)} %reshape_squeeze.7, bf16[1,384,4,64]{1,3,2,0:T(8,128)(2,1)S(1)} %bitcast.183, bf16[1,384,4,64]{1,3,2,0:T(8,128)(2,1)S(1)} %bitcast.185, ...), kind=kOutput, calls=%fused_computation.182 | convolution fusion | flops 78446976 | bytes 3153024 | tf_op jit(solution)/shard_map/sub | solution.py:65
  47.3 3.5 %fusion.75 = (bf16[3,4,128,384]{3,2,1,0:T(8,128)(2,1)S(1)}, f32[3,4,128,384]{3,2,1,0:T(8,128)}) fusion(f32[3,4,128,384]{3,2,1,0:T(8,128)} %get-tuple-element.151, f32[3,4,128]{2,1,0:T(4,128)S(1)} %get-tuple-element.150), kind=kLoop, calls=%fused_computation.175 | loop fusion | flops 1179648 | bytes 5904384 | tf_op jit(solution)/shard_map/convert_element_type | solution.py:67
  52.2 0.9 pad_maximum_fusion.7
  53.1 2.2 %collective-permute-done.6 = f32[2,384]{1,0:T(2,128)S(1)} collective-permute-done((f32[2,384]{1,0:T(2,128)S(1)}, f32[2,384]{1,0:T(2,128)S(1)}, u32[]{:S(2)}, u32[]{:S(2)}) %collective-permute-start.6) | collective-permute-done | bytes 3104 | tf_op jit(solution)/shard_map/ppermute | solution.py:22
  55.3 1.6 %collective-permute-start.7 = (f32[2,384]{1,0:T(2,128)S(1)}, f32[2,384]{1,0:T(2,128)S(1)}, u32[]{:S(2)}, u32[]{:S(2)}) collective-permute-start(f32[2,384]{1,0:T(2,128)S(1)} %fusion.100), channel_id=1, source_target_pairs={{0,1},{1,0},{2,3},{3,2},{4,5},{5,4},{6,7},{7,6},{8,9},{9,8},{10,11... | collective-permute-start | bytes 9224 | tf_op jit(solution)/shard_map/ppermute | solution.py:144
  56.9 0.9 pad_maximum_fusion.6
  59.5 1.1 copy-done.3
  60.7 0.9 multiply_convert_fusion.1
  62.9 1.2 %copy-done = f32[896,512]{0,1:T(8,128)} copy-done((f32[896,512]{0,1:T(8,128)}, f32[896,512]{0,1:T(8,128)S(1)}, u32[]{:S(2)}) %copy-start) | copy-done | bytes 1835032
  64.2 1.1 fusion.77
  69.7 2.2 %collective-permute-start.8 = (f32[256,512]{0,1:T(8,128)}, f32[256,512]{0,1:T(8,128)}, u32[]{:S(2)}, u32[]{:S(2)}) collective-permute-start(f32[256,512]{0,1:T(8,128)} %get-tuple-element.96), channel_id=1, source_target_pairs={{0,2},{2,4},{4,6},{6,8},{8,10},{10,12},{12,14},{1,3},{3,5},{5,7},{... | collective-permute-start | bytes 1572872 | tf_op jit(solution)/shard_map/ppermute | solution.py:18
  72.0 3.6 %collective-permute-start.9 = (f32[256,512]{0,1:T(8,128)}, f32[256,512]{0,1:T(8,128)}, u32[]{:S(2)}, u32[]{:S(2)}) collective-permute-start(f32[256,512]{0,1:T(8,128)} %get-tuple-element.95), channel_id=1, source_target_pairs={{2,0},{4,2},{6,4},{8,6},{10,8},{12,10},{14,12},{3,1},{5,3},{7,5},{... | collective-permute-start | bytes 1572872 | tf_op jit(solution)/shard_map/ppermute | solution.py:18
  75.6 1.1 fusion.76
  77.3 2.1 %slice.232 = f32[384,512]{0,1:T(8,128)} slice(f32[896,512]{0,1:T(8,128)} %copy-done), slice={[256:640], [0:512]} | slice | bytes 1572864 | tf_op jit(solution)/shard_map/slice | solution.py:166
  79.4 0.9 copy.53
  80.3 1.8 %convert_element_type.134 = bf16[1,384,256]{1,2,0:T(8,128)(2,1)} reshape(bf16[3,128,4,64]{1,0,3,2:T(4,128)(2,1)} %copy.53) | data formatting | bytes 393216 | tf_op jit(solution)/shard_map/convert_element_type | solution.py:170
  82.1 1.9 %collective-permute-start.10 = (f32[256,512]{0,1:T(8,128)}, f32[256,512]{0,1:T(8,128)}, u32[]{:S(2)}, u32[]{:S(2)}) collective-permute-start(f32[256,512]{0,1:T(8,128)} %get-tuple-element.94), channel_id=1, source_target_pairs={{0,2},{2,4},{4,6},{6,8},{8,10},{10,12},{12,14},{1,3},{3,5},{5,7},{... | collective-permute-start | bytes 1572872 | tf_op jit(solution)/shard_map/ppermute | solution.py:18
  84.0 3.6 %collective-permute-start.11 = (f32[256,512]{0,1:T(8,128)}, f32[256,512]{0,1:T(8,128)}, u32[]{:S(2)}, u32[]{:S(2)}) collective-permute-start(f32[256,512]{0,1:T(8,128)} %get-tuple-element.93), channel_id=1, source_target_pairs={{2,0},{4,2},{6,4},{8,6},{10,8},{12,10},{14,12},{3,1},{5,3},{7,5},{... | collective-permute-start | bytes 1572872 | tf_op jit(solution)/shard_map/ppermute | solution.py:18
  87.7 1.7 %fusion.11 = bf16[3,128,4,64]{1,3,2,0:T(8,128)(2,1)S(1)} fusion(bf16[3,384,4,64]{1,3,2,0:T(8,128)(2,1)} %pad_maximum_fusion.6, bf16[3,4,128,384]{3,2,1,0:T(8,128)(2,1)S(1)} %multiply_convert_fusion), kind=kOutput, calls=%fused_computation.32 | convolution fusion | flops 75595776 | bytes 1966080 | tf_op jit(solution)/shard_map/jhqk,jkhd->jqhd/dot_general | solution.py:88
  89.6 0.9 convert_element_type.138
  90.5 2.1 %add_dynamic-update-slice_fusion.1 = f32[384,512]{0,1:T(8,128)} fusion(f32[384,512]{0,1:T(8,128)} %slice.232, f32[256,512]{0,1:T(8,128)} %collective-permute-done.8, f32[896,512]{0,1:T(8,128)} %copy-done), kind=kLoop, calls=%fused_computation.67 | loop fusion | flops 131072 | bytes 1572864 | tf_op jit(solution)/shard_map/scatter-add | solution.py:167
  92.6 2.1 %fusion.34 = f32[384,512]{0,1:T(8,128)} fusion(f32[384,512]{0,1:T(8,128)} %add_dynamic-update-slice_fusion.1, f32[256,512]{0,1:T(8,128)} %collective-permute-done.9), kind=kLoop, calls=%fused_computation.65 | loop fusion | flops 131072 | bytes 1572864 | tf_op jit(solution)/shard_map/scatter-add | solution.py:168
  94.7 1.2 %convert.19 = bf16[384,512]{0,1:T(8,128)(2,1)S(1)} convert(f32[384,512]{0,1:T(8,128)} %fusion.34) | non-fusion elementwise | flops 196608 | bytes 1179648 | tf_op jit(solution)/shard_map/convert.14
  96.7 1.1 add_dynamic-update-slice_fusion
  97.8 1.2 %fusion.33 = f32[384,512]{0,1:T(8,128)S(1)} fusion(f32[384,512]{0,1:T(8,128)S(1)} %add_dynamic-update-slice_fusion, f32[256,512]{0,1:T(8,128)} %collective-permute-done.11), kind=kLoop, calls=%fused_computation.63 | loop fusion | flops 131072 | bytes 1572864 | tf_op jit(solution)/shard_map/scatter-add | solution.py:168
  99.3 1.6 %collective-permute-start.13 = (bf16[2,384,256]{1,2,0:T(8,128)(2,1)S(1)}, bf16[2,384,256]{1,2,0:T(8,128)(2,1)S(1)}, u32[]{:S(2)}, u32[]{:S(2)}) collective-permute-start(bf16[2,384,256]{1,2,0:T(8,128)(2,1)S(1)} %get-tuple-element.108), channel_id=1, source_target_pairs={{0,16},{16,0},{1,17},{17,1},{2,18},{18,2},{3,19},{19,3},{4,20},{20... | collective-permute-start | bytes 1179656 | tf_op jit(solution)/shard_map/ppermute | solution.py:22
  100.8 7.2 %collective-permute-done.12 = bf16[2,384,256]{1,2,0:T(8,128)(2,1)S(1)} collective-permute-done((bf16[2,384,256]{1,2,0:T(8,128)(2,1)S(1)}, bf16[2,384,256]{1,2,0:T(8,128)(2,1)S(1)}, u32[]{:S(2)}, u32[]{:S(2)}) %collective-permute-start.12) | collective-permute-done | bytes 393248 | tf_op jit(solution)/shard_map/ppermute | solution.py:22
  108.1 7.5 %collective-permute-done.13 = bf16[2,384,256]{1,2,0:T(8,128)(2,1)S(1)} collective-permute-done((bf16[2,384,256]{1,2,0:T(8,128)(2,1)S(1)}, bf16[2,384,256]{1,2,0:T(8,128)(2,1)S(1)}, u32[]{:S(2)}, u32[]{:S(2)}) %collective-permute-start.13) | collective-permute-done | bytes 393248 | tf_op jit(solution)/shard_map/ppermute | solution.py:22
  116.0 1.6 %copy.56 = bf16[1,2,384,1024]{3,2,1,0:T(8,128)(2,1)} copy(bf16[1,2,384,1024]{2,3,1,0:T(8,128)(2,1)S(1)} %maximum_select_fusion) | data formatting | bytes 3145728 | tf_op jit(solution)/shard_map/jit(_where)/select_n | solution.py:178
  (159 shorter events, 17.3 us)
Async XLA Ops:
  1.5 3.5 %copy-start.39 = (s32[12]{0:T(128)S(1)}, s32[12]{0:T(128)}, u32[]{:S(2)}) copy-start(s32[12]{0:T(128)} %param.11) | copy-start | bytes 148
  1.7 12.1 %collective-permute-start.1 = (bf16[2,384,256]{1,2,0:T(8,128)(2,1)S(1)}, bf16[2,384,256]{1,2,0:T(8,128)(2,1)S(1)}, u32[]{:S(2)}, u32[]{:S(2)}) collective-permute-start(bf16[2,384,256]{1,2,0:T(8,128)(2,1)S(1)} %bitcast.193), channel_id=1, source_target_pairs={{0,16},{16,0},{1,17},{17,1},{2,18},{18,2},{3,19},{19,3},{4,20},{20... | collective-permute-start | bytes 1179656 | tf_op jit(solution)/shard_map/ppermute | solution.py:22
  3.2 27.3 %collective-permute-start = (bf16[2,384,256]{1,2,0:T(8,128)(2,1)}, bf16[2,384,256]{1,2,0:T(8,128)(2,1)}, u32[]{:S(2)}, u32[]{:S(2)}) collective-permute-start(bf16[2,384,256]{1,2,0:T(8,128)(2,1)} %bitcast), channel_id=1, source_target_pairs={{0,16},{16,0},{1,17},{17,1},{2,18},{18,2},{3,19},{19,3},{4,20},{20... | collective-permute-start | bytes 1179656 | tf_op jit(solution)/shard_map/ppermute | solution.py:22
  14.7 8.6 %collective-permute-start.2 = (bf16[256,512]{0,1:T(8,128)(2,1)}, bf16[256,512]{0,1:T(8,128)(2,1)S(1)}, u32[]{:S(2)}, u32[]{:S(2)}) collective-permute-start(bf16[256,512]{0,1:T(8,128)(2,1)} %get-tuple-element.140), channel_id=1, source_target_pairs={{0,2},{2,4},{4,6},{6,8},{8,10},{10,12},{12,14},{1,3},{3,5},{5,7},{... | collective-permute-start | bytes 786440 | tf_op jit(solution)/shard_map/ppermute | solution.py:18
  16.6 7.5 %collective-permute-start.3 = (bf16[256,512]{0,1:T(8,128)(2,1)S(1)}, bf16[256,512]{0,1:T(8,128)(2,1)}, u32[]{:S(2)}, u32[]{:S(2)}) collective-permute-start(bf16[256,512]{0,1:T(8,128)(2,1)S(1)} %get-tuple-element.141), channel_id=1, source_target_pairs={{2,0},{4,2},{6,4},{8,6},{10,8},{12,10},{14,12},{3,1},{5,3},{7,5},{... | collective-permute-start | bytes 786440 | tf_op jit(solution)/shard_map/ppermute | solution.py:18
  25.3 2.4 %copy-start.25 = (bf16[384,256]{0,1:T(8,128)(2,1)}, bf16[384,256]{0,1:T(8,128)(2,1)S(1)}, u32[]{:S(2)}) copy-start(bf16[384,256]{0,1:T(8,128)(2,1)S(1)} %get-tuple-element.122) | copy-start | bytes 589828
  25.3 2.4 %copy-start.27 = (bf16[384,256]{0,1:T(8,128)(2,1)}, bf16[384,256]{0,1:T(8,128)(2,1)S(1)}, u32[]{:S(2)}) copy-start(bf16[384,256]{0,1:T(8,128)(2,1)S(1)} %get-tuple-element.123) | copy-start | bytes 589828
  25.3 2.4 %copy-start.29 = (bf16[384,256]{0,1:T(8,128)(2,1)}, bf16[384,256]{0,1:T(8,128)(2,1)S(1)}, u32[]{:S(2)}) copy-start(bf16[384,256]{0,1:T(8,128)(2,1)S(1)} %get-tuple-element.124) | copy-start | bytes 589828
  27.7 2.0 %copy-start.37 = (f32[3,4,128]{2,1,0:T(4,128)}, f32[3,4,128]{2,1,0:T(4,128)S(1)}, u32[]{:S(2)}) copy-start(f32[3,4,128]{2,1,0:T(4,128)S(1)} %get-tuple-element.147) | copy-start | bytes 18436
  29.8 1.8 %copy-start.31 = (bf16[384,256]{0,1:T(8,128)(2,1)}, bf16[384,256]{0,1:T(8,128)(2,1)S(1)}, u32[]{:S(2)}) copy-start(bf16[384,256]{0,1:T(8,128)(2,1)S(1)} %get-tuple-element.119) | copy-start | bytes 589828
  29.8 1.8 %copy-start.33 = (bf16[384,256]{0,1:T(8,128)(2,1)}, bf16[384,256]{0,1:T(8,128)(2,1)S(1)}, u32[]{:S(2)}) copy-start(bf16[384,256]{0,1:T(8,128)(2,1)S(1)} %get-tuple-element.120) | copy-start | bytes 589828
  29.8 1.8 %copy-start.35 = (bf16[384,256]{0,1:T(8,128)(2,1)}, bf16[384,256]{0,1:T(8,128)(2,1)S(1)}, u32[]{:S(2)}) copy-start(bf16[384,256]{0,1:T(8,128)(2,1)S(1)} %get-tuple-element.121) | copy-start | bytes 589828
  32.5 10.0 %collective-permute-start.4 = (bf16[256,512]{0,1:T(8,128)(2,1)}, bf16[256,512]{0,1:T(8,128)(2,1)}, u32[]{:S(2)}, u32[]{:S(2)}) collective-permute-start(bf16[256,512]{0,1:T(8,128)(2,1)} %get-tuple-element.134), channel_id=1, source_target_pairs={{0,2},{2,4},{4,6},{6,8},{8,10},{10,12},{12,14},{1,3},{3,5},{5,7},{... | collective-permute-start | bytes 786440 | tf_op jit(solution)/shard_map/ppermute | solution.py:18
  36.4 6.2 %collective-permute-start.5 = (bf16[256,512]{0,1:T(8,128)(2,1)}, bf16[256,512]{0,1:T(8,128)(2,1)}, u32[]{:S(2)}, u32[]{:S(2)}) collective-permute-start(bf16[256,512]{0,1:T(8,128)(2,1)} %get-tuple-element.135), channel_id=1, source_target_pairs={{2,0},{4,2},{6,4},{8,6},{10,8},{12,10},{14,12},{3,1},{5,3},{7,5},{... | collective-permute-start | bytes 786440 | tf_op jit(solution)/shard_map/ppermute | solution.py:18
  40.3 4.5 %copy-start.10 = (bf16[3,128,4,64]{1,0,3,2:T(4,128)(2,1)}, bf16[3,128,4,64]{1,0,3,2:T(4,128)(2,1)S(1)}, u32[]{:S(2)}) copy-start(bf16[3,128,4,64]{1,0,3,2:T(4,128)(2,1)S(1)} %reshape_squeeze.7) | copy-start | bytes 589828
  43.8 3.4 %copy-start.12 = (bf16[384,256]{0,1:T(8,128)(2,1)}, bf16[384,256]{0,1:T(8,128)(2,1)S(1)}, u32[]{:S(2)}) copy-start(bf16[384,256]{0,1:T(8,128)(2,1)S(1)} %get-tuple-element.116) | copy-start | bytes 589828
  43.9 3.4 %copy-start.14 = (bf16[384,256]{0,1:T(8,128)(2,1)}, bf16[384,256]{0,1:T(8,128)(2,1)S(1)}, u32[]{:S(2)}) copy-start(bf16[384,256]{0,1:T(8,128)(2,1)S(1)} %get-tuple-element.117) | copy-start | bytes 589828
  43.9 3.4 %copy-start.16 = (bf16[384,256]{0,1:T(8,128)(2,1)}, bf16[384,256]{0,1:T(8,128)(2,1)S(1)}, u32[]{:S(2)}) copy-start(bf16[384,256]{0,1:T(8,128)(2,1)S(1)} %get-tuple-element.118) | copy-start | bytes 589828
  47.3 3.6 %copy-start.18 = (bf16[384,256]{0,1:T(8,128)(2,1)S(1)}, bf16[384,256]{0,1:T(8,128)(2,1)}, u32[]{:S(2)}) copy-start(bf16[384,256]{0,1:T(8,128)(2,1)} %get-tuple-element.113) | copy-start | bytes 589828
  47.3 3.6 %copy-start.19 = (bf16[384,256]{0,1:T(8,128)(2,1)S(1)}, bf16[384,256]{0,1:T(8,128)(2,1)}, u32[]{:S(2)}) copy-start(bf16[384,256]{0,1:T(8,128)(2,1)} %get-tuple-element.114) | copy-start | bytes 589828
  47.3 3.5 %copy-start.20 = (bf16[384,256]{0,1:T(8,128)(2,1)S(1)}, bf16[384,256]{0,1:T(8,128)(2,1)}, u32[]{:S(2)}) copy-start(bf16[384,256]{0,1:T(8,128)(2,1)} %get-tuple-element.115) | copy-start | bytes 589828
  47.3 3.5 %copy-start.24 = (f32[3,128,4,64]{1,0,3,2:T(4,128)S(1)}, f32[3,128,4,64]{1,0,3,2:T(4,128)}, u32[]{:S(2)}) copy-start(f32[3,128,4,64]{1,0,3,2:T(4,128)} %reshape.575) | copy-start | bytes 1179652
  50.8 6.0 %copy-start.13 = (bf16[384,256]{0,1:T(8,128)(2,1)S(1)}, bf16[384,256]{0,1:T(8,128)(2,1)}, u32[]{:S(2)}) copy-start(bf16[384,256]{0,1:T(8,128)(2,1)} %copy-done.12) | copy-start | bytes 589828
  50.9 6.0 %copy-start.15 = (bf16[384,256]{0,1:T(8,128)(2,1)S(1)}, bf16[384,256]{0,1:T(8,128)(2,1)}, u32[]{:S(2)}) copy-start(bf16[384,256]{0,1:T(8,128)(2,1)} %copy-done.14) | copy-start | bytes 589828
  50.9 6.0 %copy-start.17 = (bf16[384,256]{0,1:T(8,128)(2,1)S(1)}, bf16[384,256]{0,1:T(8,128)(2,1)}, u32[]{:S(2)}) copy-start(bf16[384,256]{0,1:T(8,128)(2,1)} %copy-done.16) | copy-start | bytes 589828
  51.6 6.6 %copy-start.5 = (f32[3,128,4,64]{1,3,2,0:T(8,128)}, f32[3,128,4,64]{1,3,2,0:T(8,128)S(1)}, u32[]{:S(2)}) copy-start(f32[3,128,4,64]{1,3,2,0:T(8,128)S(1)} %get-tuple-element.75) | copy-start | bytes 1179652
  51.6 3.7 %collective-permute-start.6 = (f32[2,384]{1,0:T(2,128)S(1)}, f32[2,384]{1,0:T(2,128)S(1)}, u32[]{:S(2)}, u32[]{:S(2)}) collective-permute-start(f32[2,384]{1,0:T(2,128)S(1)} %maximum_add_fusion), channel_id=1, source_target_pairs={{0,16},{16,0},{1,17},{17,1},{2,18},{18,2},{3,19},{19,3},{4,20},{20... | collective-permute-start | bytes 9224 | tf_op jit(solution)/shard_map/ppermute | solution.py:22
  55.3 3.7 %collective-permute-start.7 = (f32[2,384]{1,0:T(2,128)S(1)}, f32[2,384]{1,0:T(2,128)S(1)}, u32[]{:S(2)}, u32[]{:S(2)}) collective-permute-start(f32[2,384]{1,0:T(2,128)S(1)} %fusion.100), channel_id=1, source_target_pairs={{0,1},{1,0},{2,3},{3,2},{4,5},{5,4},{6,7},{7,6},{8,9},{9,8},{10,11... | collective-permute-start | bytes 9224 | tf_op jit(solution)/shard_map/ppermute | solution.py:144
  59.0 1.7 %copy-start.3 = (f32[3,4,128,384]{3,2,1,0:T(8,128)S(1)}, f32[3,4,128,384]{3,2,1,0:T(8,128)}, u32[]{:S(2)}) copy-start(f32[3,4,128,384]{3,2,1,0:T(8,128)} %get-tuple-element.148) | copy-start | bytes 7077892
  59.0 1.7 %copy-start.32 = (bf16[384,256]{0,1:T(8,128)(2,1)S(1)}, bf16[384,256]{0,1:T(8,128)(2,1)}, u32[]{:S(2)}) copy-start(bf16[384,256]{0,1:T(8,128)(2,1)} %copy-done.31) | copy-start | bytes 589828
  59.0 1.7 %copy-start.34 = (bf16[384,256]{0,1:T(8,128)(2,1)S(1)}, bf16[384,256]{0,1:T(8,128)(2,1)}, u32[]{:S(2)}) copy-start(bf16[384,256]{0,1:T(8,128)(2,1)} %copy-done.33) | copy-start | bytes 589828
  59.0 1.7 %copy-start.36 = (bf16[384,256]{0,1:T(8,128)(2,1)S(1)}, bf16[384,256]{0,1:T(8,128)(2,1)}, u32[]{:S(2)}) copy-start(bf16[384,256]{0,1:T(8,128)(2,1)} %copy-done.35) | copy-start | bytes 589828
  59.0 1.7 %copy-start.38 = (f32[3,4,128]{2,1,0:T(4,128)S(1)}, f32[3,4,128]{2,1,0:T(4,128)}, u32[]{:S(2)}) copy-start(f32[3,4,128]{2,1,0:T(4,128)} %copy-done.37) | copy-start | bytes 18436
  66.1 1.8 %copy-start.1 = (f32[3,4,128,384]{3,2,1,0:T(8,128)S(1)}, f32[3,4,128,384]{3,2,1,0:T(8,128)}, u32[]{:S(2)}) copy-start(f32[3,4,128,384]{3,2,1,0:T(8,128)} %get-tuple-element.71) | copy-start | bytes 7077892
  69.7 7.0 %copy-start.9 = (bf16[3,4,128,384]{3,2,1,0:T(8,128)(2,1)S(1)}, bf16[3,4,128,384]{3,2,1,0:T(8,128)(2,1)}, u32[]{:S(2)}) copy-start(bf16[3,4,128,384]{3,2,1,0:T(8,128)(2,1)} %copy-done.8) | copy-start | bytes 3538948
  69.7 7.0 %copy-start.26 = (bf16[384,256]{0,1:T(8,128)(2,1)S(1)}, bf16[384,256]{0,1:T(8,128)(2,1)}, u32[]{:S(2)}) copy-start(bf16[384,256]{0,1:T(8,128)(2,1)} %copy-done.25) | copy-start | bytes 589828
  69.7 7.0 %copy-start.28 = (bf16[384,256]{0,1:T(8,128)(2,1)S(1)}, bf16[384,256]{0,1:T(8,128)(2,1)}, u32[]{:S(2)}) copy-start(bf16[384,256]{0,1:T(8,128)(2,1)} %copy-done.27) | copy-start | bytes 589828
  69.7 7.0 %copy-start.30 = (bf16[384,256]{0,1:T(8,128)(2,1)S(1)}, bf16[384,256]{0,1:T(8,128)(2,1)}, u32[]{:S(2)}) copy-start(bf16[384,256]{0,1:T(8,128)(2,1)} %copy-done.29) | copy-start | bytes 589828
  69.7 20.8 %collective-permute-start.8 = (f32[256,512]{0,1:T(8,128)}, f32[256,512]{0,1:T(8,128)}, u32[]{:S(2)}, u32[]{:S(2)}) collective-permute-start(f32[256,512]{0,1:T(8,128)} %get-tuple-element.96), channel_id=1, source_target_pairs={{0,2},{2,4},{4,6},{6,8},{8,10},{10,12},{12,14},{1,3},{3,5},{5,7},{... | collective-permute-start | bytes 1572872 | tf_op jit(solution)/shard_map/ppermute | solution.py:18
  72.0 18.5 %collective-permute-start.9 = (f32[256,512]{0,1:T(8,128)}, f32[256,512]{0,1:T(8,128)}, u32[]{:S(2)}, u32[]{:S(2)}) collective-permute-start(f32[256,512]{0,1:T(8,128)} %get-tuple-element.95), channel_id=1, source_target_pairs={{2,0},{4,2},{6,4},{8,6},{10,8},{12,10},{14,12},{3,1},{5,3},{7,5},{... | collective-permute-start | bytes 1572872 | tf_op jit(solution)/shard_map/ppermute | solution.py:18
  79.4 11.0 %copy-start.4 = (f32[1,384,256]{1,2,0:T(8,128)S(1)}, f32[1,384,256]{1,2,0:T(8,128)}, u32[]{:S(2)}) copy-start(f32[1,384,256]{1,2,0:T(8,128)} %reshape.572) | copy-start | bytes 1179652
  82.1 14.6 %collective-permute-start.10 = (f32[256,512]{0,1:T(8,128)}, f32[256,512]{0,1:T(8,128)}, u32[]{:S(2)}, u32[]{:S(2)}) collective-permute-start(f32[256,512]{0,1:T(8,128)} %get-tuple-element.94), channel_id=1, source_target_pairs={{0,2},{2,4},{4,6},{6,8},{8,10},{10,12},{12,14},{1,3},{3,5},{5,7},{... | collective-permute-start | bytes 1572872 | tf_op jit(solution)/shard_map/ppermute | solution.py:18
  84.0 13.8 %collective-permute-start.11 = (f32[256,512]{0,1:T(8,128)}, f32[256,512]{0,1:T(8,128)}, u32[]{:S(2)}, u32[]{:S(2)}) collective-permute-start(f32[256,512]{0,1:T(8,128)} %get-tuple-element.93), channel_id=1, source_target_pairs={{2,0},{4,2},{6,4},{8,6},{10,8},{12,10},{14,12},{3,1},{5,3},{7,5},{... | collective-permute-start | bytes 1572872 | tf_op jit(solution)/shard_map/ppermute | solution.py:18
  92.6 3.3 %copy-start.23 = (bf16[1,384,256]{1,2,0:T(8,128)(2,1)S(1)}, bf16[1,384,256]{1,2,0:T(8,128)(2,1)}, u32[]{:S(2)}) copy-start(bf16[1,384,256]{1,2,0:T(8,128)(2,1)} %convert_element_type.134) | copy-start | bytes 589828
  96.0 12.0 %collective-permute-start.12 = (bf16[2,384,256]{1,2,0:T(8,128)(2,1)S(1)}, bf16[2,384,256]{1,2,0:T(8,128)(2,1)S(1)}, u32[]{:S(2)}, u32[]{:S(2)}) collective-permute-start(bf16[2,384,256]{1,2,0:T(8,128)(2,1)S(1)} %get-tuple-element.106), channel_id=1, source_target_pairs={{0,16},{16,0},{1,17},{17,1},{2,18},{18,2},{3,19},{19,3},{4,20},{20... | collective-permute-start | bytes 1179656 | tf_op jit(solution)/shard_map/ppermute | solution.py:22
  97.8 1.3 %copy-start.21 = (bf16[1,384,256]{1,2,0:T(8,128)(2,1)S(1)}, bf16[1,384,256]{1,2,0:T(8,128)(2,1)}, u32[]{:S(2)}) copy-start(bf16[1,384,256]{1,2,0:T(8,128)(2,1)} %get-tuple-element.126) | copy-start | bytes 589828
  97.8 1.3 %copy-start.22 = (bf16[1,384,256]{1,2,0:T(8,128)(2,1)S(1)}, bf16[1,384,256]{1,2,0:T(8,128)(2,1)}, u32[]{:S(2)}) copy-start(bf16[1,384,256]{1,2,0:T(8,128)(2,1)} %convert_element_type.138) | copy-start | bytes 589828
  99.3 16.3 %collective-permute-start.13 = (bf16[2,384,256]{1,2,0:T(8,128)(2,1)S(1)}, bf16[2,384,256]{1,2,0:T(8,128)(2,1)S(1)}, u32[]{:S(2)}, u32[]{:S(2)}) collective-permute-start(bf16[2,384,256]{1,2,0:T(8,128)(2,1)S(1)} %get-tuple-element.108), channel_id=1, source_target_pairs={{0,16},{16,0},{1,17},{17,1},{2,18},{18,2},{3,19},{19,3},{4,20},{20... | collective-permute-start | bytes 1179656 | tf_op jit(solution)/shard_map/ppermute | solution.py:22
  (6 other events, 6.6 us)

commit v2 on v0

--- a/solution.py
+++ b/solution.py
@@ -127,7 +127,10 @@
     rel_starts, allowed = window_plan(doc_units, seq_place, unit_count, halo_units)
 
     def row_total(sums_pair):
-        return lax.psum(sums_pair, ("sec", "mp"))
+        sums = jnp.stack(sums_pair)
+        sums = sums + sec_swap(sums)
+        sums = sums + lax.ppermute(sums, "mp", [(0, 1), (1, 0)])
+        return sums[0], sums[1]
 
     grad_q, normed, total = attention_grads(
         query_cot[0],

time: 107 us -> 100 us (0.935); the launches traced: 104 us -> 99.1 us
  blocking collectives: 8.95 us -> 0 us
  waiting for transfers between devices: 46.4 us -> 52.6 us
  matrix products: 9.11 us -> 6.35 us
  starting transfers between devices: 12.1 us -> 13.4 us
    psum x1 -> x0, blocking collectives: 8.95 us -> none  [row_total(): return lax.psum(sums_pair, ('sec', 'mp'))]
    ppermute x2 -> x3, waiting for transfers between devices: 35.6 us -> 39.6 us  [sec_swap(): return lax.ppermute(value, 'sec', [(0, 1), (1, 0)])]
    ppermute x0 -> x1, waiting for transfers between devices: none -> 2.08 us  [row_total(): sums = sums + lax.ppermute(sums, 'mp', [(0, 1), (1, 0)])]
    dot_general x1, matrix products: 3.2 us -> 1.19 us  [attention_grads(): jnp.einsum('jhqk,jkhd->jqhd', dscores, keys_w, preferred_element_type=jnp...]
    ppermute x0 -> x1, starting transfers between devices: none -> 1.58 us  [row_total(): sums = sums + lax.ppermute(sums, 'mp', [(0, 1), (1, 0)])]
    slice x1, local copies, waits for them, and re-layouts: 0.1 us -> 1.66 us  [per_device(): own = total[halo:halo + rows]]
    unnamed x36 -> x12, local copies, waits for them, and re-layouts: 4.54 us -> 3.22 us
    reduce_sum x1, other arithmetic: 1.35 us -> 0.22 us  [attention_grads(): delta = jnp.sum(up4.astype(jnp.float32) * attended4, axis=3)]
  transfers between devices with their start and end apart: 6 -> 8, of which waited for: 6 -> 8; matrix products, arithmetic and copies ran while one was open for 9% -> 9% of each run, Pallas kernels for 0% -> 0%
where the time goes in v2:
time: 100 us; the launch traced here: 99.1 us
  waiting for transfers between devices  52.6 us (53%)
  local copies, waits for them, and re-layouts  13.9 us (14%)
  starting transfers between devices  13.4 us (13%)
  other arithmetic  10.6 us (11%)
  matrix products  6.35 us (6%)
  between operations  2.18 us (2%)
    ppermute x3, waiting for transfers between devices, sec_swap(): return lax.ppermute(value, 'sec', [(0, 1), (1, 0)])  39.6 us
    ppermute x4, waiting for transfers between devices, seq_shift(): lax.ppermute(value, 'seq', [(source, source + steps) for source in range(...  11 us
    ppermute x4, starting transfers between devices, seq_shift(): lax.ppermute(value, 'seq', [(source, source + steps) for source in range(...  10.1 us
    unnamed x12, local copies, waits for them, and re-layouts  3.22 us
    ppermute x1, waiting for transfers between devices, row_total(): sums = sums + lax.ppermute(sums, 'mp', [(0, 1), (1, 0)])  2.08 us
    dot_general x1, matrix products, attention_grads(): jnp.einsum('jqhd,jkhd->jhqk', up4, values_w, preferred_element_type=jnp.f...  2 us
  transfers between devices with their start and end apart: 8, of which 8 were waited for; matrix products, arithmetic and copies ran while one was open for 9% of the time, Pallas kernels for 0%

profile of v2, /device:TPU:18, one launch (start us, length us, event | category | flops | bytes accessed | tf_op | source)
XLA Modules:
  0.0 99.1 jit_solution(5533351277449408423)
XLA Ops:
  0.0 1.5 %constant_dynamic-slice_fusion.6 = (bf16[1,2,384,512]{3,2,1,0:T(8,128)(2,1)S(1)}, bf16[1,2,384,512]{3,2,1,0:T(8,128)(2,1)S(1)}) fusion(bf16[1,2,384,1024]{3,2,1,0:T(8,128)(2,1)} %param.6, s32[]{:T(128)S(6)} %select_n.91, s32[]{:T(128)S(6)} %select_n.90), kind=kLoop, calls=%fused_computation.68 | loop fusion | bytes 3145736 | tf_op jit(solution)/shard_map/dynamic_slice | solution.py:117
  1.5 0.4 copy.20
  1.9 0.6 collective-permute-start
  2.8 0.4 copy.21
  3.7 17.5 %collective-permute-done = bf16[2,384,512]{1,2,0:T(8,128)(2,1)S(1)} collective-permute-done((bf16[2,384,512]{1,2,0:T(8,128)(2,1)S(1)}, bf16[2,384,512]{1,2,0:T(8,128)(2,1)S(1)}, u32[]{:S(2)}, u32[]{:S(2)}) %collective-permute-start) | collective-permute-done | bytes 786464 | tf_op jit(solution)/shard_map/ppermute | solution.py:22
  21.4 1.0 %fusion.19 = (bf16[256,1024]{0,1:T(8,128)(2,1)}, bf16[256,1024]{0,1:T(8,128)(2,1)}) fusion(bf16[384,512]{0,1:T(8,128)(2,1)S(1)} %get-tuple-element.59, bf16[384,512]{0,1:T(8,128)(2,1)S(1)} %get-tuple-element.60), kind=kLoop, calls=%fused_computation.49 | loop fusion | flops 2097152 | bytes 1835008 | tf_op jit(solution)/shard_map/concatenate | solution.py:122
  22.5 1.9 %collective-permute-start.2 = (bf16[256,1024]{0,1:T(8,128)(2,1)}, bf16[256,1024]{0,1:T(8,128)(2,1)}, u32[]{:S(2)}, u32[]{:S(2)}) collective-permute-start(bf16[256,1024]{0,1:T(8,128)(2,1)} %get-tuple-element.58), channel_id=1, source_target_pairs={{2,0},{4,2},{6,4},{8,6},{10,8},{12,10},{14,12},{3,1},{5,3},{7,5},{... | collective-permute-start | bytes 1572872 | tf_op jit(solution)/shard_map/ppermute | solution.py:18
  24.4 2.4 %collective-permute-start.1 = (bf16[256,1024]{0,1:T(8,128)(2,1)}, bf16[256,1024]{0,1:T(8,128)(2,1)}, u32[]{:S(2)}, u32[]{:S(2)}) collective-permute-start(bf16[256,1024]{0,1:T(8,128)(2,1)} %get-tuple-element.57), channel_id=1, source_target_pairs={{0,2},{2,4},{4,6},{6,8},{8,10},{10,12},{12,14},{1,3},{3,5},{5,7},{... | collective-permute-start | bytes 1572872 | tf_op jit(solution)/shard_map/ppermute | solution.py:18
  26.8 0.6 fusion.38
  29.5 0.3 reshape.352
  29.9 1.5 %collective-permute-done.2 = bf16[256,1024]{0,1:T(8,128)(2,1)} collective-permute-done((bf16[256,1024]{0,1:T(8,128)(2,1)}, bf16[256,1024]{0,1:T(8,128)(2,1)}, u32[]{:S(2)}, u32[]{:S(2)}) %collective-permute-start.2) | collective-permute-done | bytes 524320 | tf_op jit(solution)/shard_map/ppermute | solution.py:18
  31.4 3.8 %collective-permute-done.1 = bf16[256,1024]{0,1:T(8,128)(2,1)} collective-permute-done((bf16[256,1024]{0,1:T(8,128)(2,1)}, bf16[256,1024]{0,1:T(8,128)(2,1)}, u32[]{:S(2)}, u32[]{:S(2)}) %collective-permute-start.1) | collective-permute-done | bytes 524320 | tf_op jit(solution)/shard_map/ppermute | solution.py:18
  35.2 1.4 %pad_maximum_fusion = bf16[896,1024]{0,1:T(8,128)(2,1)S(1)} fusion(bf16[256,1024]{0,1:T(8,128)(2,1)} %collective-permute-done.2, bf16[384,512]{0,1:T(8,128)(2,1)S(1)} %get-tuple-element.60, bf16[384,512]{0,1:T(8,128)(2,1)S(1)} %get-tuple-element.59, bf16[256,1024]{0,1:T(8,128)(2,1)} %collective-permute-done.1), kind=kLoop, calls=%fused_computation.14 | loop fusion | flops 7340032 | bytes 3670016 | tf_op jit(solution)/shard_map/concatenate | solution.py:125
  37.0 0.8 fusion.20
  37.9 1.7 %fusion.39 = (f32[3,8,128]{2,1,0:T(8,128)S(1)}, f32[3,8,128,384]{3,2,1,0:T(8,128)S(1)}) fusion(f32[3,8,128,384]{3,2,1,0:T(8,128)S(1)} %fusion.20, pred[3,384]{1,0:T(4,128)(4,1)S(1)} %bitcast.115), kind=kOutput, calls=%fused_computation.99 | output fusion | flops 7078271 | bytes 9450624 | tf_op jit(solution)/shard_map/sub | solution.py:66
  39.6 0.6 fusion.5
  40.2 1.2 %multiply_reduce_fusion.2 = (f32[3,128]{1,0:T(4,128)S(1)}, f32[3,128]{1,0:T(4,128)S(1)}, f32[3,128,8,64]{1,3,2,0:T(8,128)S(1)}) fusion(f32[3,128,8,64]{1,0,3,2:T(4,128)S(1)} %reshape.352, bf16[3,8,128,384]{3,2,1,0:T(8,128)(2,1)S(1)} %fusion.5, bf16[1,384,8,64]{1,3,2,0:T(8,128)(2,1)S(1)} %bitcast.100, bf16[1,384,8,64]{1,3,2,0:T(8,128)(2,1)S(1)} %bitcast.102, ...), kind=kOutput, calls=%fused_computation.47 | convolution fusion | flops 152960256 | bytes 5114880 | tf_op jit(solution)/shard_map/jhqk,jkhd->jqhd/dot_general | solution.py:69
  41.5 0.6 collective-permute-start.3
  42.1 3.1 %collective-permute-done.3 = f32[2,384]{1,0:T(2,128)S(1)} collective-permute-done((f32[2,384]{1,0:T(2,128)S(1)}, f32[2,384]{1,0:T(2,128)S(1)}, u32[]{:S(2)}, u32[]{:S(2)}) %collective-permute-start.3) | collective-permute-done | bytes 3104 | tf_op jit(solution)/shard_map/ppermute | solution.py:22
  45.1 1.6 %collective-permute-start.4 = (f32[2,384]{1,0:T(2,128)S(1)}, f32[2,384]{1,0:T(2,128)S(1)}, u32[]{:S(2)}, u32[]{:S(2)}) collective-permute-start(f32[2,384]{1,0:T(2,128)S(1)} %fusion.35), channel_id=1, source_target_pairs={{0,1},{1,0},{2,3},{3,2},{4,5},{5,4},{6,7},{7,6},{8,9},{9,8},{10,11... | collective-permute-start | bytes 9224 | tf_op jit(solution)/shard_map/ppermute | solution.py:132
  46.7 2.1 %collective-permute-done.4 = f32[2,384]{1,0:T(2,128)S(1)} collective-permute-done((f32[2,384]{1,0:T(2,128)S(1)}, f32[2,384]{1,0:T(2,128)S(1)}, u32[]{:S(2)}, u32[]{:S(2)}) %collective-permute-start.4) | collective-permute-done | bytes 3104 | tf_op jit(solution)/shard_map/ppermute | solution.py:132
  48.8 0.2 multiply_reduce_fusion
  49.1 0.6 fusion.40
  49.6 2.0 %multiply_convert_fusion = bf16[3,8,128,384]{3,2,1,0:T(8,128)(2,1)S(1)} fusion(f32[3,8,128]{2,1,0:T(8,128)S(1)} %bitcast.111, bf16[3,128,8,64]{1,3,2,0:T(8,128)(2,1)S(1)} %get-tuple-element.36, f32[3,8,128,384]{3,2,1,0:T(8,128)S(1)} %get-tuple-element.65, f32[3,8,128]{2,1,0:T(8,128)S(1)} %get-tuple-element.64, bf16[1,384,8,64]{1,3,2,0:T(8,128)(2,1)S(1)} %bitcast.101, ...), kind=kOutput, calls=%fused_computation.5 | convolution fusion | flops 158072832 | bytes 8675328 | tf_op jit(solution)/shard_map/jqhd,jkhd->jhqk/dot_general | solution.py:83
  51.7 0.6 fusion.22
  52.2 0.9 copy-done.1
  53.1 0.2 broadcast_in_dim.36
  53.4 0.3 fusion.9
  53.7 0.3 fusion.15
  54.0 1.8 %copy-done = f32[896,1024]{0,1:T(8,128)} copy-done((f32[896,1024]{0,1:T(8,128)}, f32[896,1024]{0,1:T(8,128)S(1)}, u32[]{:S(2)}) %copy-start) | copy-done | bytes 3670040
  55.8 1.6 %fusion.36 = (f32[256,1024]{0,1:T(8,128)}, f32[256,1024]{0,1:T(8,128)}) fusion(f32[896,1024]{0,1:T(8,128)S(1)} %fusion.15), kind=kLoop, calls=%fused_computation.96 | loop fusion | bytes 4194304 | tf_op jit(solution)/shard_map/slice | solution.py:146
  57.4 1.9 %collective-permute-start.5 = (f32[256,1024]{0,1:T(8,128)}, f32[256,1024]{0,1:T(8,128)}, u32[]{:S(2)}, u32[]{:S(2)}) collective-permute-start(f32[256,1024]{0,1:T(8,128)} %get-tuple-element.38), channel_id=1, source_target_pairs={{0,2},{2,4},{4,6},{6,8},{8,10},{10,12},{12,14},{1,3},{3,5},{5,7},{... | collective-permute-start | bytes 3145736 | tf_op jit(solution)/shard_map/ppermute | solution.py:18
  59.3 3.8 %collective-permute-start.6 = (f32[256,1024]{0,1:T(8,128)}, f32[256,1024]{0,1:T(8,128)}, u32[]{:S(2)}, u32[]{:S(2)}) collective-permute-start(f32[256,1024]{0,1:T(8,128)} %get-tuple-element.37), channel_id=1, source_target_pairs={{2,0},{4,2},{6,4},{8,6},{10,8},{12,10},{14,12},{3,1},{5,3},{7,5},{... | collective-permute-start | bytes 3145736 | tf_op jit(solution)/shard_map/ppermute | solution.py:18
  63.1 0.5 copy.27
  63.7 0.4 reshape.351
  64.1 1.7 %slice.147 = f32[384,1024]{0,1:T(8,128)S(1)} slice(f32[896,1024]{0,1:T(8,128)} %copy-done), slice={[256:640], [0:1024]} | slice | bytes 3145728 | tf_op jit(solution)/shard_map/slice | solution.py:147
  65.8 0.5 copy-done.2
  66.3 1.2 %fusion.16 = bf16[3,128,8,64]{1,3,2,0:T(8,128)(2,1)S(1)} fusion(bf16[3,8,128,384]{3,2,1,0:T(8,128)(2,1)S(1)} %copy-done.2, bf16[1,384,8,64]{1,3,2,0:T(8,128)(2,1)S(1)} %bitcast.93, bf16[1,384,8,64]{1,3,2,0:T(8,128)(2,1)S(1)} %bitcast.95, bf16[1,384,8,64]{1,3,2,0:T(8,128)(2,1)S(1)} %bitcast.91), kind=kOutput, calls=%fused_computation.29 | convolution fusion | flops 152371200 | bytes 3932160 | tf_op jit(solution)/shard_map/jhqk,jkhd->jqhd/dot_general | solution.py:85
  67.4 0.3 copy.26
  67.8 0.3 convert_element_type.65
  68.2 5.6 %collective-permute-done.5 = f32[256,1024]{0,1:T(8,128)} collective-permute-done((f32[256,1024]{0,1:T(8,128)}, f32[256,1024]{0,1:T(8,128)}, u32[]{:S(2)}, u32[]{:S(2)}) %collective-permute-start.5) | collective-permute-done | bytes 1048608 | tf_op jit(solution)/shard_map/ppermute | solution.py:18
  73.8 1.7 %fusion.18 = f32[384,1024]{0,1:T(8,128)S(1)} fusion(f32[384,1024]{0,1:T(8,128)S(1)} %slice.147, f32[256,1024]{0,1:T(8,128)} %collective-permute-done.5, f32[896,1024]{0,1:T(8,128)} %copy-done), kind=kLoop, calls=%fused_computation.35 | loop fusion | flops 262144 | bytes 3145728 | tf_op jit(solution)/shard_map/scatter-add | solution.py:148
  75.6 1.4 %fusion.17 = f32[384,1024]{0,1:T(8,128)S(1)} fusion(f32[384,1024]{0,1:T(8,128)S(1)} %fusion.18, f32[256,1024]{0,1:T(8,128)} %collective-permute-done.6), kind=kLoop, calls=%fused_computation.33 | loop fusion | flops 262144 | bytes 3145728 | tf_op jit(solution)/shard_map/scatter-add | solution.py:149
  77.2 0.2 select_bitcast_fusion
  77.4 0.6 collective-permute-start.7
  78.0 19.0 %collective-permute-done.7 = bf16[2,384,512]{1,2,0:T(8,128)(2,1)S(1)} collective-permute-done((bf16[2,384,512]{1,2,0:T(8,128)(2,1)S(1)}, bf16[2,384,512]{1,2,0:T(8,128)(2,1)S(1)}, u32[]{:S(2)}, u32[]{:S(2)}) %collective-permute-start.7) | collective-permute-done | bytes 786464 | tf_op jit(solution)/shard_map/ppermute | solution.py:22
  97.0 0.4 maximum_select_fusion
  97.5 1.6 %copy.28 = bf16[1,2,384,1024]{3,2,1,0:T(8,128)(2,1)} copy(bf16[1,2,384,1024]{2,3,1,0:T(8,128)(2,1)S(1)} %maximum_select_fusion) | data formatting | bytes 3145728 | tf_op jit(solution)/shard_map/jit(_where)/select_n | solution.py:157
  (34 shorter events, 2.3 us)
Async XLA Ops:
  0.0 2.5 %copy-start.3 = (s32[12]{0:T(128)S(1)}, s32[12]{0:T(128)}, u32[]{:S(2)}) copy-start(s32[12]{0:T(128)} %param.7) | copy-start | bytes 148
  1.9 19.3 %collective-permute-start = (bf16[2,384,512]{1,2,0:T(8,128)(2,1)S(1)}, bf16[2,384,512]{1,2,0:T(8,128)(2,1)S(1)}, u32[]{:S(2)}, u32[]{:S(2)}) collective-permute-start(bf16[2,384,512]{1,2,0:T(8,128)(2,1)S(1)} %bitcast.96), channel_id=1, source_target_pairs={{0,16},{16,0},{1,17},{17,1},{2,18},{18,2},{3,19},{19,3},{4,20},{20... | collective-permute-start | bytes 2359304 | tf_op jit(solution)/shard_map/ppermute | solution.py:22
  22.5 8.9 %collective-permute-start.2 = (bf16[256,1024]{0,1:T(8,128)(2,1)}, bf16[256,1024]{0,1:T(8,128)(2,1)}, u32[]{:S(2)}, u32[]{:S(2)}) collective-permute-start(bf16[256,1024]{0,1:T(8,128)(2,1)} %get-tuple-element.58), channel_id=1, source_target_pairs={{2,0},{4,2},{6,4},{8,6},{10,8},{12,10},{14,12},{3,1},{5,3},{7,5},{... | collective-permute-start | bytes 1572872 | tf_op jit(solution)/shard_map/ppermute | solution.py:18
  24.4 10.8 %collective-permute-start.1 = (bf16[256,1024]{0,1:T(8,128)(2,1)}, bf16[256,1024]{0,1:T(8,128)(2,1)}, u32[]{:S(2)}, u32[]{:S(2)}) collective-permute-start(bf16[256,1024]{0,1:T(8,128)(2,1)} %get-tuple-element.57), channel_id=1, source_target_pairs={{0,2},{2,4},{4,6},{6,8},{8,10},{10,12},{12,14},{1,3},{3,5},{5,7},{... | collective-permute-start | bytes 1572872 | tf_op jit(solution)/shard_map/ppermute | solution.py:18
  41.5 3.7 %collective-permute-start.3 = (f32[2,384]{1,0:T(2,128)S(1)}, f32[2,384]{1,0:T(2,128)S(1)}, u32[]{:S(2)}, u32[]{:S(2)}) collective-permute-start(f32[2,384]{1,0:T(2,128)S(1)} %pad_maximum_fusion.11), channel_id=1, source_target_pairs={{0,16},{16,0},{1,17},{17,1},{2,18},{18,2},{3,19},{19,3},{4,20},{20... | collective-permute-start | bytes 9224 | tf_op jit(solution)/shard_map/ppermute | solution.py:22
  45.1 3.7 %collective-permute-start.4 = (f32[2,384]{1,0:T(2,128)S(1)}, f32[2,384]{1,0:T(2,128)S(1)}, u32[]{:S(2)}, u32[]{:S(2)}) collective-permute-start(f32[2,384]{1,0:T(2,128)S(1)} %fusion.35), channel_id=1, source_target_pairs={{0,1},{1,0},{2,3},{3,2},{4,5},{5,4},{6,7},{7,6},{8,9},{9,8},{10,11... | collective-permute-start | bytes 9224 | tf_op jit(solution)/shard_map/ppermute | solution.py:132
  51.6 1.4 %copy-start.1 = (bf16[3,8,128,384]{3,2,1,0:T(8,128)(2,1)}, bf16[3,8,128,384]{3,2,1,0:T(8,128)(2,1)S(1)}, u32[]{:S(2)}) copy-start(bf16[3,8,128,384]{3,2,1,0:T(8,128)(2,1)S(1)} %multiply_convert_fusion) | copy-start | bytes 7077892
  54.0 1.8 %copy-start = (f32[896,1024]{0,1:T(8,128)}, f32[896,1024]{0,1:T(8,128)S(1)}, u32[]{:S(2)}) copy-start(f32[896,1024]{0,1:T(8,128)S(1)} %fusion.15) | copy-start | bytes 11010052
  57.4 16.4 %collective-permute-start.5 = (f32[256,1024]{0,1:T(8,128)}, f32[256,1024]{0,1:T(8,128)}, u32[]{:S(2)}, u32[]{:S(2)}) collective-permute-start(f32[256,1024]{0,1:T(8,128)} %get-tuple-element.38), channel_id=1, source_target_pairs={{0,2},{2,4},{4,6},{6,8},{8,10},{10,12},{12,14},{1,3},{3,5},{5,7},{... | collective-permute-start | bytes 3145736 | tf_op jit(solution)/shard_map/ppermute | solution.py:18
  59.3 16.3 %collective-permute-start.6 = (f32[256,1024]{0,1:T(8,128)}, f32[256,1024]{0,1:T(8,128)}, u32[]{:S(2)}, u32[]{:S(2)}) collective-permute-start(f32[256,1024]{0,1:T(8,128)} %get-tuple-element.37), channel_id=1, source_target_pairs={{2,0},{4,2},{6,4},{8,6},{10,8},{12,10},{14,12},{3,1},{5,3},{7,5},{... | collective-permute-start | bytes 3145736 | tf_op jit(solution)/shard_map/ppermute | solution.py:18
  64.1 2.1 %copy-start.2 = (bf16[3,8,128,384]{3,2,1,0:T(8,128)(2,1)S(1)}, bf16[3,8,128,384]{3,2,1,0:T(8,128)(2,1)}, u32[]{:S(2)}) copy-start(bf16[3,8,128,384]{3,2,1,0:T(8,128)(2,1)} %copy-done.1) | copy-start | bytes 7077892
  77.4 19.6 %collective-permute-start.7 = (bf16[2,384,512]{1,2,0:T(8,128)(2,1)S(1)}, bf16[2,384,512]{1,2,0:T(8,128)(2,1)S(1)}, u32[]{:S(2)}, u32[]{:S(2)}) collective-permute-start(bf16[2,384,512]{1,2,0:T(8,128)(2,1)S(1)} %get-tuple-element.42), channel_id=1, source_target_pairs={{0,16},{16,0},{1,17},{17,1},{2,18},{18,2},{3,19},{19,3},{4,20},{20... | collective-permute-start | bytes 2359304 | tf_op jit(solution)/shard_map/ppermute | solution.py:22

commit v3 on v2

--- a/solution.py
+++ b/solution.py
@@ -142,11 +142,13 @@
         row_total,
         total_cols,
     )
-    from_left = seq_shift(total[near.shape[0] - halo :], 1)
-    from_right = seq_shift(total[:halo], -1)
-    own = total[halo : halo + rows]
-    own = own.at[:halo].add(from_left)
-    own = own.at[rows - halo :].add(from_right)
+    from_left = seq_shift(total[near.shape[0] - halo :].astype(jnp.bfloat16), 1)
+    from_right = seq_shift(total[:halo].astype(jnp.bfloat16), -1)
+    own = (
+        total[halo : halo + rows]
+        + jnp.pad(from_left.astype(jnp.float32), ((0, rows - halo), (0, 0)))
+        + jnp.pad(from_right.astype(jnp.float32), ((rows - halo, 0), (0, 0)))
+    )
     grad_k = own[:, :half].astype(jnp.bfloat16)
     grad_v = own[:, half:].astype(jnp.bfloat16)
 

time: 100 us -> 97.2 us (0.972)
  waiting for transfers between devices: 52.6 us -> 47.9 us
  other arithmetic: 10.6 us -> 12.7 us
  local copies, waits for them, and re-layouts: 13.9 us -> 15.2 us
  starting transfers between devices: 13.4 us -> 12.3 us
    slice x2 -> x1, local copies, waits for them, and re-layouts: 3.21 us -> 0.07 us  [per_device(): from_left = seq_shift(total[near.shape[0] - halo:].astype(jnp.bfloat16), 1)]
    scatter-add x2 -> x0, other arithmetic: 3.12 us -> none  [the longest x1 1.68 us: per_device(): own = own.at[:halo].add(from_left)]
    unnamed x12 -> x46, local copies, waits for them, and re-layouts: 3.22 us -> 5.28 us
    ppermute x4, waiting for transfers between devices: 11 us -> 9.04 us  [seq_shift(): lax.ppermute(value, 'seq', [(source, source + steps) for source in range(...]
    ppermute x1, waiting for transfers between devices: 2.08 us -> 0.21 us  [row_total(): sums = sums + lax.ppermute(sums, 'mp', [(0, 1), (1, 0)])]
    another operation x2 -> x3, other arithmetic: 0.27 us -> 2.09 us
    another operation x1, local copies, waits for them, and re-layouts: 0.11 us -> 1.61 us  [attention_grads(): q4 = queries.reshape(unit_count, UNIT, heads, DH)]
    reduce_sum x1, other arithmetic: 0.22 us -> 1.68 us  [attention_grads(): delta = jnp.sum(up4.astype(jnp.float32) * attended4, axis=3)]
  transfers between devices with their start and end apart: 8 -> 8, of which waited for: 8 -> 7; matrix products, arithmetic and copies ran while one was open for 9% -> 9% of each run, Pallas kernels for 0% -> 0%
where the time goes in v3:
time: 97.2 us; the launch traced here: 96.8 us
  waiting for transfers between devices  47.9 us (49%)
  local copies, waits for them, and re-layouts  15.2 us (16%)
  other arithmetic  12.7 us (13%)
  starting transfers between devices  12.3 us (13%)
  matrix products  6.2 us (6%)
  between operations  2.39 us (2%)
    ppermute x3, waiting for transfers between devices, sec_swap(): return lax.ppermute(value, 'sec', [(0, 1), (1, 0)])  38.7 us
    ppermute x4, waiting for transfers between devices, seq_shift(): lax.ppermute(value, 'seq', [(source, source + steps) for source in range(...  9.04 us
    ppermute x4, starting transfers between devices, seq_shift(): lax.ppermute(value, 'seq', [(source, source + steps) for source in range(...  8.96 us
    unnamed x46, local copies, waits for them, and re-layouts  5.28 us
    another operation x3, other arithmetic  2.09 us
  transfers between devices with their start and end apart: 8, of which 7 were waited for; matrix products, arithmetic and copies ran while one was open for 9% of the time, Pallas kernels for 0%

profile of v3, /device:TPU:18, one launch (start us, length us, event | category | flops | bytes accessed | tf_op | source)
XLA Modules:
  0.0 96.8 jit_solution(13583696456603308286)
XLA Ops:
  0.0 1.5 %constant_dynamic-slice_fusion.6 = (bf16[1,2,384,512]{3,2,1,0:T(8,128)(2,1)S(1)}, bf16[1,2,384,512]{3,2,1,0:T(8,128)(2,1)S(1)}) fusion(bf16[1,2,384,1024]{3,2,1,0:T(8,128)(2,1)} %param.2, s32[]{:T(128)S(6)} %select_n.91, s32[]{:T(128)S(6)} %select_n.90), kind=kLoop, calls=%fused_computation.67 | loop fusion | bytes 3145736 | tf_op jit(solution)/shard_map/dynamic_slice | solution.py:117
  1.5 0.4 copy.20
  1.9 0.6 collective-permute-start
  2.8 0.4 copy.21
  3.7 17.6 %collective-permute-done = bf16[2,384,512]{1,2,0:T(8,128)(2,1)} collective-permute-done((bf16[2,384,512]{1,2,0:T(8,128)(2,1)S(1)}, bf16[2,384,512]{1,2,0:T(8,128)(2,1)}, u32[]{:S(2)}, u32[]{:S(2)}) %collective-permute-start) | collective-permute-done | bytes 786464 | tf_op jit(solution)/shard_map/ppermute | solution.py:22
  21.3 1.3 %bitcast_select_fusion.1 = (bf16[2,384,512]{1,2,0:T(8,128)(2,1)S(1)}, bf16[2,384,512]{1,2,0:T(8,128)(2,1)S(1)}) fusion(bf16[2,384,512]{1,2,0:T(8,128)(2,1)} %collective-permute-done, bf16[1,2,384,512]{2,3,1,0:T(8,128)(2,1)S(1)} %copy.21, pred[]{:T(512)S(6)} %eq.11), kind=kLoop, calls=%fused_computation.40 | loop fusion | flops 786432 | bytes 3145729 | tf_op jit(solution)/shard_map/jit(_where)/select_n | solution.py:120
  22.7 1.1 %fusion.19 = (bf16[256,1024]{0,1:T(8,128)(2,1)}, bf16[256,1024]{0,1:T(8,128)(2,1)}) fusion(bf16[384,512]{0,1:T(8,128)(2,1)S(1)} %get-tuple-element.35, bf16[384,512]{0,1:T(8,128)(2,1)S(1)} %get-tuple-element.36), kind=kLoop, calls=%fused_computation.48 | loop fusion | flops 2097152 | bytes 1835008 | tf_op jit(solution)/shard_map/concatenate | solution.py:122
  23.7 1.9 %collective-permute-start.2 = (bf16[256,1024]{0,1:T(8,128)(2,1)}, bf16[256,1024]{0,1:T(8,128)(2,1)}, u32[]{:S(2)}, u32[]{:S(2)}) collective-permute-start(bf16[256,1024]{0,1:T(8,128)(2,1)} %get-tuple-element.34), channel_id=1, source_target_pairs={{2,0},{4,2},{6,4},{8,6},{10,8},{12,10},{14,12},{3,1},{5,3},{7,5},{... | collective-permute-start | bytes 1572872 | tf_op jit(solution)/shard_map/ppermute | solution.py:18
  25.7 2.4 %collective-permute-start.1 = (bf16[256,1024]{0,1:T(8,128)(2,1)}, bf16[256,1024]{0,1:T(8,128)(2,1)}, u32[]{:S(2)}, u32[]{:S(2)}) collective-permute-start(bf16[256,1024]{0,1:T(8,128)(2,1)} %get-tuple-element.33), channel_id=1, source_target_pairs={{0,2},{2,4},{4,6},{6,8},{8,10},{10,12},{12,14},{1,3},{3,5},{5,7},{... | collective-permute-start | bytes 1572872 | tf_op jit(solution)/shard_map/ppermute | solution.py:18
  28.1 0.6 fusion.38
  30.7 0.8 slice_convert_fusion
  31.5 0.3 reshape.303
  31.8 1.6 %reshape_squeeze.3 = bf16[3,128,8,64]{1,0,3,2:T(4,128)(2,1)S(1)} reshape(bf16[1,384,512]{1,2,0:T(8,128)(2,1)} %get-tuple-element.32) | data formatting | bytes 786432 | tf_op jit(solution)/shard_map/reshape;squeeze | solution.py:57
  33.5 3.0 %collective-permute-done.1 = bf16[256,1024]{0,1:T(8,128)(2,1)} collective-permute-done((bf16[256,1024]{0,1:T(8,128)(2,1)}, bf16[256,1024]{0,1:T(8,128)(2,1)}, u32[]{:S(2)}, u32[]{:S(2)}) %collective-permute-start.1) | collective-permute-done | bytes 524320 | tf_op jit(solution)/shard_map/ppermute | solution.py:18
  36.5 1.4 %pad_maximum_fusion = bf16[896,1024]{0,1:T(8,128)(2,1)S(1)} fusion(bf16[256,1024]{0,1:T(8,128)(2,1)} %collective-permute-done.2, bf16[384,512]{0,1:T(8,128)(2,1)S(1)} %get-tuple-element.36, bf16[384,512]{0,1:T(8,128)(2,1)S(1)} %get-tuple-element.35, bf16[256,1024]{0,1:T(8,128)(2,1)} %collective-permute-done.1), kind=kLoop, calls=%fused_computation.14 | loop fusion | flops 7340032 | bytes 3670016 | tf_op jit(solution)/shard_map/concatenate | solution.py:125
  38.4 0.8 fusion.20
  39.2 1.7 %fusion.39 = (f32[3,8,128]{2,1,0:T(8,128)S(1)}, f32[3,8,128,384]{3,2,1,0:T(8,128)S(1)}) fusion(f32[3,8,128,384]{3,2,1,0:T(8,128)S(1)} %fusion.20, pred[3,384]{1,0:T(4,128)(4,1)S(1)} %bitcast.115), kind=kOutput, calls=%fused_computation.98 | output fusion | flops 7078271 | bytes 9450624 | tf_op jit(solution)/shard_map/sub | solution.py:66
  41.0 0.6 fusion.5
  41.6 1.5 %copy-done.1 = f32[3,8,128,384]{3,2,1,0:T(8,128)} copy-done((f32[3,8,128,384]{3,2,1,0:T(8,128)}, f32[3,8,128,384]{3,2,1,0:T(8,128)S(1)}, u32[]{:S(2)}) %copy-start.1) | copy-done | bytes 4718616
  43.1 1.2 %multiply_reduce_fusion.2 = (f32[3,128]{1,0:T(4,128)S(1)}, f32[3,128]{1,0:T(4,128)S(1)}, f32[3,128,8,64]{1,3,2,0:T(8,128)S(1)}) fusion(f32[3,128,8,64]{1,0,3,2:T(4,128)S(1)} %reshape.303, bf16[3,8,128,384]{3,2,1,0:T(8,128)(2,1)S(1)} %fusion.5, bf16[1,384,8,64]{1,3,2,0:T(8,128)(2,1)S(1)} %bitcast.100, bf16[1,384,8,64]{1,3,2,0:T(8,128)(2,1)S(1)} %bitcast.102, ...), kind=kOutput, calls=%fused_computation.46 | convolution fusion | flops 152960256 | bytes 5114880 | tf_op jit(solution)/shard_map/jhqk,jkhd->jqhd/dot_general | solution.py:69
  44.4 0.6 collective-permute-start.3
  45.0 3.1 %collective-permute-done.3 = f32[2,384]{1,0:T(2,128)S(1)} collective-permute-done((f32[2,384]{1,0:T(2,128)S(1)}, f32[2,384]{1,0:T(2,128)S(1)}, u32[]{:S(2)}, u32[]{:S(2)}) %collective-permute-start.3) | collective-permute-done | bytes 3104 | tf_op jit(solution)/shard_map/ppermute | solution.py:22
  48.0 1.6 %collective-permute-start.4 = (f32[2,384]{1,0:T(2,128)S(1)}, f32[2,384]{1,0:T(2,128)S(1)}, u32[]{:S(2)}, u32[]{:S(2)}) collective-permute-start(f32[2,384]{1,0:T(2,128)S(1)} %fusion.35), channel_id=1, source_target_pairs={{0,1},{1,0},{2,3},{3,2},{4,5},{5,4},{6,7},{7,6},{8,9},{9,8},{10,11... | collective-permute-start | bytes 9224 | tf_op jit(solution)/shard_map/ppermute | solution.py:132
  49.6 0.5 copy.27
  50.2 1.3 %reshape.302 = f32[1,384,512]{1,2,0:T(8,128)} reshape(f32[3,128,8,64]{1,0,3,2:T(4,128)S(1)} %copy.27) | data formatting | bytes 1572864 | tf_op jit(solution)/shard_map/reshape | solution.py:70
  51.5 0.2 collective-permute-done.4
  51.7 1.7 %multiply_reduce_fusion = (f32[3,128,8]{1,2,0:T(8,128)S(1)}, bf16[3,128,8,64]{1,3,2,0:T(8,128)(2,1)S(1)}) fusion(f32[3,128,8,64]{1,3,2,0:T(8,128)} %copy-done.7, f32[3,128]{1,0:T(4,128)S(1)} %bitcast.112, f32[3,128]{1,0:T(4,128)S(1)} %bitcast.110, f32[3,128,8,64]{1,0,3,2:T(4,128)} %copy-done.3), kind=kLoop, calls=%fused_computation.43 | loop fusion | flops 1569792 | bytes 1981440 | tf_op jit(solution)/shard_map/reduce_sum | solution.py:81
  53.5 0.6 fusion.40
  54.0 1.7 %copy-done.2 = f32[3,8,128,384]{3,2,1,0:T(8,128)S(1)} copy-done((f32[3,8,128,384]{3,2,1,0:T(8,128)S(1)}, f32[3,8,128,384]{3,2,1,0:T(8,128)}, u32[]{:S(2)}) %copy-start.2) | copy-done | bytes 4718616
  56.1 1.9 %multiply_convert_fusion = bf16[3,8,128,384]{3,2,1,0:T(8,128)(2,1)S(1)} fusion(f32[3,8,128]{2,1,0:T(8,128)S(1)} %bitcast.111, bf16[3,128,8,64]{1,3,2,0:T(8,128)(2,1)S(1)} %get-tuple-element.12, f32[3,8,128,384]{3,2,1,0:T(8,128)S(1)} %copy-done.2, f32[3,8,128]{2,1,0:T(8,128)S(1)} %get-tuple-element.40, bf16[1,384,8,64]{1,3,2,0:T(8,128)(2,1)S(1)} %bitcast.101, ...), kind=kOutput, calls=%fused_computation.5 | convolution fusion | flops 158072832 | bytes 8675328 | tf_op jit(solution)/shard_map/jqhd,jkhd->jhqk/dot_general | solution.py:83
  58.0 0.6 fusion.22
  58.5 0.2 broadcast_in_dim.36
  58.9 0.3 fusion.9
  59.2 0.3 fusion.17
  59.7 1.6 %copy-done = f32[896,1024]{0,1:T(8,128)} copy-done((f32[896,1024]{0,1:T(8,128)}, f32[896,1024]{0,1:T(8,128)S(1)}, u32[]{:S(2)}) %copy-start) | copy-done | bytes 3670040
  61.4 1.9 %collective-permute-start.6 = (bf16[256,1024]{0,1:T(8,128)(2,1)S(1)}, bf16[256,1024]{0,1:T(8,128)(2,1)S(1)}, u32[]{:S(2)}, u32[]{:S(2)}) collective-permute-start(bf16[256,1024]{0,1:T(8,128)(2,1)S(1)} %get-tuple-element.14), channel_id=1, source_target_pairs={{2,0},{4,2},{6,4},{8,6},{10,8},{12,10},{14,12},{3,1},{5,3},{7,5},{... | collective-permute-start | bytes 1572872 | tf_op jit(solution)/shard_map/ppermute | solution.py:18
  63.3 2.7 %collective-permute-start.5 = (bf16[256,1024]{0,1:T(8,128)(2,1)S(1)}, bf16[256,1024]{0,1:T(8,128)(2,1)}, u32[]{:S(2)}, u32[]{:S(2)}) collective-permute-start(bf16[256,1024]{0,1:T(8,128)(2,1)S(1)} %get-tuple-element.13), channel_id=1, source_target_pairs={{0,2},{2,4},{4,6},{6,8},{8,10},{10,12},{12,14},{1,3},{3,5},{5,7},{... | collective-permute-start | bytes 1572872 | tf_op jit(solution)/shard_map/ppermute | solution.py:18
  66.1 1.2 %fusion.18 = bf16[3,128,8,64]{1,3,2,0:T(8,128)(2,1)S(1)} fusion(bf16[3,8,128,384]{3,2,1,0:T(8,128)(2,1)S(1)} %multiply_convert_fusion, bf16[1,384,8,64]{1,3,2,0:T(8,128)(2,1)S(1)} %bitcast.93, bf16[1,384,8,64]{1,3,2,0:T(8,128)(2,1)S(1)} %bitcast.95, bf16[1,384,8,64]{1,3,2,0:T(8,128)(2,1)S(1)} %bitcast.91), kind=kOutput, calls=%fused_computation.32 | convolution fusion | flops 152371200 | bytes 3932160 | tf_op jit(solution)/shard_map/jhqk,jkhd->jqhd/dot_general | solution.py:85
  67.2 0.3 copy.26
  67.6 0.3 convert_element_type.73
  68.0 2.0 %collective-permute-done.6 = bf16[256,1024]{0,1:T(8,128)(2,1)S(1)} collective-permute-done((bf16[256,1024]{0,1:T(8,128)(2,1)S(1)}, bf16[256,1024]{0,1:T(8,128)(2,1)S(1)}, u32[]{:S(2)}, u32[]{:S(2)}) %collective-permute-start.6) | collective-permute-done | bytes 524320 | tf_op jit(solution)/shard_map/ppermute | solution.py:18
  70.0 4.1 %collective-permute-done.5 = bf16[256,1024]{0,1:T(8,128)(2,1)} collective-permute-done((bf16[256,1024]{0,1:T(8,128)(2,1)S(1)}, bf16[256,1024]{0,1:T(8,128)(2,1)}, u32[]{:S(2)}, u32[]{:S(2)}) %collective-permute-start.5) | collective-permute-done | bytes 524320 | tf_op jit(solution)/shard_map/ppermute | solution.py:18
  74.0 1.7 %fusion.14 = bf16[384,1024]{0,1:T(8,128)(2,1)S(1)} fusion(f32[896,1024]{0,1:T(8,128)} %copy-done, bf16[256,1024]{0,1:T(8,128)(2,1)S(1)} %collective-permute-done.6, bf16[256,1024]{0,1:T(8,128)(2,1)} %collective-permute-done.5), kind=kLoop, calls=%fused_computation.24 | loop fusion | flops 1966080 | bytes 3407872 | tf_op jit(solution)/shard_map/convert.6
  75.8 0.2 select_bitcast_fusion
  76.1 0.6 collective-permute-start.7
  76.7 18.0 %collective-permute-done.7 = bf16[2,384,512]{1,2,0:T(8,128)(2,1)S(1)} collective-permute-done((bf16[2,384,512]{1,2,0:T(8,128)(2,1)S(1)}, bf16[2,384,512]{1,2,0:T(8,128)(2,1)S(1)}, u32[]{:S(2)}, u32[]{:S(2)}) %collective-permute-start.7) | collective-permute-done | bytes 786464 | tf_op jit(solution)/shard_map/ppermute | solution.py:22
  94.7 0.4 maximum_select_fusion
  95.1 1.6 %copy.28 = bf16[1,2,384,1024]{3,2,1,0:T(8,128)(2,1)} copy(bf16[1,2,384,1024]{2,3,1,0:T(8,128)(2,1)S(1)} %maximum_select_fusion) | data formatting | bytes 3145728 | tf_op jit(solution)/shard_map/jit(_where)/select_n | solution.py:159
  (66 shorter events, 2.4 us)
Async XLA Ops:
  0.0 2.5 %copy-start.20 = (s32[12]{0:T(128)S(1)}, s32[12]{0:T(128)}, u32[]{:S(2)}) copy-start(s32[12]{0:T(128)} %param.3) | copy-start | bytes 148
  1.9 19.5 %collective-permute-start = (bf16[2,384,512]{1,2,0:T(8,128)(2,1)S(1)}, bf16[2,384,512]{1,2,0:T(8,128)(2,1)}, u32[]{:S(2)}, u32[]{:S(2)}) collective-permute-start(bf16[2,384,512]{1,2,0:T(8,128)(2,1)S(1)} %bitcast.96), channel_id=1, source_target_pairs={{0,16},{16,0},{1,17},{17,1},{2,18},{18,2},{3,19},{19,3},{4,20},{20... | collective-permute-start | bytes 2359304 | tf_op jit(solution)/shard_map/ppermute | solution.py:22
  23.7 9.7 %collective-permute-start.2 = (bf16[256,1024]{0,1:T(8,128)(2,1)}, bf16[256,1024]{0,1:T(8,128)(2,1)}, u32[]{:S(2)}, u32[]{:S(2)}) collective-permute-start(bf16[256,1024]{0,1:T(8,128)(2,1)} %get-tuple-element.34), channel_id=1, source_target_pairs={{2,0},{4,2},{6,4},{8,6},{10,8},{12,10},{14,12},{3,1},{5,3},{7,5},{... | collective-permute-start | bytes 1572872 | tf_op jit(solution)/shard_map/ppermute | solution.py:18
  25.7 10.8 %collective-permute-start.1 = (bf16[256,1024]{0,1:T(8,128)(2,1)}, bf16[256,1024]{0,1:T(8,128)(2,1)}, u32[]{:S(2)}, u32[]{:S(2)}) collective-permute-start(bf16[256,1024]{0,1:T(8,128)(2,1)} %get-tuple-element.33), channel_id=1, source_target_pairs={{0,2},{2,4},{4,6},{6,8},{8,10},{10,12},{12,14},{1,3},{3,5},{5,7},{... | collective-permute-start | bytes 1572872 | tf_op jit(solution)/shard_map/ppermute | solution.py:18
  31.8 11.2 %copy-start.3 = (f32[3,128,8,64]{1,0,3,2:T(4,128)}, f32[3,128,8,64]{1,0,3,2:T(4,128)S(1)}, u32[]{:S(2)}) copy-start(f32[3,128,8,64]{1,0,3,2:T(4,128)S(1)} %reshape.303) | copy-start | bytes 2359300
  33.4 4.9 %copy-start.4 = (bf16[3,128,8,64]{1,0,3,2:T(4,128)(2,1)}, bf16[3,128,8,64]{1,0,3,2:T(4,128)(2,1)S(1)}, u32[]{:S(2)}) copy-start(bf16[3,128,8,64]{1,0,3,2:T(4,128)(2,1)S(1)} %reshape_squeeze.3) | copy-start | bytes 1179652
  38.1 1.0 %copy-start.8 = (bf16[384,512]{0,1:T(8,128)(2,1)}, bf16[384,512]{0,1:T(8,128)(2,1)S(1)}, u32[]{:S(2)}) copy-start(bf16[384,512]{0,1:T(8,128)(2,1)S(1)} %get-tuple-element.26) | copy-start | bytes 1179652
  38.2 1.0 %copy-start.10 = (bf16[384,512]{0,1:T(8,128)(2,1)}, bf16[384,512]{0,1:T(8,128)(2,1)S(1)}, u32[]{:S(2)}) copy-start(bf16[384,512]{0,1:T(8,128)(2,1)S(1)} %get-tuple-element.27) | copy-start | bytes 1179652
  38.2 1.0 %copy-start.12 = (bf16[384,512]{0,1:T(8,128)(2,1)}, bf16[384,512]{0,1:T(8,128)(2,1)S(1)}, u32[]{:S(2)}) copy-start(bf16[384,512]{0,1:T(8,128)(2,1)S(1)} %get-tuple-element.28) | copy-start | bytes 1179652
  38.3 4.8 %copy-start.14 = (bf16[384,512]{0,1:T(8,128)(2,1)}, bf16[384,512]{0,1:T(8,128)(2,1)S(1)}, u32[]{:S(2)}) copy-start(bf16[384,512]{0,1:T(8,128)(2,1)S(1)} %get-tuple-element.23) | copy-start | bytes 1179652
  38.3 4.8 %copy-start.16 = (bf16[384,512]{0,1:T(8,128)(2,1)}, bf16[384,512]{0,1:T(8,128)(2,1)S(1)}, u32[]{:S(2)}) copy-start(bf16[384,512]{0,1:T(8,128)(2,1)S(1)} %get-tuple-element.24) | copy-start | bytes 1179652
  38.3 4.7 %copy-start.18 = (bf16[384,512]{0,1:T(8,128)(2,1)}, bf16[384,512]{0,1:T(8,128)(2,1)S(1)}, u32[]{:S(2)}) copy-start(bf16[384,512]{0,1:T(8,128)(2,1)S(1)} %get-tuple-element.25) | copy-start | bytes 1179652
  40.9 2.1 %copy-start.1 = (f32[3,8,128,384]{3,2,1,0:T(8,128)}, f32[3,8,128,384]{3,2,1,0:T(8,128)S(1)}, u32[]{:S(2)}) copy-start(f32[3,8,128,384]{3,2,1,0:T(8,128)S(1)} %get-tuple-element.41) | copy-start | bytes 14155780
  44.3 5.3 %copy-start.7 = (f32[3,128,8,64]{1,3,2,0:T(8,128)}, f32[3,128,8,64]{1,3,2,0:T(8,128)S(1)}, u32[]{:S(2)}) copy-start(f32[3,128,8,64]{1,3,2,0:T(8,128)S(1)} %get-tuple-element.42) | copy-start | bytes 2359300
  44.4 3.7 %collective-permute-start.3 = (f32[2,384]{1,0:T(2,128)S(1)}, f32[2,384]{1,0:T(2,128)S(1)}, u32[]{:S(2)}, u32[]{:S(2)}) collective-permute-start(f32[2,384]{1,0:T(2,128)S(1)} %pad_maximum_fusion.11), channel_id=1, source_target_pairs={{0,16},{16,0},{1,17},{17,1},{2,18},{18,2},{3,19},{19,3},{4,20},{20... | collective-permute-start | bytes 9224 | tf_op jit(solution)/shard_map/ppermute | solution.py:22
  48.0 3.7 %collective-permute-start.4 = (f32[2,384]{1,0:T(2,128)S(1)}, f32[2,384]{1,0:T(2,128)S(1)}, u32[]{:S(2)}, u32[]{:S(2)}) collective-permute-start(f32[2,384]{1,0:T(2,128)S(1)} %fusion.35), channel_id=1, source_target_pairs={{0,1},{1,0},{2,3},{3,2},{4,5},{5,4},{6,7},{7,6},{8,9},{9,8},{10,11... | collective-permute-start | bytes 9224 | tf_op jit(solution)/shard_map/ppermute | solution.py:132
  53.4 2.3 %copy-start.2 = (f32[3,8,128,384]{3,2,1,0:T(8,128)S(1)}, f32[3,8,128,384]{3,2,1,0:T(8,128)}, u32[]{:S(2)}) copy-start(f32[3,8,128,384]{3,2,1,0:T(8,128)} %copy-done.1) | copy-start | bytes 14155780
  53.4 2.4 %copy-start.15 = (bf16[384,512]{0,1:T(8,128)(2,1)S(1)}, bf16[384,512]{0,1:T(8,128)(2,1)}, u32[]{:S(2)}) copy-start(bf16[384,512]{0,1:T(8,128)(2,1)} %copy-done.14) | copy-start | bytes 1179652
  53.4 2.5 %copy-start.17 = (bf16[384,512]{0,1:T(8,128)(2,1)S(1)}, bf16[384,512]{0,1:T(8,128)(2,1)}, u32[]{:S(2)}) copy-start(bf16[384,512]{0,1:T(8,128)(2,1)} %copy-done.16) | copy-start | bytes 1179652
  53.4 2.6 %copy-start.19 = (bf16[384,512]{0,1:T(8,128)(2,1)S(1)}, bf16[384,512]{0,1:T(8,128)(2,1)}, u32[]{:S(2)}) copy-start(bf16[384,512]{0,1:T(8,128)(2,1)} %copy-done.18) | copy-start | bytes 1179652
  56.1 1.9 %copy-start.5 = (bf16[3,128,8,64]{1,0,3,2:T(4,128)(2,1)S(1)}, bf16[3,128,8,64]{1,0,3,2:T(4,128)(2,1)}, u32[]{:S(2)}) copy-start(bf16[3,128,8,64]{1,0,3,2:T(4,128)(2,1)} %copy-done.4) | copy-start | bytes 1179652
  59.5 1.8 %copy-start = (f32[896,1024]{0,1:T(8,128)}, f32[896,1024]{0,1:T(8,128)S(1)}, u32[]{:S(2)}) copy-start(f32[896,1024]{0,1:T(8,128)S(1)} %fusion.17) | copy-start | bytes 11010052
  59.5 6.5 %copy-start.9 = (bf16[384,512]{0,1:T(8,128)(2,1)S(1)}, bf16[384,512]{0,1:T(8,128)(2,1)}, u32[]{:S(2)}) copy-start(bf16[384,512]{0,1:T(8,128)(2,1)} %copy-done.8) | copy-start | bytes 1179652
  59.5 6.5 %copy-start.11 = (bf16[384,512]{0,1:T(8,128)(2,1)S(1)}, bf16[384,512]{0,1:T(8,128)(2,1)}, u32[]{:S(2)}) copy-start(bf16[384,512]{0,1:T(8,128)(2,1)} %copy-done.10) | copy-start | bytes 1179652
  59.5 6.5 %copy-start.13 = (bf16[384,512]{0,1:T(8,128)(2,1)S(1)}, bf16[384,512]{0,1:T(8,128)(2,1)}, u32[]{:S(2)}) copy-start(bf16[384,512]{0,1:T(8,128)(2,1)} %copy-done.12) | copy-start | bytes 1179652
  61.4 8.6 %collective-permute-start.6 = (bf16[256,1024]{0,1:T(8,128)(2,1)S(1)}, bf16[256,1024]{0,1:T(8,128)(2,1)S(1)}, u32[]{:S(2)}, u32[]{:S(2)}) collective-permute-start(bf16[256,1024]{0,1:T(8,128)(2,1)S(1)} %get-tuple-element.14), channel_id=1, source_target_pairs={{2,0},{4,2},{6,4},{8,6},{10,8},{12,10},{14,12},{3,1},{5,3},{7,5},{... | collective-permute-start | bytes 1572872 | tf_op jit(solution)/shard_map/ppermute | solution.py:18
  63.3 4.6 %copy-start.6 = (f32[1,384,512]{1,2,0:T(8,128)S(1)}, f32[1,384,512]{1,2,0:T(8,128)}, u32[]{:S(2)}) copy-start(f32[1,384,512]{1,2,0:T(8,128)} %reshape.302) | copy-start | bytes 2359300
  63.3 10.7 %collective-permute-start.5 = (bf16[256,1024]{0,1:T(8,128)(2,1)S(1)}, bf16[256,1024]{0,1:T(8,128)(2,1)}, u32[]{:S(2)}, u32[]{:S(2)}) collective-permute-start(bf16[256,1024]{0,1:T(8,128)(2,1)S(1)} %get-tuple-element.13), channel_id=1, source_target_pairs={{0,2},{2,4},{4,6},{6,8},{8,10},{10,12},{12,14},{1,3},{3,5},{5,7},{... | collective-permute-start | bytes 1572872 | tf_op jit(solution)/shard_map/ppermute | solution.py:18
  76.1 18.6 %collective-permute-start.7 = (bf16[2,384,512]{1,2,0:T(8,128)(2,1)S(1)}, bf16[2,384,512]{1,2,0:T(8,128)(2,1)S(1)}, u32[]{:S(2)}, u32[]{:S(2)}) collective-permute-start(bf16[2,384,512]{1,2,0:T(8,128)(2,1)S(1)} %get-tuple-element.18), channel_id=1, source_target_pairs={{0,16},{16,0},{1,17},{17,1},{2,18},{18,2},{3,19},{19,3},{4,20},{20... | collective-permute-start | bytes 2359304 | tf_op jit(solution)/shard_map/ppermute | solution.py:22

commit v4 on v3

--- a/solution.py
+++ b/solution.py
@@ -1,6 +1,8 @@
 import jax
 import jax.numpy as jnp
 from jax import lax
+from jax.experimental import pallas as pl
+from jax.experimental.pallas import tpu as pltpu
 from jax.sharding import PartitionSpec as P
 
 UNIT = 128
@@ -36,39 +38,126 @@
     ).astype(jnp.int32)
     key_units = starts[:, None] + jnp.arange(MAX_DOC_UNITS, dtype=jnp.int32)[None, :]
     allowed = unit_doc(key_units.reshape(-1)).reshape(key_units.shape) == unit_doc(query_units)[:, None]
-    return starts - (first_unit - halo_units), allowed
-
-
-def attention_grads(queries, cotangent, near_keys, near_values, rel_starts, allowed, total_fn, total_cols):
-    rows, head_cols = queries.shape
-    heads = head_cols // DH
-    unit_count = rows // UNIT
+    near_units = unit_count + 2 * halo_units
+    rel_starts = jnp.clip(starts - (first_unit - halo_units), 0, near_units - MAX_DOC_UNITS)
+    return rel_starts, allowed
+
+
+PAIR = 2 * DH
+
+
+def pair_softmax(q_pair, k_pair, mask, lane_low):
+    score_scale = DH ** (-0.5)
+    result = []
+    for chosen in (lane_low, jnp.logical_not(lane_low)):
+        q_one = jnp.where(chosen, q_pair, jnp.zeros_like(q_pair))
+        scores = (
+            lax.dot_general(q_one, k_pair, (((1,), (1,)), ((), ())), preferred_element_type=jnp.float32)
+            * score_scale
+        )
+        scores = jnp.where(mask, scores, -jnp.inf)
+        row_max = jnp.max(scores, axis=1, keepdims=True)
+        expven = jnp.exp(scores - row_max)
+        result.append((chosen, expven / jnp.sum(expven, axis=1, keepdims=True)))
+    return result
+
+
+def window_mask(allow_ref, j):
+    window = MAX_DOC_UNITS * UNIT
+    block = lax.broadcasted_iota(jnp.int32, (UNIT, window), 1) // UNIT
+    mask = jnp.zeros((UNIT, window), jnp.bool_)
+    for w in range(MAX_DOC_UNITS):
+        mask = jnp.logical_or(mask, jnp.logical_and(block == w, allow_ref[j * MAX_DOC_UNITS + w] != 0))
+    return mask
+
+
+def forward_kernel(rel_ref, allow_ref, q_ref, kv_ref, out_ref):
+    rows, head_cols = q_ref.shape
+    window = MAX_DOC_UNITS * UNIT
+    lane_low = lax.broadcasted_iota(jnp.int32, (UNIT, PAIR), 1) < DH
+    for j in range(rows // UNIT):
+        start = pl.multiple_of(rel_ref[j] * UNIT, UNIT)
+        mask = window_mask(allow_ref, j)
+        for p in range(head_cols // PAIR):
+            q_pair = q_ref[pl.ds(j * UNIT, UNIT), pl.ds(p * PAIR, PAIR)]
+            k_pair = kv_ref[pl.ds(start, window), pl.ds(p * PAIR, PAIR)]
+            v_pair = kv_ref[pl.ds(start, window), pl.ds(head_cols + p * PAIR, PAIR)]
+            outs = [
+                jnp.dot(weights.astype(jnp.bfloat16), v_pair, preferred_element_type=jnp.float32)
+                for _, weights in pair_softmax(q_pair, k_pair, mask, lane_low)
+            ]
+            out_ref[pl.ds(j * UNIT, UNIT), pl.ds(p * PAIR, PAIR)] = jnp.where(lane_low, outs[0], outs[1])
+
+
+def backward_kernel(rel_ref, allow_ref, q_ref, up_ref, att_ref, kv_ref, dq_ref, dkv_ref):
+    rows, head_cols = q_ref.shape
     window = MAX_DOC_UNITS * UNIT
     score_scale = DH ** (-0.5)
-
-    def windows(near):
-        pieces = [
-            lax.dynamic_slice_in_dim(near, rel_starts[j] * UNIT, window, 0) for j in range(unit_count)
-        ]
-        return jnp.stack(pieces).reshape(unit_count, window, heads, DH)
-
-    keys_w = windows(near_keys)
-    values_w = windows(near_values)
-    q4 = queries.reshape(unit_count, UNIT, heads, DH)
+    lane_low = lax.broadcasted_iota(jnp.int32, (UNIT, PAIR), 1) < DH
+    wide_low = lax.broadcasted_iota(jnp.int32, (window, PAIR), 1) < DH
+    dkv_ref[...] = jnp.zeros(dkv_ref.shape, dkv_ref.dtype)
+    contract_rows = (((0,), (0,)), ((), ()))
+    for j in range(rows // UNIT):
+        start = pl.multiple_of(rel_ref[j] * UNIT, UNIT)
+        mask = window_mask(allow_ref, j)
+        for p in range(head_cols // PAIR):
+            q_pair = q_ref[pl.ds(j * UNIT, UNIT), pl.ds(p * PAIR, PAIR)]
+            up_pair = up_ref[pl.ds(j * UNIT, UNIT), pl.ds(p * PAIR, PAIR)]
+            att_pair = att_ref[pl.ds(j * UNIT, UNIT), pl.ds(p * PAIR, PAIR)]
+            k_pair = kv_ref[pl.ds(start, window), pl.ds(p * PAIR, PAIR)]
+            v_pair = kv_ref[pl.ds(start, window), pl.ds(head_cols + p * PAIR, PAIR)]
+            product = up_pair.astype(jnp.float32) * att_pair
+            grads = []
+            for chosen, weights in pair_softmax(q_pair, k_pair, mask, lane_low):
+                delta = jnp.sum(jnp.where(chosen, product, 0.0), axis=1, keepdims=True)
+                up_one = jnp.where(chosen, up_pair, jnp.zeros_like(up_pair))
+                dprobs = lax.dot_general(
+                    up_one, v_pair, (((1,), (1,)), ((), ())), preferred_element_type=jnp.float32
+                )
+                dscores = (weights * (dprobs - delta) * score_scale).astype(jnp.bfloat16)
+                grads.append(
+                    (
+                        jnp.dot(dscores, k_pair, preferred_element_type=jnp.float32),
+                        lax.dot_general(dscores, q_pair, contract_rows, preferred_element_type=jnp.float32),
+                        lax.dot_general(
+                            weights.astype(jnp.bfloat16), up_pair, contract_rows,
+                            preferred_element_type=jnp.float32,
+                        ),
+                    )
+                )
+            (dq_a, dk_a, dv_a), (dq_b, dk_b, dv_b) = grads
+            dq_ref[pl.ds(j * UNIT, UNIT), pl.ds(p * PAIR, PAIR)] = jnp.where(lane_low, dq_a, dq_b)
+            k_rows = (pl.ds(start, window), pl.ds(p * PAIR, PAIR))
+            v_rows = (pl.ds(start, window), pl.ds(head_cols + p * PAIR, PAIR))
+            dkv_ref[k_rows] = dkv_ref[k_rows] + jnp.where(wide_low, dk_a, dk_b)
+            dkv_ref[v_rows] = dkv_ref[v_rows] + jnp.where(wide_low, dv_a, dv_b)
+
+
+def whole_call(kernel, scalars, arrays, outs):
+    def spec(shape):
+        return pl.BlockSpec(shape, lambda i, *_: (0,) * len(shape))
+
+    return pl.pallas_call(
+        kernel,
+        grid_spec=pltpu.PrefetchScalarGridSpec(
+            num_scalar_prefetch=len(scalars),
+            grid=(1,),
+            in_specs=[spec(a.shape) for a in arrays],
+            out_specs=[spec(o.shape) for o in outs],
+        ),
+        out_shape=outs,
+    )(*scalars, *arrays)
+
+
+def attention_grads(queries, cotangent, near, rel_starts, allowed, total_fn, total_cols):
+    rows, head_cols = queries.shape
+    near_rows = near.shape[0]
+    allow_flat = allowed.reshape(-1).astype(jnp.int32)
+    scalars = (rel_starts.astype(jnp.int32), allow_flat)
+    (attended,) = whole_call(
+        forward_kernel, scalars, (queries, near), [jax.ShapeDtypeStruct((rows, head_cols), jnp.float32)]
+    )
     cot_float = cotangent.astype(jnp.float32)
-
-    mask = jnp.repeat(allowed, UNIT, axis=1)[:, None, None, :]
-    scores = (
-        jnp.einsum("jqhd,jkhd->jhqk", q4, keys_w, preferred_element_type=jnp.float32) * score_scale
-    )
-    scores = jnp.where(mask, scores, -jnp.inf)
-    row_max = jnp.max(scores, axis=3, keepdims=True)
-    expven = jnp.exp(scores - row_max)
-    weights = expven / jnp.sum(expven, axis=3, keepdims=True)
-    rounded = weights.astype(jnp.bfloat16)
-    attended4 = jnp.einsum("jhqk,jkhd->jqhd", rounded, values_w, preferred_element_type=jnp.float32)
-    attended = attended4.reshape(rows, head_cols)
-
     squares, crosses = total_fn(
         (jnp.sum(attended * attended, axis=1), jnp.sum(cot_float * attended, axis=1))
     )
@@ -76,27 +165,16 @@
     normed = attended / spread[:, None]
     shared = crosses / total_cols / spread
     upstream = ((cot_float - normed * shared[:, None]) / spread[:, None]).astype(jnp.bfloat16)
-    up4 = upstream.reshape(unit_count, UNIT, heads, DH)
-
-    delta = jnp.sum(up4.astype(jnp.float32) * attended4, axis=3)
-    delta = jnp.transpose(delta, (0, 2, 1))[..., None]
-    dprobs = jnp.einsum("jqhd,jkhd->jhqk", up4, values_w, preferred_element_type=jnp.float32)
-    dscores = (weights * (dprobs - delta) * score_scale).astype(jnp.bfloat16)
-    grad_q = jnp.einsum("jhqk,jkhd->jqhd", dscores, keys_w, preferred_element_type=jnp.float32)
-    grad_kw = jnp.einsum("jhqk,jqhd->jkhd", dscores, q4, preferred_element_type=jnp.float32)
-    grad_vw = jnp.einsum("jhqk,jqhd->jkhd", rounded, up4, preferred_element_type=jnp.float32)
-    grad_kvw = jnp.concatenate(
-        [grad_kw.reshape(unit_count, window, head_cols), grad_vw.reshape(unit_count, window, head_cols)],
-        axis=2,
-    )
-    near_rows = near_keys.shape[0]
-    total = jnp.zeros((near_rows, 2 * head_cols), jnp.float32)
-    for j in range(unit_count):
-        start = rel_starts[j] * UNIT
-        total = lax.dynamic_update_slice_in_dim(
-            total, lax.dynamic_slice_in_dim(total, start, window, 0) + grad_kvw[j], start, 0
-        )
-    return grad_q.reshape(rows, head_cols), normed, total
+    grad_q, total = whole_call(
+        backward_kernel,
+        scalars,
+        (queries, upstream, attended, near),
+        [
+            jax.ShapeDtypeStruct((rows, head_cols), jnp.float32),
+            jax.ShapeDtypeStruct((near_rows, 2 * head_cols), jnp.float32),
+        ],
+    )
+    return grad_q, normed, total
 
 
 def per_device(heads_in, doc_units):
@@ -135,8 +213,7 @@
     grad_q, normed, total = attention_grads(
         query_cot[0],
         query_cot[1],
-        near[:, :half],
-        near[:, half:],
+        near,
         rel_starts,
         allowed,
         row_total,

time: 97.2 us -> 108 us (1.11)
  Pallas kernels: 0 us -> 22 us
  local copies, waits for them, and re-layouts: 15.2 us -> 2.53 us
  matrix products: 6.2 us -> 0 us
  waiting for transfers between devices: 47.9 us -> 52.8 us
  starting transfers between devices: 12.3 us -> 14.6 us
  between operations: 2.39 us -> 0.15 us
  other arithmetic: 12.7 us -> 14.5 us
    pallas_call x0 -> x2, Pallas kernels: none -> 22 us  [whole_call(): pl.pallas_call(kernel, grid_spec=pltpu.PrefetchScalarGridSpec(num_scalar_...]
    dot_general x6 -> x0, matrix products: 6.2 us -> none  [the longest x1 1.87 us: attention_grads(): jnp.einsum('jqhd,jkhd->jhqk', up4, values_w, preferred_element_type=jnp.f...]
    unnamed x46 -> x4, local copies, waits for them, and re-layouts: 5.28 us -> 0.01 us
    another operation x3 -> x4, other arithmetic: 2.09 us -> 4.91 us
    ppermute x4, waiting for transfers between devices: 9.04 us -> 11.6 us  [seq_shift(): lax.ppermute(value, 'seq', [(source, source + steps) for source in range(...]
    ppermute x4, starting transfers between devices: 8.96 us -> 11.2 us  [seq_shift(): lax.ppermute(value, 'seq', [(source, source + steps) for source in range(...]
    dynamic_slice x4 -> x0, local copies, waits for them, and re-layouts: 2.1 us -> none  [the longest x2 1.84 us: per_device(): kept = lax.dynamic_slice_in_dim(local_heads, keep_offset, half, 2)]
    ppermute x1, waiting for transfers between devices: 0.21 us -> 2.08 us  [row_total(): sums = sums + lax.ppermute(sums, 'mp', [(0, 1), (1, 0)])]
  transfers between devices with their start and end apart: 8 -> 8, of which waited for: 7 -> 8; matrix products, arithmetic and copies ran while one was open for 9% -> 3% of each run, Pallas kernels for 0% -> 0%
where the time goes in v4:
time: 108 us; the launch traced here: 107 us
  waiting for transfers between devices  52.8 us (49%)
  Pallas kernels  22 us (20%)
  starting transfers between devices  14.6 us (14%)
  other arithmetic  14.5 us (13%)
  local copies, waits for them, and re-layouts  2.53 us (2%)
    ppermute x3, waiting for transfers between devices, sec_swap(): return lax.ppermute(value, 'sec', [(0, 1), (1, 0)])  39.1 us
    pallas_call x2, Pallas kernels, whole_call(): pl.pallas_call(kernel, grid_spec=pltpu.PrefetchScalarGridSpec(num_scalar_...  22 us
    ppermute x4, waiting for transfers between devices, seq_shift(): lax.ppermute(value, 'seq', [(source, source + steps) for source in range(...  11.6 us
    ppermute x4, starting transfers between devices, seq_shift(): lax.ppermute(value, 'seq', [(source, source + steps) for source in range(...  11.2 us
    another operation x3, other arithmetic  4.86 us
  transfers between devices with their start and end apart: 8, of which 8 were waited for; matrix products, arithmetic and copies ran while one was open for 3% of the time, Pallas kernels for 0%

profile of v4, /device:TPU:18, one launch (start us, length us, event | category | flops | bytes accessed | tf_op | source)
XLA Modules:
  0.0 106.6 jit_solution(6355277049773223370)
XLA Ops:
  0.0 0.0 copy-start
  0.0 1.3 %dynamic-slice_bitcast_fusion = bf16[2,384,512]{2,1,0:T(8,128)(2,1)S(1)} fusion(bf16[1,2,384,1024]{3,2,1,0:T(8,128)(2,1)} %param.2, s32[]{:T(128)S(6)} %select_n.73), kind=kLoop, calls=%fused_computation.16 | loop fusion | bytes 1572868 | tf_op jit(solution)/shard_map/dynamic_slice | solution.py:194
  1.3 0.6 collective-permute-start
  1.9 0.8 reduce-window.8
  2.7 0.2 fusion.5
  2.9 0.1 iota_add_fusion
  3.0 0.1 add.78
  3.1 0.5 subtract_clamp_fusion.rel_ref
  3.6 17.0 %collective-permute-done = bf16[2,384,512]{2,1,0:T(8,128)(2,1)S(1)} collective-permute-done((bf16[2,384,512]{2,1,0:T(8,128)(2,1)S(1)}, bf16[2,384,512]{2,1,0:T(8,128)(2,1)S(1)}, u32[]{:S(2)}, u32[]{:S(2)}) %collective-permute-start) | collective-permute-done | bytes 786464 | tf_op jit(solution)/shard_map/ppermute | solution.py:24
  20.7 0.0 copy-done
  20.7 0.4 bitcast_select_fusion
  21.0 0.1 slice_bitcast_fusion.3
  21.1 0.9 fusion.3
  22.0 1.9 %collective-permute-start.1 = (bf16[256,1024]{1,0:T(8,128)(2,1)}, bf16[256,1024]{1,0:T(8,128)(2,1)S(1)}, u32[]{:S(2)}, u32[]{:S(2)}) collective-permute-start(bf16[256,1024]{1,0:T(8,128)(2,1)} %get-tuple-element.25), channel_id=1, source_target_pairs={{0,2},{2,4},{4,6},{6,8},{8,10},{10,12},{12,14},{1,3},{3,5},{5,7},{... | collective-permute-start | bytes 1572872 | tf_op jit(solution)/shard_map/ppermute | solution.py:20
  23.9 3.6 %collective-permute-start.2 = (bf16[256,1024]{1,0:T(8,128)(2,1)S(1)}, bf16[256,1024]{1,0:T(8,128)(2,1)S(1)}, u32[]{:S(2)}, u32[]{:S(2)}) collective-permute-start(bf16[256,1024]{1,0:T(8,128)(2,1)S(1)} %get-tuple-element.26), channel_id=1, source_target_pairs={{2,0},{4,2},{6,4},{8,6},{10,8},{12,10},{14,12},{3,1},{5,3},{7,5},{... | collective-permute-start | bytes 1572872 | tf_op jit(solution)/shard_map/ppermute | solution.py:20
  27.6 0.2 convert_reduce_fusion
  27.8 0.1 eq.15
  27.8 0.1 eq.16
  27.9 0.6 compare_convert_fusion.1.allow_ref
  28.5 0.8 slice_bitcast_fusion.5.q_ref
  29.3 3.4 %collective-permute-done.1 = bf16[256,1024]{1,0:T(8,128)(2,1)S(1)} collective-permute-done((bf16[256,1024]{1,0:T(8,128)(2,1)}, bf16[256,1024]{1,0:T(8,128)(2,1)S(1)}, u32[]{:S(2)}, u32[]{:S(2)}) %collective-permute-start.1) | collective-permute-done | bytes 524320 | tf_op jit(solution)/shard_map/ppermute | solution.py:20
  32.7 1.5 %collective-permute-done.2 = bf16[256,1024]{1,0:T(8,128)(2,1)S(1)} collective-permute-done((bf16[256,1024]{1,0:T(8,128)(2,1)S(1)}, bf16[256,1024]{1,0:T(8,128)(2,1)S(1)}, u32[]{:S(2)}, u32[]{:S(2)}) %collective-permute-start.2) | collective-permute-done | bytes 524320 | tf_op jit(solution)/shard_map/ppermute | solution.py:20
  34.3 1.4 %pad_maximum_fusion.kv_ref = bf16[896,1024]{1,0:T(8,128)(2,1)} fusion(bf16[256,1024]{1,0:T(8,128)(2,1)S(1)} %collective-permute-done.2, bf16[384,512]{1,0:T(8,128)(2,1)S(1)} %get-tuple-element.28, bf16[384,512]{1,0:T(8,128)(2,1)S(1)} %get-tuple-element.27, bf16[256,1024]{1,0:T(8,128)(2,1)S(1)} %collective-permute-done.1), kind=kLoop, calls=%fused_computation | loop fusion | flops 7340032 | bytes 3670016 | tf_op jit(solution)/shard_map/concatenate | solution.py:203
  35.7 8.2 %shard_map.28.att_ref = f32[384,512]{1,0:T(8,128)} custom-call(s32[3]{0:T(128)} %subtract_clamp_fusion.rel_ref, s32[9]{0:T(128)} %compare_convert_fusion.1.allow_ref, bf16[384,512]{1,0:T(8,128)(2,1)} %slice_bitcast_fusion.5.q_ref, bf16[896,1024]{1,0:T(8,128)(2,1)} %pad_maximum_fusion.kv_ref), custom_call_target="tpu_custom_call" | custom-call | tf_op jit(solution)/shard_map/pallas_call | solution.py:140
  44.0 1.3 %multiply_reduce_fusion = (f32[384]{0:T(512)S(1)}, f32[384]{0:T(512)S(1)}) fusion(f32[384,512]{1,0:T(8,128)} %shard_map.28.att_ref, bf16[2,384,512]{2,1,0:T(8,128)(2,1)S(1)} %get-tuple-element.16), kind=kLoop, calls=%fused_computation.15 | loop fusion | flops 982272 | bytes 1182720 | tf_op jit(solution)/shard_map/reduce_sum | solution.py:162
  45.3 0.6 collective-permute-start.3
  45.9 3.1 %collective-permute-done.3 = f32[2,384]{1,0:T(2,128)S(1)} collective-permute-done((f32[2,384]{1,0:T(2,128)S(1)}, f32[2,384]{1,0:T(2,128)S(1)}, u32[]{:S(2)}, u32[]{:S(2)}) %collective-permute-start.3) | collective-permute-done | bytes 3104 | tf_op jit(solution)/shard_map/ppermute | solution.py:24
  49.0 1.6 %collective-permute-start.4 = (f32[2,384]{1,0:T(2,128)S(1)}, f32[2,384]{1,0:T(2,128)S(1)}, u32[]{:S(2)}, u32[]{:S(2)}) collective-permute-start(f32[2,384]{1,0:T(2,128)S(1)} %fusion.9), channel_id=1, source_target_pairs={{0,1},{1,0},{2,3},{3,2},{4,5},{5,4},{6,7},{7,6},{8,9},{9,8},{10,11... | collective-permute-start | bytes 9224 | tf_op jit(solution)/shard_map/ppermute | solution.py:210
  50.6 2.1 %collective-permute-done.4 = f32[2,384]{1,0:T(2,128)S(1)} collective-permute-done((f32[2,384]{1,0:T(2,128)S(1)}, f32[2,384]{1,0:T(2,128)S(1)}, u32[]{:S(2)}, u32[]{:S(2)}) %collective-permute-start.4) | collective-permute-done | bytes 3104 | tf_op jit(solution)/shard_map/ppermute | solution.py:210
  52.7 2.1 %fusion.2 = (bf16[384,512]{1,0:T(8,128)(2,1)}, bf16[1,384,512]{2,1,0:T(8,128)(2,1)S(1)}) fusion(f32[384]{0:T(512)S(1)} %get-tuple-element.11, f32[384]{0:T(512)S(1)} %get-tuple-element.12, bf16[2,384,512]{2,1,0:T(8,128)(2,1)S(1)} %get-tuple-element.16, f32[384,512]{1,0:T(8,128)} %shard_map.28.att_ref), kind=kLoop, calls=%fused_computation.7 | loop fusion | flops 1376256 | bytes 1969152 | tf_op jit(solution)/shard_map/convert_element_type | solution.py:167
  54.9 13.8 %shard_map.29 = (f32[384,512]{1,0:T(8,128)}, f32[896,1024]{1,0:T(8,128)}) custom-call(s32[3]{0:T(128)} %subtract_clamp_fusion.rel_ref, s32[9]{0:T(128)} %compare_convert_fusion.1.allow_ref, bf16[384,512]{1,0:T(8,128)(2,1)} %slice_bitcast_fusion.5.q_ref, bf16[384,512]{1,0:T(8,128)(2,1)} %get-tuple-element.21.up_ref, f32[384,512]{1,0:T(8,128)} %shard_map.28.att_ref, ...), custom_call_target="tpu_custom_call" | custom-call | tf_op jit(solution)/shard_map/pallas_call | solution.py:140
  68.6 2.3 %convert.13 = bf16[896,1024]{1,0:T(8,128)(2,1)S(1)} convert(f32[896,1024]{1,0:T(8,128)} %get-tuple-element.7) | non-fusion elementwise | flops 917504 | bytes 5505024 | tf_op jit(solution)/shard_map/convert.8
  71.0 0.0 copy-start.1
  71.0 0.1 fusion.10
  71.0 2.1 %collective-permute-start.5 = (bf16[256,1024]{1,0:T(8,128)(2,1)S(1)}, bf16[256,1024]{1,0:T(8,128)(2,1)S(1)}, u32[]{:S(2)}, u32[]{:S(2)}) collective-permute-start(bf16[256,1024]{1,0:T(8,128)(2,1)S(1)} %get-tuple-element.17), channel_id=1, source_target_pairs={{0,2},{2,4},{4,6},{6,8},{8,10},{10,12},{12,14},{1,3},{3,5},{5,7},{... | collective-permute-start | bytes 1572872 | tf_op jit(solution)/shard_map/ppermute | solution.py:20
  73.1 3.6 %collective-permute-start.6 = (bf16[256,1024]{1,0:T(8,128)(2,1)S(1)}, bf16[256,1024]{1,0:T(8,128)(2,1)S(1)}, u32[]{:S(2)}, u32[]{:S(2)}) collective-permute-start(bf16[256,1024]{1,0:T(8,128)(2,1)S(1)} %get-tuple-element.18), channel_id=1, source_target_pairs={{2,0},{4,2},{6,4},{8,6},{10,8},{12,10},{14,12},{3,1},{5,3},{7,5},{... | collective-permute-start | bytes 1572872 | tf_op jit(solution)/shard_map/ppermute | solution.py:20
  76.7 0.0 copy-done.1
  76.8 0.1 convert_bitcast_fusion.1
  76.8 4.9 %collective-permute-done.5 = bf16[256,1024]{1,0:T(8,128)(2,1)S(1)} collective-permute-done((bf16[256,1024]{1,0:T(8,128)(2,1)S(1)}, bf16[256,1024]{1,0:T(8,128)(2,1)S(1)}, u32[]{:S(2)}, u32[]{:S(2)}) %collective-permute-start.5) | collective-permute-done | bytes 524320 | tf_op jit(solution)/shard_map/ppermute | solution.py:20
  81.7 1.8 %collective-permute-done.6 = bf16[256,1024]{1,0:T(8,128)(2,1)S(1)} collective-permute-done((bf16[256,1024]{1,0:T(8,128)(2,1)S(1)}, bf16[256,1024]{1,0:T(8,128)(2,1)S(1)}, u32[]{:S(2)}, u32[]{:S(2)}) %collective-permute-start.6) | collective-permute-done | bytes 524320 | tf_op jit(solution)/shard_map/ppermute | solution.py:20
  83.4 1.7 %add_convert_fusion = bf16[384,1024]{1,0:T(8,128)(2,1)S(1)} fusion(f32[896,1024]{1,0:T(8,128)} %get-tuple-element.7, bf16[256,1024]{1,0:T(8,128)(2,1)S(1)} %collective-permute-done.6, bf16[256,1024]{1,0:T(8,128)(2,1)S(1)} %collective-permute-done.5), kind=kLoop, calls=%fused_computation.2 | loop fusion | flops 1966080 | bytes 3407872 | tf_op jit(solution)/shard_map/convert.6
  85.1 0.1 slice_bitcast_fusion.1
  85.2 0.2 select_bitcast_fusion
  85.4 0.6 collective-permute-start.7
  86.0 19.0 %collective-permute-done.7 = bf16[2,384,512]{2,1,0:T(8,128)(2,1)S(1)} collective-permute-done((bf16[2,384,512]{2,1,0:T(8,128)(2,1)S(1)}, bf16[2,384,512]{2,1,0:T(8,128)(2,1)S(1)}, u32[]{:S(2)}, u32[]{:S(2)}) %collective-permute-start.7) | collective-permute-done | bytes 786464 | tf_op jit(solution)/shard_map/ppermute | solution.py:24
  105.0 1.6 %maximum_select_fusion = bf16[1,2,384,1024]{3,2,1,0:T(8,128)(2,1)} fusion(bf16[1,2,384,512]{3,2,1,0:T(8,128)(2,1)S(1)} %bitcast.31, bf16[1,2,384,512]{3,2,1,0:T(8,128)(2,1)S(1)} %get-tuple-element.19, pred[]{:T(512)S(6)} %eq.14), kind=kLoop, calls=%fused_computation.1 | loop fusion | flops 7077888 | bytes 3145729 | tf_op jit(solution)/shard_map/jit(_where)/select_n | solution.py:236
  (8 shorter events, 0.1 us)
Async XLA Ops:
  0.0 20.7 %copy-start = (bf16[1,2,384,1024]{3,2,1,0:T(8,128)(2,1)S(1)}, bf16[1,2,384,1024]{3,2,1,0:T(8,128)(2,1)}, u32[]{:S(2)}) copy-start(bf16[1,2,384,1024]{3,2,1,0:T(8,128)(2,1)} %param.2) | copy-start | bytes 4718596
  1.3 19.3 %collective-permute-start = (bf16[2,384,512]{2,1,0:T(8,128)(2,1)S(1)}, bf16[2,384,512]{2,1,0:T(8,128)(2,1)S(1)}, u32[]{:S(2)}, u32[]{:S(2)}) collective-permute-start(bf16[2,384,512]{2,1,0:T(8,128)(2,1)S(1)} %dynamic-slice_bitcast_fusion), channel_id=1, source_target_pairs={{0,16},{16,0},{1,17},{17,1},{2,18},{18,2},{3,19},{19,3},{4,20},{20... | collective-permute-start | bytes 2359304 | tf_op jit(solution)/shard_map/ppermute | solution.py:24
  22.0 10.7 %collective-permute-start.1 = (bf16[256,1024]{1,0:T(8,128)(2,1)}, bf16[256,1024]{1,0:T(8,128)(2,1)S(1)}, u32[]{:S(2)}, u32[]{:S(2)}) collective-permute-start(bf16[256,1024]{1,0:T(8,128)(2,1)} %get-tuple-element.25), channel_id=1, source_target_pairs={{0,2},{2,4},{4,6},{6,8},{8,10},{10,12},{12,14},{1,3},{3,5},{5,7},{... | collective-permute-start | bytes 1572872 | tf_op jit(solution)/shard_map/ppermute | solution.py:20
  23.9 10.3 %collective-permute-start.2 = (bf16[256,1024]{1,0:T(8,128)(2,1)S(1)}, bf16[256,1024]{1,0:T(8,128)(2,1)S(1)}, u32[]{:S(2)}, u32[]{:S(2)}) collective-permute-start(bf16[256,1024]{1,0:T(8,128)(2,1)S(1)} %get-tuple-element.26), channel_id=1, source_target_pairs={{2,0},{4,2},{6,4},{8,6},{10,8},{12,10},{14,12},{3,1},{5,3},{7,5},{... | collective-permute-start | bytes 1572872 | tf_op jit(solution)/shard_map/ppermute | solution.py:20
  45.3 3.7 %collective-permute-start.3 = (f32[2,384]{1,0:T(2,128)S(1)}, f32[2,384]{1,0:T(2,128)S(1)}, u32[]{:S(2)}, u32[]{:S(2)}) collective-permute-start(f32[2,384]{1,0:T(2,128)S(1)} %pad_maximum_fusion.4), channel_id=1, source_target_pairs={{0,16},{16,0},{1,17},{17,1},{2,18},{18,2},{3,19},{19,3},{4,20},{20... | collective-permute-start | bytes 9224 | tf_op jit(solution)/shard_map/ppermute | solution.py:24
  49.0 3.7 %collective-permute-start.4 = (f32[2,384]{1,0:T(2,128)S(1)}, f32[2,384]{1,0:T(2,128)S(1)}, u32[]{:S(2)}, u32[]{:S(2)}) collective-permute-start(f32[2,384]{1,0:T(2,128)S(1)} %fusion.9), channel_id=1, source_target_pairs={{0,1},{1,0},{2,3},{3,2},{4,5},{5,4},{6,7},{7,6},{8,9},{9,8},{10,11... | collective-permute-start | bytes 9224 | tf_op jit(solution)/shard_map/ppermute | solution.py:210
  71.0 5.8 %copy-start.1 = (f32[384,512]{1,0:T(8,128)S(1)}, f32[384,512]{1,0:T(8,128)}, u32[]{:S(2)}) copy-start(f32[384,512]{1,0:T(8,128)} %get-tuple-element.8) | copy-start | bytes 2359300
  71.0 10.6 %collective-permute-start.5 = (bf16[256,1024]{1,0:T(8,128)(2,1)S(1)}, bf16[256,1024]{1,0:T(8,128)(2,1)S(1)}, u32[]{:S(2)}, u32[]{:S(2)}) collective-permute-start(bf16[256,1024]{1,0:T(8,128)(2,1)S(1)} %get-tuple-element.17), channel_id=1, source_target_pairs={{0,2},{2,4},{4,6},{6,8},{8,10},{10,12},{12,14},{1,3},{3,5},{5,7},{... | collective-permute-start | bytes 1572872 | tf_op jit(solution)/shard_map/ppermute | solution.py:20
  73.1 10.3 %collective-permute-start.6 = (bf16[256,1024]{1,0:T(8,128)(2,1)S(1)}, bf16[256,1024]{1,0:T(8,128)(2,1)S(1)}, u32[]{:S(2)}, u32[]{:S(2)}) collective-permute-start(bf16[256,1024]{1,0:T(8,128)(2,1)S(1)} %get-tuple-element.18), channel_id=1, source_target_pairs={{2,0},{4,2},{6,4},{8,6},{10,8},{12,10},{14,12},{3,1},{5,3},{7,5},{... | collective-permute-start | bytes 1572872 | tf_op jit(solution)/shard_map/ppermute | solution.py:20
  85.4 19.6 %collective-permute-start.7 = (bf16[2,384,512]{2,1,0:T(8,128)(2,1)S(1)}, bf16[2,384,512]{2,1,0:T(8,128)(2,1)S(1)}, u32[]{:S(2)}, u32[]{:S(2)}) collective-permute-start(bf16[2,384,512]{2,1,0:T(8,128)(2,1)S(1)} %get-tuple-element.20), channel_id=1, source_target_pairs={{0,16},{16,0},{1,17},{17,1},{2,18},{18,2},{3,19},{19,3},{4,20},{20... | collective-permute-start | bytes 2359304 | tf_op jit(solution)/shard_map/ppermute | solution.py:24

commit v5 on v3

--- a/solution.py
+++ b/solution.py
@@ -127,9 +127,10 @@
     rel_starts, allowed = window_plan(doc_units, seq_place, unit_count, halo_units)
 
     def row_total(sums_pair):
-        sums = jnp.stack(sums_pair)
-        sums = sums + sec_swap(sums)
-        sums = sums + lax.ppermute(sums, "mp", [(0, 1), (1, 0)])
+        gathered = lax.all_gather(jnp.stack(sums_pair), ("sec", "mp"))
+        sums = gathered[0]
+        for more in range(1, gathered.shape[0]):
+            sums = sums + gathered[more]
         return sums[0], sums[1]
 
     grad_q, normed, total = attention_grads(

time: 97.2 us -> 101 us (1.039)
  blocking collectives: 0 us -> 8.15 us
  waiting for transfers between devices: 47.9 us -> 44.7 us
  starting transfers between devices: 12.3 us -> 10.2 us
    all_gather x0 -> x1, blocking collectives: none -> 8.15 us  [row_total(): gathered = lax.all_gather(jnp.stack(sums_pair), ('sec', 'mp'))]
    ppermute x3 -> x2, waiting for transfers between devices: 38.7 us -> 35.6 us  [sec_swap(): return lax.ppermute(value, 'sec', [(0, 1), (1, 0)])]
    ppermute x1 -> x0, starting transfers between devices: 1.58 us -> none  [row_total(): sums = sums + lax.ppermute(sums, 'mp', [(0, 1), (1, 0)])]
    another operation x4 -> x3, other arithmetic: 2.1 us -> 2.09 us
  transfers between devices with their start and end apart: 8 -> 6, of which waited for: 7 -> 5; matrix products, arithmetic and copies ran while one was open for 9% -> 7% of each run, Pallas kernels for 0% -> 0%
where the time goes in v5:
time: 101 us; the launch traced here: 100 us
  waiting for transfers between devices  44.7 us (44%)
  local copies, waits for them, and re-layouts  16.1 us (16%)
  other arithmetic  12.6 us (12%)
  starting transfers between devices  10.2 us (10%)
  blocking collectives  8.15 us (8%)
  matrix products  6.19 us (6%)
  between operations  2.28 us (2%)
    ppermute x2, waiting for transfers between devices, sec_swap(): return lax.ppermute(value, 'sec', [(0, 1), (1, 0)])  35.6 us
    ppermute x4, waiting for transfers between devices, seq_shift(): lax.ppermute(value, 'seq', [(source, source + steps) for source in range(...  9.13 us
    ppermute x4, starting transfers between devices, seq_shift(): lax.ppermute(value, 'seq', [(source, source + steps) for source in range(...  8.96 us
    all_gather x1, blocking collectives, row_total(): gathered = lax.all_gather(jnp.stack(sums_pair), ('sec', 'mp'))  8.15 us
    unnamed x46, local copies, waits for them, and re-layouts  6.15 us
    another operation x3, other arithmetic  2.09 us
  transfers between devices with their start and end apart: 6, of which 5 were waited for; matrix products, arithmetic and copies ran while one was open for 7% of the time, Pallas kernels for 0%

profile of v5, /device:TPU:18, one launch (start us, length us, event | category | flops | bytes accessed | tf_op | source)
XLA Modules:
  0.0 100.3 jit_solution(5036439623805423193)
XLA Ops:
  0.0 1.5 %constant_dynamic-slice_fusion.6 = (bf16[1,2,384,512]{3,2,1,0:T(8,128)(2,1)S(1)}, bf16[1,2,384,512]{3,2,1,0:T(8,128)(2,1)S(1)}) fusion(bf16[1,2,384,1024]{3,2,1,0:T(8,128)(2,1)} %param.2, s32[]{:T(128)S(6)} %select_n.91, s32[]{:T(128)S(6)} %select_n.90), kind=kLoop, calls=%fused_computation.67 | loop fusion | bytes 3145736 | tf_op jit(solution)/shard_map/dynamic_slice | solution.py:117
  1.5 0.4 copy.29
  1.9 0.6 collective-permute-start
  2.6 0.2 fusion.25
  2.8 0.4 copy.30
  3.7 17.6 %collective-permute-done = bf16[2,384,512]{1,2,0:T(8,128)(2,1)} collective-permute-done((bf16[2,384,512]{1,2,0:T(8,128)(2,1)S(1)}, bf16[2,384,512]{1,2,0:T(8,128)(2,1)}, u32[]{:S(2)}, u32[]{:S(2)}) %collective-permute-start) | collective-permute-done | bytes 786464 | tf_op jit(solution)/shard_map/ppermute | solution.py:22
  21.3 1.3 %bitcast_select_fusion.1 = (bf16[2,384,512]{1,2,0:T(8,128)(2,1)S(1)}, bf16[2,384,512]{1,2,0:T(8,128)(2,1)S(1)}) fusion(bf16[2,384,512]{1,2,0:T(8,128)(2,1)} %collective-permute-done, bf16[1,2,384,512]{2,3,1,0:T(8,128)(2,1)S(1)} %copy.30, pred[]{:T(512)S(6)} %eq.11), kind=kLoop, calls=%fused_computation.40 | loop fusion | flops 786432 | bytes 3145729 | tf_op jit(solution)/shard_map/jit(_where)/select_n | solution.py:120
  22.7 1.1 %fusion.19 = (bf16[256,1024]{0,1:T(8,128)(2,1)}, bf16[256,1024]{0,1:T(8,128)(2,1)}) fusion(bf16[384,512]{0,1:T(8,128)(2,1)S(1)} %get-tuple-element.35, bf16[384,512]{0,1:T(8,128)(2,1)S(1)} %get-tuple-element.36), kind=kLoop, calls=%fused_computation.48 | loop fusion | flops 2097152 | bytes 1835008 | tf_op jit(solution)/shard_map/concatenate | solution.py:122
  23.7 1.9 %collective-permute-start.2 = (bf16[256,1024]{0,1:T(8,128)(2,1)}, bf16[256,1024]{0,1:T(8,128)(2,1)}, u32[]{:S(2)}, u32[]{:S(2)}) collective-permute-start(bf16[256,1024]{0,1:T(8,128)(2,1)} %get-tuple-element.34), channel_id=1, source_target_pairs={{2,0},{4,2},{6,4},{8,6},{10,8},{12,10},{14,12},{3,1},{5,3},{7,5},{... | collective-permute-start | bytes 1572872 | tf_op jit(solution)/shard_map/ppermute | solution.py:18
  25.7 2.4 %collective-permute-start.1 = (bf16[256,1024]{0,1:T(8,128)(2,1)}, bf16[256,1024]{0,1:T(8,128)(2,1)}, u32[]{:S(2)}, u32[]{:S(2)}) collective-permute-start(bf16[256,1024]{0,1:T(8,128)(2,1)} %get-tuple-element.33), channel_id=1, source_target_pairs={{0,2},{2,4},{4,6},{6,8},{8,10},{10,12},{12,14},{1,3},{3,5},{5,7},{... | collective-permute-start | bytes 1572872 | tf_op jit(solution)/shard_map/ppermute | solution.py:18
  28.1 0.6 fusion.37
  30.6 0.8 slice_convert_fusion
  31.4 0.3 reshape.314
  31.7 1.6 %reshape_squeeze.3 = bf16[3,128,8,64]{1,0,3,2:T(4,128)(2,1)S(1)} reshape(bf16[1,384,512]{1,2,0:T(8,128)(2,1)} %get-tuple-element.32) | data formatting | bytes 786432 | tf_op jit(solution)/shard_map/reshape;squeeze | solution.py:57
  33.4 3.1 %collective-permute-done.1 = bf16[256,1024]{0,1:T(8,128)(2,1)} collective-permute-done((bf16[256,1024]{0,1:T(8,128)(2,1)}, bf16[256,1024]{0,1:T(8,128)(2,1)}, u32[]{:S(2)}, u32[]{:S(2)}) %collective-permute-start.1) | collective-permute-done | bytes 524320 | tf_op jit(solution)/shard_map/ppermute | solution.py:18
  36.5 1.4 %pad_maximum_fusion = bf16[896,1024]{0,1:T(8,128)(2,1)S(1)} fusion(bf16[256,1024]{0,1:T(8,128)(2,1)} %collective-permute-done.2, bf16[384,512]{0,1:T(8,128)(2,1)S(1)} %get-tuple-element.36, bf16[384,512]{0,1:T(8,128)(2,1)S(1)} %get-tuple-element.35, bf16[256,1024]{0,1:T(8,128)(2,1)} %collective-permute-done.1), kind=kLoop, calls=%fused_computation.14 | loop fusion | flops 7340032 | bytes 3670016 | tf_op jit(solution)/shard_map/concatenate | solution.py:125
  38.4 0.8 fusion.20
  39.2 1.7 %fusion.38 = (f32[3,8,128]{2,1,0:T(8,128)S(1)}, f32[3,8,128,384]{3,2,1,0:T(8,128)S(1)}) fusion(f32[3,8,128,384]{3,2,1,0:T(8,128)S(1)} %fusion.20, pred[3,384]{1,0:T(4,128)(4,1)S(1)} %bitcast.113), kind=kOutput, calls=%fused_computation.100 | output fusion | flops 7078271 | bytes 9450624 | tf_op jit(solution)/shard_map/sub | solution.py:66
  41.0 0.6 fusion.5
  41.6 1.5 %copy-done.1 = f32[3,8,128,384]{3,2,1,0:T(8,128)} copy-done((f32[3,8,128,384]{3,2,1,0:T(8,128)}, f32[3,8,128,384]{3,2,1,0:T(8,128)S(1)}, u32[]{:S(2)}) %copy-start.1) | copy-done | bytes 4718616
  43.1 1.2 %multiply_reduce_fusion.2 = (f32[3,128]{1,0:T(4,128)S(1)}, f32[3,128]{1,0:T(4,128)S(1)}, f32[3,128,8,64]{1,3,2,0:T(8,128)S(1)}) fusion(f32[3,128,8,64]{1,0,3,2:T(4,128)S(1)} %reshape.314, bf16[3,8,128,384]{3,2,1,0:T(8,128)(2,1)S(1)} %fusion.5, bf16[1,384,8,64]{1,3,2,0:T(8,128)(2,1)S(1)} %bitcast.102, bf16[1,384,8,64]{1,3,2,0:T(8,128)(2,1)S(1)} %bitcast.104, ...), kind=kOutput, calls=%fused_computation.46 | convolution fusion | flops 152960256 | bytes 5114880 | tf_op jit(solution)/shard_map/jhqk,jkhd->jqhd/dot_general | solution.py:69
  44.3 0.9 copy-done.7
  45.2 0.5 copy.36
  45.7 1.3 %reshape.313 = f32[1,384,512]{1,2,0:T(8,128)} reshape(f32[3,128,8,64]{1,0,3,2:T(4,128)S(1)} %copy.36) | data formatting | bytes 1572864 | tf_op jit(solution)/shard_map/reshape | solution.py:70
  47.1 8.1 %all-gather.1 = f32[4,2,384]{2,1,0:T(2,128)S(1)} all-gather(f32[1,2,384]{2,1,0:T(2,128)S(1)} %maximum_bitcast_fusion), channel_id=2, replica_groups=mesh['sec'=2,'seq'=8,'mp'=2] {'sec','mp'}, dimensions={0}, use_global_device_ids=true | all-gather | bytes 15360 | tf_op jit(solution)/shard_map/all_gather | solution.py:130
  55.3 1.7 %multiply_reduce_fusion = (f32[3,128,8]{1,2,0:T(8,128)S(1)}, bf16[3,128,8,64]{1,3,2,0:T(8,128)(2,1)S(1)}) fusion(f32[3,128,8,64]{1,3,2,0:T(8,128)} %copy-done.7, f32[3,128]{1,0:T(4,128)S(1)} %bitcast.108, f32[3,128]{1,0:T(4,128)S(1)} %bitcast.106, f32[3,128,8,64]{1,0,3,2:T(4,128)} %copy-done.3), kind=kLoop, calls=%fused_computation.43 | loop fusion | flops 1569792 | bytes 1981440 | tf_op jit(solution)/shard_map/reduce_sum | solution.py:81
  57.0 0.6 fusion.39
  57.6 1.7 %copy-done.2 = f32[3,8,128,384]{3,2,1,0:T(8,128)S(1)} copy-done((f32[3,8,128,384]{3,2,1,0:T(8,128)S(1)}, f32[3,8,128,384]{3,2,1,0:T(8,128)}, u32[]{:S(2)}) %copy-start.2) | copy-done | bytes 4718616
  59.6 1.9 %multiply_convert_fusion = bf16[3,8,128,384]{3,2,1,0:T(8,128)(2,1)S(1)} fusion(f32[3,8,128]{2,1,0:T(8,128)S(1)} %bitcast.107, bf16[3,128,8,64]{1,3,2,0:T(8,128)(2,1)S(1)} %get-tuple-element.12, f32[3,8,128,384]{3,2,1,0:T(8,128)S(1)} %copy-done.2, f32[3,8,128]{2,1,0:T(8,128)S(1)} %get-tuple-element.40, bf16[1,384,8,64]{1,3,2,0:T(8,128)(2,1)S(1)} %bitcast.103, ...), kind=kOutput, calls=%fused_computation.5 | convolution fusion | flops 158072832 | bytes 8675328 | tf_op jit(solution)/shard_map/jqhd,jkhd->jhqk/dot_general | solution.py:83
  61.5 0.6 fusion.22
  62.1 0.2 broadcast_in_dim.36
  62.4 0.3 fusion.9
  62.7 0.3 fusion.17
  63.1 0.2 convert.13
  63.3 1.6 %copy-done = f32[896,1024]{0,1:T(8,128)} copy-done((f32[896,1024]{0,1:T(8,128)}, f32[896,1024]{0,1:T(8,128)S(1)}, u32[]{:S(2)}) %copy-start) | copy-done | bytes 3670040
  64.9 1.9 %collective-permute-start.4 = (bf16[256,1024]{0,1:T(8,128)(2,1)S(1)}, bf16[256,1024]{0,1:T(8,128)(2,1)S(1)}, u32[]{:S(2)}, u32[]{:S(2)}) collective-permute-start(bf16[256,1024]{0,1:T(8,128)(2,1)S(1)} %get-tuple-element.14), channel_id=1, source_target_pairs={{2,0},{4,2},{6,4},{8,6},{10,8},{12,10},{14,12},{3,1},{5,3},{7,5},{... | collective-permute-start | bytes 1572872 | tf_op jit(solution)/shard_map/ppermute | solution.py:18
  66.8 2.7 %collective-permute-start.3 = (bf16[256,1024]{0,1:T(8,128)(2,1)S(1)}, bf16[256,1024]{0,1:T(8,128)(2,1)}, u32[]{:S(2)}, u32[]{:S(2)}) collective-permute-start(bf16[256,1024]{0,1:T(8,128)(2,1)S(1)} %get-tuple-element.13), channel_id=1, source_target_pairs={{0,2},{2,4},{4,6},{6,8},{8,10},{10,12},{12,14},{1,3},{3,5},{5,7},{... | collective-permute-start | bytes 1572872 | tf_op jit(solution)/shard_map/ppermute | solution.py:18
  69.6 1.2 %fusion.18 = bf16[3,128,8,64]{1,3,2,0:T(8,128)(2,1)S(1)} fusion(bf16[3,8,128,384]{3,2,1,0:T(8,128)(2,1)S(1)} %multiply_convert_fusion, bf16[1,384,8,64]{1,3,2,0:T(8,128)(2,1)S(1)} %bitcast.95, bf16[1,384,8,64]{1,3,2,0:T(8,128)(2,1)S(1)} %bitcast.97, bf16[1,384,8,64]{1,3,2,0:T(8,128)(2,1)S(1)} %bitcast.93), kind=kOutput, calls=%fused_computation.32 | convolution fusion | flops 152371200 | bytes 3932160 | tf_op jit(solution)/shard_map/jhqk,jkhd->jqhd/dot_general | solution.py:85
  70.8 0.3 copy.35
  71.1 0.3 convert_element_type.73
  71.6 2.0 %collective-permute-done.4 = bf16[256,1024]{0,1:T(8,128)(2,1)S(1)} collective-permute-done((bf16[256,1024]{0,1:T(8,128)(2,1)S(1)}, bf16[256,1024]{0,1:T(8,128)(2,1)S(1)}, u32[]{:S(2)}, u32[]{:S(2)}) %collective-permute-start.4) | collective-permute-done | bytes 524320 | tf_op jit(solution)/shard_map/ppermute | solution.py:18
  73.5 4.1 %collective-permute-done.3 = bf16[256,1024]{0,1:T(8,128)(2,1)} collective-permute-done((bf16[256,1024]{0,1:T(8,128)(2,1)S(1)}, bf16[256,1024]{0,1:T(8,128)(2,1)}, u32[]{:S(2)}, u32[]{:S(2)}) %collective-permute-start.3) | collective-permute-done | bytes 524320 | tf_op jit(solution)/shard_map/ppermute | solution.py:18
  77.6 1.7 %fusion.14 = bf16[384,1024]{0,1:T(8,128)(2,1)S(1)} fusion(f32[896,1024]{0,1:T(8,128)} %copy-done, bf16[256,1024]{0,1:T(8,128)(2,1)S(1)} %collective-permute-done.4, bf16[256,1024]{0,1:T(8,128)(2,1)} %collective-permute-done.3), kind=kLoop, calls=%fused_computation.24 | loop fusion | flops 1966080 | bytes 3407872 | tf_op jit(solution)/shard_map/convert.6
  79.4 0.2 select_bitcast_fusion
  79.6 0.6 collective-permute-start.5
  80.2 18.0 %collective-permute-done.5 = bf16[2,384,512]{1,2,0:T(8,128)(2,1)S(1)} collective-permute-done((bf16[2,384,512]{1,2,0:T(8,128)(2,1)S(1)}, bf16[2,384,512]{1,2,0:T(8,128)(2,1)S(1)}, u32[]{:S(2)}, u32[]{:S(2)}) %collective-permute-start.5) | collective-permute-done | bytes 786464 | tf_op jit(solution)/shard_map/ppermute | solution.py:22
  98.2 0.4 maximum_select_fusion
  98.7 1.6 %copy.37 = bf16[1,2,384,1024]{3,2,1,0:T(8,128)(2,1)} copy(bf16[1,2,384,1024]{2,3,1,0:T(8,128)(2,1)S(1)} %maximum_select_fusion) | data formatting | bytes 3145728 | tf_op jit(solution)/shard_map/jit(_where)/select_n | solution.py:160
  (62 shorter events, 2.0 us)
Async XLA Ops:
  0.0 2.5 %copy-start.20 = (s32[12]{0:T(128)S(1)}, s32[12]{0:T(128)}, u32[]{:S(2)}) copy-start(s32[12]{0:T(128)} %param.3) | copy-start | bytes 148
  1.9 19.5 %collective-permute-start = (bf16[2,384,512]{1,2,0:T(8,128)(2,1)S(1)}, bf16[2,384,512]{1,2,0:T(8,128)(2,1)}, u32[]{:S(2)}, u32[]{:S(2)}) collective-permute-start(bf16[2,384,512]{1,2,0:T(8,128)(2,1)S(1)} %bitcast.98), channel_id=1, source_target_pairs={{0,16},{16,0},{1,17},{17,1},{2,18},{18,2},{3,19},{19,3},{4,20},{20... | collective-permute-start | bytes 2359304 | tf_op jit(solution)/shard_map/ppermute | solution.py:22
  23.7 9.6 %collective-permute-start.2 = (bf16[256,1024]{0,1:T(8,128)(2,1)}, bf16[256,1024]{0,1:T(8,128)(2,1)}, u32[]{:S(2)}, u32[]{:S(2)}) collective-permute-start(bf16[256,1024]{0,1:T(8,128)(2,1)} %get-tuple-element.34), channel_id=1, source_target_pairs={{2,0},{4,2},{6,4},{8,6},{10,8},{12,10},{14,12},{3,1},{5,3},{7,5},{... | collective-permute-start | bytes 1572872 | tf_op jit(solution)/shard_map/ppermute | solution.py:18
  25.7 10.8 %collective-permute-start.1 = (bf16[256,1024]{0,1:T(8,128)(2,1)}, bf16[256,1024]{0,1:T(8,128)(2,1)}, u32[]{:S(2)}, u32[]{:S(2)}) collective-permute-start(bf16[256,1024]{0,1:T(8,128)(2,1)} %get-tuple-element.33), channel_id=1, source_target_pairs={{0,2},{2,4},{4,6},{6,8},{8,10},{10,12},{12,14},{1,3},{3,5},{5,7},{... | collective-permute-start | bytes 1572872 | tf_op jit(solution)/shard_map/ppermute | solution.py:18
  31.7 11.4 %copy-start.3 = (f32[3,128,8,64]{1,0,3,2:T(4,128)}, f32[3,128,8,64]{1,0,3,2:T(4,128)S(1)}, u32[]{:S(2)}) copy-start(f32[3,128,8,64]{1,0,3,2:T(4,128)S(1)} %reshape.314) | copy-start | bytes 2359300
  33.3 5.0 %copy-start.4 = (bf16[3,128,8,64]{1,0,3,2:T(4,128)(2,1)}, bf16[3,128,8,64]{1,0,3,2:T(4,128)(2,1)S(1)}, u32[]{:S(2)}) copy-start(bf16[3,128,8,64]{1,0,3,2:T(4,128)(2,1)S(1)} %reshape_squeeze.3) | copy-start | bytes 1179652
  38.1 1.0 %copy-start.8 = (bf16[384,512]{0,1:T(8,128)(2,1)}, bf16[384,512]{0,1:T(8,128)(2,1)S(1)}, u32[]{:S(2)}) copy-start(bf16[384,512]{0,1:T(8,128)(2,1)S(1)} %get-tuple-element.26) | copy-start | bytes 1179652
  38.2 1.0 %copy-start.10 = (bf16[384,512]{0,1:T(8,128)(2,1)}, bf16[384,512]{0,1:T(8,128)(2,1)S(1)}, u32[]{:S(2)}) copy-start(bf16[384,512]{0,1:T(8,128)(2,1)S(1)} %get-tuple-element.27) | copy-start | bytes 1179652
  38.2 1.0 %copy-start.12 = (bf16[384,512]{0,1:T(8,128)(2,1)}, bf16[384,512]{0,1:T(8,128)(2,1)S(1)}, u32[]{:S(2)}) copy-start(bf16[384,512]{0,1:T(8,128)(2,1)S(1)} %get-tuple-element.28) | copy-start | bytes 1179652
  38.3 4.8 %copy-start.14 = (bf16[384,512]{0,1:T(8,128)(2,1)}, bf16[384,512]{0,1:T(8,128)(2,1)S(1)}, u32[]{:S(2)}) copy-start(bf16[384,512]{0,1:T(8,128)(2,1)S(1)} %get-tuple-element.23) | copy-start | bytes 1179652
  38.3 4.8 %copy-start.16 = (bf16[384,512]{0,1:T(8,128)(2,1)}, bf16[384,512]{0,1:T(8,128)(2,1)S(1)}, u32[]{:S(2)}) copy-start(bf16[384,512]{0,1:T(8,128)(2,1)S(1)} %get-tuple-element.24) | copy-start | bytes 1179652
  38.3 4.8 %copy-start.18 = (bf16[384,512]{0,1:T(8,128)(2,1)}, bf16[384,512]{0,1:T(8,128)(2,1)S(1)}, u32[]{:S(2)}) copy-start(bf16[384,512]{0,1:T(8,128)(2,1)S(1)} %get-tuple-element.25) | copy-start | bytes 1179652
  40.9 2.1 %copy-start.1 = (f32[3,8,128,384]{3,2,1,0:T(8,128)}, f32[3,8,128,384]{3,2,1,0:T(8,128)S(1)}, u32[]{:S(2)}) copy-start(f32[3,8,128,384]{3,2,1,0:T(8,128)S(1)} %get-tuple-element.41) | copy-start | bytes 14155780
  44.3 0.9 copy-start.7
  57.0 2.3 %copy-start.2 = (f32[3,8,128,384]{3,2,1,0:T(8,128)S(1)}, f32[3,8,128,384]{3,2,1,0:T(8,128)}, u32[]{:S(2)}) copy-start(f32[3,8,128,384]{3,2,1,0:T(8,128)} %copy-done.1) | copy-start | bytes 14155780
  57.0 2.4 %copy-start.15 = (bf16[384,512]{0,1:T(8,128)(2,1)S(1)}, bf16[384,512]{0,1:T(8,128)(2,1)}, u32[]{:S(2)}) copy-start(bf16[384,512]{0,1:T(8,128)(2,1)} %copy-done.14) | copy-start | bytes 1179652
  57.0 2.5 %copy-start.17 = (bf16[384,512]{0,1:T(8,128)(2,1)S(1)}, bf16[384,512]{0,1:T(8,128)(2,1)}, u32[]{:S(2)}) copy-start(bf16[384,512]{0,1:T(8,128)(2,1)} %copy-done.16) | copy-start | bytes 1179652
  57.0 2.6 %copy-start.19 = (bf16[384,512]{0,1:T(8,128)(2,1)S(1)}, bf16[384,512]{0,1:T(8,128)(2,1)}, u32[]{:S(2)}) copy-start(bf16[384,512]{0,1:T(8,128)(2,1)} %copy-done.18) | copy-start | bytes 1179652
  59.6 1.9 %copy-start.5 = (bf16[3,128,8,64]{1,0,3,2:T(4,128)(2,1)S(1)}, bf16[3,128,8,64]{1,0,3,2:T(4,128)(2,1)}, u32[]{:S(2)}) copy-start(bf16[3,128,8,64]{1,0,3,2:T(4,128)(2,1)} %copy-done.4) | copy-start | bytes 1179652
  63.0 1.8 %copy-start = (f32[896,1024]{0,1:T(8,128)}, f32[896,1024]{0,1:T(8,128)S(1)}, u32[]{:S(2)}) copy-start(f32[896,1024]{0,1:T(8,128)S(1)} %fusion.17) | copy-start | bytes 11010052
  63.0 6.5 %copy-start.9 = (bf16[384,512]{0,1:T(8,128)(2,1)S(1)}, bf16[384,512]{0,1:T(8,128)(2,1)}, u32[]{:S(2)}) copy-start(bf16[384,512]{0,1:T(8,128)(2,1)} %copy-done.8) | copy-start | bytes 1179652
  63.1 6.5 %copy-start.11 = (bf16[384,512]{0,1:T(8,128)(2,1)S(1)}, bf16[384,512]{0,1:T(8,128)(2,1)}, u32[]{:S(2)}) copy-start(bf16[384,512]{0,1:T(8,128)(2,1)} %copy-done.10) | copy-start | bytes 1179652
  63.1 6.5 %copy-start.13 = (bf16[384,512]{0,1:T(8,128)(2,1)S(1)}, bf16[384,512]{0,1:T(8,128)(2,1)}, u32[]{:S(2)}) copy-start(bf16[384,512]{0,1:T(8,128)(2,1)} %copy-done.12) | copy-start | bytes 1179652
  64.9 8.6 %collective-permute-start.4 = (bf16[256,1024]{0,1:T(8,128)(2,1)S(1)}, bf16[256,1024]{0,1:T(8,128)(2,1)S(1)}, u32[]{:S(2)}, u32[]{:S(2)}) collective-permute-start(bf16[256,1024]{0,1:T(8,128)(2,1)S(1)} %get-tuple-element.14), channel_id=1, source_target_pairs={{2,0},{4,2},{6,4},{8,6},{10,8},{12,10},{14,12},{3,1},{5,3},{7,5},{... | collective-permute-start | bytes 1572872 | tf_op jit(solution)/shard_map/ppermute | solution.py:18
  66.8 4.6 %copy-start.6 = (f32[1,384,512]{1,2,0:T(8,128)S(1)}, f32[1,384,512]{1,2,0:T(8,128)}, u32[]{:S(2)}) copy-start(f32[1,384,512]{1,2,0:T(8,128)} %reshape.313) | copy-start | bytes 2359300
  66.8 10.7 %collective-permute-start.3 = (bf16[256,1024]{0,1:T(8,128)(2,1)S(1)}, bf16[256,1024]{0,1:T(8,128)(2,1)}, u32[]{:S(2)}, u32[]{:S(2)}) collective-permute-start(bf16[256,1024]{0,1:T(8,128)(2,1)S(1)} %get-tuple-element.13), channel_id=1, source_target_pairs={{0,2},{2,4},{4,6},{6,8},{8,10},{10,12},{12,14},{1,3},{3,5},{5,7},{... | collective-permute-start | bytes 1572872 | tf_op jit(solution)/shard_map/ppermute | solution.py:18
  79.6 18.6 %collective-permute-start.5 = (bf16[2,384,512]{1,2,0:T(8,128)(2,1)S(1)}, bf16[2,384,512]{1,2,0:T(8,128)(2,1)S(1)}, u32[]{:S(2)}, u32[]{:S(2)}) collective-permute-start(bf16[2,384,512]{1,2,0:T(8,128)(2,1)S(1)} %get-tuple-element.18), channel_id=1, source_target_pairs={{0,16},{16,0},{1,17},{17,1},{2,18},{18,2},{3,19},{19,3},{4,20},{20... | collective-permute-start | bytes 2359304 | tf_op jit(solution)/shard_map/ppermute | solution.py:22

commit v6 on v3

--- a/solution.py
+++ b/solution.py
@@ -1,6 +1,7 @@
 import jax
 import jax.numpy as jnp
 from jax import lax
+from jax.experimental.layout import Layout, with_layout_constraint
 from jax.sharding import PartitionSpec as P
 
 UNIT = 128
@@ -155,7 +156,9 @@
     kv_pair = jnp.stack([grad_k, grad_v])
     qn_pair = jnp.stack([grad_q.astype(jnp.bfloat16), normed.astype(jnp.bfloat16)])
     keep_pair = jnp.where(is_first, kv_pair, qn_pair)
-    back = sec_swap(jnp.where(is_first, qn_pair, kv_pair))
+    leaving = with_layout_constraint(jnp.where(is_first, qn_pair, kv_pair), Layout((0, 1, 2)))
+    keep_pair = with_layout_constraint(keep_pair, Layout((0, 1, 2)))
+    back = sec_swap(leaving)
     result = jnp.where(
         is_first,
         jnp.concatenate([keep_pair, back], axis=2),

time: 97.2 us -> 121 us (1.24)
  local copies, waits for them, and re-layouts: 15.2 us -> 32.9 us
  matrix products: 6.2 us -> 10.2 us
  other arithmetic: 12.7 us -> 15.6 us
    dynamic_slice x2 -> x8, local copies, waits for them, and re-layouts: 0.26 us -> 10.6 us  [windows(): lax.dynamic_slice_in_dim(near, rel_starts[j] * UNIT, window, 0)]
    reshape x0 -> x2, local copies, waits for them, and re-layouts: none -> 5.18 us  [the longest x1 3.13 us: attention_grads(): grad_vw.reshape(unit_count, window, head_cols)]
    reshape x1 -> x2, local copies, waits for them, and re-layouts: 1.32 us -> 4.58 us  [attention_grads(): attended = attended4.reshape(rows, head_cols)]
    dynamic_slice x2 -> x0, local copies, waits for them, and re-layouts: 1.84 us -> none  [per_device(): kept = lax.dynamic_slice_in_dim(local_heads, keep_offset, half, 2)]
    dot_general x1, matrix products: 0.55 us -> 2.18 us  [attention_grads(): jnp.einsum('jhqk,jqhd->jkhd', dscores, q4, preferred_element_type=jnp.flo...]
    select_n x1 -> x0, local copies, waits for them, and re-layouts: 1.63 us -> none  [per_device(): jnp.where(is_first, jnp.concatenate([keep_pair, back], axis=2), jnp.conca...]
    dot_general x1, matrix products: 0.55 us -> 2.01 us  [attention_grads(): jnp.einsum('jhqk,jqhd->jkhd', rounded, up4, preferred_element_type=jnp.fl...]
    unnamed x46 -> x48, local copies, waits for them, and re-layouts: 5.28 us -> 6.39 us
  transfers between devices with their start and end apart: 8 -> 8, of which waited for: 7 -> 6; matrix products, arithmetic and copies ran while one was open for 9% -> 10% of each run, Pallas kernels for 0% -> 0%
where the time goes in v6:
time: 121 us; the launch traced here: 120 us
  waiting for transfers between devices  46.8 us (39%)
  local copies, waits for them, and re-layouts  32.9 us (27%)
  other arithmetic  15.6 us (13%)
  starting transfers between devices  11.9 us (10%)
  matrix products  10.2 us (8%)
  between operations  2.48 us (2%)
    ppermute x3, waiting for transfers between devices, sec_swap(): return lax.ppermute(value, 'sec', [(0, 1), (1, 0)])  38.3 us
    dynamic_slice x8, local copies, waits for them, and re-layouts, windows(): lax.dynamic_slice_in_dim(near, rel_starts[j] * UNIT, window, 0)  10.6 us
    ppermute x4, starting transfers between devices, seq_shift(): lax.ppermute(value, 'seq', [(source, source + steps) for source in range(...  8.63 us
    ppermute x4, waiting for transfers between devices, seq_shift(): lax.ppermute(value, 'seq', [(source, source + steps) for source in range(...  8.53 us
    unnamed x48, local copies, waits for them, and re-layouts  6.39 us
    reshape x2, local copies, waits for them, and re-layouts, attention_grads(): attended = attended4.reshape(rows, head_cols)  4.58 us
    reshape x1, local copies, waits for them, and re-layouts, attention_grads(): grad_vw.reshape(unit_count, window, head_cols)  3.13 us
    another operation x3, other arithmetic  2.91 us
  transfers between devices with their start and end apart: 8, of which 6 were waited for; matrix products, arithmetic and copies ran while one was open for 10% of the time, Pallas kernels for 0%

profile of v6, /device:TPU:18, one launch (start us, length us, event | category | flops | bytes accessed | tf_op | source)
XLA Modules:
  0.0 119.9 jit_solution(10566538920018181512)
XLA Ops:
  0.0 1.2 dynamic-slice_bitcast_fusion
  1.2 0.6 collective-permute-start
  1.8 0.8 reduce-window.8
  3.3 17.2 %collective-permute-done = bf16[2,384,512]{2,1,0:T(8,128)(2,1)S(1)} collective-permute-done((bf16[2,384,512]{2,1,0:T(8,128)(2,1)S(1)}, bf16[2,384,512]{2,1,0:T(8,128)(2,1)S(1)}, u32[]{:S(2)}, u32[]{:S(2)}) %collective-permute-start) | collective-permute-done | bytes 786464 | tf_op jit(solution)/shard_map/ppermute | solution.py:23
  20.5 1.4 %bitcast_select_fusion = (bf16[2,384,512]{2,1,0:T(8,128)(2,1)S(1)}, bf16[2,384,512]{2,1,0:T(8,128)(2,1)S(1)}) fusion(bf16[2,384,512]{2,1,0:T(8,128)(2,1)S(1)} %collective-permute-done, pred[]{:T(512)S(6)} %eq.11, bf16[1,2,384,1024]{3,2,1,0:T(8,128)(2,1)} %param.2, s32[]{:T(128)S(6)} %select_n.82), kind=kLoop, calls=%fused_computation.39 | loop fusion | flops 786432 | bytes 3145733 | tf_op jit(solution)/shard_map/jit(_where)/select_n | solution.py:120
  22.0 1.1 fusion.19
  23.1 1.9 %collective-permute-start.2 = (bf16[256,1024]{1,0:T(8,128)(2,1)}, bf16[256,1024]{1,0:T(8,128)(2,1)}, u32[]{:S(2)}, u32[]{:S(2)}) collective-permute-start(bf16[256,1024]{1,0:T(8,128)(2,1)} %get-tuple-element.32), channel_id=1, source_target_pairs={{2,0},{4,2},{6,4},{8,6},{10,8},{12,10},{14,12},{3,1},{5,3},{7,5},{... | collective-permute-start | bytes 1572872 | tf_op jit(solution)/shard_map/ppermute | solution.py:19
  25.0 2.4 %collective-permute-start.1 = (bf16[256,1024]{1,0:T(8,128)(2,1)}, bf16[256,1024]{1,0:T(8,128)(2,1)}, u32[]{:S(2)}, u32[]{:S(2)}) collective-permute-start(bf16[256,1024]{1,0:T(8,128)(2,1)} %get-tuple-element.31), channel_id=1, source_target_pairs={{0,2},{2,4},{4,6},{6,8},{8,10},{10,12},{12,14},{1,3},{3,5},{5,7},{... | collective-permute-start | bytes 1572872 | tf_op jit(solution)/shard_map/ppermute | solution.py:19
  27.4 0.7 fusion.35
  30.2 0.9 slice_convert_fusion
  33.3 2.6 %collective-permute-done.1 = bf16[256,1024]{1,0:T(8,128)(2,1)} collective-permute-done((bf16[256,1024]{1,0:T(8,128)(2,1)}, bf16[256,1024]{1,0:T(8,128)(2,1)}, u32[]{:S(2)}, u32[]{:S(2)}) %collective-permute-start.1) | collective-permute-done | bytes 524320 | tf_op jit(solution)/shard_map/ppermute | solution.py:19
  35.8 1.4 %pad_maximum_fusion = bf16[896,1024]{1,0:T(8,128)(2,1)S(1)} fusion(bf16[256,1024]{1,0:T(8,128)(2,1)} %collective-permute-done.2, bf16[384,512]{1,0:T(8,128)(2,1)S(1)} %get-tuple-element.34, bf16[384,512]{1,0:T(8,128)(2,1)S(1)} %get-tuple-element.33, bf16[256,1024]{1,0:T(8,128)(2,1)} %collective-permute-done.1), kind=kLoop, calls=%fused_computation.14 | loop fusion | flops 7340032 | bytes 3670016 | tf_op jit(solution)/shard_map/concatenate | solution.py:126
  37.4 1.0 constant_dynamic-slice_fusion.5
  38.4 1.2 %copy.32 = bf16[384,512]{0,1:T(8,128)(2,1)S(1)} copy(bf16[384,512]{1,0:T(8,128)(2,1)} %get-tuple-element.25) | data formatting | bytes 786432 | tf_op jit(solution)/shard_map/dynamic_slice | solution.py:52
  39.8 1.4 %copy.30 = bf16[384,512]{0,1:T(8,128)(2,1)S(1)} copy(bf16[384,512]{1,0:T(8,128)(2,1)} %get-tuple-element.24) | data formatting | bytes 786432 | tf_op jit(solution)/shard_map/dynamic_slice | solution.py:52
  41.2 1.1 constant_dynamic-slice_fusion.2
  42.3 1.9 %copy.37 = bf16[384,512]{0,1:T(8,128)(2,1)} copy(bf16[384,512]{1,0:T(8,128)(2,1)} %get-tuple-element.22) | data formatting | bytes 786432 | tf_op jit(solution)/shard_map/dynamic_slice | solution.py:52
  44.2 1.9 %copy.36 = bf16[384,512]{0,1:T(8,128)(2,1)} copy(bf16[384,512]{1,0:T(8,128)(2,1)} %get-tuple-element.23) | data formatting | bytes 786432 | tf_op jit(solution)/shard_map/dynamic_slice | solution.py:52
  46.1 1.9 %copy.35 = bf16[384,512]{0,1:T(8,128)(2,1)} copy(bf16[384,512]{1,0:T(8,128)(2,1)} %get-tuple-element.21) | data formatting | bytes 786432 | tf_op jit(solution)/shard_map/dynamic_slice | solution.py:52
  48.1 0.8 fusion.20
  48.9 1.7 %fusion.36 = (f32[3,8,128]{2,1,0:T(8,128)S(1)}, f32[3,8,128,384]{3,2,1,0:T(8,128)S(1)}) fusion(f32[3,8,128,384]{3,2,1,0:T(8,128)S(1)} %fusion.20, pred[3,384]{1,0:T(4,128)(4,1)S(1)} %bitcast.109), kind=kOutput, calls=%fused_computation.94 | output fusion | flops 7078271 | bytes 9450624 | tf_op jit(solution)/shard_map/sub | solution.py:67
  50.7 0.6 fusion.5
  51.3 1.5 %copy-done.2 = f32[3,8,128,384]{3,2,1,0:T(8,128)} copy-done((f32[3,8,128,384]{3,2,1,0:T(8,128)}, f32[3,8,128,384]{3,2,1,0:T(8,128)S(1)}, u32[]{:S(2)}) %copy-start.2) | copy-done | bytes 4718616
  52.8 2.1 %multiply_reduce_fusion.2 = (f32[3,128]{1,0:T(4,128)S(1)}, f32[3,128]{1,0:T(4,128)S(1)}, f32[3,128,8,64]{1,3,2,0:T(8,128)}) fusion(f32[3,128,8,64]{1,3,2,0:T(8,128)S(1)} %copy.39, bf16[3,8,128,384]{3,2,1,0:T(8,128)(2,1)S(1)} %fusion.5, bf16[1,384,8,64]{1,3,2,0:T(8,128)(2,1)S(1)} %bitcast.92, bf16[1,384,8,64]{1,3,2,0:T(8,128)(2,1)S(1)} %bitcast.94, ...), kind=kOutput, calls=%fused_computation.46 | convolution fusion | flops 152960256 | bytes 5114880 | tf_op jit(solution)/shard_map/jhqk,jkhd->jqhd/dot_general | solution.py:70
  55.6 3.1 %collective-permute-done.3 = f32[2,384]{1,0:T(2,128)S(1)} collective-permute-done((f32[2,384]{1,0:T(2,128)S(1)}, f32[2,384]{1,0:T(2,128)S(1)}, u32[]{:S(2)}, u32[]{:S(2)}) %collective-permute-start.3) | collective-permute-done | bytes 3104 | tf_op jit(solution)/shard_map/ppermute | solution.py:23
  58.7 0.6 fusion.32
  59.3 1.5 %collective-permute-start.4 = (f32[2,384]{1,0:T(2,128)}, f32[2,384]{1,0:T(2,128)S(1)}, u32[]{:S(2)}, u32[]{:S(2)}) collective-permute-start(f32[2,384]{1,0:T(2,128)} %fusion.32), channel_id=1, source_target_pairs={{0,1},{1,0},{2,3},{3,2},{4,5},{5,4},{6,7},{7,6},{8,9},{9,8},{10,11... | collective-permute-start | bytes 9224 | tf_op jit(solution)/shard_map/ppermute | solution.py:133
  60.8 2.8 %copy.48 = f32[3,128,8,64]{3,2,1,0:T(8,128)} copy(f32[3,128,8,64]{1,3,2,0:T(8,128)} %get-tuple-element.40) | data formatting | bytes 1572864 | tf_op jit(solution)/shard_map/reshape | solution.py:71
  63.5 1.8 %reshape.251 = f32[1,384,512]{2,1,0:T(8,128)S(1)} reshape(f32[3,128,8,64]{3,2,1,0:T(8,128)} %copy.48) | data formatting | bytes 1572864 | tf_op jit(solution)/shard_map/reshape | solution.py:71
  65.4 1.6 %multiply_reduce_fusion = (f32[3,128,8]{1,2,0:T(8,128)S(1)}, bf16[3,128,8,64]{1,3,2,0:T(8,128)(2,1)S(1)}) fusion(f32[3,128,8,64]{1,3,2,0:T(8,128)} %get-tuple-element.40, f32[3,128,8,64]{1,3,2,0:T(8,128)} %copy-done.6, f32[3,128]{1,0:T(4,128)S(1)} %bitcast.106, f32[3,128]{1,0:T(4,128)S(1)} %bitcast.104), kind=kLoop, calls=%fused_computation.43 | loop fusion | flops 1569792 | bytes 1981440 | tf_op jit(solution)/shard_map/reduce_sum | solution.py:82
  67.1 2.0 %fusion.38 = f32[3,8,64,384]{3,2,1,0:T(8,128)} fusion(bf16[3,128,8,64]{1,3,2,0:T(8,128)(2,1)S(1)} %get-tuple-element.12, bf16[3,8,128,384]{3,2,1,0:T(8,128)(2,1)S(1)} %fusion.5), kind=kOutput, calls=%fused_computation.96 | convolution fusion | flops 150994944 | bytes 5111808 | tf_op jit(solution)/shard_map/jhqk,jqhd->jkhd/dot_general | solution.py:88
  69.1 1.1 copy-done.3
  70.5 1.9 %multiply_convert_fusion = bf16[3,8,128,384]{3,2,1,0:T(8,128)(2,1)S(1)} fusion(f32[3,8,128]{2,1,0:T(8,128)S(1)} %bitcast.105, bf16[3,128,8,64]{1,3,2,0:T(8,128)(2,1)S(1)} %get-tuple-element.12, f32[3,8,128,384]{3,2,1,0:T(8,128)S(1)} %copy-done.3, f32[3,8,128]{2,1,0:T(8,128)S(1)} %copy-done.21, bf16[1,384,8,64]{1,3,2,0:T(8,128)(2,1)S(1)} %bitcast.93, ...), kind=kOutput, calls=%fused_computation.5 | convolution fusion | flops 158072832 | bytes 8675328 | tf_op jit(solution)/shard_map/jqhd,jkhd->jhqk/dot_general | solution.py:84
  72.4 2.2 %fusion.37 = f32[3,8,64,384]{3,2,1,0:T(8,128)} fusion(bf16[3,128,8,64]{1,3,2,0:T(8,128)(2,1)S(1)} %copy.40, bf16[3,8,128,384]{3,2,1,0:T(8,128)(2,1)S(1)} %multiply_convert_fusion), kind=kOutput, calls=%fused_computation.95 | convolution fusion | flops 150994944 | bytes 5111808 | tf_op jit(solution)/shard_map/jhqk,jqhd->jkhd/dot_general | solution.py:87
  74.6 2.0 %copy.41 = f32[3,384,512]{2,1,0:T(8,128)S(1)} copy(f32[3,384,512]{1,2,0:T(8,128)} %bitcast.84) | data formatting | bytes 4718592 | tf_op jit(solution)/shard_map/reshape | solution.py:90
  76.6 3.1 %copy.42 = f32[3,384,512]{2,1,0:T(8,128)} copy(f32[3,384,512]{1,2,0:T(8,128)} %bitcast.83) | data formatting | bytes 4718592 | tf_op jit(solution)/shard_map/reshape | solution.py:90
  80.2 1.2 %copy-done.1 = f32[3,384,512]{2,1,0:T(8,128)S(1)} copy-done((f32[3,384,512]{2,1,0:T(8,128)S(1)}, f32[3,384,512]{2,1,0:T(8,128)}, u32[]{:S(2)}) %copy-start.1) | copy-done | bytes 2359320
  82.7 1.5 %copy-done = f32[896,1024]{1,0:T(8,128)} copy-done((f32[896,1024]{1,0:T(8,128)}, f32[896,1024]{1,0:T(8,128)S(1)}, u32[]{:S(2)}) %copy-start) | copy-done | bytes 3670040
  84.2 0.9 fusion.33
  85.1 1.9 %collective-permute-start.6 = (bf16[256,1024]{1,0:T(8,128)(2,1)}, bf16[256,1024]{1,0:T(8,128)(2,1)S(1)}, u32[]{:S(2)}, u32[]{:S(2)}) collective-permute-start(bf16[256,1024]{1,0:T(8,128)(2,1)} %get-tuple-element.16), channel_id=1, source_target_pairs={{2,0},{4,2},{6,4},{8,6},{10,8},{12,10},{14,12},{3,1},{5,3},{7,5},{... | collective-permute-start | bytes 1572872 | tf_op jit(solution)/shard_map/ppermute | solution.py:19
  87.0 2.4 %collective-permute-start.5 = (bf16[256,1024]{1,0:T(8,128)(2,1)S(1)}, bf16[256,1024]{1,0:T(8,128)(2,1)}, u32[]{:S(2)}, u32[]{:S(2)}) collective-permute-start(bf16[256,1024]{1,0:T(8,128)(2,1)S(1)} %get-tuple-element.15), channel_id=1, source_target_pairs={{0,2},{2,4},{4,6},{6,8},{8,10},{10,12},{12,14},{1,3},{3,5},{5,7},{... | collective-permute-start | bytes 1572872 | tf_op jit(solution)/shard_map/ppermute | solution.py:19
  89.5 1.2 fusion.18
  91.7 2.3 %collective-permute-done.6 = bf16[256,1024]{1,0:T(8,128)(2,1)S(1)} collective-permute-done((bf16[256,1024]{1,0:T(8,128)(2,1)}, bf16[256,1024]{1,0:T(8,128)(2,1)S(1)}, u32[]{:S(2)}, u32[]{:S(2)}) %collective-permute-start.6) | collective-permute-done | bytes 524320 | tf_op jit(solution)/shard_map/ppermute | solution.py:19
  94.0 3.6 %collective-permute-done.5 = bf16[256,1024]{1,0:T(8,128)(2,1)} collective-permute-done((bf16[256,1024]{1,0:T(8,128)(2,1)S(1)}, bf16[256,1024]{1,0:T(8,128)(2,1)}, u32[]{:S(2)}, u32[]{:S(2)}) %collective-permute-start.5) | collective-permute-done | bytes 524320 | tf_op jit(solution)/shard_map/ppermute | solution.py:19
  97.6 1.8 %fusion.14 = bf16[384,1024]{1,0:T(8,128)(2,1)S(1)} fusion(f32[896,1024]{1,0:T(8,128)} %copy-done, bf16[256,1024]{1,0:T(8,128)(2,1)S(1)} %collective-permute-done.6, bf16[256,1024]{1,0:T(8,128)(2,1)} %collective-permute-done.5), kind=kLoop, calls=%fused_computation.24 | loop fusion | flops 1966080 | bytes 3407872 | tf_op jit(solution)/shard_map/convert.6
  99.7 0.6 collective-permute-start.7
  100.3 18.0 %collective-permute-done.7 = bf16[2,384,512]{2,1,0:T(8,128)(2,1)S(1)} collective-permute-done((bf16[2,384,512]{2,1,0:T(8,128)(2,1)S(1)}, bf16[2,384,512]{2,1,0:T(8,128)(2,1)S(1)}, u32[]{:S(2)}, u32[]{:S(2)}) %collective-permute-start.7) | collective-permute-done | bytes 786464 | tf_op jit(solution)/shard_map/ppermute | solution.py:23
  118.3 1.6 %maximum_select_fusion = bf16[1,2,384,1024]{3,2,1,0:T(8,128)(2,1)} fusion(bf16[1,2,384,512]{3,2,1,0:T(8,128)(2,1)S(1)} %bitcast.91, bf16[1,2,384,512]{3,2,1,0:T(8,128)(2,1)S(1)} %get-tuple-element.19, pred[]{:T(512)S(6)} %eq.11), kind=kLoop, calls=%fused_computation.29 | loop fusion | flops 7077888 | bytes 3145729 | tf_op jit(solution)/shard_map/jit(_where)/select_n | solution.py:162
  (75 shorter events, 7.3 us)
Async XLA Ops:
  1.2 19.3 %collective-permute-start = (bf16[2,384,512]{2,1,0:T(8,128)(2,1)S(1)}, bf16[2,384,512]{2,1,0:T(8,128)(2,1)S(1)}, u32[]{:S(2)}, u32[]{:S(2)}) collective-permute-start(bf16[2,384,512]{2,1,0:T(8,128)(2,1)S(1)} %dynamic-slice_bitcast_fusion), channel_id=1, source_target_pairs={{0,16},{16,0},{1,17},{17,1},{2,18},{18,2},{3,19},{19,3},{4,20},{20... | collective-permute-start | bytes 2359304 | tf_op jit(solution)/shard_map/ppermute | solution.py:23
  23.1 10.1 %collective-permute-start.2 = (bf16[256,1024]{1,0:T(8,128)(2,1)}, bf16[256,1024]{1,0:T(8,128)(2,1)}, u32[]{:S(2)}, u32[]{:S(2)}) collective-permute-start(bf16[256,1024]{1,0:T(8,128)(2,1)} %get-tuple-element.32), channel_id=1, source_target_pairs={{2,0},{4,2},{6,4},{8,6},{10,8},{12,10},{14,12},{3,1},{5,3},{7,5},{... | collective-permute-start | bytes 1572872 | tf_op jit(solution)/shard_map/ppermute | solution.py:19
  25.0 10.8 %collective-permute-start.1 = (bf16[256,1024]{1,0:T(8,128)(2,1)}, bf16[256,1024]{1,0:T(8,128)(2,1)}, u32[]{:S(2)}, u32[]{:S(2)}) collective-permute-start(bf16[256,1024]{1,0:T(8,128)(2,1)} %get-tuple-element.31), channel_id=1, source_target_pairs={{0,2},{2,4},{4,6},{6,8},{8,10},{10,12},{12,14},{1,3},{3,5},{5,7},{... | collective-permute-start | bytes 1572872 | tf_op jit(solution)/shard_map/ppermute | solution.py:19
  31.4 1.0 copy-start.13
  31.9 21.0 %copy-start.6 = (f32[3,128,8,64]{1,3,2,0:T(8,128)}, f32[3,128,8,64]{1,3,2,0:T(8,128)S(1)}, u32[]{:S(2)}) copy-start(f32[3,128,8,64]{1,3,2,0:T(8,128)S(1)} %copy.39) | copy-start | bytes 2359300
  39.6 8.5 %copy-start.7 = (bf16[384,512]{0,1:T(8,128)(2,1)}, bf16[384,512]{0,1:T(8,128)(2,1)S(1)}, u32[]{:S(2)}) copy-start(bf16[384,512]{0,1:T(8,128)(2,1)S(1)} %copy.32) | copy-start | bytes 1179652
  39.8 8.3 %copy-start.9 = (bf16[384,512]{0,1:T(8,128)(2,1)}, bf16[384,512]{0,1:T(8,128)(2,1)S(1)}, u32[]{:S(2)}) copy-start(bf16[384,512]{0,1:T(8,128)(2,1)S(1)} %copy.31) | copy-start | bytes 1179652
  41.2 6.9 %copy-start.11 = (bf16[384,512]{0,1:T(8,128)(2,1)}, bf16[384,512]{0,1:T(8,128)(2,1)S(1)}, u32[]{:S(2)}) copy-start(bf16[384,512]{0,1:T(8,128)(2,1)S(1)} %copy.30) | copy-start | bytes 1179652
  50.6 2.2 %copy-start.2 = (f32[3,8,128,384]{3,2,1,0:T(8,128)}, f32[3,8,128,384]{3,2,1,0:T(8,128)S(1)}, u32[]{:S(2)}) copy-start(f32[3,8,128,384]{3,2,1,0:T(8,128)S(1)} %get-tuple-element.39) | copy-start | bytes 14155780
  50.6 2.2 %copy-start.20 = (f32[3,8,128]{2,1,0:T(8,128)}, f32[3,8,128]{2,1,0:T(8,128)S(1)}, u32[]{:S(2)}) copy-start(f32[3,8,128]{2,1,0:T(8,128)S(1)} %get-tuple-element.38) | copy-start | bytes 36868
  50.6 2.2 %copy-start.14 = (bf16[384,512]{0,1:T(8,128)(2,1)S(1)}, bf16[384,512]{0,1:T(8,128)(2,1)}, u32[]{:S(2)}) copy-start(bf16[384,512]{0,1:T(8,128)(2,1)} %copy.37) | copy-start | bytes 1179652
  50.7 2.2 %copy-start.16 = (bf16[384,512]{0,1:T(8,128)(2,1)S(1)}, bf16[384,512]{0,1:T(8,128)(2,1)}, u32[]{:S(2)}) copy-start(bf16[384,512]{0,1:T(8,128)(2,1)} %copy.36) | copy-start | bytes 1179652
  50.7 2.2 %copy-start.18 = (bf16[384,512]{0,1:T(8,128)(2,1)S(1)}, bf16[384,512]{0,1:T(8,128)(2,1)}, u32[]{:S(2)}) copy-start(bf16[384,512]{0,1:T(8,128)(2,1)} %copy.35) | copy-start | bytes 1179652
  55.0 3.7 %collective-permute-start.3 = (f32[2,384]{1,0:T(2,128)S(1)}, f32[2,384]{1,0:T(2,128)S(1)}, u32[]{:S(2)}, u32[]{:S(2)}) collective-permute-start(f32[2,384]{1,0:T(2,128)S(1)} %pad_maximum_fusion.11), channel_id=1, source_target_pairs={{0,16},{16,0},{1,17},{17,1},{2,18},{18,2},{3,19},{19,3},{4,20},{20... | collective-permute-start | bytes 9224 | tf_op jit(solution)/shard_map/ppermute | solution.py:23
  59.3 6.1 %collective-permute-start.4 = (f32[2,384]{1,0:T(2,128)}, f32[2,384]{1,0:T(2,128)S(1)}, u32[]{:S(2)}, u32[]{:S(2)}) collective-permute-start(f32[2,384]{1,0:T(2,128)} %fusion.32), channel_id=1, source_target_pairs={{0,1},{1,0},{2,3},{3,2},{4,5},{5,4},{6,7},{7,6},{8,9},{9,8},{10,11... | collective-permute-start | bytes 9224 | tf_op jit(solution)/shard_map/ppermute | solution.py:133
  67.0 3.2 %copy-start.3 = (f32[3,8,128,384]{3,2,1,0:T(8,128)S(1)}, f32[3,8,128,384]{3,2,1,0:T(8,128)}, u32[]{:S(2)}) copy-start(f32[3,8,128,384]{3,2,1,0:T(8,128)} %copy-done.2) | copy-start | bytes 14155780
  67.0 3.3 %copy-start.15 = (bf16[384,512]{0,1:T(8,128)(2,1)S(1)}, bf16[384,512]{0,1:T(8,128)(2,1)}, u32[]{:S(2)}) copy-start(bf16[384,512]{0,1:T(8,128)(2,1)} %copy.37) | copy-start | bytes 1179652
  67.0 3.4 %copy-start.17 = (bf16[384,512]{0,1:T(8,128)(2,1)S(1)}, bf16[384,512]{0,1:T(8,128)(2,1)}, u32[]{:S(2)}) copy-start(bf16[384,512]{0,1:T(8,128)(2,1)} %copy.36) | copy-start | bytes 1179652
  67.1 3.5 %copy-start.19 = (bf16[384,512]{0,1:T(8,128)(2,1)S(1)}, bf16[384,512]{0,1:T(8,128)(2,1)}, u32[]{:S(2)}) copy-start(bf16[384,512]{0,1:T(8,128)(2,1)} %copy.35) | copy-start | bytes 1179652
  67.1 3.5 %copy-start.21 = (f32[3,8,128]{2,1,0:T(8,128)S(1)}, f32[3,8,128]{2,1,0:T(8,128)}, u32[]{:S(2)}) copy-start(f32[3,8,128]{2,1,0:T(8,128)} %copy-done.20) | copy-start | bytes 36868
  72.4 2.2 %copy-start.4 = (bf16[3,8,128,384]{3,2,1,0:T(8,128)(2,1)}, bf16[3,8,128,384]{3,2,1,0:T(8,128)(2,1)S(1)}, u32[]{:S(2)}) copy-start(bf16[3,8,128,384]{3,2,1,0:T(8,128)(2,1)S(1)} %multiply_convert_fusion) | copy-start | bytes 7077892
  79.8 1.7 %copy-start.1 = (f32[3,384,512]{2,1,0:T(8,128)S(1)}, f32[3,384,512]{2,1,0:T(8,128)}, u32[]{:S(2)}) copy-start(f32[3,384,512]{2,1,0:T(8,128)} %copy.42) | copy-start | bytes 7077892
  82.4 1.9 %copy-start = (f32[896,1024]{1,0:T(8,128)}, f32[896,1024]{1,0:T(8,128)S(1)}, u32[]{:S(2)}) copy-start(f32[896,1024]{1,0:T(8,128)S(1)} %fusion.17) | copy-start | bytes 11010052
  82.4 7.1 %copy-start.5 = (bf16[3,8,128,384]{3,2,1,0:T(8,128)(2,1)S(1)}, bf16[3,8,128,384]{3,2,1,0:T(8,128)(2,1)}, u32[]{:S(2)}) copy-start(bf16[3,8,128,384]{3,2,1,0:T(8,128)(2,1)} %copy-done.4) | copy-start | bytes 7077892
  82.4 7.1 %copy-start.8 = (bf16[384,512]{0,1:T(8,128)(2,1)S(1)}, bf16[384,512]{0,1:T(8,128)(2,1)}, u32[]{:S(2)}) copy-start(bf16[384,512]{0,1:T(8,128)(2,1)} %copy-done.7) | copy-start | bytes 1179652
  82.4 7.1 %copy-start.10 = (bf16[384,512]{0,1:T(8,128)(2,1)S(1)}, bf16[384,512]{0,1:T(8,128)(2,1)}, u32[]{:S(2)}) copy-start(bf16[384,512]{0,1:T(8,128)(2,1)} %copy-done.9) | copy-start | bytes 1179652
  82.4 7.1 %copy-start.12 = (bf16[384,512]{0,1:T(8,128)(2,1)S(1)}, bf16[384,512]{0,1:T(8,128)(2,1)}, u32[]{:S(2)}) copy-start(bf16[384,512]{0,1:T(8,128)(2,1)} %copy-done.11) | copy-start | bytes 1179652
  85.1 8.9 %collective-permute-start.6 = (bf16[256,1024]{1,0:T(8,128)(2,1)}, bf16[256,1024]{1,0:T(8,128)(2,1)S(1)}, u32[]{:S(2)}, u32[]{:S(2)}) collective-permute-start(bf16[256,1024]{1,0:T(8,128)(2,1)} %get-tuple-element.16), channel_id=1, source_target_pairs={{2,0},{4,2},{6,4},{8,6},{10,8},{12,10},{14,12},{3,1},{5,3},{7,5},{... | collective-permute-start | bytes 1572872 | tf_op jit(solution)/shard_map/ppermute | solution.py:19
  87.0 10.6 %collective-permute-start.5 = (bf16[256,1024]{1,0:T(8,128)(2,1)S(1)}, bf16[256,1024]{1,0:T(8,128)(2,1)}, u32[]{:S(2)}, u32[]{:S(2)}) collective-permute-start(bf16[256,1024]{1,0:T(8,128)(2,1)S(1)} %get-tuple-element.15), channel_id=1, source_target_pairs={{0,2},{2,4},{4,6},{6,8},{8,10},{10,12},{12,14},{1,3},{3,5},{5,7},{... | collective-permute-start | bytes 1572872 | tf_op jit(solution)/shard_map/ppermute | solution.py:19
  99.7 18.6 %collective-permute-start.7 = (bf16[2,384,512]{2,1,0:T(8,128)(2,1)S(1)}, bf16[2,384,512]{2,1,0:T(8,128)(2,1)S(1)}, u32[]{:S(2)}, u32[]{:S(2)}) collective-permute-start(bf16[2,384,512]{2,1,0:T(8,128)(2,1)S(1)} %get-tuple-element.20), channel_id=1, source_target_pairs={{0,16},{16,0},{1,17},{17,1},{2,18},{18,2},{3,19},{19,3},{4,20},{20... | collective-permute-start | bytes 2359304 | tf_op jit(solution)/shard_map/ppermute | solution.py:23

commit v7 on v3

--- a/solution.py
+++ b/solution.py
@@ -82,7 +82,6 @@
     delta = jnp.transpose(delta, (0, 2, 1))[..., None]
     dprobs = jnp.einsum("jqhd,jkhd->jhqk", up4, values_w, preferred_element_type=jnp.float32)
     dscores = (weights * (dprobs - delta) * score_scale).astype(jnp.bfloat16)
-    grad_q = jnp.einsum("jhqk,jkhd->jqhd", dscores, keys_w, preferred_element_type=jnp.float32)
     grad_kw = jnp.einsum("jhqk,jqhd->jkhd", dscores, q4, preferred_element_type=jnp.float32)
     grad_vw = jnp.einsum("jhqk,jqhd->jkhd", rounded, up4, preferred_element_type=jnp.float32)
     grad_kvw = jnp.concatenate(
@@ -96,7 +95,7 @@
         total = lax.dynamic_update_slice_in_dim(
             total, lax.dynamic_slice_in_dim(total, start, window, 0) + grad_kvw[j], start, 0
         )
-    return grad_q.reshape(rows, head_cols), normed, total
+    return (dscores, keys_w), normed, total
 
 
 def per_device(heads_in, doc_units):
@@ -142,8 +141,14 @@
         row_total,
         total_cols,
     )
-    from_left = seq_shift(total[near.shape[0] - halo :].astype(jnp.bfloat16), 1)
-    from_right = seq_shift(total[:halo].astype(jnp.bfloat16), -1)
+    to_left = total[near.shape[0] - halo :]
+    to_right = total[:halo]
+    dscores, keys_w, to_left, to_right = lax.optimization_barrier((*grad_q, to_left, to_right))
+    grad_q = jnp.einsum(
+        "jhqk,jkhd->jqhd", dscores, keys_w, preferred_element_type=jnp.float32
+    ).reshape(rows, half)
+    from_left = seq_shift(to_left.astype(jnp.bfloat16), 1)
+    from_right = seq_shift(to_right.astype(jnp.bfloat16), -1)
     own = (
         total[halo : halo + rows]
         + jnp.pad(from_left.astype(jnp.float32), ((0, rows - halo), (0, 0)))

time: 97.2 us -> 102 us (1.049)
  matrix products: 6.2 us -> 10.3 us
  starting transfers between devices: 12.3 us -> 14.7 us
  waiting for transfers between devices: 47.9 us -> 46.1 us
    unnamed x46, local copies, waits for them, and re-layouts: 5.28 us -> 0.81 us
    sub x0 -> x1, matrix products: none -> 3.65 us  [attention_grads(): expven = jnp.exp(scores - row_max)]
    ppermute x4, waiting for transfers between devices: 9.04 us -> 6.56 us  [seq_shift(): lax.ppermute(value, 'seq', [(source, source + steps) for source in range(...]
    ppermute x4, starting transfers between devices: 8.96 us -> 11.4 us  [seq_shift(): lax.ppermute(value, 'seq', [(source, source + steps) for source in range(...]
    convert_element_type x1, other arithmetic: 0.6 us -> 2.78 us  [attention_grads(): rounded = weights.astype(jnp.bfloat16)]
    sub x1 -> x0, other arithmetic: 1.72 us -> none  [attention_grads(): expven = jnp.exp(scores - row_max)]
    dot_general x1, matrix products: 1.87 us -> 3.18 us  [attention_grads(): jnp.einsum('jqhd,jkhd->jhqk', up4, values_w, preferred_element_type=jnp.f...]
    select_n x1, other arithmetic: 1.28 us -> 0.15 us  [per_device(): key_value = jnp.where(is_first, kept, arrived)]
  transfers between devices with their start and end apart: 8 -> 8, of which waited for: 7 -> 6; matrix products, arithmetic and copies ran while one was open for 9% -> 10% of each run, Pallas kernels for 0% -> 0%
where the time goes in v7:
time: 102 us; the launch traced here: 101 us
  waiting for transfers between devices  46.1 us (45%)
  local copies, waits for them, and re-layouts  14.8 us (15%)
  starting transfers between devices  14.7 us (14%)
  other arithmetic  12.6 us (12%)
  matrix products  10.3 us (10%)
  between operations  2.3 us (2%)
    ppermute x3, waiting for transfers between devices, sec_swap(): return lax.ppermute(value, 'sec', [(0, 1), (1, 0)])  39.5 us
    ppermute x4, starting transfers between devices, seq_shift(): lax.ppermute(value, 'seq', [(source, source + steps) for source in range(...  11.4 us
    ppermute x4, waiting for transfers between devices, seq_shift(): lax.ppermute(value, 'seq', [(source, source + steps) for source in range(...  6.56 us
    sub x1, matrix products, attention_grads(): expven = jnp.exp(scores - row_max)  3.65 us
    dot_general x1, matrix products, attention_grads(): jnp.einsum('jqhd,jkhd->jhqk', up4, values_w, preferred_element_type=jnp.f...  3.18 us
    convert_element_type x1, other arithmetic, attention_grads(): rounded = weights.astype(jnp.bfloat16)  2.78 us
    reshape x1, local copies, waits for them, and re-layouts, attention_grads(): attended = attended4.reshape(rows, head_cols)  2.35 us
  transfers between devices with their start and end apart: 8, of which 6 were waited for; matrix products, arithmetic and copies ran while one was open for 10% of the time, Pallas kernels for 0%

profile of v7, /device:TPU:18, one launch (start us, length us, event | category | flops | bytes accessed | tf_op | source)
XLA Modules:
  0.0 100.9 jit_solution(8392617814181139922)
XLA Ops:
  0.0 1.5 %constant_dynamic-slice_fusion.6 = (bf16[1,2,384,512]{3,2,1,0:T(8,128)(2,1)S(1)}, bf16[1,2,384,512]{3,2,1,0:T(8,128)(2,1)S(1)}) fusion(bf16[1,2,384,1024]{3,2,1,0:T(8,128)(2,1)} %param.2, s32[]{:T(128)S(6)} %select_n.91, s32[]{:T(128)S(6)} %select_n.90), kind=kLoop, calls=%fused_computation.69 | loop fusion | bytes 3145736 | tf_op jit(solution)/shard_map/dynamic_slice | solution.py:116
  1.5 0.4 copy.20
  1.9 0.6 collective-permute-start
  2.5 0.2 reduce-window.8
  2.6 0.2 fusion.32
  3.3 0.4 copy.21
  3.7 17.5 %collective-permute-done = bf16[2,384,512]{1,2,0:T(8,128)(2,1)S(1)} collective-permute-done((bf16[2,384,512]{1,2,0:T(8,128)(2,1)S(1)}, bf16[2,384,512]{1,2,0:T(8,128)(2,1)S(1)}, u32[]{:S(2)}, u32[]{:S(2)}) %collective-permute-start) | collective-permute-done | bytes 786464 | tf_op jit(solution)/shard_map/ppermute | solution.py:22
  21.4 1.1 %fusion.19 = (bf16[256,1024]{0,1:T(8,128)(2,1)}, bf16[256,1024]{0,1:T(8,128)(2,1)}) fusion(bf16[384,512]{0,1:T(8,128)(2,1)S(1)} %get-tuple-element.43, bf16[384,512]{0,1:T(8,128)(2,1)S(1)} %get-tuple-element.44), kind=kLoop, calls=%fused_computation.48 | loop fusion | flops 2097152 | bytes 1835008 | tf_op jit(solution)/shard_map/concatenate | solution.py:121
  22.5 1.9 %collective-permute-start.1 = (bf16[256,1024]{0,1:T(8,128)(2,1)}, bf16[256,1024]{0,1:T(8,128)(2,1)}, u32[]{:S(2)}, u32[]{:S(2)}) collective-permute-start(bf16[256,1024]{0,1:T(8,128)(2,1)} %get-tuple-element.41), channel_id=1, source_target_pairs={{0,2},{2,4},{4,6},{6,8},{8,10},{10,12},{12,14},{1,3},{3,5},{5,7},{... | collective-permute-start | bytes 1572872 | tf_op jit(solution)/shard_map/ppermute | solution.py:18
  24.4 3.6 %collective-permute-start.2 = (bf16[256,1024]{0,1:T(8,128)(2,1)}, bf16[256,1024]{0,1:T(8,128)(2,1)}, u32[]{:S(2)}, u32[]{:S(2)}) collective-permute-start(bf16[256,1024]{0,1:T(8,128)(2,1)} %get-tuple-element.42), channel_id=1, source_target_pairs={{2,0},{4,2},{6,4},{8,6},{10,8},{12,10},{14,12},{3,1},{5,3},{7,5},{... | collective-permute-start | bytes 1572872 | tf_op jit(solution)/shard_map/ppermute | solution.py:18
  28.1 0.6 fusion.43
  30.6 0.8 slice_convert_fusion
  31.4 0.3 reshape.303
  31.8 1.6 %reshape_squeeze.3 = bf16[3,128,8,64]{1,0,3,2:T(4,128)(2,1)S(1)} reshape(bf16[1,384,512]{1,2,0:T(8,128)(2,1)} %get-tuple-element.40) | data formatting | bytes 786432 | tf_op jit(solution)/shard_map/reshape;squeeze | solution.py:57
  33.4 1.7 %collective-permute-done.2 = bf16[256,1024]{0,1:T(8,128)(2,1)} collective-permute-done((bf16[256,1024]{0,1:T(8,128)(2,1)}, bf16[256,1024]{0,1:T(8,128)(2,1)}, u32[]{:S(2)}, u32[]{:S(2)}) %collective-permute-start.2) | collective-permute-done | bytes 524320 | tf_op jit(solution)/shard_map/ppermute | solution.py:18
  35.1 1.4 %pad_maximum_fusion = bf16[896,1024]{0,1:T(8,128)(2,1)S(1)} fusion(bf16[256,1024]{0,1:T(8,128)(2,1)} %collective-permute-done.2, bf16[384,512]{0,1:T(8,128)(2,1)S(1)} %get-tuple-element.44, bf16[384,512]{0,1:T(8,128)(2,1)S(1)} %get-tuple-element.43, bf16[256,1024]{0,1:T(8,128)(2,1)} %collective-permute-done.1), kind=kLoop, calls=%fused_computation.14 | loop fusion | flops 7340032 | bytes 3670016 | tf_op jit(solution)/shard_map/concatenate | solution.py:124
  36.6 1.1 %constant_dynamic-slice_fusion.2 = (bf16[384,512]{0,1:T(8,128)(2,1)}, bf16[384,512]{0,1:T(8,128)(2,1)}, bf16[384,512]{0,1:T(8,128)(2,1)}) fusion(bf16[896,512]{0,1:T(8,128)(2,1)S(1)} %get-tuple-element.23, s32[]{:T(128)S(6)} %select_n.97, s32[]{:T(128)S(6)} %select_n.99, s32[]{:T(128)S(6)} %select_n.98), kind=kLoop, calls=%fused_computation.65 | loop fusion | bytes 2359308 | tf_op jit(solution)/shard_map/dynamic_slice | solution.py:51
  37.9 3.7 %fusion.44 = (f32[3,8,128]{2,1,0:T(8,128)S(1)}, f32[3,8,128,384]{3,2,1,0:T(8,128)}) fusion(pred[3,384]{1,0:T(4,128)(4,1)S(1)} %bitcast.116, bf16[3,128,8,64]{1,0,3,2:T(4,128)(2,1)S(1)} %reshape_squeeze.3, bf16[1,384,8,64]{1,3,2,0:T(8,128)(2,1)S(1)} %bitcast.93, bf16[1,384,8,64]{1,3,2,0:T(8,128)(2,1)S(1)} %bitcast.95, bf16[1,384,8,64]{1,3,2,0:T(8,128)(2,1)S(1)} %bitcast.91), kind=kOutput, calls=%fused_computation.98 | convolution fusion | flops 156893568 | bytes 6304896 | tf_op jit(solution)/shard_map/sub | solution.py:66
  41.6 2.8 %fusion.5 = bf16[3,8,128,384]{3,2,1,0:T(8,128)(2,1)S(1)} fusion(f32[3,8,128,384]{3,2,1,0:T(8,128)} %get-tuple-element.49, f32[3,8,128]{2,1,0:T(8,128)S(1)} %get-tuple-element.48), kind=kLoop, calls=%fused_computation.13 | loop fusion | flops 2359296 | bytes 7090176 | tf_op jit(solution)/shard_map/convert_element_type | solution.py:68
  44.5 1.2 %multiply_reduce_fusion.2 = (f32[3,128]{1,0:T(4,128)S(1)}, f32[3,128]{1,0:T(4,128)S(1)}, f32[3,128,8,64]{1,3,2,0:T(8,128)S(1)}) fusion(f32[3,128,8,64]{1,0,3,2:T(4,128)S(1)} %reshape.303, bf16[3,8,128,384]{3,2,1,0:T(8,128)(2,1)S(1)} %fusion.5, bf16[1,384,8,64]{1,3,2,0:T(8,128)(2,1)S(1)} %bitcast.101, bf16[1,384,8,64]{1,3,2,0:T(8,128)(2,1)S(1)} %bitcast.103, ...), kind=kOutput, calls=%fused_computation.46 | convolution fusion | flops 152960256 | bytes 5114880 | tf_op jit(solution)/shard_map/jhqk,jkhd->jqhd/dot_general | solution.py:69
  45.7 0.6 collective-permute-start.3
  46.3 3.0 %collective-permute-done.3 = f32[2,384]{1,0:T(2,128)S(1)} collective-permute-done((f32[2,384]{1,0:T(2,128)S(1)}, f32[2,384]{1,0:T(2,128)S(1)}, u32[]{:S(2)}, u32[]{:S(2)}) %collective-permute-start.3) | collective-permute-done | bytes 3104 | tf_op jit(solution)/shard_map/ppermute | solution.py:22
  49.4 0.6 fusion.40
  50.0 1.5 %collective-permute-start.4 = (f32[2,384]{1,0:T(2,128)}, f32[2,384]{1,0:T(2,128)S(1)}, u32[]{:S(2)}, u32[]{:S(2)}) collective-permute-start(f32[2,384]{1,0:T(2,128)} %fusion.40), channel_id=1, source_target_pairs={{0,1},{1,0},{2,3},{3,2},{4,5},{5,4},{6,7},{7,6},{8,9},{9,8},{10,11... | collective-permute-start | bytes 9224 | tf_op jit(solution)/shard_map/ppermute | solution.py:131
  51.7 1.5 %copy.27 = f32[3,128,8,64]{1,0,3,2:T(4,128)} copy(f32[3,128,8,64]{1,3,2,0:T(8,128)S(1)} %get-tuple-element.50) | data formatting | bytes 1572864 | tf_op jit(solution)/shard_map/jhqk,jkhd->jqhd/transpose | solution.py:69
  53.2 2.3 %reshape.302 = f32[1,384,512]{1,2,0:T(8,128)} reshape(f32[3,128,8,64]{1,0,3,2:T(4,128)} %copy.27) | data formatting | bytes 1572864 | tf_op jit(solution)/shard_map/reshape | solution.py:70
  55.6 1.7 %multiply_reduce_fusion = (f32[3,128,8]{1,2,0:T(8,128)S(1)}, bf16[3,128,8,64]{1,3,2,0:T(8,128)(2,1)S(1)}) fusion(f32[3,128,8,64]{1,3,2,0:T(8,128)} %copy-done.3, f32[3,128]{1,0:T(4,128)S(1)} %bitcast.113, f32[3,128]{1,0:T(4,128)S(1)} %bitcast.111, f32[3,128,8,64]{1,0,3,2:T(4,128)} %copy-done.1), kind=kLoop, calls=%fused_computation.43 | loop fusion | flops 1569792 | bytes 1981440 | tf_op jit(solution)/shard_map/reduce_sum | solution.py:81
  57.3 0.6 fusion.49
  57.9 0.4 copy-done.13
  58.5 3.2 %multiply_convert_fusion = bf16[3,8,128,384]{3,2,1,0:T(8,128)(2,1)S(1)} fusion(f32[3,8,128]{2,1,0:T(8,128)S(1)} %bitcast.112, bf16[3,128,8,64]{1,3,2,0:T(8,128)(2,1)S(1)} %get-tuple-element.20, f32[3,8,128,384]{3,2,1,0:T(8,128)} %get-tuple-element.49, f32[3,8,128]{2,1,0:T(8,128)S(1)} %copy-done.19, bf16[1,384,8,64]{1,3,2,0:T(8,128)(2,1)S(1)} %bitcast.102, ...), kind=kOutput, calls=%fused_computation.5 | convolution fusion | flops 158072832 | bytes 8675328 | tf_op jit(solution)/shard_map/jqhd,jkhd->jhqk/dot_general | solution.py:83
  61.7 0.6 fusion.27
  62.3 0.2 broadcast_in_dim.36
  62.6 0.3 fusion.9
  63.0 0.3 fusion.17
  63.3 1.2 %fusion.41 = (bf16[256,1024]{0,1:T(8,128)(2,1)}, bf16[256,1024]{0,1:T(8,128)(2,1)}) fusion(f32[896,1024]{0,1:T(8,128)S(1)} %fusion.17), kind=kLoop, calls=%fused_computation.95 | loop fusion | bytes 2097152 | tf_op jit(solution)/shard_map/slice | solution.py:145
  64.4 2.4 %collective-permute-start.5 = (bf16[256,1024]{0,1:T(8,128)(2,1)}, bf16[256,1024]{0,1:T(8,128)(2,1)S(1)}, u32[]{:S(2)}, u32[]{:S(2)}) collective-permute-start(bf16[256,1024]{0,1:T(8,128)(2,1)} %get-tuple-element.9), channel_id=1, source_target_pairs={{0,2},{2,4},{4,6},{6,8},{8,10},{10,12},{12,14},{1,3},{3,5},{5,7},{... | collective-permute-start | bytes 1572872 | tf_op jit(solution)/shard_map/ppermute | solution.py:18
  66.9 3.4 %collective-permute-start.6 = (bf16[256,1024]{0,1:T(8,128)(2,1)}, bf16[256,1024]{0,1:T(8,128)(2,1)}, u32[]{:S(2)}, u32[]{:S(2)}) collective-permute-start(bf16[256,1024]{0,1:T(8,128)(2,1)} %get-tuple-element.10), channel_id=1, source_target_pairs={{2,0},{4,2},{6,4},{8,6},{10,8},{12,10},{14,12},{3,1},{5,3},{7,5},{... | collective-permute-start | bytes 1572872 | tf_op jit(solution)/shard_map/ppermute | solution.py:18
  70.3 1.1 %fusion.18 = bf16[3,128,8,64]{1,3,2,0:T(8,128)(2,1)S(1)} fusion(bf16[3,384,8,64]{1,3,2,0:T(8,128)(2,1)S(1)} %pad_maximum_fusion.2, bf16[3,8,128,384]{3,2,1,0:T(8,128)(2,1)S(1)} %multiply_convert_fusion), kind=kOutput, calls=%fused_computation.32 | convolution fusion | flops 151191552 | bytes 3932160 | tf_op jit(solution)/shard_map/jhqk,jkhd->jqhd/dot_general | solution.py:147
  71.5 0.3 copy.26
  71.8 0.3 convert_element_type.79
  72.3 3.0 %collective-permute-done.5 = bf16[256,1024]{0,1:T(8,128)(2,1)S(1)} collective-permute-done((bf16[256,1024]{0,1:T(8,128)(2,1)}, bf16[256,1024]{0,1:T(8,128)(2,1)S(1)}, u32[]{:S(2)}, u32[]{:S(2)}) %collective-permute-start.5) | collective-permute-done | bytes 524320 | tf_op jit(solution)/shard_map/ppermute | solution.py:18
  75.3 1.9 %collective-permute-done.6 = bf16[256,1024]{0,1:T(8,128)(2,1)} collective-permute-done((bf16[256,1024]{0,1:T(8,128)(2,1)}, bf16[256,1024]{0,1:T(8,128)(2,1)}, u32[]{:S(2)}, u32[]{:S(2)}) %collective-permute-start.6) | collective-permute-done | bytes 524320 | tf_op jit(solution)/shard_map/ppermute | solution.py:18
  77.1 1.7 %fusion.14 = bf16[384,1024]{0,1:T(8,128)(2,1)S(1)} fusion(f32[896,1024]{0,1:T(8,128)} %copy-done, bf16[256,1024]{0,1:T(8,128)(2,1)} %collective-permute-done.6, bf16[256,1024]{0,1:T(8,128)(2,1)S(1)} %collective-permute-done.5), kind=kLoop, calls=%fused_computation.24 | loop fusion | flops 1966080 | bytes 3407872 | tf_op jit(solution)/shard_map/convert.6
  78.9 0.2 select_bitcast_fusion
  79.2 0.6 collective-permute-start.7
  79.8 19.0 %collective-permute-done.7 = bf16[2,384,512]{1,2,0:T(8,128)(2,1)S(1)} collective-permute-done((bf16[2,384,512]{1,2,0:T(8,128)(2,1)S(1)}, bf16[2,384,512]{1,2,0:T(8,128)(2,1)S(1)}, u32[]{:S(2)}, u32[]{:S(2)}) %collective-permute-start.7) | collective-permute-done | bytes 786464 | tf_op jit(solution)/shard_map/ppermute | solution.py:22
  98.8 0.4 maximum_select_fusion
  99.2 1.6 %copy.28 = bf16[1,2,384,1024]{3,2,1,0:T(8,128)(2,1)} copy(bf16[1,2,384,1024]{2,3,1,0:T(8,128)(2,1)S(1)} %maximum_select_fusion) | data formatting | bytes 3145728 | tf_op jit(solution)/shard_map/jit(_where)/select_n | solution.py:164
  (65 shorter events, 1.9 us)
Async XLA Ops:
  0.0 2.5 %copy-start.20 = (s32[12]{0:T(128)S(1)}, s32[12]{0:T(128)}, u32[]{:S(2)}) copy-start(s32[12]{0:T(128)} %param.3) | copy-start | bytes 148
  1.9 19.3 %collective-permute-start = (bf16[2,384,512]{1,2,0:T(8,128)(2,1)S(1)}, bf16[2,384,512]{1,2,0:T(8,128)(2,1)S(1)}, u32[]{:S(2)}, u32[]{:S(2)}) collective-permute-start(bf16[2,384,512]{1,2,0:T(8,128)(2,1)S(1)} %bitcast.97), channel_id=1, source_target_pairs={{0,16},{16,0},{1,17},{17,1},{2,18},{18,2},{3,19},{19,3},{4,20},{20... | collective-permute-start | bytes 2359304 | tf_op jit(solution)/shard_map/ppermute | solution.py:22
  22.5 10.9 %collective-permute-start.1 = (bf16[256,1024]{0,1:T(8,128)(2,1)}, bf16[256,1024]{0,1:T(8,128)(2,1)}, u32[]{:S(2)}, u32[]{:S(2)}) collective-permute-start(bf16[256,1024]{0,1:T(8,128)(2,1)} %get-tuple-element.41), channel_id=1, source_target_pairs={{0,2},{2,4},{4,6},{6,8},{8,10},{10,12},{12,14},{1,3},{3,5},{5,7},{... | collective-permute-start | bytes 1572872 | tf_op jit(solution)/shard_map/ppermute | solution.py:18
  24.4 10.6 %collective-permute-start.2 = (bf16[256,1024]{0,1:T(8,128)(2,1)}, bf16[256,1024]{0,1:T(8,128)(2,1)}, u32[]{:S(2)}, u32[]{:S(2)}) collective-permute-start(bf16[256,1024]{0,1:T(8,128)(2,1)} %get-tuple-element.42), channel_id=1, source_target_pairs={{2,0},{4,2},{6,4},{8,6},{10,8},{12,10},{14,12},{3,1},{5,3},{7,5},{... | collective-permute-start | bytes 1572872 | tf_op jit(solution)/shard_map/ppermute | solution.py:18
  31.7 12.6 %copy-start.1 = (f32[3,128,8,64]{1,0,3,2:T(4,128)}, f32[3,128,8,64]{1,0,3,2:T(4,128)S(1)}, u32[]{:S(2)}) copy-start(f32[3,128,8,64]{1,0,3,2:T(4,128)S(1)} %reshape.303) | copy-start | bytes 2359300
  33.4 4.5 %copy-start.4 = (bf16[3,128,8,64]{1,0,3,2:T(4,128)(2,1)}, bf16[3,128,8,64]{1,0,3,2:T(4,128)(2,1)S(1)}, u32[]{:S(2)}) copy-start(bf16[3,128,8,64]{1,0,3,2:T(4,128)(2,1)S(1)} %reshape_squeeze.3) | copy-start | bytes 1179652
  37.8 3.7 %copy-start.6 = (bf16[384,512]{0,1:T(8,128)(2,1)}, bf16[384,512]{0,1:T(8,128)(2,1)S(1)}, u32[]{:S(2)}) copy-start(bf16[384,512]{0,1:T(8,128)(2,1)S(1)} %get-tuple-element.34) | copy-start | bytes 1179652
  37.9 3.7 %copy-start.8 = (bf16[384,512]{0,1:T(8,128)(2,1)}, bf16[384,512]{0,1:T(8,128)(2,1)S(1)}, u32[]{:S(2)}) copy-start(bf16[384,512]{0,1:T(8,128)(2,1)S(1)} %get-tuple-element.35) | copy-start | bytes 1179652
  37.9 3.7 %copy-start.10 = (bf16[384,512]{0,1:T(8,128)(2,1)}, bf16[384,512]{0,1:T(8,128)(2,1)S(1)}, u32[]{:S(2)}) copy-start(bf16[384,512]{0,1:T(8,128)(2,1)S(1)} %get-tuple-element.36) | copy-start | bytes 1179652
  41.5 2.8 %copy-start.18 = (f32[3,8,128]{2,1,0:T(8,128)}, f32[3,8,128]{2,1,0:T(8,128)S(1)}, u32[]{:S(2)}) copy-start(f32[3,8,128]{2,1,0:T(8,128)S(1)} %get-tuple-element.48) | copy-start | bytes 36868
  41.6 2.8 %copy-start.12 = (bf16[384,512]{0,1:T(8,128)(2,1)S(1)}, bf16[384,512]{0,1:T(8,128)(2,1)}, u32[]{:S(2)}) copy-start(bf16[384,512]{0,1:T(8,128)(2,1)} %get-tuple-element.31) | copy-start | bytes 1179652
  41.6 2.8 %copy-start.14 = (bf16[384,512]{0,1:T(8,128)(2,1)S(1)}, bf16[384,512]{0,1:T(8,128)(2,1)}, u32[]{:S(2)}) copy-start(bf16[384,512]{0,1:T(8,128)(2,1)} %get-tuple-element.32) | copy-start | bytes 1179652
  41.6 2.8 %copy-start.16 = (bf16[384,512]{0,1:T(8,128)(2,1)S(1)}, bf16[384,512]{0,1:T(8,128)(2,1)}, u32[]{:S(2)}) copy-start(bf16[384,512]{0,1:T(8,128)(2,1)} %get-tuple-element.33) | copy-start | bytes 1179652
  44.4 7.1 %copy-start.7 = (bf16[384,512]{0,1:T(8,128)(2,1)S(1)}, bf16[384,512]{0,1:T(8,128)(2,1)}, u32[]{:S(2)}) copy-start(bf16[384,512]{0,1:T(8,128)(2,1)} %copy-done.6) | copy-start | bytes 1179652
  44.4 7.1 %copy-start.9 = (bf16[384,512]{0,1:T(8,128)(2,1)S(1)}, bf16[384,512]{0,1:T(8,128)(2,1)}, u32[]{:S(2)}) copy-start(bf16[384,512]{0,1:T(8,128)(2,1)} %copy-done.8) | copy-start | bytes 1179652
  44.4 7.1 %copy-start.11 = (bf16[384,512]{0,1:T(8,128)(2,1)S(1)}, bf16[384,512]{0,1:T(8,128)(2,1)}, u32[]{:S(2)}) copy-start(bf16[384,512]{0,1:T(8,128)(2,1)} %copy-done.10) | copy-start | bytes 1179652
  45.7 6.0 %copy-start.3 = (f32[3,128,8,64]{1,3,2,0:T(8,128)}, f32[3,128,8,64]{1,3,2,0:T(8,128)S(1)}, u32[]{:S(2)}) copy-start(f32[3,128,8,64]{1,3,2,0:T(8,128)S(1)} %get-tuple-element.50) | copy-start | bytes 2359300
  45.7 3.7 %collective-permute-start.3 = (f32[2,384]{1,0:T(2,128)S(1)}, f32[2,384]{1,0:T(2,128)S(1)}, u32[]{:S(2)}, u32[]{:S(2)}) collective-permute-start(f32[2,384]{1,0:T(2,128)S(1)} %pad_maximum_fusion.9), channel_id=1, source_target_pairs={{0,16},{16,0},{1,17},{17,1},{2,18},{18,2},{3,19},{19,3},{4,20},{20... | collective-permute-start | bytes 9224 | tf_op jit(solution)/shard_map/ppermute | solution.py:22
  50.0 5.6 %collective-permute-start.4 = (f32[2,384]{1,0:T(2,128)}, f32[2,384]{1,0:T(2,128)S(1)}, u32[]{:S(2)}, u32[]{:S(2)}) collective-permute-start(f32[2,384]{1,0:T(2,128)} %fusion.40), channel_id=1, source_target_pairs={{0,1},{1,0},{2,3},{3,2},{4,5},{5,4},{6,7},{7,6},{8,9},{9,8},{10,11... | collective-permute-start | bytes 9224 | tf_op jit(solution)/shard_map/ppermute | solution.py:131
  57.3 1.0 copy-start.13
  57.3 1.1 %copy-start.15 = (bf16[384,512]{0,1:T(8,128)(2,1)S(1)}, bf16[384,512]{0,1:T(8,128)(2,1)}, u32[]{:S(2)}) copy-start(bf16[384,512]{0,1:T(8,128)(2,1)} %get-tuple-element.32) | copy-start | bytes 1179652
  57.3 1.2 %copy-start.17 = (bf16[384,512]{0,1:T(8,128)(2,1)S(1)}, bf16[384,512]{0,1:T(8,128)(2,1)}, u32[]{:S(2)}) copy-start(bf16[384,512]{0,1:T(8,128)(2,1)} %get-tuple-element.33) | copy-start | bytes 1179652
  57.3 1.2 %copy-start.19 = (f32[3,8,128]{2,1,0:T(8,128)S(1)}, f32[3,8,128]{2,1,0:T(8,128)}, u32[]{:S(2)}) copy-start(f32[3,8,128]{2,1,0:T(8,128)} %copy-done.18) | copy-start | bytes 36868
  58.5 3.2 %copy-start.5 = (bf16[3,128,8,64]{1,0,3,2:T(4,128)(2,1)S(1)}, bf16[3,128,8,64]{1,0,3,2:T(4,128)(2,1)}, u32[]{:S(2)}) copy-start(bf16[3,128,8,64]{1,0,3,2:T(4,128)(2,1)} %copy-done.4) | copy-start | bytes 1179652
  63.3 8.2 %copy-start = (f32[896,1024]{0,1:T(8,128)}, f32[896,1024]{0,1:T(8,128)S(1)}, u32[]{:S(2)}) copy-start(f32[896,1024]{0,1:T(8,128)S(1)} %fusion.17) | copy-start | bytes 11010052
  64.4 7.7 %copy-start.2 = (f32[1,384,512]{1,2,0:T(8,128)S(1)}, f32[1,384,512]{1,2,0:T(8,128)}, u32[]{:S(2)}) copy-start(f32[1,384,512]{1,2,0:T(8,128)} %reshape.302) | copy-start | bytes 2359300
  64.4 10.8 %collective-permute-start.5 = (bf16[256,1024]{0,1:T(8,128)(2,1)}, bf16[256,1024]{0,1:T(8,128)(2,1)S(1)}, u32[]{:S(2)}, u32[]{:S(2)}) collective-permute-start(bf16[256,1024]{0,1:T(8,128)(2,1)} %get-tuple-element.9), channel_id=1, source_target_pairs={{0,2},{2,4},{4,6},{6,8},{8,10},{10,12},{12,14},{1,3},{3,5},{5,7},{... | collective-permute-start | bytes 1572872 | tf_op jit(solution)/shard_map/ppermute | solution.py:18
  66.9 10.3 %collective-permute-start.6 = (bf16[256,1024]{0,1:T(8,128)(2,1)}, bf16[256,1024]{0,1:T(8,128)(2,1)}, u32[]{:S(2)}, u32[]{:S(2)}) collective-permute-start(bf16[256,1024]{0,1:T(8,128)(2,1)} %get-tuple-element.10), channel_id=1, source_target_pairs={{2,0},{4,2},{6,4},{8,6},{10,8},{12,10},{14,12},{3,1},{5,3},{7,5},{... | collective-permute-start | bytes 1572872 | tf_op jit(solution)/shard_map/ppermute | solution.py:18
  79.2 19.6 %collective-permute-start.7 = (bf16[2,384,512]{1,2,0:T(8,128)(2,1)S(1)}, bf16[2,384,512]{1,2,0:T(8,128)(2,1)S(1)}, u32[]{:S(2)}, u32[]{:S(2)}) collective-permute-start(bf16[2,384,512]{1,2,0:T(8,128)(2,1)S(1)} %get-tuple-element.26), channel_id=1, source_target_pairs={{0,16},{16,0},{1,17},{17,1},{2,18},{18,2},{3,19},{19,3},{4,20},{20... | collective-permute-start | bytes 2359304 | tf_op jit(solution)/shard_map/ppermute | solution.py:22

commit v8 on v3

--- a/solution.py
+++ b/solution.py
@@ -39,21 +39,27 @@
     return starts - (first_unit - halo_units), allowed
 
 
-def attention_grads(queries, cotangent, near_keys, near_values, rel_starts, allowed, total_fn, total_cols):
+def attention_grads(queries, cotangent, pieces, rel_starts, allowed, total_fn, total_cols):
     rows, head_cols = queries.shape
     heads = head_cols // DH
     unit_count = rows // UNIT
     window = MAX_DOC_UNITS * UNIT
     score_scale = DH ** (-0.5)
+    units = [piece[u * UNIT : (u + 1) * UNIT] for piece in pieces for u in range(piece.shape[0] // UNIT)]
 
-    def windows(near):
-        pieces = [
-            lax.dynamic_slice_in_dim(near, rel_starts[j] * UNIT, window, 0) for j in range(unit_count)
-        ]
-        return jnp.stack(pieces).reshape(unit_count, window, heads, DH)
+    def candidate(first):
+        return jnp.concatenate(units[first : first + MAX_DOC_UNITS], axis=0)
 
-    keys_w = windows(near_keys)
-    values_w = windows(near_values)
+    joined_w = []
+    for j in range(unit_count):
+        offset = rel_starts[j] - j
+        chosen = candidate(j + MAX_DOC_UNITS - 1)
+        for shift in range(MAX_DOC_UNITS - 2, -1, -1):
+            chosen = jnp.where(offset == shift, candidate(j + shift), chosen)
+        joined_w.append(chosen)
+    joined_w = jnp.stack(joined_w)
+    keys_w = joined_w[:, :, :head_cols].reshape(unit_count, window, heads, DH)
+    values_w = joined_w[:, :, head_cols:].reshape(unit_count, window, heads, DH)
     q4 = queries.reshape(unit_count, UNIT, heads, DH)
     cot_float = cotangent.astype(jnp.float32)
 
@@ -89,7 +95,7 @@
         [grad_kw.reshape(unit_count, window, head_cols), grad_vw.reshape(unit_count, window, head_cols)],
         axis=2,
     )
-    near_rows = near_keys.shape[0]
+    near_rows = sum(piece.shape[0] for piece in pieces)
     total = jnp.zeros((near_rows, 2 * head_cols), jnp.float32)
     for j in range(unit_count):
         start = rel_starts[j] * UNIT
@@ -122,7 +128,6 @@
     joined = jnp.concatenate([key_value[0], key_value[1]], axis=1)
     low = seq_shift(joined[rows - halo :], 1)
     high = seq_shift(joined[:halo], -1)
-    near = jnp.concatenate([low, joined, high], axis=0)
 
     rel_starts, allowed = window_plan(doc_units, seq_place, unit_count, halo_units)
 
@@ -135,14 +140,13 @@
     grad_q, normed, total = attention_grads(
         query_cot[0],
         query_cot[1],
-        near[:, :half],
-        near[:, half:],
+        (low, joined, high),
         rel_starts,
         allowed,
         row_total,
         total_cols,
     )
-    from_left = seq_shift(total[near.shape[0] - halo :].astype(jnp.bfloat16), 1)
+    from_left = seq_shift(total[rows + halo :].astype(jnp.bfloat16), 1)
     from_right = seq_shift(total[:halo].astype(jnp.bfloat16), -1)
     own = (
         total[halo : halo + rows]

time: 97.2 us -> 107 us (1.10)
  matrix products: 6.2 us -> 11.1 us
  local copies, waits for them, and re-layouts: 15.2 us -> 18.8 us
  between operations: 2.39 us -> 4.9 us
  waiting for transfers between devices: 47.9 us -> 45.6 us
  other arithmetic: 12.7 us -> 13.8 us
    sub x0 -> x1, matrix products: none -> 3.57 us  [attention_grads(): expven = jnp.exp(scores - row_max)]
    select_n x0 -> x2, other arithmetic: none -> 3.1 us  [attention_grads(): chosen = jnp.where(offset == shift, candidate(j + shift), chosen)]
    unnamed x46 -> x22, local copies, waits for them, and re-layouts: 5.28 us -> 2.41 us
    ppermute x4, waiting for transfers between devices: 9.04 us -> 6.18 us  [seq_shift(): lax.ppermute(value, 'seq', [(source, source + steps) for source in range(...]
    convert_element_type x1, other arithmetic: 0.6 us -> 2.78 us  [attention_grads(): rounded = weights.astype(jnp.bfloat16)]
    transpose x1, local copies, waits for them, and re-layouts: 0.54 us -> 2.67 us  [attention_grads(): jnp.einsum('jhqk,jkhd->jqhd', rounded, values_w, preferred_element_type=j...]
    concatenate x0 -> x2, local copies, waits for them, and re-layouts: none -> 1.94 us  [candidate(): return jnp.concatenate(units[first:first + MAX_DOC_UNITS], axis=0)]
    sub x1 -> x0, other arithmetic: 1.72 us -> none  [attention_grads(): expven = jnp.exp(scores - row_max)]
  transfers between devices with their start and end apart: 8 -> 8, of which waited for: 7 -> 6; matrix products, arithmetic and copies ran while one was open for 9% -> 13% of each run, Pallas kernels for 0% -> 0%
where the time goes in v8:
time: 107 us
  waiting for transfers between devices  45.6 us (43%)
  local copies, waits for them, and re-layouts  18.8 us (18%)
  other arithmetic  13.8 us (13%)
  starting transfers between devices  12.5 us (12%)
  matrix products  11.1 us (10%)
  between operations  4.9 us (5%)
    ppermute x3, waiting for transfers between devices, sec_swap(): return lax.ppermute(value, 'sec', [(0, 1), (1, 0)])  39.4 us
    ppermute x4, starting transfers between devices, seq_shift(): lax.ppermute(value, 'seq', [(source, source + steps) for source in range(...  9.08 us
    ppermute x4, waiting for transfers between devices, seq_shift(): lax.ppermute(value, 'seq', [(source, source + steps) for source in range(...  6.18 us
    sub x1, matrix products, attention_grads(): expven = jnp.exp(scores - row_max)  3.57 us
    dot_general x1, matrix products, attention_grads(): jnp.einsum('jqhd,jkhd->jhqk', up4, values_w, preferred_element_type=jnp.f...  3.14 us
    select_n x2, other arithmetic, attention_grads(): chosen = jnp.where(offset == shift, candidate(j + shift), chosen)  3.1 us
    convert_element_type x1, other arithmetic, attention_grads(): rounded = weights.astype(jnp.bfloat16)  2.78 us
    transpose x1, local copies, waits for them, and re-layouts, attention_grads(): jnp.einsum('jhqk,jkhd->jqhd', rounded, values_w, preferred_element_type=j...  2.67 us
  transfers between devices with their start and end apart: 8, of which 6 were waited for; matrix products, arithmetic and copies ran while one was open for 13% of the time, Pallas kernels for 0%

profile of v8, /device:TPU:18, one launch (start us, length us, event | category | flops | bytes accessed | tf_op | source)
XLA Modules:
  0.0 106.6 jit_solution(7333814725463002778)
XLA Ops:
  0.0 1.5 %constant_dynamic-slice_fusion = (bf16[1,2,384,512]{3,2,1,0:T(8,128)(2,1)S(1)}, bf16[1,2,384,512]{3,2,1,0:T(8,128)(2,1)S(1)}) fusion(bf16[1,2,384,1024]{3,2,1,0:T(8,128)(2,1)} %param.2, s32[]{:T(128)S(6)} %select_n.165, s32[]{:T(128)S(6)} %select_n.164), kind=kLoop, calls=%fused_computation.85 | loop fusion | bytes 3145736 | tf_op jit(solution)/shard_map/dynamic_slice | solution.py:123
  1.5 0.4 copy.16
  1.9 0.6 collective-permute-start
  2.5 0.4 copy.17
  3.6 17.6 %collective-permute-done = bf16[2,384,512]{1,2,0:T(8,128)(2,1)S(1)} collective-permute-done((bf16[2,384,512]{1,2,0:T(8,128)(2,1)S(1)}, bf16[2,384,512]{1,2,0:T(8,128)(2,1)S(1)}, u32[]{:S(2)}, u32[]{:S(2)}) %collective-permute-start) | collective-permute-done | bytes 786464 | tf_op jit(solution)/shard_map/ppermute | solution.py:22
  21.4 1.1 %slice_convert_fusion = (f32[1,384,512]{1,2,0:T(8,128)}, bf16[1,384,512]{1,2,0:T(8,128)(2,1)S(1)}, bf16[1,384,512]{1,2,0:T(8,128)(2,1)S(1)}, bf16[384,512]{0,1:T...) fusion(bf16[2,384,512]{1,2,0:T(8,128)(2,1)S(1)} %get-tuple-element.19, ...), kind=kLoop, calls=%fused_computation.61 | loop fusion | flops 196608 | bytes 4325376 | tf_op jit(solution)/shard_map/convert_element_type | solution.py:64
  22.5 0.9 fusion.21
  23.3 1.9 %collective-permute-start.2 = (bf16[256,1024]{0,1:T(8,128)(2,1)}, bf16[256,1024]{0,1:T(8,128)(2,1)}, u32[]{:S(2)}, u32[]{:S(2)}) collective-permute-start(bf16[256,1024]{0,1:T(8,128)(2,1)} %get-tuple-element.36), channel_id=1, source_target_pairs={{2,0},{4,2},{6,4},{8,6},{10,8},{12,10},{14,12},{3,1},{5,3},{7,5},{... | collective-permute-start | bytes 1572872 | tf_op jit(solution)/shard_map/ppermute | solution.py:18
  25.4 2.4 %collective-permute-start.1 = (bf16[256,1024]{0,1:T(8,128)(2,1)S(1)}, bf16[256,1024]{0,1:T(8,128)(2,1)}, u32[]{:S(2)}, u32[]{:S(2)}) collective-permute-start(bf16[256,1024]{0,1:T(8,128)(2,1)S(1)} %get-tuple-element.35), channel_id=1, source_target_pairs={{0,2},{2,4},{4,6},{6,8},{8,10},{10,12},{12,14},{1,3},{3,5},{5,7},{... | collective-permute-start | bytes 1572872 | tf_op jit(solution)/shard_map/ppermute | solution.py:18
  27.8 0.7 fusion.47
  31.1 1.4 %reshape.553 = f32[3,128,8,64]{1,0,3,2:T(4,128)S(1)} reshape(f32[1,384,512]{1,2,0:T(8,128)} %get-tuple-element.27) | data formatting | bytes 1572864 | tf_op jit(solution)/shard_map/convert_element_type | solution.py:64
  32.5 1.0 reshape_squeeze.3
  33.5 1.0 slice_bitcast_fusion.2
  34.5 1.4 %fusion.19 = bf16[1,384,1024]{1,2,0:T(8,128)(2,1)S(1)} fusion(bf16[1,256,1024]{1,2,0:T(8,128)(2,1)} %bitcast.19, bf16[1,128,1024]{1,2,0:T(8,128)(2,1)S(1)} %get-tuple-element.30, pred[]{:T(512)} %bitcast.17, pred[]{:T(512)} %bitcast.16, bf16[1,128,1024]{1,2,0:T(8,128)(2,1)S(1)} %slice_bitcast_fusion.2, bf16[1,256,1024]{1,2,0:T(8,128)(2,1)S(1)} %bitcast.109, ...), kind=kLoop, calls=%fused_computation.44 | loop fusion | flops 5505024 | bytes 3145730 | tf_op jit(solution)/shard_map/jit(_where)/select_n | solution.py:58
  36.0 1.0 slice_bitcast_fusion.3
  37.0 1.7 %maximum_select_fusion.1 = (bf16[1,384,1024]{1,2,0:T(8,128)(2,1)S(1)}, bf16[1,384,1024]{1,2,0:T(8,128)(2,1)S(1)}) fusion(bf16[1,128,1024]{1,2,0:T(8,128)(2,1)S(1)} %get-tuple-element.29, bf16[1,256,1024]{1,2,0:T(8,128)(2,1)} %bitcast.7, pred[]{:T(512)} %bitcast.9, pred[]{:T(512)} %bitcast.4, bf16[1,256,1024]{1,2,0:T(8,128)(2,1)} %bitcast.11, ...), kind=kLoop, calls=%fused_computation.39 | loop fusion | flops 7864320 | bytes 4718596 | tf_op jit(solution)/shard_map/jit(_where)/select_n | solution.py:58
  38.7 0.3 pad_maximum_fusion
  39.0 1.3 %fusion.44 = (bf16[3,384,512]{1,2,0:T(8,128)(2,1)S(1)}, bf16[3,384,512]{1,2,0:T(8,128)(2,1)}) fusion(bf16[3,384,1024]{1,2,0:T(8,128)(2,1)S(1)} %pad_maximum_fusion), kind=kLoop, calls=%fused_computation.102 | loop fusion | bytes 4718592 | tf_op jit(solution)/shard_map/slice | solution.py:61
  40.3 3.6 %fusion.48 = (f32[3,8,128]{2,1,0:T(8,128)S(1)}, f32[3,8,128,384]{3,2,1,0:T(8,128)}) fusion(pred[3,384]{1,0:T(4,128)(4,1)S(1)} %bitcast.128, bf16[3,384,8,64]{1,3,2,0:T(8,128)(2,1)S(1)} %bitcast.111, bf16[3,128,8,64]{1,0,3,2:T(4,128)(2,1)S(1)} %copy-done.6), kind=kOutput, calls=%fused_computation.106 | convolution fusion | flops 155713920 | bytes 6304896 | tf_op jit(solution)/shard_map/sub | solution.py:72
  43.9 2.8 %fusion.5 = bf16[3,8,128,384]{3,2,1,0:T(8,128)(2,1)S(1)} fusion(f32[3,8,128,384]{3,2,1,0:T(8,128)} %get-tuple-element.41, f32[3,8,128]{2,1,0:T(8,128)S(1)} %get-tuple-element.40), kind=kLoop, calls=%fused_computation.14 | loop fusion | flops 2359296 | bytes 7090176 | tf_op jit(solution)/shard_map/convert_element_type | solution.py:74
  46.7 2.1 %multiply_reduce_fusion.2 = (f32[3,128]{1,0:T(4,128)S(1)}, f32[3,128]{1,0:T(4,128)S(1)}, f32[3,128,8,64]{1,3,2,0:T(8,128)}) fusion(f32[3,128,8,64]{1,0,3,2:T(4,128)S(1)} %reshape.553, bf16[3,384,8,64]{1,3,2,0:T(8,128)(2,1)S(1)} %bitcast.113, bf16[3,8,128,384]{3,2,1,0:T(8,128)(2,1)S(1)} %fusion.5), kind=kOutput, calls=%fused_computation.54 | convolution fusion | flops 151780608 | bytes 5114880 | tf_op jit(solution)/shard_map/jhqk,jkhd->jqhd/dot_general | solution.py:75
  48.8 0.6 collective-permute-start.3
  49.4 3.1 %collective-permute-done.3 = f32[2,384]{1,0:T(2,128)S(1)} collective-permute-done((f32[2,384]{1,0:T(2,128)S(1)}, f32[2,384]{1,0:T(2,128)S(1)}, u32[]{:S(2)}, u32[]{:S(2)}) %collective-permute-start.3) | collective-permute-done | bytes 3104 | tf_op jit(solution)/shard_map/ppermute | solution.py:22
  52.5 1.6 %collective-permute-start.4 = (f32[2,384]{1,0:T(2,128)S(1)}, f32[2,384]{1,0:T(2,128)S(1)}, u32[]{:S(2)}, u32[]{:S(2)}) collective-permute-start(f32[2,384]{1,0:T(2,128)S(1)} %fusion.43), channel_id=1, source_target_pairs={{0,1},{1,0},{2,3},{3,2},{4,5},{5,4},{6,7},{7,6},{8,9},{9,8},{10,11... | collective-permute-start | bytes 9224 | tf_op jit(solution)/shard_map/ppermute | solution.py:137
  56.0 2.7 %copy.23 = f32[3,128,8,64]{1,0,3,2:T(4,128)} copy(f32[3,128,8,64]{1,3,2,0:T(8,128)} %get-tuple-element.42) | data formatting | bytes 1572864 | tf_op jit(solution)/shard_map/jhqk,jkhd->jqhd/transpose | solution.py:75
  58.7 2.4 %reshape.552 = f32[1,384,512]{1,2,0:T(8,128)} reshape(f32[3,128,8,64]{1,0,3,2:T(4,128)} %copy.23) | data formatting | bytes 1572864 | tf_op jit(solution)/shard_map/reshape | solution.py:76
  61.1 1.3 %multiply_reduce_fusion = (f32[3,128,8]{1,2,0:T(8,128)S(1)}, bf16[3,128,8,64]{1,3,2,0:T(8,128)(2,1)S(1)}) fusion(f32[3,128,8,64]{1,3,2,0:T(8,128)} %get-tuple-element.42, f32[3,128]{1,0:T(4,128)S(1)} %bitcast.127, f32[3,128]{1,0:T(4,128)S(1)} %bitcast.123, f32[3,128,8,64]{1,0,3,2:T(4,128)S(1)} %reshape.553), kind=kLoop, calls=%fused_computation.51 | loop fusion | flops 1569792 | bytes 1981440 | tf_op jit(solution)/shard_map/reduce_sum | solution.py:87
  62.5 0.6 fusion.53
  63.1 0.7 copy-done.4
  63.8 3.1 %multiply_convert_fusion = bf16[3,8,128,384]{3,2,1,0:T(8,128)(2,1)S(1)} fusion(f32[3,8,128]{2,1,0:T(8,128)S(1)} %bitcast.124, bf16[3,128,8,64]{1,3,2,0:T(8,128)(2,1)S(1)} %get-tuple-element.12, bf16[3,384,8,64]{1,3,2,0:T(8,128)(2,1)S(1)} %bitcast.114, f32[3,8,128,384]{3,2,1,0:T(8,128)} %get-tuple-element.41, f32[3,8,128]{2,1,0:T(8,128)S(1)} %get-tuple-element.40), kind=kOutput, calls=%fused_computation.5 | convolution fusion | flops 156893184 | bytes 8675328 | tf_op jit(solution)/shard_map/jqhd,jkhd->jhqk/dot_general | solution.py:89
  66.9 0.6 fusion.32
  67.5 0.2 broadcast_in_dim.36
  67.9 0.3 fusion.9
  68.2 0.3 fusion.17
  68.7 1.6 %copy-done = f32[896,1024]{0,1:T(8,128)} copy-done((f32[896,1024]{0,1:T(8,128)}, f32[896,1024]{0,1:T(8,128)S(1)}, u32[]{:S(2)}) %copy-start) | copy-done | bytes 3670040
  70.3 2.1 %collective-permute-start.6 = (bf16[256,1024]{0,1:T(8,128)(2,1)S(1)}, bf16[256,1024]{0,1:T(8,128)(2,1)S(1)}, u32[]{:S(2)}, u32[]{:S(2)}) collective-permute-start(bf16[256,1024]{0,1:T(8,128)(2,1)S(1)} %get-tuple-element.16), channel_id=1, source_target_pairs={{2,0},{4,2},{6,4},{8,6},{10,8},{12,10},{14,12},{3,1},{5,3},{7,5},{... | collective-permute-start | bytes 1572872 | tf_op jit(solution)/shard_map/ppermute | solution.py:18
  72.4 2.7 %collective-permute-start.5 = (bf16[256,1024]{0,1:T(8,128)(2,1)S(1)}, bf16[256,1024]{0,1:T(8,128)(2,1)}, u32[]{:S(2)}, u32[]{:S(2)}) collective-permute-start(bf16[256,1024]{0,1:T(8,128)(2,1)S(1)} %get-tuple-element.15), channel_id=1, source_target_pairs={{0,2},{2,4},{4,6},{6,8},{8,10},{10,12},{12,14},{1,3},{3,5},{5,7},{... | collective-permute-start | bytes 1572872 | tf_op jit(solution)/shard_map/ppermute | solution.py:18
  75.1 1.2 %fusion.18 = bf16[3,128,8,64]{1,3,2,0:T(8,128)(2,1)S(1)} fusion(bf16[3,384,8,64]{1,3,2,0:T(8,128)(2,1)S(1)} %bitcast.112, bf16[3,8,128,384]{3,2,1,0:T(8,128)(2,1)S(1)} %multiply_convert_fusion), kind=kOutput, calls=%fused_computation.32 | convolution fusion | flops 151191552 | bytes 3932160 | tf_op jit(solution)/shard_map/jhqk,jkhd->jqhd/dot_general | solution.py:91
  76.3 0.3 copy.22
  76.6 0.3 convert_element_type.73
  77.1 2.0 %collective-permute-done.6 = bf16[256,1024]{0,1:T(8,128)(2,1)S(1)} collective-permute-done((bf16[256,1024]{0,1:T(8,128)(2,1)S(1)}, bf16[256,1024]{0,1:T(8,128)(2,1)S(1)}, u32[]{:S(2)}, u32[]{:S(2)}) %collective-permute-start.6) | collective-permute-done | bytes 524320 | tf_op jit(solution)/shard_map/ppermute | solution.py:18
  79.1 4.1 %collective-permute-done.5 = bf16[256,1024]{0,1:T(8,128)(2,1)} collective-permute-done((bf16[256,1024]{0,1:T(8,128)(2,1)S(1)}, bf16[256,1024]{0,1:T(8,128)(2,1)}, u32[]{:S(2)}, u32[]{:S(2)}) %collective-permute-start.5) | collective-permute-done | bytes 524320 | tf_op jit(solution)/shard_map/ppermute | solution.py:18
  83.1 1.7 %fusion.14 = bf16[384,1024]{0,1:T(8,128)(2,1)S(1)} fusion(f32[896,1024]{0,1:T(8,128)} %copy-done, bf16[256,1024]{0,1:T(8,128)(2,1)S(1)} %collective-permute-done.6, bf16[256,1024]{0,1:T(8,128)(2,1)} %collective-permute-done.5), kind=kLoop, calls=%fused_computation.24 | loop fusion | flops 1966080 | bytes 3407872 | tf_op jit(solution)/shard_map/convert.6
  84.9 0.2 select_bitcast_fusion
  85.2 0.6 collective-permute-start.7
  85.8 18.7 %collective-permute-done.7 = bf16[2,384,512]{1,2,0:T(8,128)(2,1)S(1)} collective-permute-done((bf16[2,384,512]{1,2,0:T(8,128)(2,1)S(1)}, bf16[2,384,512]{1,2,0:T(8,128)(2,1)S(1)}, u32[]{:S(2)}, u32[]{:S(2)}) %collective-permute-start.7) | collective-permute-done | bytes 786464 | tf_op jit(solution)/shard_map/ppermute | solution.py:22
  104.5 0.4 maximum_select_fusion
  104.9 1.6 %copy.24 = bf16[1,2,384,1024]{3,2,1,0:T(8,128)(2,1)} copy(bf16[1,2,384,1024]{2,3,1,0:T(8,128)(2,1)S(1)} %maximum_select_fusion) | data formatting | bytes 3145728 | tf_op jit(solution)/shard_map/jit(_where)/select_n | solution.py:163
  (43 shorter events, 1.9 us)
Async XLA Ops:
  1.5 1.3 %copy-start.8 = (s32[12]{0:T(128)S(1)}, s32[12]{0:T(128)}, u32[]{:S(2)}) copy-start(s32[12]{0:T(128)} %param.3) | copy-start | bytes 148
  1.9 19.3 %collective-permute-start = (bf16[2,384,512]{1,2,0:T(8,128)(2,1)S(1)}, bf16[2,384,512]{1,2,0:T(8,128)(2,1)S(1)}, u32[]{:S(2)}, u32[]{:S(2)}) collective-permute-start(bf16[2,384,512]{1,2,0:T(8,128)(2,1)S(1)} %bitcast.115), channel_id=1, source_target_pairs={{0,16},{16,0},{1,17},{17,1},{2,18},{18,2},{3,19},{19,3},{4,20},{20... | collective-permute-start | bytes 2359304 | tf_op jit(solution)/shard_map/ppermute | solution.py:22
  23.3 10.2 %collective-permute-start.2 = (bf16[256,1024]{0,1:T(8,128)(2,1)}, bf16[256,1024]{0,1:T(8,128)(2,1)}, u32[]{:S(2)}, u32[]{:S(2)}) collective-permute-start(bf16[256,1024]{0,1:T(8,128)(2,1)} %get-tuple-element.36), channel_id=1, source_target_pairs={{2,0},{4,2},{6,4},{8,6},{10,8},{12,10},{14,12},{3,1},{5,3},{7,5},{... | collective-permute-start | bytes 1572872 | tf_op jit(solution)/shard_map/ppermute | solution.py:18
  25.4 10.6 %collective-permute-start.1 = (bf16[256,1024]{0,1:T(8,128)(2,1)S(1)}, bf16[256,1024]{0,1:T(8,128)(2,1)}, u32[]{:S(2)}, u32[]{:S(2)}) collective-permute-start(bf16[256,1024]{0,1:T(8,128)(2,1)S(1)} %get-tuple-element.35), channel_id=1, source_target_pairs={{0,2},{2,4},{4,6},{6,8},{8,10},{10,12},{12,14},{1,3},{3,5},{5,7},{... | collective-permute-start | bytes 1572872 | tf_op jit(solution)/shard_map/ppermute | solution.py:18
  39.0 1.3 %copy-start.6 = (bf16[3,128,8,64]{1,0,3,2:T(4,128)(2,1)S(1)}, bf16[3,128,8,64]{1,0,3,2:T(4,128)(2,1)}, u32[]{:S(2)}) copy-start(bf16[3,128,8,64]{1,0,3,2:T(4,128)(2,1)} %reshape_squeeze.3) | copy-start | bytes 1179652
  40.3 3.6 %copy-start.1 = (bf16[3,384,512]{1,2,0:T(8,128)(2,1)}, bf16[3,384,512]{1,2,0:T(8,128)(2,1)S(1)}, u32[]{:S(2)}) copy-start(bf16[3,384,512]{1,2,0:T(8,128)(2,1)S(1)} %get-tuple-element.13) | copy-start | bytes 3538948
  43.9 2.8 %copy-start.3 = (bf16[3,384,512]{1,2,0:T(8,128)(2,1)S(1)}, bf16[3,384,512]{1,2,0:T(8,128)(2,1)}, u32[]{:S(2)}) copy-start(bf16[3,384,512]{1,2,0:T(8,128)(2,1)} %get-tuple-element.14) | copy-start | bytes 3538948
  48.8 3.7 %collective-permute-start.3 = (f32[2,384]{1,0:T(2,128)S(1)}, f32[2,384]{1,0:T(2,128)S(1)}, u32[]{:S(2)}, u32[]{:S(2)}) collective-permute-start(f32[2,384]{1,0:T(2,128)S(1)} %pad_maximum_fusion.8), channel_id=1, source_target_pairs={{0,16},{16,0},{1,17},{17,1},{2,18},{18,2},{3,19},{19,3},{4,20},{20... | collective-permute-start | bytes 9224 | tf_op jit(solution)/shard_map/ppermute | solution.py:22
  52.5 8.6 %collective-permute-start.4 = (f32[2,384]{1,0:T(2,128)S(1)}, f32[2,384]{1,0:T(2,128)S(1)}, u32[]{:S(2)}, u32[]{:S(2)}) collective-permute-start(f32[2,384]{1,0:T(2,128)S(1)} %fusion.43), channel_id=1, source_target_pairs={{0,1},{1,0},{2,3},{3,2},{4,5},{5,4},{6,7},{7,6},{8,9},{9,8},{10,11... | collective-permute-start | bytes 9224 | tf_op jit(solution)/shard_map/ppermute | solution.py:137
  62.5 1.3 %copy-start.4 = (bf16[3,384,512]{1,2,0:T(8,128)(2,1)S(1)}, bf16[3,384,512]{1,2,0:T(8,128)(2,1)}, u32[]{:S(2)}) copy-start(bf16[3,384,512]{1,2,0:T(8,128)(2,1)} %get-tuple-element.14) | copy-start | bytes 3538948
  63.8 3.2 %copy-start.7 = (bf16[3,128,8,64]{1,0,3,2:T(4,128)(2,1)S(1)}, bf16[3,128,8,64]{1,0,3,2:T(4,128)(2,1)}, u32[]{:S(2)}) copy-start(bf16[3,128,8,64]{1,0,3,2:T(4,128)(2,1)} %reshape_squeeze.3) | copy-start | bytes 1179652
  68.5 1.8 %copy-start = (f32[896,1024]{0,1:T(8,128)}, f32[896,1024]{0,1:T(8,128)S(1)}, u32[]{:S(2)}) copy-start(f32[896,1024]{0,1:T(8,128)S(1)} %fusion.17) | copy-start | bytes 11010052
  70.2 4.9 %copy-start.2 = (bf16[3,384,512]{1,2,0:T(8,128)(2,1)S(1)}, bf16[3,384,512]{1,2,0:T(8,128)(2,1)}, u32[]{:S(2)}) copy-start(bf16[3,384,512]{1,2,0:T(8,128)(2,1)} %copy-done.1) | copy-start | bytes 3538948
  70.3 8.7 %collective-permute-start.6 = (bf16[256,1024]{0,1:T(8,128)(2,1)S(1)}, bf16[256,1024]{0,1:T(8,128)(2,1)S(1)}, u32[]{:S(2)}, u32[]{:S(2)}) collective-permute-start(bf16[256,1024]{0,1:T(8,128)(2,1)S(1)} %get-tuple-element.16), channel_id=1, source_target_pairs={{2,0},{4,2},{6,4},{8,6},{10,8},{12,10},{14,12},{3,1},{5,3},{7,5},{... | collective-permute-start | bytes 1572872 | tf_op jit(solution)/shard_map/ppermute | solution.py:18
  72.4 4.6 %copy-start.5 = (f32[1,384,512]{1,2,0:T(8,128)S(1)}, f32[1,384,512]{1,2,0:T(8,128)}, u32[]{:S(2)}) copy-start(f32[1,384,512]{1,2,0:T(8,128)} %reshape.552) | copy-start | bytes 2359300
  72.4 10.7 %collective-permute-start.5 = (bf16[256,1024]{0,1:T(8,128)(2,1)S(1)}, bf16[256,1024]{0,1:T(8,128)(2,1)}, u32[]{:S(2)}, u32[]{:S(2)}) collective-permute-start(bf16[256,1024]{0,1:T(8,128)(2,1)S(1)} %get-tuple-element.15), channel_id=1, source_target_pairs={{0,2},{2,4},{4,6},{6,8},{8,10},{10,12},{12,14},{1,3},{3,5},{5,7},{... | collective-permute-start | bytes 1572872 | tf_op jit(solution)/shard_map/ppermute | solution.py:18
  85.2 19.3 %collective-permute-start.7 = (bf16[2,384,512]{1,2,0:T(8,128)(2,1)S(1)}, bf16[2,384,512]{1,2,0:T(8,128)(2,1)S(1)}, u32[]{:S(2)}, u32[]{:S(2)}) collective-permute-start(bf16[2,384,512]{1,2,0:T(8,128)(2,1)S(1)} %get-tuple-element.18), channel_id=1, source_target_pairs={{0,16},{16,0},{1,17},{17,1},{2,18},{18,2},{3,19},{19,3},{4,20},{20... | collective-permute-start | bytes 2359304 | tf_op jit(solution)/shard_map/ppermute | solution.py:22

commit v9 on v3

--- a/solution.py
+++ b/solution.py
@@ -64,7 +64,7 @@
     scores = jnp.where(mask, scores, -jnp.inf)
     row_max = jnp.max(scores, axis=3, keepdims=True)
     expven = jnp.exp(scores - row_max)
-    weights = expven / jnp.sum(expven, axis=3, keepdims=True)
+    weights = expven * (1.0 / jnp.sum(expven, axis=3, keepdims=True))
     rounded = weights.astype(jnp.bfloat16)
     attended4 = jnp.einsum("jhqk,jkhd->jqhd", rounded, values_w, preferred_element_type=jnp.float32)
     attended = attended4.reshape(rows, head_cols)
@@ -73,9 +73,10 @@
         (jnp.sum(attended * attended, axis=1), jnp.sum(cot_float * attended, axis=1))
     )
     spread = jnp.sqrt(squares / total_cols + epsilon)
-    normed = attended / spread[:, None]
-    shared = crosses / total_cols / spread
-    upstream = ((cot_float - normed * shared[:, None]) / spread[:, None]).astype(jnp.bfloat16)
+    inverse = 1.0 / spread
+    normed = attended * inverse[:, None]
+    shared = crosses / total_cols * inverse
+    upstream = ((cot_float - normed * shared[:, None]) * inverse[:, None]).astype(jnp.bfloat16)
     up4 = upstream.reshape(unit_count, UNIT, heads, DH)
 
     delta = jnp.sum(up4.astype(jnp.float32) * attended4, axis=3)

time: 97.2 us -> 112 us (1.15)
  matrix products: 6.2 us -> 24.4 us
  local copies, waits for them, and re-layouts: 15.2 us -> 11.1 us
  waiting for transfers between devices: 47.9 us -> 50.1 us
  other arithmetic: 12.7 us -> 11.2 us
    dot_general x1, matrix products: 0.55 us -> 9.34 us  [attention_grads(): jnp.einsum('jhqk,jqhd->jkhd', rounded, up4, preferred_element_type=jnp.fl...]
    dot_general x1, matrix products: 1.22 us -> 8.49 us  [attention_grads(): jnp.einsum('jhqk,jkhd->jqhd', rounded, values_w, preferred_element_type=j...]
    unnamed x46 -> x30, local copies, waits for them, and re-layouts: 5.28 us -> 1.85 us
    ppermute x4, waiting for transfers between devices: 9.04 us -> 11.3 us  [seq_shift(): lax.ppermute(value, 'seq', [(source, source + steps) for source in range(...]
    dot_general x1, matrix products: 1.87 us -> 4.01 us  [attention_grads(): jnp.einsum('jqhd,jkhd->jhqk', up4, values_w, preferred_element_type=jnp.f...]
    sub x1, other arithmetic: 1.72 us -> 3.53 us  [attention_grads(): expven = jnp.exp(scores - row_max)]
    another operation x1, local copies, waits for them, and re-layouts: 1.61 us -> 0.11 us  [attention_grads(): q4 = queries.reshape(unit_count, UNIT, heads, DH)]
    select_n x1, other arithmetic: 1.28 us -> 0.15 us  [per_device(): query_cot = jnp.where(is_first, arrived, kept)]
  transfers between devices with their start and end apart: 8 -> 8, of which waited for: 7 -> 8; matrix products, arithmetic and copies ran while one was open for 9% -> 6% of each run, Pallas kernels for 0% -> 0%
where the time goes in v9:
time: 112 us; the launch traced here: 111 us
  waiting for transfers between devices  50.1 us (45%)
  matrix products  24.4 us (22%)
  starting transfers between devices  12.4 us (11%)
  other arithmetic  11.2 us (10%)
  local copies, waits for them, and re-layouts  11.1 us (10%)
  between operations  2.21 us (2%)
    ppermute x3, waiting for transfers between devices, sec_swap(): return lax.ppermute(value, 'sec', [(0, 1), (1, 0)])  38.6 us
    ppermute x4, waiting for transfers between devices, seq_shift(): lax.ppermute(value, 'seq', [(source, source + steps) for source in range(...  11.3 us
    dot_general x1, matrix products, attention_grads(): jnp.einsum('jhqk,jqhd->jkhd', rounded, up4, preferred_element_type=jnp.fl...  9.34 us
    ppermute x4, starting transfers between devices, seq_shift(): lax.ppermute(value, 'seq', [(source, source + steps) for source in range(...  9 us
    dot_general x1, matrix products, attention_grads(): jnp.einsum('jhqk,jkhd->jqhd', rounded, values_w, preferred_element_type=j...  8.49 us
    dot_general x1, matrix products, attention_grads(): jnp.einsum('jqhd,jkhd->jhqk', up4, values_w, preferred_element_type=jnp.f...  4.01 us
    sub x1, other arithmetic, attention_grads(): expven = jnp.exp(scores - row_max)  3.53 us
  transfers between devices with their start and end apart: 8, of which 8 were waited for; matrix products, arithmetic and copies ran while one was open for 6% of the time, Pallas kernels for 0%

profile of v9, /device:TPU:18, one launch (start us, length us, event | category | flops | bytes accessed | tf_op | source)
XLA Modules:
  0.0 111.4 jit_solution(4041882377382414390)
XLA Ops:
  0.0 1.5 %constant_dynamic-slice_fusion.6 = (bf16[1,2,384,512]{3,2,1,0:T(8,128)(2,1)S(1)}, bf16[1,2,384,512]{3,2,1,0:T(8,128)(2,1)S(1)}) fusion(bf16[1,2,384,1024]{3,2,1,0:T(8,128)(2,1)} %param.2, s32[]{:T(128)S(6)} %select_n.91, s32[]{:T(128)S(6)} %select_n.90), kind=kLoop, calls=%fused_computation.68 | loop fusion | bytes 3145736 | tf_op jit(solution)/shard_map/dynamic_slice | solution.py:118
  1.5 0.4 copy.20
  1.9 0.6 collective-permute-start
  2.5 0.2 reduce-window.8
  2.6 0.2 fusion.25
  2.8 0.4 copy.21
  3.4 0.2 convert_reduce_fusion
  3.7 17.5 %collective-permute-done = bf16[2,384,512]{1,2,0:T(8,128)(2,1)S(1)} collective-permute-done((bf16[2,384,512]{1,2,0:T(8,128)(2,1)S(1)}, bf16[2,384,512]{1,2,0:T(8,128)(2,1)S(1)}, u32[]{:S(2)}, u32[]{:S(2)}) %collective-permute-start) | collective-permute-done | bytes 786464 | tf_op jit(solution)/shard_map/ppermute | solution.py:22
  21.4 1.0 fusion.19
  22.5 1.9 %collective-permute-start.2 = (bf16[256,1024]{0,1:T(8,128)(2,1)}, bf16[256,1024]{0,1:T(8,128)(2,1)}, u32[]{:S(2)}, u32[]{:S(2)}) collective-permute-start(bf16[256,1024]{0,1:T(8,128)(2,1)} %get-tuple-element.34), channel_id=1, source_target_pairs={{2,0},{4,2},{6,4},{8,6},{10,8},{12,10},{14,12},{3,1},{5,3},{7,5},{... | collective-permute-start | bytes 1572872 | tf_op jit(solution)/shard_map/ppermute | solution.py:18
  24.4 2.4 %collective-permute-start.1 = (bf16[256,1024]{0,1:T(8,128)(2,1)}, bf16[256,1024]{0,1:T(8,128)(2,1)}, u32[]{:S(2)}, u32[]{:S(2)}) collective-permute-start(bf16[256,1024]{0,1:T(8,128)(2,1)} %get-tuple-element.33), channel_id=1, source_target_pairs={{0,2},{2,4},{4,6},{6,8},{8,10},{10,12},{12,14},{1,3},{3,5},{5,7},{... | collective-permute-start | bytes 1572872 | tf_op jit(solution)/shard_map/ppermute | solution.py:18
  26.8 0.7 fusion.47
  29.5 0.3 reshape.303
  29.9 1.5 %collective-permute-done.2 = bf16[256,1024]{0,1:T(8,128)(2,1)} collective-permute-done((bf16[256,1024]{0,1:T(8,128)(2,1)}, bf16[256,1024]{0,1:T(8,128)(2,1)}, u32[]{:S(2)}, u32[]{:S(2)}) %collective-permute-start.2) | collective-permute-done | bytes 524320 | tf_op jit(solution)/shard_map/ppermute | solution.py:18
  31.4 3.8 %collective-permute-done.1 = bf16[256,1024]{0,1:T(8,128)(2,1)} collective-permute-done((bf16[256,1024]{0,1:T(8,128)(2,1)}, bf16[256,1024]{0,1:T(8,128)(2,1)}, u32[]{:S(2)}, u32[]{:S(2)}) %collective-permute-start.1) | collective-permute-done | bytes 524320 | tf_op jit(solution)/shard_map/ppermute | solution.py:18
  35.2 1.4 %pad_maximum_fusion = bf16[896,1024]{0,1:T(8,128)(2,1)S(1)} fusion(bf16[256,1024]{0,1:T(8,128)(2,1)} %collective-permute-done.2, bf16[384,512]{0,1:T(8,128)(2,1)S(1)} %get-tuple-element.36, bf16[384,512]{0,1:T(8,128)(2,1)S(1)} %get-tuple-element.35, bf16[256,1024]{0,1:T(8,128)(2,1)} %collective-permute-done.1), kind=kLoop, calls=%fused_computation.13 | loop fusion | flops 7340032 | bytes 3670016 | tf_op jit(solution)/shard_map/concatenate | solution.py:126
  36.9 0.8 fusion.20
  37.9 3.5 %fusion.48 = (f32[3,8,128]{2,1,0:T(8,128)S(1)}, f32[3,8,128,384]{3,2,1,0:T(8,128)}) fusion(f32[3,8,128,384]{3,2,1,0:T(8,128)S(1)} %fusion.20, pred[3,384]{1,0:T(4,128)(4,1)S(1)} %bitcast.114), kind=kOutput, calls=%fused_computation.104 | output fusion | flops 7078271 | bytes 9450624 | tf_op jit(solution)/shard_map/sub | solution.py:66
  41.5 0.9 constant_dynamic-slice_fusion.2
  42.4 8.5 %multiply_reduce_fusion.2 = (f32[3,128]{1,0:T(4,128)S(1)}, f32[3,128]{1,0:T(4,128)S(1)}, f32[3,128,8,64]{1,3,2,0:T(8,128)S(1)}) fusion(f32[3,128,8,64]{1,0,3,2:T(4,128)S(1)} %reshape.303, f32[3,8,128]{2,1,0:T(8,128)S(1)} %broadcast_divide_fusion, f32[3,8,128,384]{3,2,1,0:T(8,128)} %copy-done.1, pred[3,384]{1,0:T(4,128)(4,1)S(1)} %bitcast.115, ...), kind=kOutput, calls=%fused_computation.46 | convolution fusion | flops 161221248 | bytes 7487616 | tf_op jit(solution)/shard_map/jhqk,jkhd->jqhd/dot_general | solution.py:69
  50.9 0.6 collective-permute-start.3
  51.5 3.1 %collective-permute-done.3 = f32[2,384]{1,0:T(2,128)S(1)} collective-permute-done((f32[2,384]{1,0:T(2,128)S(1)}, f32[2,384]{1,0:T(2,128)S(1)}, u32[]{:S(2)}, u32[]{:S(2)}) %collective-permute-start.3) | collective-permute-done | bytes 3104 | tf_op jit(solution)/shard_map/ppermute | solution.py:22
  54.6 1.6 %collective-permute-start.4 = (f32[2,384]{1,0:T(2,128)S(1)}, f32[2,384]{1,0:T(2,128)S(1)}, u32[]{:S(2)}, u32[]{:S(2)}) collective-permute-start(f32[2,384]{1,0:T(2,128)S(1)} %fusion.44), channel_id=1, source_target_pairs={{0,1},{1,0},{2,3},{3,2},{4,5},{5,4},{6,7},{7,6},{8,9},{9,8},{10,11... | collective-permute-start | bytes 9224 | tf_op jit(solution)/shard_map/ppermute | solution.py:133
  56.2 0.5 copy.27
  56.7 1.3 %reshape.302 = f32[1,384,512]{1,2,0:T(8,128)} reshape(f32[3,128,8,64]{1,0,3,2:T(4,128)S(1)} %copy.27) | data formatting | bytes 1572864 | tf_op jit(solution)/shard_map/reshape | solution.py:70
  58.0 0.2 collective-permute-done.4
  58.3 1.0 multiply_reduce_fusion
  59.3 9.3 %fusion.18 = f32[3,8,64,384]{3,2,1,0:T(8,128)S(1)} fusion(bf16[3,128,8,64]{1,3,2,0:T(8,128)(2,1)} %get-tuple-element.12, f32[3,8,128]{2,1,0:T(8,128)S(1)} %broadcast_divide_fusion, f32[3,8,128,384]{3,2,1,0:T(8,128)} %copy-done.1, pred[3,384]{1,0:T(4,128)(4,1)S(1)} %bitcast.116), kind=kOutput, calls=%fused_computation.34 | convolution fusion | flops 159255936 | bytes 7484544 | tf_op jit(solution)/shard_map/jhqk,jqhd->jkhd/dot_general | solution.py:88
  68.6 4.0 %multiply_convert_fusion = bf16[3,8,128,384]{3,2,1,0:T(8,128)(2,1)S(1)} fusion(f32[3,8,128,384]{3,2,1,0:T(8,128)} %get-tuple-element.41, f32[3,8,128]{2,1,0:T(8,128)S(1)} %bitcast.104, f32[3,8,128]{2,1,0:T(8,128)S(1)} %broadcast_divide_fusion, bf16[3,128,8,64]{1,3,2,0:T(8,128)(2,1)} %get-tuple-element.12, bf16[1,384,8,64]{1,3,2,0:T(8,128)(2,1)} %bitcast.93, ...), kind=kOutput, calls=%fused_computation.5 | convolution fusion | flops 158072832 | bytes 8675328 | tf_op jit(solution)/shard_map/jqhd,jkhd->jhqk/dot_general | solution.py:84
  72.6 0.6 fusion.22
  73.2 0.2 broadcast_in_dim.36
  73.6 0.3 fusion.8
  73.9 0.3 fusion.16
  74.2 0.2 convert.13
  74.4 1.6 %copy-done = f32[896,1024]{0,1:T(8,128)} copy-done((f32[896,1024]{0,1:T(8,128)}, f32[896,1024]{0,1:T(8,128)S(1)}, u32[]{:S(2)}) %copy-start) | copy-done | bytes 3670040
  76.0 1.9 %collective-permute-start.6 = (bf16[256,1024]{0,1:T(8,128)(2,1)S(1)}, bf16[256,1024]{0,1:T(8,128)(2,1)S(1)}, u32[]{:S(2)}, u32[]{:S(2)}) collective-permute-start(bf16[256,1024]{0,1:T(8,128)(2,1)S(1)} %get-tuple-element.14), channel_id=1, source_target_pairs={{2,0},{4,2},{6,4},{8,6},{10,8},{12,10},{14,12},{3,1},{5,3},{7,5},{... | collective-permute-start | bytes 1572872 | tf_op jit(solution)/shard_map/ppermute | solution.py:18
  78.0 2.8 %collective-permute-start.5 = (bf16[256,1024]{0,1:T(8,128)(2,1)S(1)}, bf16[256,1024]{0,1:T(8,128)(2,1)}, u32[]{:S(2)}, u32[]{:S(2)}) collective-permute-start(bf16[256,1024]{0,1:T(8,128)(2,1)S(1)} %get-tuple-element.13), channel_id=1, source_target_pairs={{0,2},{2,4},{4,6},{6,8},{8,10},{10,12},{12,14},{1,3},{3,5},{5,7},{... | collective-permute-start | bytes 1572872 | tf_op jit(solution)/shard_map/ppermute | solution.py:18
  80.8 1.2 %fusion.17 = bf16[3,128,8,64]{1,3,2,0:T(8,128)(2,1)S(1)} fusion(bf16[3,8,128,384]{3,2,1,0:T(8,128)(2,1)S(1)} %multiply_convert_fusion, bf16[1,384,8,64]{1,3,2,0:T(8,128)(2,1)S(1)} %bitcast.99, bf16[1,384,8,64]{1,3,2,0:T(8,128)(2,1)S(1)} %bitcast.101, bf16[1,384,8,64]{1,3,2,0:T(8,128)(2,1)S(1)} %bitcast.97), kind=kOutput, calls=%fused_computation.31 | convolution fusion | flops 152371200 | bytes 3932160 | tf_op jit(solution)/shard_map/jhqk,jkhd->jqhd/dot_general | solution.py:86
  81.9 0.3 copy.26
  82.3 0.3 convert_element_type.73
  82.7 1.9 %collective-permute-done.6 = bf16[256,1024]{0,1:T(8,128)(2,1)S(1)} collective-permute-done((bf16[256,1024]{0,1:T(8,128)(2,1)S(1)}, bf16[256,1024]{0,1:T(8,128)(2,1)S(1)}, u32[]{:S(2)}, u32[]{:S(2)}) %collective-permute-start.6) | collective-permute-done | bytes 524320 | tf_op jit(solution)/shard_map/ppermute | solution.py:18
  84.6 4.1 %collective-permute-done.5 = bf16[256,1024]{0,1:T(8,128)(2,1)} collective-permute-done((bf16[256,1024]{0,1:T(8,128)(2,1)S(1)}, bf16[256,1024]{0,1:T(8,128)(2,1)}, u32[]{:S(2)}, u32[]{:S(2)}) %collective-permute-start.5) | collective-permute-done | bytes 524320 | tf_op jit(solution)/shard_map/ppermute | solution.py:18
  88.7 1.7 %fusion.13 = bf16[384,1024]{0,1:T(8,128)(2,1)S(1)} fusion(f32[896,1024]{0,1:T(8,128)} %copy-done, bf16[256,1024]{0,1:T(8,128)(2,1)S(1)} %collective-permute-done.6, bf16[256,1024]{0,1:T(8,128)(2,1)} %collective-permute-done.5), kind=kLoop, calls=%fused_computation.23 | loop fusion | flops 1966080 | bytes 3407872 | tf_op jit(solution)/shard_map/convert.6
  90.5 0.2 select_bitcast_fusion
  90.8 0.6 collective-permute-start.7
  91.4 18.0 %collective-permute-done.7 = bf16[2,384,512]{1,2,0:T(8,128)(2,1)S(1)} collective-permute-done((bf16[2,384,512]{1,2,0:T(8,128)(2,1)S(1)}, bf16[2,384,512]{1,2,0:T(8,128)(2,1)S(1)}, u32[]{:S(2)}, u32[]{:S(2)}) %collective-permute-start.7) | collective-permute-done | bytes 786464 | tf_op jit(solution)/shard_map/ppermute | solution.py:22
  109.4 0.4 maximum_select_fusion
  109.8 1.6 %copy.28 = bf16[1,2,384,1024]{3,2,1,0:T(8,128)(2,1)} copy(bf16[1,2,384,1024]{2,3,1,0:T(8,128)(2,1)S(1)} %maximum_select_fusion) | data formatting | bytes 3145728 | tf_op jit(solution)/shard_map/jit(_where)/select_n | solution.py:160
  (51 shorter events, 1.7 us)
Async XLA Ops:
  0.0 2.5 %copy-start.12 = (s32[12]{0:T(128)S(1)}, s32[12]{0:T(128)}, u32[]{:S(2)}) copy-start(s32[12]{0:T(128)} %param.3) | copy-start | bytes 148
  1.9 19.3 %collective-permute-start = (bf16[2,384,512]{1,2,0:T(8,128)(2,1)S(1)}, bf16[2,384,512]{1,2,0:T(8,128)(2,1)S(1)}, u32[]{:S(2)}, u32[]{:S(2)}) collective-permute-start(bf16[2,384,512]{1,2,0:T(8,128)(2,1)S(1)} %bitcast.102), channel_id=1, source_target_pairs={{0,16},{16,0},{1,17},{17,1},{2,18},{18,2},{3,19},{19,3},{4,20},{20... | collective-permute-start | bytes 2359304 | tf_op jit(solution)/shard_map/ppermute | solution.py:22
  22.5 8.9 %collective-permute-start.2 = (bf16[256,1024]{0,1:T(8,128)(2,1)}, bf16[256,1024]{0,1:T(8,128)(2,1)}, u32[]{:S(2)}, u32[]{:S(2)}) collective-permute-start(bf16[256,1024]{0,1:T(8,128)(2,1)} %get-tuple-element.34), channel_id=1, source_target_pairs={{2,0},{4,2},{6,4},{8,6},{10,8},{12,10},{14,12},{3,1},{5,3},{7,5},{... | collective-permute-start | bytes 1572872 | tf_op jit(solution)/shard_map/ppermute | solution.py:18
  24.4 10.8 %collective-permute-start.1 = (bf16[256,1024]{0,1:T(8,128)(2,1)}, bf16[256,1024]{0,1:T(8,128)(2,1)}, u32[]{:S(2)}, u32[]{:S(2)}) collective-permute-start(bf16[256,1024]{0,1:T(8,128)(2,1)} %get-tuple-element.33), channel_id=1, source_target_pairs={{0,2},{2,4},{4,6},{6,8},{8,10},{10,12},{12,14},{1,3},{3,5},{5,7},{... | collective-permute-start | bytes 1572872 | tf_op jit(solution)/shard_map/ppermute | solution.py:18
  36.9 0.9 copy-start.6
  36.9 0.9 copy-start.8
  36.9 1.0 copy-start.10
  37.9 3.5 %copy-start.1 = (f32[3,8,128,384]{3,2,1,0:T(8,128)}, f32[3,8,128,384]{3,2,1,0:T(8,128)S(1)}, u32[]{:S(2)}) copy-start(f32[3,8,128,384]{3,2,1,0:T(8,128)S(1)} %fusion.20) | copy-start | bytes 14155780
  42.4 8.5 %copy-start.3 = (bf16[384,512]{0,1:T(8,128)(2,1)}, bf16[384,512]{0,1:T(8,128)(2,1)S(1)}, u32[]{:S(2)}) copy-start(bf16[384,512]{0,1:T(8,128)(2,1)S(1)} %get-tuple-element.23) | copy-start | bytes 1179652
  42.4 8.5 %copy-start.5 = (bf16[384,512]{0,1:T(8,128)(2,1)}, bf16[384,512]{0,1:T(8,128)(2,1)S(1)}, u32[]{:S(2)}) copy-start(bf16[384,512]{0,1:T(8,128)(2,1)S(1)} %get-tuple-element.24) | copy-start | bytes 1179652
  50.9 3.7 %collective-permute-start.3 = (f32[2,384]{1,0:T(2,128)S(1)}, f32[2,384]{1,0:T(2,128)S(1)}, u32[]{:S(2)}, u32[]{:S(2)}) collective-permute-start(f32[2,384]{1,0:T(2,128)S(1)} %pad_maximum_fusion.11), channel_id=1, source_target_pairs={{0,16},{16,0},{1,17},{17,1},{2,18},{18,2},{3,19},{19,3},{4,20},{20... | collective-permute-start | bytes 9224 | tf_op jit(solution)/shard_map/ppermute | solution.py:22
  54.6 3.7 %collective-permute-start.4 = (f32[2,384]{1,0:T(2,128)S(1)}, f32[2,384]{1,0:T(2,128)S(1)}, u32[]{:S(2)}, u32[]{:S(2)}) collective-permute-start(f32[2,384]{1,0:T(2,128)S(1)} %fusion.44), channel_id=1, source_target_pairs={{0,1},{1,0},{2,3},{3,2},{4,5},{5,4},{6,7},{7,6},{8,9},{9,8},{10,11... | collective-permute-start | bytes 9224 | tf_op jit(solution)/shard_map/ppermute | solution.py:133
  59.3 9.3 %copy-start.4 = (bf16[384,512]{0,1:T(8,128)(2,1)S(1)}, bf16[384,512]{0,1:T(8,128)(2,1)}, u32[]{:S(2)}) copy-start(bf16[384,512]{0,1:T(8,128)(2,1)} %copy-done.3) | copy-start | bytes 1179652
  74.2 1.8 %copy-start = (f32[896,1024]{0,1:T(8,128)}, f32[896,1024]{0,1:T(8,128)S(1)}, u32[]{:S(2)}) copy-start(f32[896,1024]{0,1:T(8,128)S(1)} %fusion.16) | copy-start | bytes 11010052
  74.2 6.6 %copy-start.7 = (bf16[384,512]{0,1:T(8,128)(2,1)S(1)}, bf16[384,512]{0,1:T(8,128)(2,1)}, u32[]{:S(2)}) copy-start(bf16[384,512]{0,1:T(8,128)(2,1)} %copy-done.6) | copy-start | bytes 1179652
  74.2 6.6 %copy-start.9 = (bf16[384,512]{0,1:T(8,128)(2,1)S(1)}, bf16[384,512]{0,1:T(8,128)(2,1)}, u32[]{:S(2)}) copy-start(bf16[384,512]{0,1:T(8,128)(2,1)} %copy-done.8) | copy-start | bytes 1179652
  74.2 6.6 %copy-start.11 = (bf16[384,512]{0,1:T(8,128)(2,1)S(1)}, bf16[384,512]{0,1:T(8,128)(2,1)}, u32[]{:S(2)}) copy-start(bf16[384,512]{0,1:T(8,128)(2,1)} %copy-done.10) | copy-start | bytes 1179652
  76.0 8.6 %collective-permute-start.6 = (bf16[256,1024]{0,1:T(8,128)(2,1)S(1)}, bf16[256,1024]{0,1:T(8,128)(2,1)S(1)}, u32[]{:S(2)}, u32[]{:S(2)}) collective-permute-start(bf16[256,1024]{0,1:T(8,128)(2,1)S(1)} %get-tuple-element.14), channel_id=1, source_target_pairs={{2,0},{4,2},{6,4},{8,6},{10,8},{12,10},{14,12},{3,1},{5,3},{7,5},{... | collective-permute-start | bytes 1572872 | tf_op jit(solution)/shard_map/ppermute | solution.py:18
  78.0 4.7 %copy-start.2 = (f32[1,384,512]{1,2,0:T(8,128)S(1)}, f32[1,384,512]{1,2,0:T(8,128)}, u32[]{:S(2)}) copy-start(f32[1,384,512]{1,2,0:T(8,128)} %reshape.302) | copy-start | bytes 2359300
  78.0 10.7 %collective-permute-start.5 = (bf16[256,1024]{0,1:T(8,128)(2,1)S(1)}, bf16[256,1024]{0,1:T(8,128)(2,1)}, u32[]{:S(2)}, u32[]{:S(2)}) collective-permute-start(bf16[256,1024]{0,1:T(8,128)(2,1)S(1)} %get-tuple-element.13), channel_id=1, source_target_pairs={{0,2},{2,4},{4,6},{6,8},{8,10},{10,12},{12,14},{1,3},{3,5},{5,7},{... | collective-permute-start | bytes 1572872 | tf_op jit(solution)/shard_map/ppermute | solution.py:18
  90.8 18.6 %collective-permute-start.7 = (bf16[2,384,512]{1,2,0:T(8,128)(2,1)S(1)}, bf16[2,384,512]{1,2,0:T(8,128)(2,1)S(1)}, u32[]{:S(2)}, u32[]{:S(2)}) collective-permute-start(bf16[2,384,512]{1,2,0:T(8,128)(2,1)S(1)} %get-tuple-element.18), channel_id=1, source_target_pairs={{0,16},{16,0},{1,17},{17,1},{2,18},{18,2},{3,19},{19,3},{4,20},{20... | collective-permute-start | bytes 2359304 | tf_op jit(solution)/shard_map/ppermute | solution.py:22

commit v10 on v3

--- a/solution.py
+++ b/solution.py
@@ -114,8 +114,9 @@
     keep_offset = section * half
     send_offset = (1 - section) * half
     sent = lax.dynamic_slice_in_dim(local_heads, send_offset, half, 2)
-    kept = lax.dynamic_slice_in_dim(local_heads, keep_offset, half, 2)
     arrived = sec_swap(sent)
+    arrived, later_heads = lax.optimization_barrier((arrived, local_heads))
+    kept = lax.dynamic_slice_in_dim(later_heads, keep_offset, half, 2)
     key_value = jnp.where(is_first, kept, arrived)
     query_cot = jnp.where(is_first, arrived, kept)
 

time: 97.2 us -> 98.1 us (level)
  local copies, waits for them, and re-layouts: 15.2 us -> 16.4 us
    dynamic_slice x1 -> x2, local copies, waits for them, and re-layouts: 0.36 us -> 2.46 us  [per_device(): sent = lax.dynamic_slice_in_dim(local_heads, send_offset, half, 2)]
    dynamic_slice x2 -> x0, local copies, waits for them, and re-layouts: 1.84 us -> none  [per_device(): kept = lax.dynamic_slice_in_dim(local_heads, keep_offset, half, 2)]
    unnamed x46 -> x49, local copies, waits for them, and re-layouts: 5.28 us -> 6.15 us
where the time goes in v10:
time: 98.1 us; the launch traced here: 97.7 us
  waiting for transfers between devices  47.6 us (49%)
  local copies, waits for them, and re-layouts  16.4 us (17%)
  other arithmetic  12.8 us (13%)
  starting transfers between devices  12.3 us (13%)
  matrix products  6.2 us (6%)
  between operations  2.4 us (2%)
    ppermute x3, waiting for transfers between devices, sec_swap(): return lax.ppermute(value, 'sec', [(0, 1), (1, 0)])  38.4 us
    ppermute x4, waiting for transfers between devices, seq_shift(): lax.ppermute(value, 'seq', [(source, source + steps) for source in range(...  9.04 us
    ppermute x4, starting transfers between devices, seq_shift(): lax.ppermute(value, 'seq', [(source, source + steps) for source in range(...  8.96 us
    unnamed x49, local copies, waits for them, and re-layouts  6.15 us
    dynamic_slice x2, local copies, waits for them, and re-layouts, per_device(): sent = lax.dynamic_slice_in_dim(local_heads, send_offset, half, 2)  2.46 us
    another operation x3, other arithmetic  2.09 us
  transfers between devices with their start and end apart: 8, of which 7 were waited for; matrix products, arithmetic and copies ran while one was open for 9% of the time, Pallas kernels for 0%

profile of v10, /device:TPU:18, one launch (start us, length us, event | category | flops | bytes accessed | tf_op | source)
XLA Modules:
  0.0 97.7 jit_solution(7322545514052677514)
XLA Ops:
  0.0 1.3 %constant_dynamic-slice_fusion.6 = bf16[1,2,384,512]{3,2,1,0:T(8,128)(2,1)S(1)} fusion(bf16[1,2,384,1024]{3,2,1,0:T(8,128)(2,1)} %param.2, s32[]{:T(128)S(6)} %select_n.90), kind=kLoop, calls=%fused_computation.67 | loop fusion | bytes 1572868 | tf_op jit(solution)/shard_map/dynamic_slice | solution.py:116
  1.3 1.2 %copy.20 = bf16[1,2,384,512]{2,3,1,0:T(8,128)(2,1)} copy(bf16[1,2,384,512]{3,2,1,0:T(8,128)(2,1)S(1)} %constant_dynamic-slice_fusion.6) | data formatting | bytes 1572864 | tf_op jit(solution)/shard_map/dynamic_slice | solution.py:116
  2.5 0.5 collective-permute-start
  3.0 0.9 copy.21
  4.8 17.3 %collective-permute-done = bf16[2,384,512]{1,2,0:T(8,128)(2,1)} collective-permute-done((bf16[2,384,512]{1,2,0:T(8,128)(2,1)}, bf16[2,384,512]{1,2,0:T(8,128)(2,1)}, u32[]{:S(2)}, u32[]{:S(2)}) %collective-permute-start) | collective-permute-done | bytes 786464 | tf_op jit(solution)/shard_map/ppermute | solution.py:22
  22.1 1.4 %broadcast_select_fusion.2 = (bf16[2,384,512]{1,2,0:T(8,128)(2,1)S(1)}, bf16[2,384,512]{1,2,0:T(8,128)(2,1)S(1)}) fusion(bf16[2,384,512]{1,2,0:T(8,128)(2,1)} %collective-permute-done, pred[]{:T(512)S(6)} %eq.11, bf16[2,384,1024]{1,2,0:T(8,128)(2,1)S(1)} %bitcast.88, s32[]{:T(128)S(6)} %select_n.91), kind=kLoop, calls=%fused_computation.47 | loop fusion | flops 786432 | bytes 3145733 | tf_op jit(solution)/shard_map/jit(_where)/select_n | solution.py:121
  23.6 1.1 %fusion.19 = (bf16[256,1024]{0,1:T(8,128)(2,1)}, bf16[256,1024]{0,1:T(8,128)(2,1)}) fusion(bf16[384,512]{0,1:T(8,128)(2,1)S(1)} %get-tuple-element.37, bf16[384,512]{0,1:T(8,128)(2,1)S(1)} %get-tuple-element.38), kind=kLoop, calls=%fused_computation.48 | loop fusion | flops 2097152 | bytes 1835008 | tf_op jit(solution)/shard_map/concatenate | solution.py:123
  24.7 1.9 %collective-permute-start.2 = (bf16[256,1024]{0,1:T(8,128)(2,1)}, bf16[256,1024]{0,1:T(8,128)(2,1)}, u32[]{:S(2)}, u32[]{:S(2)}) collective-permute-start(bf16[256,1024]{0,1:T(8,128)(2,1)} %get-tuple-element.36), channel_id=1, source_target_pairs={{2,0},{4,2},{6,4},{8,6},{10,8},{12,10},{14,12},{3,1},{5,3},{7,5},{... | collective-permute-start | bytes 1572872 | tf_op jit(solution)/shard_map/ppermute | solution.py:18
  26.6 2.4 %collective-permute-start.1 = (bf16[256,1024]{0,1:T(8,128)(2,1)}, bf16[256,1024]{0,1:T(8,128)(2,1)}, u32[]{:S(2)}, u32[]{:S(2)}) collective-permute-start(bf16[256,1024]{0,1:T(8,128)(2,1)} %get-tuple-element.35), channel_id=1, source_target_pairs={{0,2},{2,4},{4,6},{6,8},{8,10},{10,12},{12,14},{1,3},{3,5},{5,7},{... | collective-permute-start | bytes 1572872 | tf_op jit(solution)/shard_map/ppermute | solution.py:18
  29.0 0.6 fusion.38
  31.6 0.8 slice_convert_fusion
  32.4 0.3 reshape.302
  32.8 1.6 %reshape_squeeze.3 = bf16[3,128,8,64]{1,0,3,2:T(4,128)(2,1)S(1)} reshape(bf16[1,384,512]{1,2,0:T(8,128)(2,1)} %get-tuple-element.34) | data formatting | bytes 786432 | tf_op jit(solution)/shard_map/reshape;squeeze | solution.py:57
  34.4 3.0 %collective-permute-done.1 = bf16[256,1024]{0,1:T(8,128)(2,1)} collective-permute-done((bf16[256,1024]{0,1:T(8,128)(2,1)}, bf16[256,1024]{0,1:T(8,128)(2,1)}, u32[]{:S(2)}, u32[]{:S(2)}) %collective-permute-start.1) | collective-permute-done | bytes 524320 | tf_op jit(solution)/shard_map/ppermute | solution.py:18
  37.4 1.4 %pad_maximum_fusion = bf16[896,1024]{0,1:T(8,128)(2,1)S(1)} fusion(bf16[256,1024]{0,1:T(8,128)(2,1)} %collective-permute-done.2, bf16[384,512]{0,1:T(8,128)(2,1)S(1)} %get-tuple-element.38, bf16[384,512]{0,1:T(8,128)(2,1)S(1)} %get-tuple-element.37, bf16[256,1024]{0,1:T(8,128)(2,1)} %collective-permute-done.1), kind=kLoop, calls=%fused_computation.14 | loop fusion | flops 7340032 | bytes 3670016 | tf_op jit(solution)/shard_map/concatenate | solution.py:126
  39.3 0.8 fusion.20
  40.1 1.7 %fusion.39 = (f32[3,8,128]{2,1,0:T(8,128)S(1)}, f32[3,8,128,384]{3,2,1,0:T(8,128)S(1)}) fusion(f32[3,8,128,384]{3,2,1,0:T(8,128)S(1)} %fusion.20, pred[3,384]{1,0:T(4,128)(4,1)S(1)} %bitcast.113), kind=kOutput, calls=%fused_computation.97 | output fusion | flops 7078271 | bytes 9450624 | tf_op jit(solution)/shard_map/sub | solution.py:66
  41.9 0.6 fusion.5
  42.5 1.5 %copy-done.1 = f32[3,8,128,384]{3,2,1,0:T(8,128)} copy-done((f32[3,8,128,384]{3,2,1,0:T(8,128)}, f32[3,8,128,384]{3,2,1,0:T(8,128)S(1)}, u32[]{:S(2)}) %copy-start.1) | copy-done | bytes 4718616
  44.0 1.2 %multiply_reduce_fusion.2 = (f32[3,128]{1,0:T(4,128)S(1)}, f32[3,128]{1,0:T(4,128)S(1)}, f32[3,128,8,64]{1,3,2,0:T(8,128)S(1)}) fusion(f32[3,128,8,64]{1,0,3,2:T(4,128)S(1)} %reshape.302, bf16[3,8,128,384]{3,2,1,0:T(8,128)(2,1)S(1)} %fusion.5, bf16[1,384,8,64]{1,3,2,0:T(8,128)(2,1)S(1)} %bitcast.98, bf16[1,384,8,64]{1,3,2,0:T(8,128)(2,1)S(1)} %bitcast.100, ...), kind=kOutput, calls=%fused_computation.44 | convolution fusion | flops 152960256 | bytes 5114880 | tf_op jit(solution)/shard_map/jhqk,jkhd->jqhd/dot_general | solution.py:69
  45.3 0.6 collective-permute-start.3
  45.9 3.1 %collective-permute-done.3 = f32[2,384]{1,0:T(2,128)S(1)} collective-permute-done((f32[2,384]{1,0:T(2,128)S(1)}, f32[2,384]{1,0:T(2,128)S(1)}, u32[]{:S(2)}, u32[]{:S(2)}) %collective-permute-start.3) | collective-permute-done | bytes 3104 | tf_op jit(solution)/shard_map/ppermute | solution.py:22
  48.9 1.6 %collective-permute-start.4 = (f32[2,384]{1,0:T(2,128)S(1)}, f32[2,384]{1,0:T(2,128)S(1)}, u32[]{:S(2)}, u32[]{:S(2)}) collective-permute-start(f32[2,384]{1,0:T(2,128)S(1)} %fusion.35), channel_id=1, source_target_pairs={{0,1},{1,0},{2,3},{3,2},{4,5},{5,4},{6,7},{7,6},{8,9},{9,8},{10,11... | collective-permute-start | bytes 9224 | tf_op jit(solution)/shard_map/ppermute | solution.py:133
  50.5 0.5 copy.27
  51.1 1.3 %reshape.301 = f32[1,384,512]{1,2,0:T(8,128)} reshape(f32[3,128,8,64]{1,0,3,2:T(4,128)S(1)} %copy.27) | data formatting | bytes 1572864 | tf_op jit(solution)/shard_map/reshape | solution.py:70
  52.4 0.2 collective-permute-done.4
  52.6 1.7 %multiply_reduce_fusion = (f32[3,128,8]{1,2,0:T(8,128)S(1)}, bf16[3,128,8,64]{1,3,2,0:T(8,128)(2,1)S(1)}) fusion(f32[3,128,8,64]{1,3,2,0:T(8,128)} %copy-done.8, f32[3,128]{1,0:T(4,128)S(1)} %bitcast.110, f32[3,128]{1,0:T(4,128)S(1)} %bitcast.108, f32[3,128,8,64]{1,0,3,2:T(4,128)} %copy-done.3), kind=kLoop, calls=%fused_computation.41 | loop fusion | flops 1569792 | bytes 1981440 | tf_op jit(solution)/shard_map/reduce_sum | solution.py:81
  54.4 0.6 fusion.40
  54.9 1.7 %copy-done.2 = f32[3,8,128,384]{3,2,1,0:T(8,128)S(1)} copy-done((f32[3,8,128,384]{3,2,1,0:T(8,128)S(1)}, f32[3,8,128,384]{3,2,1,0:T(8,128)}, u32[]{:S(2)}) %copy-start.2) | copy-done | bytes 4718616
  57.0 1.9 %multiply_convert_fusion = bf16[3,8,128,384]{3,2,1,0:T(8,128)(2,1)S(1)} fusion(f32[3,8,128]{2,1,0:T(8,128)S(1)} %bitcast.109, bf16[3,128,8,64]{1,3,2,0:T(8,128)(2,1)S(1)} %get-tuple-element.16, f32[3,8,128,384]{3,2,1,0:T(8,128)S(1)} %copy-done.2, f32[3,8,128]{2,1,0:T(8,128)S(1)} %get-tuple-element.42, bf16[1,384,8,64]{1,3,2,0:T(8,128)(2,1)S(1)} %bitcast.99, ...), kind=kOutput, calls=%fused_computation.5 | convolution fusion | flops 158072832 | bytes 8675328 | tf_op jit(solution)/shard_map/jqhd,jkhd->jhqk/dot_general | solution.py:83
  58.9 0.6 fusion.22
  59.4 0.2 broadcast_in_dim.36
  59.8 0.3 fusion.9
  60.1 0.3 fusion.17
  60.6 1.6 %copy-done = f32[896,1024]{0,1:T(8,128)} copy-done((f32[896,1024]{0,1:T(8,128)}, f32[896,1024]{0,1:T(8,128)S(1)}, u32[]{:S(2)}) %copy-start) | copy-done | bytes 3670040
  62.3 1.9 %collective-permute-start.6 = (bf16[256,1024]{0,1:T(8,128)(2,1)S(1)}, bf16[256,1024]{0,1:T(8,128)(2,1)S(1)}, u32[]{:S(2)}, u32[]{:S(2)}) collective-permute-start(bf16[256,1024]{0,1:T(8,128)(2,1)S(1)} %get-tuple-element.20), channel_id=1, source_target_pairs={{2,0},{4,2},{6,4},{8,6},{10,8},{12,10},{14,12},{3,1},{5,3},{7,5},{... | collective-permute-start | bytes 1572872 | tf_op jit(solution)/shard_map/ppermute | solution.py:18
  64.2 2.7 %collective-permute-start.5 = (bf16[256,1024]{0,1:T(8,128)(2,1)S(1)}, bf16[256,1024]{0,1:T(8,128)(2,1)}, u32[]{:S(2)}, u32[]{:S(2)}) collective-permute-start(bf16[256,1024]{0,1:T(8,128)(2,1)S(1)} %get-tuple-element.19), channel_id=1, source_target_pairs={{0,2},{2,4},{4,6},{6,8},{8,10},{10,12},{12,14},{1,3},{3,5},{5,7},{... | collective-permute-start | bytes 1572872 | tf_op jit(solution)/shard_map/ppermute | solution.py:18
  67.0 1.2 %fusion.18 = bf16[3,128,8,64]{1,3,2,0:T(8,128)(2,1)S(1)} fusion(bf16[3,8,128,384]{3,2,1,0:T(8,128)(2,1)S(1)} %multiply_convert_fusion, bf16[1,384,8,64]{1,3,2,0:T(8,128)(2,1)S(1)} %bitcast.92, bf16[1,384,8,64]{1,3,2,0:T(8,128)(2,1)S(1)} %bitcast.94, bf16[1,384,8,64]{1,3,2,0:T(8,128)(2,1)S(1)} %bitcast.90), kind=kOutput, calls=%fused_computation.32 | convolution fusion | flops 152371200 | bytes 3932160 | tf_op jit(solution)/shard_map/jhqk,jkhd->jqhd/dot_general | solution.py:85
  68.2 0.3 copy.26
  68.5 0.3 convert_element_type.73
  68.9 2.0 %collective-permute-done.6 = bf16[256,1024]{0,1:T(8,128)(2,1)S(1)} collective-permute-done((bf16[256,1024]{0,1:T(8,128)(2,1)S(1)}, bf16[256,1024]{0,1:T(8,128)(2,1)S(1)}, u32[]{:S(2)}, u32[]{:S(2)}) %collective-permute-start.6) | collective-permute-done | bytes 524320 | tf_op jit(solution)/shard_map/ppermute | solution.py:18
  70.9 4.1 %collective-permute-done.5 = bf16[256,1024]{0,1:T(8,128)(2,1)} collective-permute-done((bf16[256,1024]{0,1:T(8,128)(2,1)S(1)}, bf16[256,1024]{0,1:T(8,128)(2,1)}, u32[]{:S(2)}, u32[]{:S(2)}) %collective-permute-start.5) | collective-permute-done | bytes 524320 | tf_op jit(solution)/shard_map/ppermute | solution.py:18
  75.0 1.7 %fusion.14 = bf16[384,1024]{0,1:T(8,128)(2,1)S(1)} fusion(f32[896,1024]{0,1:T(8,128)} %copy-done, bf16[256,1024]{0,1:T(8,128)(2,1)S(1)} %collective-permute-done.6, bf16[256,1024]{0,1:T(8,128)(2,1)} %collective-permute-done.5), kind=kLoop, calls=%fused_computation.24 | loop fusion | flops 1966080 | bytes 3407872 | tf_op jit(solution)/shard_map/convert.6
  76.8 0.2 select_bitcast_fusion
  77.0 0.6 collective-permute-start.7
  77.6 18.0 %collective-permute-done.7 = bf16[2,384,512]{1,2,0:T(8,128)(2,1)S(1)} collective-permute-done((bf16[2,384,512]{1,2,0:T(8,128)(2,1)S(1)}, bf16[2,384,512]{1,2,0:T(8,128)(2,1)S(1)}, u32[]{:S(2)}, u32[]{:S(2)}) %collective-permute-start.7) | collective-permute-done | bytes 786464 | tf_op jit(solution)/shard_map/ppermute | solution.py:22
  95.6 0.4 maximum_select_fusion
  96.0 1.6 %copy.28 = bf16[1,2,384,1024]{3,2,1,0:T(8,128)(2,1)} copy(bf16[1,2,384,1024]{2,3,1,0:T(8,128)(2,1)S(1)} %maximum_select_fusion) | data formatting | bytes 3145728 | tf_op jit(solution)/shard_map/jit(_where)/select_n | solution.py:160
  (68 shorter events, 2.4 us)
Async XLA Ops:
  0.0 3.0 %copy-start.6 = (bf16[1,2,384,1024]{3,2,1,0:T(8,128)(2,1)S(1)}, bf16[1,2,384,1024]{3,2,1,0:T(8,128)(2,1)}, u32[]{:S(2)}) copy-start(bf16[1,2,384,1024]{3,2,1,0:T(8,128)(2,1)} %param.2) | copy-start | bytes 4718596
  1.3 2.6 %copy-start.21 = (s32[12]{0:T(128)S(1)}, s32[12]{0:T(128)}, u32[]{:S(2)}) copy-start(s32[12]{0:T(128)} %param.3) | copy-start | bytes 148
  2.5 19.6 %collective-permute-start = (bf16[2,384,512]{1,2,0:T(8,128)(2,1)}, bf16[2,384,512]{1,2,0:T(8,128)(2,1)}, u32[]{:S(2)}, u32[]{:S(2)}) collective-permute-start(bf16[2,384,512]{1,2,0:T(8,128)(2,1)} %bitcast), channel_id=1, source_target_pairs={{0,16},{16,0},{1,17},{17,1},{2,18},{18,2},{3,19},{19,3},{4,20},{20... | collective-permute-start | bytes 2359304 | tf_op jit(solution)/shard_map/ppermute | solution.py:22
  24.7 9.7 %collective-permute-start.2 = (bf16[256,1024]{0,1:T(8,128)(2,1)}, bf16[256,1024]{0,1:T(8,128)(2,1)}, u32[]{:S(2)}, u32[]{:S(2)}) collective-permute-start(bf16[256,1024]{0,1:T(8,128)(2,1)} %get-tuple-element.36), channel_id=1, source_target_pairs={{2,0},{4,2},{6,4},{8,6},{10,8},{12,10},{14,12},{3,1},{5,3},{7,5},{... | collective-permute-start | bytes 1572872 | tf_op jit(solution)/shard_map/ppermute | solution.py:18
  26.6 10.8 %collective-permute-start.1 = (bf16[256,1024]{0,1:T(8,128)(2,1)}, bf16[256,1024]{0,1:T(8,128)(2,1)}, u32[]{:S(2)}, u32[]{:S(2)}) collective-permute-start(bf16[256,1024]{0,1:T(8,128)(2,1)} %get-tuple-element.35), channel_id=1, source_target_pairs={{0,2},{2,4},{4,6},{6,8},{8,10},{10,12},{12,14},{1,3},{3,5},{5,7},{... | collective-permute-start | bytes 1572872 | tf_op jit(solution)/shard_map/ppermute | solution.py:18
  32.7 11.2 %copy-start.3 = (f32[3,128,8,64]{1,0,3,2:T(4,128)}, f32[3,128,8,64]{1,0,3,2:T(4,128)S(1)}, u32[]{:S(2)}) copy-start(f32[3,128,8,64]{1,0,3,2:T(4,128)S(1)} %reshape.302) | copy-start | bytes 2359300
  34.4 4.9 %copy-start.4 = (bf16[3,128,8,64]{1,0,3,2:T(4,128)(2,1)}, bf16[3,128,8,64]{1,0,3,2:T(4,128)(2,1)S(1)}, u32[]{:S(2)}) copy-start(bf16[3,128,8,64]{1,0,3,2:T(4,128)(2,1)S(1)} %reshape_squeeze.3) | copy-start | bytes 1179652
  39.1 1.0 %copy-start.9 = (bf16[384,512]{0,1:T(8,128)(2,1)}, bf16[384,512]{0,1:T(8,128)(2,1)S(1)}, u32[]{:S(2)}) copy-start(bf16[384,512]{0,1:T(8,128)(2,1)S(1)} %get-tuple-element.28) | copy-start | bytes 1179652
  39.1 1.0 %copy-start.11 = (bf16[384,512]{0,1:T(8,128)(2,1)}, bf16[384,512]{0,1:T(8,128)(2,1)S(1)}, u32[]{:S(2)}) copy-start(bf16[384,512]{0,1:T(8,128)(2,1)S(1)} %get-tuple-element.29) | copy-start | bytes 1179652
  39.1 1.0 %copy-start.13 = (bf16[384,512]{0,1:T(8,128)(2,1)}, bf16[384,512]{0,1:T(8,128)(2,1)S(1)}, u32[]{:S(2)}) copy-start(bf16[384,512]{0,1:T(8,128)(2,1)S(1)} %get-tuple-element.30) | copy-start | bytes 1179652
  39.2 4.8 %copy-start.15 = (bf16[384,512]{0,1:T(8,128)(2,1)}, bf16[384,512]{0,1:T(8,128)(2,1)S(1)}, u32[]{:S(2)}) copy-start(bf16[384,512]{0,1:T(8,128)(2,1)S(1)} %get-tuple-element.25) | copy-start | bytes 1179652
  39.2 4.8 %copy-start.17 = (bf16[384,512]{0,1:T(8,128)(2,1)}, bf16[384,512]{0,1:T(8,128)(2,1)S(1)}, u32[]{:S(2)}) copy-start(bf16[384,512]{0,1:T(8,128)(2,1)S(1)} %get-tuple-element.26) | copy-start | bytes 1179652
  39.3 4.7 %copy-start.19 = (bf16[384,512]{0,1:T(8,128)(2,1)}, bf16[384,512]{0,1:T(8,128)(2,1)S(1)}, u32[]{:S(2)}) copy-start(bf16[384,512]{0,1:T(8,128)(2,1)S(1)} %get-tuple-element.27) | copy-start | bytes 1179652
  41.9 2.1 %copy-start.1 = (f32[3,8,128,384]{3,2,1,0:T(8,128)}, f32[3,8,128,384]{3,2,1,0:T(8,128)S(1)}, u32[]{:S(2)}) copy-start(f32[3,8,128,384]{3,2,1,0:T(8,128)S(1)} %get-tuple-element.43) | copy-start | bytes 14155780
  45.2 5.3 %copy-start.8 = (f32[3,128,8,64]{1,3,2,0:T(8,128)}, f32[3,128,8,64]{1,3,2,0:T(8,128)S(1)}, u32[]{:S(2)}) copy-start(f32[3,128,8,64]{1,3,2,0:T(8,128)S(1)} %get-tuple-element.44) | copy-start | bytes 2359300
  45.3 3.7 %collective-permute-start.3 = (f32[2,384]{1,0:T(2,128)S(1)}, f32[2,384]{1,0:T(2,128)S(1)}, u32[]{:S(2)}, u32[]{:S(2)}) collective-permute-start(f32[2,384]{1,0:T(2,128)S(1)} %pad_maximum_fusion.11), channel_id=1, source_target_pairs={{0,16},{16,0},{1,17},{17,1},{2,18},{18,2},{3,19},{19,3},{4,20},{20... | collective-permute-start | bytes 9224 | tf_op jit(solution)/shard_map/ppermute | solution.py:22
  48.9 3.7 %collective-permute-start.4 = (f32[2,384]{1,0:T(2,128)S(1)}, f32[2,384]{1,0:T(2,128)S(1)}, u32[]{:S(2)}, u32[]{:S(2)}) collective-permute-start(f32[2,384]{1,0:T(2,128)S(1)} %fusion.35), channel_id=1, source_target_pairs={{0,1},{1,0},{2,3},{3,2},{4,5},{5,4},{6,7},{7,6},{8,9},{9,8},{10,11... | collective-permute-start | bytes 9224 | tf_op jit(solution)/shard_map/ppermute | solution.py:133
  54.3 2.3 %copy-start.2 = (f32[3,8,128,384]{3,2,1,0:T(8,128)S(1)}, f32[3,8,128,384]{3,2,1,0:T(8,128)}, u32[]{:S(2)}) copy-start(f32[3,8,128,384]{3,2,1,0:T(8,128)} %copy-done.1) | copy-start | bytes 14155780
  54.3 2.4 %copy-start.16 = (bf16[384,512]{0,1:T(8,128)(2,1)S(1)}, bf16[384,512]{0,1:T(8,128)(2,1)}, u32[]{:S(2)}) copy-start(bf16[384,512]{0,1:T(8,128)(2,1)} %copy-done.15) | copy-start | bytes 1179652
  54.4 2.5 %copy-start.18 = (bf16[384,512]{0,1:T(8,128)(2,1)S(1)}, bf16[384,512]{0,1:T(8,128)(2,1)}, u32[]{:S(2)}) copy-start(bf16[384,512]{0,1:T(8,128)(2,1)} %copy-done.17) | copy-start | bytes 1179652
  54.4 2.6 %copy-start.20 = (bf16[384,512]{0,1:T(8,128)(2,1)S(1)}, bf16[384,512]{0,1:T(8,128)(2,1)}, u32[]{:S(2)}) copy-start(bf16[384,512]{0,1:T(8,128)(2,1)} %copy-done.19) | copy-start | bytes 1179652
  57.0 1.9 %copy-start.5 = (bf16[3,128,8,64]{1,0,3,2:T(4,128)(2,1)S(1)}, bf16[3,128,8,64]{1,0,3,2:T(4,128)(2,1)}, u32[]{:S(2)}) copy-start(bf16[3,128,8,64]{1,0,3,2:T(4,128)(2,1)} %copy-done.4) | copy-start | bytes 1179652
  60.4 1.8 %copy-start = (f32[896,1024]{0,1:T(8,128)}, f32[896,1024]{0,1:T(8,128)S(1)}, u32[]{:S(2)}) copy-start(f32[896,1024]{0,1:T(8,128)S(1)} %fusion.17) | copy-start | bytes 11010052
  60.4 6.5 %copy-start.10 = (bf16[384,512]{0,1:T(8,128)(2,1)S(1)}, bf16[384,512]{0,1:T(8,128)(2,1)}, u32[]{:S(2)}) copy-start(bf16[384,512]{0,1:T(8,128)(2,1)} %copy-done.9) | copy-start | bytes 1179652
  60.4 6.5 %copy-start.12 = (bf16[384,512]{0,1:T(8,128)(2,1)S(1)}, bf16[384,512]{0,1:T(8,128)(2,1)}, u32[]{:S(2)}) copy-start(bf16[384,512]{0,1:T(8,128)(2,1)} %copy-done.11) | copy-start | bytes 1179652
  60.4 6.5 %copy-start.14 = (bf16[384,512]{0,1:T(8,128)(2,1)S(1)}, bf16[384,512]{0,1:T(8,128)(2,1)}, u32[]{:S(2)}) copy-start(bf16[384,512]{0,1:T(8,128)(2,1)} %copy-done.13) | copy-start | bytes 1179652
  62.3 8.6 %collective-permute-start.6 = (bf16[256,1024]{0,1:T(8,128)(2,1)S(1)}, bf16[256,1024]{0,1:T(8,128)(2,1)S(1)}, u32[]{:S(2)}, u32[]{:S(2)}) collective-permute-start(bf16[256,1024]{0,1:T(8,128)(2,1)S(1)} %get-tuple-element.20), channel_id=1, source_target_pairs={{2,0},{4,2},{6,4},{8,6},{10,8},{12,10},{14,12},{3,1},{5,3},{7,5},{... | collective-permute-start | bytes 1572872 | tf_op jit(solution)/shard_map/ppermute | solution.py:18
  64.2 4.6 %copy-start.7 = (f32[1,384,512]{1,2,0:T(8,128)S(1)}, f32[1,384,512]{1,2,0:T(8,128)}, u32[]{:S(2)}) copy-start(f32[1,384,512]{1,2,0:T(8,128)} %reshape.301) | copy-start | bytes 2359300
  64.2 10.7 %collective-permute-start.5 = (bf16[256,1024]{0,1:T(8,128)(2,1)S(1)}, bf16[256,1024]{0,1:T(8,128)(2,1)}, u32[]{:S(2)}, u32[]{:S(2)}) collective-permute-start(bf16[256,1024]{0,1:T(8,128)(2,1)S(1)} %get-tuple-element.19), channel_id=1, source_target_pairs={{0,2},{2,4},{4,6},{6,8},{8,10},{10,12},{12,14},{1,3},{3,5},{5,7},{... | collective-permute-start | bytes 1572872 | tf_op jit(solution)/shard_map/ppermute | solution.py:18
  77.0 18.6 %collective-permute-start.7 = (bf16[2,384,512]{1,2,0:T(8,128)(2,1)S(1)}, bf16[2,384,512]{1,2,0:T(8,128)(2,1)S(1)}, u32[]{:S(2)}, u32[]{:S(2)}) collective-permute-start(bf16[2,384,512]{1,2,0:T(8,128)(2,1)S(1)} %get-tuple-element.24), channel_id=1, source_target_pairs={{0,16},{16,0},{1,17},{17,1},{2,18},{18,2},{3,19},{19,3},{4,20},{20... | collective-permute-start | bytes 2359304 | tf_op jit(solution)/shard_map/ppermute | solution.py:22

commit v11 on v3

--- a/solution.py
+++ b/solution.py
@@ -105,19 +105,22 @@
     is_first = section == 0
     local_heads = heads_in[0]
     _, rows, cols = local_heads.shape
-    half = cols // 2
+    heads = cols // DH
+    heads_first = -(-heads * 3 // 5)
+    width = heads_first * DH
+    width_second = cols - width
     unit_count = rows // UNIT
     halo_units = MAX_DOC_UNITS - 1
     halo = halo_units * UNIT
     total_cols = cols * lax.axis_size("mp")
 
-    keep_offset = section * half
-    send_offset = (1 - section) * half
-    sent = lax.dynamic_slice_in_dim(local_heads, send_offset, half, 2)
-    kept = lax.dynamic_slice_in_dim(local_heads, keep_offset, half, 2)
-    arrived = sec_swap(sent)
-    key_value = jnp.where(is_first, kept, arrived)
-    query_cot = jnp.where(is_first, arrived, kept)
+    to_first = local_heads[:, :, :width]
+    to_second = local_heads[:, :, width:]
+    got_first = lax.ppermute(to_first, "sec", [(1, 0)])
+    got_second = lax.ppermute(to_second, "sec", [(0, 1)])
+    pad = jnp.zeros((2, rows, width - width_second), local_heads.dtype)
+    key_value = jnp.where(is_first, to_first, jnp.concatenate([got_second, pad], axis=2))
+    query_cot = jnp.where(is_first, got_first, jnp.concatenate([to_second, pad], axis=2))
 
     joined = jnp.concatenate([key_value[0], key_value[1]], axis=1)
     low = seq_shift(joined[rows - halo :], 1)
@@ -135,13 +138,15 @@
     grad_q, normed, total = attention_grads(
         query_cot[0],
         query_cot[1],
-        near[:, :half],
-        near[:, half:],
+        near[:, :width],
+        near[:, width:],
         rel_starts,
         allowed,
         row_total,
         total_cols,
     )
+    normed = normed.astype(jnp.bfloat16)
+    normed_first = lax.ppermute(normed, "sec", [(0, 1)])
     from_left = seq_shift(total[near.shape[0] - halo :].astype(jnp.bfloat16), 1)
     from_right = seq_shift(total[:halo].astype(jnp.bfloat16), -1)
     own = (
@@ -149,19 +154,30 @@
         + jnp.pad(from_left.astype(jnp.float32), ((0, rows - halo), (0, 0)))
         + jnp.pad(from_right.astype(jnp.float32), ((rows - halo, 0), (0, 0)))
     )
-    grad_k = own[:, :half].astype(jnp.bfloat16)
-    grad_v = own[:, half:].astype(jnp.bfloat16)
+    grad_k = own[:, :width].astype(jnp.bfloat16)
+    grad_v = own[:, width:].astype(jnp.bfloat16)
+    grad_q = grad_q.astype(jnp.bfloat16)
 
-    kv_pair = jnp.stack([grad_k, grad_v])
-    qn_pair = jnp.stack([grad_q.astype(jnp.bfloat16), normed.astype(jnp.bfloat16)])
-    keep_pair = jnp.where(is_first, kv_pair, qn_pair)
-    back = sec_swap(jnp.where(is_first, qn_pair, kv_pair))
-    result = jnp.where(
-        is_first,
-        jnp.concatenate([keep_pair, back], axis=2),
-        jnp.concatenate([back, keep_pair], axis=2),
+    common = max(width, 2 * width_second)
+
+    def widened(value):
+        return jnp.pad(value, ((0, 0), (0, common - value.shape[1])))
+
+    second_out = jnp.concatenate([grad_k[:, :width_second], grad_v[:, :width_second]], axis=1)
+    back = sec_swap(jnp.where(is_first, widened(grad_q), widened(second_out)))
+    first_result = jnp.stack(
+        [
+            jnp.concatenate([grad_k, back[:, :width_second]], axis=1),
+            jnp.concatenate([grad_v, back[:, width_second : 2 * width_second]], axis=1),
+        ]
     )
-    return result[None]
+    second_result = jnp.stack(
+        [
+            jnp.concatenate([back[:, :width], grad_q[:, :width_second]], axis=1),
+            jnp.concatenate([normed_first, normed[:, :width_second]], axis=1),
+        ]
+    )
+    return jnp.where(is_first, first_result, second_result)[None]
 
 
 def solution(mesh):

time: 97.2 us -> 115 us (1.18); the launches traced: 96.8 us -> 113 us
  starting transfers between devices: 12.3 us -> 23.9 us
  waiting for transfers between devices: 47.9 us -> 51.4 us
  matrix products: 6.2 us -> 8.85 us
  other arithmetic: 12.7 us -> 11.3 us
    ppermute x0 -> x3, waiting for transfers between devices: none -> 32.2 us  [the longest x1 14.1 us: per_device(): got_second = lax.ppermute(to_second, 'sec', [(0, 1)])]
    ppermute x3 -> x2, waiting for transfers between devices: 38.7 us -> 11.8 us  [sec_swap(): return lax.ppermute(value, 'sec', [(0, 1), (1, 0)])]
    dynamic_slice x2 -> x8, local copies, waits for them, and re-layouts: 0.26 us -> 6.27 us  [windows(): lax.dynamic_slice_in_dim(near, rel_starts[j] * UNIT, window, 0)]
    ppermute x0 -> x3, starting transfers between devices: none -> 5 us  [the longest x1 2.42 us: per_device(): got_first = lax.ppermute(to_first, 'sec', [(1, 0)])]
    ppermute x3 -> x2, starting transfers between devices: 1.8 us -> 5.84 us  [sec_swap(): return lax.ppermute(value, 'sec', [(0, 1), (1, 0)])]
    unnamed x46 -> x21, local copies, waits for them, and re-layouts: 5.28 us -> 1.42 us
    ppermute x4, waiting for transfers between devices: 9.04 us -> 5.29 us  [seq_shift(): lax.ppermute(value, 'seq', [(source, source + steps) for source in range(...]
    ppermute x4, starting transfers between devices: 8.96 us -> 11.4 us  [seq_shift(): lax.ppermute(value, 'seq', [(source, source + steps) for source in range(...]
  transfers between devices with their start and end apart: 8 -> 10, of which waited for: 7 -> 9; matrix products, arithmetic and copies ran while one was open for 9% -> 12% of each run, Pallas kernels for 0% -> 0%
where the time goes in v11:
time: 115 us; the launch traced here: 113 us
  waiting for transfers between devices  51.4 us (45%)
  starting transfers between devices  23.9 us (21%)
  local copies, waits for them, and re-layouts  15.1 us (13%)
  other arithmetic  11.3 us (10%)
  matrix products  8.85 us (8%)
  between operations  2.34 us (2%)
    ppermute x1, waiting for transfers between devices, per_device(): got_second = lax.ppermute(to_second, 'sec', [(0, 1)])  14.1 us
    ppermute x2, waiting for transfers between devices, sec_swap(): return lax.ppermute(value, 'sec', [(0, 1), (1, 0)])  11.8 us
    ppermute x4, starting transfers between devices, seq_shift(): lax.ppermute(value, 'seq', [(source, source + steps) for source in range(...  11.4 us
    ppermute x1, waiting for transfers between devices, per_device(): got_first = lax.ppermute(to_first, 'sec', [(1, 0)])  9.87 us
    ppermute x1, waiting for transfers between devices, per_device(): normed_first = lax.ppermute(normed, 'sec', [(0, 1)])  8.27 us
    dynamic_slice x8, local copies, waits for them, and re-layouts, windows(): lax.dynamic_slice_in_dim(near, rel_starts[j] * UNIT, window, 0)  6.27 us
    ppermute x2, starting transfers between devices, sec_swap(): return lax.ppermute(value, 'sec', [(0, 1), (1, 0)])  5.84 us
    ppermute x4, waiting for transfers between devices, seq_shift(): lax.ppermute(value, 'seq', [(source, source + steps) for source in range(...  5.29 us
  transfers between devices with their start and end apart: 10, of which 9 were waited for; matrix products, arithmetic and copies ran while one was open for 12% of the time, Pallas kernels for 0%

profile of v11, /device:TPU:18, one launch (start us, length us, event | category | flops | bytes accessed | tf_op | source)
XLA Modules:
  0.0 112.9 jit_solution(15401505401026355401)
XLA Ops:
  0.0 1.1 slice.133
  1.1 1.3 %collective-permute-start.1 = (bf16[2,384,384]{2,1,0:T(8,128)(2,1)S(1)}, bf16[2,384,384]{2,1,0:T(8,128)(2,1)S(1)}, u32[]{:S(2)}, u32[]{:S(2)}) collective-permute-start(bf16[2,384,384]{2,1,0:T(8,128)(2,1)S(1)} %slice.133), channel_id=1, source_target_pairs={{0,16},{1,17},{2,18},{3,19},{4,20},{5,21},{6,22},{7,23},{8,24},{9,... | collective-permute-start | bytes 1769480 | tf_op jit(solution)/shard_map/ppermute | solution.py:120
  2.4 0.8 reduce-window.8
  3.5 0.4 copy-done.6
  4.0 14.1 %collective-permute-done.1 = bf16[2,384,384]{2,1,0:T(8,128)(2,1)S(1)} collective-permute-done((bf16[2,384,384]{2,1,0:T(8,128)(2,1)S(1)}, bf16[2,384,384]{2,1,0:T(8,128)(2,1)S(1)}, u32[]{:S(2)}, u32[]{:S(2)}) %collective-permute-start.1) | collective-permute-done | bytes 589856 | tf_op jit(solution)/shard_map/ppermute | solution.py:120
  18.1 2.4 %fusion.39 = (bf16[2,384,640]{2,1,0:T(8,128)(2,1)}, bf16[2,384,640]{2,1,0:T(8,128)(2,1)S(1)}) fusion(bf16[2,384,1024]{2,1,0:T(8,128)(2,1)} %bitcast.110, bf16[2,384,384]{2,1,0:T(8,128)(2,1)S(1)} %collective-permute-done.1, pred[]{:T(512)S(6)} %eq.11), kind=kLoop, calls=%fused_computation.96 | loop fusion | flops 491520 | bytes 3538945 | tf_op jit(solution)/shard_map/slice | solution.py:117
  20.6 0.9 fusion.20
  21.5 1.9 %collective-permute-start.2 = (bf16[256,1280]{1,0:T(8,128)(2,1)}, bf16[256,1280]{1,0:T(8,128)(2,1)S(1)}, u32[]{:S(2)}, u32[]{:S(2)}) collective-permute-start(bf16[256,1280]{1,0:T(8,128)(2,1)} %get-tuple-element.31), channel_id=1, source_target_pairs={{0,2},{2,4},{4,6},{6,8},{8,10},{10,12},{12,14},{1,3},{3,5},{5,7},{... | collective-permute-start | bytes 1966088 | tf_op jit(solution)/shard_map/ppermute | solution.py:18
  23.4 3.6 %collective-permute-start.3 = (bf16[256,1280]{1,0:T(8,128)(2,1)S(1)}, bf16[256,1280]{1,0:T(8,128)(2,1)S(1)}, u32[]{:S(2)}, u32[]{:S(2)}) collective-permute-start(bf16[256,1280]{1,0:T(8,128)(2,1)S(1)} %get-tuple-element.32), channel_id=1, source_target_pairs={{2,0},{4,2},{6,4},{8,6},{10,8},{12,10},{14,12},{3,1},{5,3},{7,5},{... | collective-permute-start | bytes 1966088 | tf_op jit(solution)/shard_map/ppermute | solution.py:18
  27.1 0.7 convert_reduce_fusion
  27.8 0.7 reduce_sum.57
  28.7 2.4 %collective-permute-start = (bf16[2,384,640]{2,1,0:T(8,128)(2,1)}, bf16[2,384,640]{2,1,0:T(8,128)(2,1)}, u32[]{:S(2)}, u32[]{:S(2)}) collective-permute-start(bf16[2,384,640]{2,1,0:T(8,128)(2,1)} %get-tuple-element.17), channel_id=1, source_target_pairs={{16,0},{17,1},{18,2},{19,3},{20,4},{21,5},{22,6},{23,7},{24,8},{25... | collective-permute-start | bytes 2949128 | tf_op jit(solution)/shard_map/ppermute | solution.py:119
  31.1 0.7 fusion.43
  33.7 1.5 %collective-permute-done.3 = bf16[256,1280]{1,0:T(8,128)(2,1)S(1)} collective-permute-done((bf16[256,1280]{1,0:T(8,128)(2,1)S(1)}, bf16[256,1280]{1,0:T(8,128)(2,1)S(1)}, u32[]{:S(2)}, u32[]{:S(2)}) %collective-permute-start.3) | collective-permute-done | bytes 655392 | tf_op jit(solution)/shard_map/ppermute | solution.py:18
  35.7 1.0 copy.29
  36.7 1.0 copy.27
  37.7 1.0 copy.28
  38.8 1.0 copy.32
  39.8 1.0 copy.33
  40.8 1.0 copy.34
  41.8 9.9 %collective-permute-done = bf16[2,384,640]{2,1,0:T(8,128)(2,1)} collective-permute-done((bf16[2,384,640]{2,1,0:T(8,128)(2,1)}, bf16[2,384,640]{2,1,0:T(8,128)(2,1)}, u32[]{:S(2)}, u32[]{:S(2)}) %collective-permute-start) | collective-permute-done | bytes 983072 | tf_op jit(solution)/shard_map/ppermute | solution.py:119
  52.4 0.3 copy.31
  52.8 0.4 reshape.209
  53.5 2.1 %fusion.21 = f32[3,10,128,384]{3,2,1,0:T(8,128)S(1)} fusion(bf16[1,384,10,64]{1,3,2,0:T(8,128)(2,1)S(1)} %bitcast.103, bf16[1,384,10,64]{1,3,2,0:T(8,128)(2,1)} %bitcast.107, bf16[1,384,10,64]{1,3,2,0:T(8,128)(2,1)} %bitcast.105, bf16[3,128,10,64]{1,0,3,2:T(4,128)(2,1)S(1)} %reshape_squeeze.3), kind=kOutput, calls=%fused_computation.51 | convolution fusion | flops 190218240 | bytes 7864320 | tf_op jit(solution)/shard_map/jqhd,jkhd->jhqk/dot_general | solution.py:62
  55.6 2.1 %fusion.44 = (f32[3,10,128]{2,1,0:T(8,128)S(1)}, f32[3,10,128,384]{3,2,1,0:T(8,128)S(1)}) fusion(f32[3,10,128,384]{3,2,1,0:T(8,128)S(1)} %fusion.21, pred[3,384]{1,0:T(4,128)(4,1)S(1)} %bitcast.128), kind=kOutput, calls=%fused_computation.101 | output fusion | flops 8847743 | bytes 11812992 | tf_op jit(solution)/shard_map/sub | solution.py:66
  57.8 0.7 fusion.5
  59.1 1.5 %multiply_reduce_fusion.2 = (f32[3,128]{1,0:T(4,128)S(1)}, f32[3,128]{1,0:T(4,128)S(1)}, f32[3,128,10,64]{1,3,2,0:T(8,128)S(1)}) fusion(f32[3,128,10,64]{1,0,3,2:T(4,128)S(1)} %reshape.209, bf16[3,10,128,384]{3,2,1,0:T(8,128)(2,1)S(1)} %fusion.5, bf16[1,384,10,64]{1,3,2,0:T(8,128)(2,1)S(1)} %bitcast.115, bf16[1,384,10,64]{1,3,2,0:T(8,128)(2,1)S(1)} %bitcast.113, ...), kind=kOutput, calls=%fused_computation.42 | convolution fusion | flops 191200512 | bytes 6392832 | tf_op jit(solution)/shard_map/jhqk,jkhd->jqhd/dot_general | solution.py:69
  60.6 3.7 %collective-permute-start.4 = (f32[2,384]{1,0:T(2,128)S(1)}, f32[2,384]{1,0:T(2,128)S(1)}, u32[]{:S(2)}, u32[]{:S(2)}) collective-permute-start(f32[2,384]{1,0:T(2,128)S(1)} %pad_maximum_fusion.9), channel_id=1, source_target_pairs={{0,16},{16,0},{1,17},{17,1},{2,18},{18,2},{3,19},{19,3},{4,20},{20... | collective-permute-start | bytes 9224 | tf_op jit(solution)/shard_map/ppermute | solution.py:22
  64.4 1.6 %collective-permute-done.4 = f32[2,384]{1,0:T(2,128)S(1)} collective-permute-done((f32[2,384]{1,0:T(2,128)S(1)}, f32[2,384]{1,0:T(2,128)S(1)}, u32[]{:S(2)}, u32[]{:S(2)}) %collective-permute-start.4) | collective-permute-done | bytes 3104 | tf_op jit(solution)/shard_map/ppermute | solution.py:22
  66.0 1.6 %collective-permute-start.5 = (f32[2,384]{1,0:T(2,128)S(1)}, f32[2,384]{1,0:T(2,128)S(1)}, u32[]{:S(2)}, u32[]{:S(2)}) collective-permute-start(f32[2,384]{1,0:T(2,128)S(1)} %fusion.36), channel_id=1, source_target_pairs={{0,1},{1,0},{2,3},{3,2},{4,5},{5,4},{6,7},{7,6},{8,9},{9,8},{10,11... | collective-permute-start | bytes 9224 | tf_op jit(solution)/shard_map/ppermute | solution.py:135
  67.5 2.1 %collective-permute-done.5 = f32[2,384]{1,0:T(2,128)S(1)} collective-permute-done((f32[2,384]{1,0:T(2,128)S(1)}, f32[2,384]{1,0:T(2,128)S(1)}, u32[]{:S(2)}, u32[]{:S(2)}) %collective-permute-start.5) | collective-permute-done | bytes 3104 | tf_op jit(solution)/shard_map/ppermute | solution.py:135
  69.9 0.7 fusion.45
  70.6 2.4 %multiply_convert_fusion = bf16[3,10,128,384]{3,2,1,0:T(8,128)(2,1)S(1)} fusion(f32[3,10,128]{2,1,0:T(8,128)S(1)} %bitcast.117, bf16[3,128,10,64]{1,3,2,0:T(8,128)(2,1)S(1)} %get-tuple-element.12, f32[3,10,128,384]{3,2,1,0:T(8,128)S(1)} %get-tuple-element.41, f32[3,10,128]{2,1,0:T(8,128)S(1)} %get-tuple-element.40, ...), kind=kOutput, calls=%fused_computation.5 | convolution fusion | flops 197591040 | bytes 10844160 | tf_op jit(solution)/shard_map/jqhd,jkhd->jhqk/dot_general | solution.py:83
  73.0 0.7 fusion.23
  74.2 0.5 fusion.9
  74.6 0.5 fusion.17
  75.4 2.1 %collective-permute-start.6 = (bf16[256,1280]{0,1:T(8,128)(2,1)S(1)}, bf16[256,1280]{0,1:T(8,128)(2,1)S(1)}, u32[]{:S(2)}, u32[]{:S(2)}) collective-permute-start(bf16[256,1280]{0,1:T(8,128)(2,1)S(1)} %get-tuple-element.13), channel_id=1, source_target_pairs={{0,2},{2,4},{4,6},{6,8},{8,10},{10,12},{12,14},{1,3},{3,5},{5,7},{... | collective-permute-start | bytes 1966088 | tf_op jit(solution)/shard_map/ppermute | solution.py:18
  77.5 3.8 %collective-permute-start.7 = (bf16[256,1280]{0,1:T(8,128)(2,1)S(1)}, bf16[256,1280]{0,1:T(8,128)(2,1)S(1)}, u32[]{:S(2)}, u32[]{:S(2)}) collective-permute-start(bf16[256,1280]{0,1:T(8,128)(2,1)S(1)} %get-tuple-element.14), channel_id=1, source_target_pairs={{2,0},{4,2},{6,4},{8,6},{10,8},{12,10},{14,12},{3,1},{5,3},{7,5},{... | collective-permute-start | bytes 1966088 | tf_op jit(solution)/shard_map/ppermute | solution.py:18
  81.3 0.7 copy.39
  82.0 1.4 %fusion.18 = bf16[3,128,10,64]{1,3,2,0:T(8,128)(2,1)S(1)} fusion(bf16[3,10,128,384]{3,2,1,0:T(8,128)(2,1)S(1)} %multiply_convert_fusion, bf16[1,384,10,64]{1,3,2,0:T(8,128)(2,1)S(1)} %bitcast.104, bf16[1,384,10,64]{1,3,2,0:T(8,128)(2,1)S(1)} %bitcast.108, bf16[1,384,10,64]{1,3,2,0:T(8,128)(2,1)S(1)} %bitcast.106), kind=kOutput, calls=%fused_computation.34 | convolution fusion | flops 190464000 | bytes 4915200 | tf_op jit(solution)/shard_map/jhqk,jkhd->jqhd/dot_general | solution.py:85
  83.5 0.4 copy.38
  84.1 1.3 %collective-permute-start.9 = (bf16[384,640]{0,1:T(8,128)(2,1)S(1)}, bf16[384,640]{0,1:T(8,128)(2,1)S(1)}, u32[]{:S(2)}, u32[]{:S(2)}) collective-permute-start(bf16[384,640]{0,1:T(8,128)(2,1)S(1)} %fusion.19), channel_id=1, source_target_pairs={{0,16},{1,17},{2,18},{3,19},{4,20},{5,21},{6,22},{7,23},{8,24},{9,... | collective-permute-start | bytes 1474568 | tf_op jit(solution)/shard_map/ppermute | solution.py:149
  85.4 2.0 %collective-permute-done.6 = bf16[256,1280]{0,1:T(8,128)(2,1)S(1)} collective-permute-done((bf16[256,1280]{0,1:T(8,128)(2,1)S(1)}, bf16[256,1280]{0,1:T(8,128)(2,1)S(1)}, u32[]{:S(2)}, u32[]{:S(2)}) %collective-permute-start.6) | collective-permute-done | bytes 655392 | tf_op jit(solution)/shard_map/ppermute | solution.py:18
  87.5 1.8 %collective-permute-done.7 = bf16[256,1280]{0,1:T(8,128)(2,1)S(1)} collective-permute-done((bf16[256,1280]{0,1:T(8,128)(2,1)S(1)}, bf16[256,1280]{0,1:T(8,128)(2,1)S(1)}, u32[]{:S(2)}, u32[]{:S(2)}) %collective-permute-start.7) | collective-permute-done | bytes 655392 | tf_op jit(solution)/shard_map/ppermute | solution.py:18
  89.8 2.1 %collective-permute-start.8 = (bf16[384,768]{0,1:T(8,128)(2,1)S(1)}, bf16[384,768]{0,1:T(8,128)(2,1)S(1)}, u32[]{:S(2)}, u32[]{:S(2)}) collective-permute-start(bf16[384,768]{0,1:T(8,128)(2,1)S(1)} %maximum_select_fusion.1), channel_id=1, source_target_pairs={{0,16},{16,0},{1,17},{17,1},{2,18},{18,2},{3,19},{19,3},{4,20},{20... | collective-permute-start | bytes 1769480 | tf_op jit(solution)/shard_map/ppermute | solution.py:22
  91.9 8.3 %collective-permute-done.9 = bf16[384,640]{0,1:T(8,128)(2,1)S(1)} collective-permute-done((bf16[384,640]{0,1:T(8,128)(2,1)S(1)}, bf16[384,640]{0,1:T(8,128)(2,1)S(1)}, u32[]{:S(2)}, u32[]{:S(2)}) %collective-permute-start.9) | collective-permute-done | bytes 491552 | tf_op jit(solution)/shard_map/ppermute | solution.py:149
  100.4 10.2 %collective-permute-done.8 = bf16[384,768]{0,1:T(8,128)(2,1)S(1)} collective-permute-done((bf16[384,768]{0,1:T(8,128)(2,1)S(1)}, bf16[384,768]{0,1:T(8,128)(2,1)S(1)}, u32[]{:S(2)}, u32[]{:S(2)}) %collective-permute-start.8) | collective-permute-done | bytes 589856 | tf_op jit(solution)/shard_map/ppermute | solution.py:22
  111.3 1.6 %copy.40 = bf16[1,2,384,1024]{3,2,1,0:T(8,128)(2,1)} copy(bf16[1,2,384,1024]{2,3,1,0:T(8,128)(2,1)S(1)} %maximum_select_fusion) | data formatting | bytes 3145728 | tf_op jit(solution)/shard_map/jit(_where)/select_n | solution.py:180
  (59 shorter events, 5.5 us)
Async XLA Ops:
  1.1 17.0 %collective-permute-start.1 = (bf16[2,384,384]{2,1,0:T(8,128)(2,1)S(1)}, bf16[2,384,384]{2,1,0:T(8,128)(2,1)S(1)}, u32[]{:S(2)}, u32[]{:S(2)}) collective-permute-start(bf16[2,384,384]{2,1,0:T(8,128)(2,1)S(1)} %slice.133), channel_id=1, source_target_pairs={{0,16},{1,17},{2,18},{3,19},{4,20},{5,21},{6,22},{7,23},{8,24},{9,... | collective-permute-start | bytes 1769480 | tf_op jit(solution)/shard_map/ppermute | solution.py:120
  3.3 0.5 copy-start.6
  20.5 6.6 %copy-start.7 = (s32[12,1]{0,1:T(1,128)S(1)}, s32[12,1]{0,1:T(1,128)}, u32[]{:S(2)}) copy-start(s32[12,1]{0,1:T(1,128)} %copy-done.6) | copy-start | bytes 148
  21.5 12.1 %collective-permute-start.2 = (bf16[256,1280]{1,0:T(8,128)(2,1)}, bf16[256,1280]{1,0:T(8,128)(2,1)S(1)}, u32[]{:S(2)}, u32[]{:S(2)}) collective-permute-start(bf16[256,1280]{1,0:T(8,128)(2,1)} %get-tuple-element.31), channel_id=1, source_target_pairs={{0,2},{2,4},{4,6},{6,8},{8,10},{10,12},{12,14},{1,3},{3,5},{5,7},{... | collective-permute-start | bytes 1966088 | tf_op jit(solution)/shard_map/ppermute | solution.py:18
  23.4 11.7 %collective-permute-start.3 = (bf16[256,1280]{1,0:T(8,128)(2,1)S(1)}, bf16[256,1280]{1,0:T(8,128)(2,1)S(1)}, u32[]{:S(2)}, u32[]{:S(2)}) collective-permute-start(bf16[256,1280]{1,0:T(8,128)(2,1)S(1)} %get-tuple-element.32), channel_id=1, source_target_pairs={{2,0},{4,2},{6,4},{8,6},{10,8},{12,10},{14,12},{3,1},{5,3},{7,5},{... | collective-permute-start | bytes 1966088 | tf_op jit(solution)/shard_map/ppermute | solution.py:18
  28.7 23.0 %collective-permute-start = (bf16[2,384,640]{2,1,0:T(8,128)(2,1)}, bf16[2,384,640]{2,1,0:T(8,128)(2,1)}, u32[]{:S(2)}, u32[]{:S(2)}) collective-permute-start(bf16[2,384,640]{2,1,0:T(8,128)(2,1)} %get-tuple-element.17), channel_id=1, source_target_pairs={{16,0},{17,1},{18,2},{19,3},{20,4},{21,5},{22,6},{23,7},{24,8},{25... | collective-permute-start | bytes 2949128 | tf_op jit(solution)/shard_map/ppermute | solution.py:119
  52.4 1.0 copy-start
  57.7 1.0 copy-start.3
  57.7 1.2 %copy-start.4 = (bf16[384,640]{0,1:T(8,128)(2,1)S(1)}, bf16[384,640]{0,1:T(8,128)(2,1)}, u32[]{:S(2)}) copy-start(bf16[384,640]{0,1:T(8,128)(2,1)} %copy.33) | copy-start | bytes 1474564
  57.8 1.3 %copy-start.5 = (bf16[384,640]{0,1:T(8,128)(2,1)S(1)}, bf16[384,640]{0,1:T(8,128)(2,1)}, u32[]{:S(2)}) copy-start(bf16[384,640]{0,1:T(8,128)(2,1)} %copy.34) | copy-start | bytes 1474564
  60.6 5.3 %collective-permute-start.4 = (f32[2,384]{1,0:T(2,128)S(1)}, f32[2,384]{1,0:T(2,128)S(1)}, u32[]{:S(2)}, u32[]{:S(2)}) collective-permute-start(f32[2,384]{1,0:T(2,128)S(1)} %pad_maximum_fusion.9), channel_id=1, source_target_pairs={{0,16},{16,0},{1,17},{17,1},{2,18},{18,2},{3,19},{19,3},{4,20},{20... | collective-permute-start | bytes 9224 | tf_op jit(solution)/shard_map/ppermute | solution.py:22
  66.0 3.7 %collective-permute-start.5 = (f32[2,384]{1,0:T(2,128)S(1)}, f32[2,384]{1,0:T(2,128)S(1)}, u32[]{:S(2)}, u32[]{:S(2)}) collective-permute-start(f32[2,384]{1,0:T(2,128)S(1)} %fusion.36), channel_id=1, source_target_pairs={{0,1},{1,0},{2,3},{3,2},{4,5},{5,4},{6,7},{7,6},{8,9},{9,8},{10,11... | collective-permute-start | bytes 9224 | tf_op jit(solution)/shard_map/ppermute | solution.py:135
  75.3 6.7 %copy-start.1 = (bf16[384,640]{0,1:T(8,128)(2,1)S(1)}, bf16[384,640]{0,1:T(8,128)(2,1)}, u32[]{:S(2)}) copy-start(bf16[384,640]{0,1:T(8,128)(2,1)} %copy.27) | copy-start | bytes 1474564
  75.3 6.7 %copy-start.2 = (bf16[384,640]{0,1:T(8,128)(2,1)S(1)}, bf16[384,640]{0,1:T(8,128)(2,1)}, u32[]{:S(2)}) copy-start(bf16[384,640]{0,1:T(8,128)(2,1)} %copy.28) | copy-start | bytes 1474564
  75.4 12.0 %collective-permute-start.6 = (bf16[256,1280]{0,1:T(8,128)(2,1)S(1)}, bf16[256,1280]{0,1:T(8,128)(2,1)S(1)}, u32[]{:S(2)}, u32[]{:S(2)}) collective-permute-start(bf16[256,1280]{0,1:T(8,128)(2,1)S(1)} %get-tuple-element.13), channel_id=1, source_target_pairs={{0,2},{2,4},{4,6},{6,8},{8,10},{10,12},{12,14},{1,3},{3,5},{5,7},{... | collective-permute-start | bytes 1966088 | tf_op jit(solution)/shard_map/ppermute | solution.py:18
  77.5 11.7 %collective-permute-start.7 = (bf16[256,1280]{0,1:T(8,128)(2,1)S(1)}, bf16[256,1280]{0,1:T(8,128)(2,1)S(1)}, u32[]{:S(2)}, u32[]{:S(2)}) collective-permute-start(bf16[256,1280]{0,1:T(8,128)(2,1)S(1)} %get-tuple-element.14), channel_id=1, source_target_pairs={{2,0},{4,2},{6,4},{8,6},{10,8},{12,10},{14,12},{3,1},{5,3},{7,5},{... | collective-permute-start | bytes 1966088 | tf_op jit(solution)/shard_map/ppermute | solution.py:18
  84.1 16.1 %collective-permute-start.9 = (bf16[384,640]{0,1:T(8,128)(2,1)S(1)}, bf16[384,640]{0,1:T(8,128)(2,1)S(1)}, u32[]{:S(2)}, u32[]{:S(2)}) collective-permute-start(bf16[384,640]{0,1:T(8,128)(2,1)S(1)} %fusion.19), channel_id=1, source_target_pairs={{0,16},{1,17},{2,18},{3,19},{4,20},{5,21},{6,22},{7,23},{8,24},{9,... | collective-permute-start | bytes 1474568 | tf_op jit(solution)/shard_map/ppermute | solution.py:149
  89.8 20.8 %collective-permute-start.8 = (bf16[384,768]{0,1:T(8,128)(2,1)S(1)}, bf16[384,768]{0,1:T(8,128)(2,1)S(1)}, u32[]{:S(2)}, u32[]{:S(2)}) collective-permute-start(bf16[384,768]{0,1:T(8,128)(2,1)S(1)} %maximum_select_fusion.1), channel_id=1, source_target_pairs={{0,16},{16,0},{1,17},{17,1},{2,18},{18,2},{3,19},{19,3},{4,20},{20... | collective-permute-start | bytes 1769480 | tf_op jit(solution)/shard_map/ppermute | solution.py:22

commit v12 on v3

--- a/solution.py
+++ b/solution.py
@@ -16,6 +16,18 @@
     count = lax.axis_size("seq")
     initial, last = (max(0, -steps), min(count, count - steps))
     return lax.ppermute(value, "seq", [(source, source + steps) for source in range(initial, last)])
+
+
+def halo_swap(top, bottom):
+    count = lax.axis_size("seq")
+    even = lax.axis_index("seq") % 2 == 0
+    inside = [(i, i ^ 1) for i in range(count) if (i ^ 1) < count]
+    between = [(i, i + 1) for i in range(1, count - 1, 2)] + [(i + 1, i) for i in range(1, count - 1, 2)]
+    within = lax.ppermute(jnp.where(even, bottom, top), "seq", inside)
+    across = lax.ppermute(jnp.where(even, top, bottom), "seq", between)
+    from_below = jnp.where(even, across, within)
+    from_above = jnp.where(even, within, across)
+    return from_below, from_above
 
 
 def sec_swap(value):
@@ -120,8 +132,7 @@
     query_cot = jnp.where(is_first, arrived, kept)
 
     joined = jnp.concatenate([key_value[0], key_value[1]], axis=1)
-    low = seq_shift(joined[rows - halo :], 1)
-    high = seq_shift(joined[:halo], -1)
+    low, high = halo_swap(joined[:halo], joined[rows - halo :])
     near = jnp.concatenate([low, joined, high], axis=0)
 
     rel_starts, allowed = window_plan(doc_units, seq_place, unit_count, halo_units)
@@ -142,8 +153,9 @@
         row_total,
         total_cols,
     )
-    from_left = seq_shift(total[near.shape[0] - halo :].astype(jnp.bfloat16), 1)
-    from_right = seq_shift(total[:halo].astype(jnp.bfloat16), -1)
+    from_left, from_right = halo_swap(
+        total[:halo].astype(jnp.bfloat16), total[near.shape[0] - halo :].astype(jnp.bfloat16)
+    )
     own = (
         total[halo : halo + rows]
         + jnp.pad(from_left.astype(jnp.float32), ((0, rows - halo), (0, 0)))

time: 97.2 us -> 93.9 us (0.966)
  starting transfers between devices: 12.3 us -> 10.9 us
  waiting for transfers between devices: 47.9 us -> 46.5 us
    select_n x0 -> x4, other arithmetic: none -> 3.38 us  [the longest x2 2.04 us: halo_swap(): across = lax.ppermute(jnp.where(even, top, bottom), 'seq', between)]
    ppermute x4, waiting for transfers between devices: 9.04 us -> 6.72 us  [the longest x2 6.72 us: halo_swap(): across = lax.ppermute(jnp.where(even, top, bottom), 'seq', between)]
    ppermute x4, starting transfers between devices: 8.96 us -> 7.48 us  [the longest x2 4 us: halo_swap(): across = lax.ppermute(jnp.where(even, top, bottom), 'seq', between)]
    concatenate x1, other arithmetic: 1.37 us -> 0.17 us  [per_device(): near = jnp.concatenate([low, joined, high], axis=0)]
    select_n x1, other arithmetic: 1.28 us -> 0.15 us  [per_device(): query_cot = jnp.where(is_first, arrived, kept)]
    concatenate x1 -> x0, other arithmetic: 1.07 us -> none  [per_device(): joined = jnp.concatenate([key_value[0], key_value[1]], axis=1)]
  transfers between devices with their start and end apart: 8 -> 8, of which waited for: 7 -> 6; matrix products, arithmetic and copies ran while one was open for 9% -> 9% of each run, Pallas kernels for 0% -> 0%
where the time goes in v12:
time: 93.9 us; the launch traced here: 93.6 us
  waiting for transfers between devices  46.5 us (50%)
  local copies, waits for them, and re-layouts  15.2 us (16%)
  other arithmetic  12.6 us (13%)
  starting transfers between devices  10.9 us (12%)
  matrix products  6.2 us (7%)
  between operations  2.33 us (2%)
    ppermute x3, waiting for transfers between devices, sec_swap(): return lax.ppermute(value, 'sec', [(0, 1), (1, 0)])  39.6 us
    ppermute x2, waiting for transfers between devices, halo_swap(): across = lax.ppermute(jnp.where(even, top, bottom), 'seq', between)  6.72 us
    unnamed x46, local copies, waits for them, and re-layouts  5.29 us
    ppermute x2, starting transfers between devices, halo_swap(): across = lax.ppermute(jnp.where(even, top, bottom), 'seq', between)  4 us
    ppermute x2, starting transfers between devices, halo_swap(): within = lax.ppermute(jnp.where(even, bottom, top), 'seq', inside)  3.48 us
    select_n x2, other arithmetic, halo_swap(): across = lax.ppermute(jnp.where(even, top, bottom), 'seq', between)  2.04 us
    another operation x3, other arithmetic  2.02 us
  transfers between devices with their start and end apart: 8, of which 6 were waited for; matrix products, arithmetic and copies ran while one was open for 9% of the time, Pallas kernels for 0%

profile of v12, /device:TPU:18, one launch (start us, length us, event | category | flops | bytes accessed | tf_op | source)
XLA Modules:
  0.0 93.6 jit_solution(17355363218315009366)
XLA Ops:
  0.0 1.5 %constant_dynamic-slice_fusion.6 = (bf16[1,2,384,512]{3,2,1,0:T(8,128)(2,1)S(1)}, bf16[1,2,384,512]{3,2,1,0:T(8,128)(2,1)S(1)}) fusion(bf16[1,2,384,1024]{3,2,1,0:T(8,128)(2,1)} %param.2, s32[]{:T(128)S(6)} %select_n.136, s32[]{:T(128)S(6)} %select_n.135), kind=kLoop, calls=%fused_computation.75 | loop fusion | bytes 3145736 | tf_op jit(solution)/shard_map/dynamic_slice | solution.py:129
  1.5 0.4 copy.20
  1.9 0.6 collective-permute-start
  2.5 0.4 copy.21
  3.7 17.5 %collective-permute-done = bf16[2,384,512]{1,2,0:T(8,128)(2,1)S(1)} collective-permute-done((bf16[2,384,512]{1,2,0:T(8,128)(2,1)S(1)}, bf16[2,384,512]{1,2,0:T(8,128)(2,1)S(1)}, u32[]{:S(2)}, u32[]{:S(2)}) %collective-permute-start) | collective-permute-done | bytes 786464 | tf_op jit(solution)/shard_map/ppermute | solution.py:34
  21.4 1.2 %broadcast_select_fusion.8 = (bf16[256,1024]{0,1:T(8,128)(2,1)}, bf16[256,1024]{0,1:T(8,128)(2,1)}) fusion(pred[]{:T(512)S(6)} %eq.21, bf16[384,512]{0,1:T(8,128)(2,1)S(1)} %get-tuple-element.40, bf16[384,512]{0,1:T(8,128)(2,1)S(1)} %get-tuple-element.39), kind=kLoop, calls=%fused_computation.57 | loop fusion | flops 3670016 | bytes 1835009 | tf_op jit(solution)/shard_map/jit(_where)/select_n | solution.py:27
  22.6 1.9 %collective-permute-start.1 = (bf16[256,1024]{0,1:T(8,128)(2,1)}, bf16[256,1024]{0,1:T(8,128)(2,1)}, u32[]{:S(2)}, u32[]{:S(2)}) collective-permute-start(bf16[256,1024]{0,1:T(8,128)(2,1)} %get-tuple-element.37), channel_id=1, source_target_pairs={{2,4},{6,8},{10,12},{4,2},{8,6},{12,10},{3,5},{7,9},{11,13},{5,3},... | collective-permute-start | bytes 1572872 | tf_op jit(solution)/shard_map/ppermute | solution.py:27
  24.5 1.7 %collective-permute-start.2 = (bf16[256,1024]{0,1:T(8,128)(2,1)}, bf16[256,1024]{0,1:T(8,128)(2,1)}, u32[]{:S(2)}, u32[]{:S(2)}) collective-permute-start(bf16[256,1024]{0,1:T(8,128)(2,1)} %get-tuple-element.38), channel_id=1, source_target_pairs={{0,2},{2,0},{4,6},{6,4},{8,10},{10,8},{12,14},{14,12},{1,3},{3,1},... | collective-permute-start | bytes 1572872 | tf_op jit(solution)/shard_map/ppermute | solution.py:26
  26.3 0.6 fusion.37
  28.8 0.8 slice_convert_fusion
  29.6 0.3 reshape.303
  30.0 1.6 %reshape_squeeze.3 = bf16[3,128,8,64]{1,0,3,2:T(4,128)(2,1)S(1)} reshape(bf16[1,384,512]{1,2,0:T(8,128)(2,1)} %get-tuple-element.36) | data formatting | bytes 786432 | tf_op jit(solution)/shard_map/reshape;squeeze | solution.py:69
  31.6 1.8 %collective-permute-done.1 = bf16[256,1024]{0,1:T(8,128)(2,1)} collective-permute-done((bf16[256,1024]{0,1:T(8,128)(2,1)}, bf16[256,1024]{0,1:T(8,128)(2,1)}, u32[]{:S(2)}, u32[]{:S(2)}) %collective-permute-start.1) | collective-permute-done | bytes 524320 | tf_op jit(solution)/shard_map/ppermute | solution.py:27
  33.4 1.3 %broadcast_select_fusion.6 = (bf16[256,1024]{0,1:T(8,128)(2,1)S(1)}, bf16[256,1024]{0,1:T(8,128)(2,1)S(1)}) fusion(bf16[256,1024]{0,1:T(8,128)(2,1)} %collective-permute-done.1, bf16[256,1024]{0,1:T(8,128)(2,1)} %collective-permute-done.2, pred[]{:T(512)S(6)} %eq.21), kind=kLoop, calls=%fused_computation.55 | loop fusion | flops 524288 | bytes 2097153 | tf_op jit(solution)/shard_map/jit(_where)/select_n | solution.py:28
  35.4 0.8 fusion.20
  36.2 1.7 %fusion.38 = (f32[3,8,128]{2,1,0:T(8,128)S(1)}, f32[3,8,128,384]{3,2,1,0:T(8,128)S(1)}) fusion(f32[3,8,128,384]{3,2,1,0:T(8,128)S(1)} %fusion.20, pred[3,384]{1,0:T(4,128)(4,1)S(1)} %bitcast.115), kind=kOutput, calls=%fused_computation.105 | output fusion | flops 7078271 | bytes 9450624 | tf_op jit(solution)/shard_map/sub | solution.py:78
  38.0 0.6 fusion.5
  38.6 1.5 %copy-done.1 = f32[3,8,128,384]{3,2,1,0:T(8,128)} copy-done((f32[3,8,128,384]{3,2,1,0:T(8,128)}, f32[3,8,128,384]{3,2,1,0:T(8,128)S(1)}, u32[]{:S(2)}) %copy-start.1) | copy-done | bytes 4718616
  40.1 1.2 %multiply_reduce_fusion.2 = (f32[3,128]{1,0:T(4,128)S(1)}, f32[3,128]{1,0:T(4,128)S(1)}, f32[3,128,8,64]{1,3,2,0:T(8,128)S(1)}) fusion(f32[3,128,8,64]{1,0,3,2:T(4,128)S(1)} %reshape.303, bf16[3,8,128,384]{3,2,1,0:T(8,128)(2,1)S(1)} %fusion.5, bf16[1,384,8,64]{1,3,2,0:T(8,128)(2,1)S(1)} %bitcast.100, bf16[1,384,8,64]{1,3,2,0:T(8,128)(2,1)S(1)} %bitcast.102, ...), kind=kOutput, calls=%fused_computation.46 | convolution fusion | flops 152960256 | bytes 5114880 | tf_op jit(solution)/shard_map/jhqk,jkhd->jqhd/dot_general | solution.py:81
  41.4 0.6 collective-permute-start.3
  42.0 3.1 %collective-permute-done.3 = f32[2,384]{1,0:T(2,128)S(1)} collective-permute-done((f32[2,384]{1,0:T(2,128)S(1)}, f32[2,384]{1,0:T(2,128)S(1)}, u32[]{:S(2)}, u32[]{:S(2)}) %collective-permute-start.3) | collective-permute-done | bytes 3104 | tf_op jit(solution)/shard_map/ppermute | solution.py:34
  45.1 1.6 %collective-permute-start.4 = (f32[2,384]{1,0:T(2,128)S(1)}, f32[2,384]{1,0:T(2,128)S(1)}, u32[]{:S(2)}, u32[]{:S(2)}) collective-permute-start(f32[2,384]{1,0:T(2,128)S(1)} %fusion.35), channel_id=1, source_target_pairs={{0,1},{1,0},{2,3},{3,2},{4,5},{5,4},{6,7},{7,6},{8,9},{9,8},{10,11... | collective-permute-start | bytes 9224 | tf_op jit(solution)/shard_map/ppermute | solution.py:143
  46.7 0.5 copy.27
  47.2 1.3 %reshape.302 = f32[1,384,512]{1,2,0:T(8,128)} reshape(f32[3,128,8,64]{1,0,3,2:T(4,128)S(1)} %copy.27) | data formatting | bytes 1572864 | tf_op jit(solution)/shard_map/reshape | solution.py:82
  48.5 0.2 collective-permute-done.4
  48.8 1.7 %multiply_reduce_fusion = (f32[3,128,8]{1,2,0:T(8,128)S(1)}, bf16[3,128,8,64]{1,3,2,0:T(8,128)(2,1)S(1)}) fusion(f32[3,128,8,64]{1,3,2,0:T(8,128)} %copy-done.7, f32[3,128]{1,0:T(4,128)S(1)} %bitcast.112, f32[3,128]{1,0:T(4,128)S(1)} %bitcast.110, f32[3,128,8,64]{1,0,3,2:T(4,128)} %copy-done.3), kind=kLoop, calls=%fused_computation.43 | loop fusion | flops 1569792 | bytes 1981440 | tf_op jit(solution)/shard_map/reduce_sum | solution.py:93
  50.5 0.6 fusion.39
  51.1 1.7 %copy-done.2 = f32[3,8,128,384]{3,2,1,0:T(8,128)S(1)} copy-done((f32[3,8,128,384]{3,2,1,0:T(8,128)S(1)}, f32[3,8,128,384]{3,2,1,0:T(8,128)}, u32[]{:S(2)}) %copy-start.2) | copy-done | bytes 4718616
  53.1 1.9 %multiply_convert_fusion = bf16[3,8,128,384]{3,2,1,0:T(8,128)(2,1)S(1)} fusion(f32[3,8,128]{2,1,0:T(8,128)S(1)} %bitcast.111, bf16[3,128,8,64]{1,3,2,0:T(8,128)(2,1)S(1)} %get-tuple-element.12, f32[3,8,128,384]{3,2,1,0:T(8,128)S(1)} %copy-done.2, f32[3,8,128]{2,1,0:T(8,128)S(1)} %get-tuple-element.44, bf16[1,384,8,64]{1,3,2,0:T(8,128)(2,1)S(1)} %bitcast.101, ...), kind=kOutput, calls=%fused_computation.5 | convolution fusion | flops 158072832 | bytes 8675328 | tf_op jit(solution)/shard_map/jqhd,jkhd->jhqk/dot_general | solution.py:95
  55.0 0.6 fusion.22
  55.6 0.2 broadcast_in_dim.36
  55.9 0.3 fusion.9
  56.2 0.3 fusion.17
  56.6 0.2 convert.13
  56.8 1.6 %copy-done = f32[896,1024]{0,1:T(8,128)} copy-done((f32[896,1024]{0,1:T(8,128)}, f32[896,1024]{0,1:T(8,128)S(1)}, u32[]{:S(2)}) %copy-start) | copy-done | bytes 3670040
  58.3 0.9 broadcast_select_fusion.4
  59.2 2.1 %collective-permute-start.5 = (bf16[256,1024]{0,1:T(8,128)(2,1)}, bf16[256,1024]{0,1:T(8,128)(2,1)S(1)}, u32[]{:S(2)}, u32[]{:S(2)}) collective-permute-start(bf16[256,1024]{0,1:T(8,128)(2,1)} %get-tuple-element.13), channel_id=1, source_target_pairs={{2,4},{6,8},{10,12},{4,2},{8,6},{12,10},{3,5},{7,9},{11,13},{5,3},... | collective-permute-start | bytes 1572872 | tf_op jit(solution)/shard_map/ppermute | solution.py:27
  61.3 1.7 %collective-permute-start.6 = (bf16[256,1024]{0,1:T(8,128)(2,1)S(1)}, bf16[256,1024]{0,1:T(8,128)(2,1)S(1)}, u32[]{:S(2)}, u32[]{:S(2)}) collective-permute-start(bf16[256,1024]{0,1:T(8,128)(2,1)S(1)} %get-tuple-element.14), channel_id=1, source_target_pairs={{0,2},{2,0},{4,6},{6,4},{8,10},{10,8},{12,14},{14,12},{1,3},{3,1},... | collective-permute-start | bytes 1572872 | tf_op jit(solution)/shard_map/ppermute | solution.py:26
  63.0 1.2 %fusion.18 = bf16[3,128,8,64]{1,3,2,0:T(8,128)(2,1)S(1)} fusion(bf16[3,8,128,384]{3,2,1,0:T(8,128)(2,1)S(1)} %multiply_convert_fusion, bf16[1,384,8,64]{1,3,2,0:T(8,128)(2,1)S(1)} %bitcast.93, bf16[1,384,8,64]{1,3,2,0:T(8,128)(2,1)S(1)} %bitcast.95, bf16[1,384,8,64]{1,3,2,0:T(8,128)(2,1)S(1)} %bitcast.91), kind=kOutput, calls=%fused_computation.32 | convolution fusion | flops 152371200 | bytes 3932160 | tf_op jit(solution)/shard_map/jhqk,jkhd->jqhd/dot_general | solution.py:97
  64.2 0.3 copy.26
  64.6 0.3 convert_element_type.73
  65.0 4.9 %collective-permute-done.5 = bf16[256,1024]{0,1:T(8,128)(2,1)S(1)} collective-permute-done((bf16[256,1024]{0,1:T(8,128)(2,1)}, bf16[256,1024]{0,1:T(8,128)(2,1)S(1)}, u32[]{:S(2)}, u32[]{:S(2)}) %collective-permute-start.5) | collective-permute-done | bytes 524320 | tf_op jit(solution)/shard_map/ppermute | solution.py:27
  70.0 1.6 %fusion.14 = bf16[384,1024]{0,1:T(8,128)(2,1)S(1)} fusion(f32[896,1024]{0,1:T(8,128)} %copy-done, bf16[256,1024]{0,1:T(8,128)(2,1)S(1)} %get-tuple-element.24, bf16[256,1024]{0,1:T(8,128)(2,1)S(1)} %get-tuple-element.23), kind=kLoop, calls=%fused_computation.24 | loop fusion | flops 1966080 | bytes 3407872 | tf_op jit(solution)/shard_map/convert.6
  71.7 0.2 select_bitcast_fusion
  71.9 0.6 collective-permute-start.7
  72.5 19.0 %collective-permute-done.7 = bf16[2,384,512]{1,2,0:T(8,128)(2,1)S(1)} collective-permute-done((bf16[2,384,512]{1,2,0:T(8,128)(2,1)S(1)}, bf16[2,384,512]{1,2,0:T(8,128)(2,1)S(1)}, u32[]{:S(2)}, u32[]{:S(2)}) %collective-permute-start.7) | collective-permute-done | bytes 786464 | tf_op jit(solution)/shard_map/ppermute | solution.py:34
  91.6 0.4 maximum_select_fusion
  92.0 1.6 %copy.28 = bf16[1,2,384,1024]{3,2,1,0:T(8,128)(2,1)} copy(bf16[1,2,384,1024]{2,3,1,0:T(8,128)(2,1)S(1)} %maximum_select_fusion) | data formatting | bytes 3145728 | tf_op jit(solution)/shard_map/jit(_where)/select_n | solution.py:171
  (68 shorter events, 2.6 us)
Async XLA Ops:
  1.5 1.3 %copy-start.20 = (s32[12]{0:T(128)S(1)}, s32[12]{0:T(128)}, u32[]{:S(2)}) copy-start(s32[12]{0:T(128)} %param.3) | copy-start | bytes 148
  1.9 19.3 %collective-permute-start = (bf16[2,384,512]{1,2,0:T(8,128)(2,1)S(1)}, bf16[2,384,512]{1,2,0:T(8,128)(2,1)S(1)}, u32[]{:S(2)}, u32[]{:S(2)}) collective-permute-start(bf16[2,384,512]{1,2,0:T(8,128)(2,1)S(1)} %bitcast.96), channel_id=1, source_target_pairs={{0,16},{16,0},{1,17},{17,1},{2,18},{18,2},{3,19},{19,3},{4,20},{20... | collective-permute-start | bytes 2359304 | tf_op jit(solution)/shard_map/ppermute | solution.py:34
  22.6 10.8 %collective-permute-start.1 = (bf16[256,1024]{0,1:T(8,128)(2,1)}, bf16[256,1024]{0,1:T(8,128)(2,1)}, u32[]{:S(2)}, u32[]{:S(2)}) collective-permute-start(bf16[256,1024]{0,1:T(8,128)(2,1)} %get-tuple-element.37), channel_id=1, source_target_pairs={{2,4},{6,8},{10,12},{4,2},{8,6},{12,10},{3,5},{7,9},{11,13},{5,3},... | collective-permute-start | bytes 1572872 | tf_op jit(solution)/shard_map/ppermute | solution.py:27
  24.5 8.9 %collective-permute-start.2 = (bf16[256,1024]{0,1:T(8,128)(2,1)}, bf16[256,1024]{0,1:T(8,128)(2,1)}, u32[]{:S(2)}, u32[]{:S(2)}) collective-permute-start(bf16[256,1024]{0,1:T(8,128)(2,1)} %get-tuple-element.38), channel_id=1, source_target_pairs={{0,2},{2,0},{4,6},{6,4},{8,10},{10,8},{12,14},{14,12},{1,3},{3,1},... | collective-permute-start | bytes 1572872 | tf_op jit(solution)/shard_map/ppermute | solution.py:26
  30.0 10.2 %copy-start.3 = (f32[3,128,8,64]{1,0,3,2:T(4,128)}, f32[3,128,8,64]{1,0,3,2:T(4,128)S(1)}, u32[]{:S(2)}) copy-start(f32[3,128,8,64]{1,0,3,2:T(4,128)S(1)} %reshape.303) | copy-start | bytes 2359300
  31.6 3.8 %copy-start.4 = (bf16[3,128,8,64]{1,0,3,2:T(4,128)(2,1)}, bf16[3,128,8,64]{1,0,3,2:T(4,128)(2,1)S(1)}, u32[]{:S(2)}) copy-start(bf16[3,128,8,64]{1,0,3,2:T(4,128)(2,1)S(1)} %reshape_squeeze.3) | copy-start | bytes 1179652
  35.2 1.0 %copy-start.8 = (bf16[384,512]{0,1:T(8,128)(2,1)}, bf16[384,512]{0,1:T(8,128)(2,1)S(1)}, u32[]{:S(2)}) copy-start(bf16[384,512]{0,1:T(8,128)(2,1)S(1)} %get-tuple-element.30) | copy-start | bytes 1179652
  35.2 1.0 %copy-start.10 = (bf16[384,512]{0,1:T(8,128)(2,1)}, bf16[384,512]{0,1:T(8,128)(2,1)S(1)}, u32[]{:S(2)}) copy-start(bf16[384,512]{0,1:T(8,128)(2,1)S(1)} %get-tuple-element.31) | copy-start | bytes 1179652
  35.2 1.0 %copy-start.12 = (bf16[384,512]{0,1:T(8,128)(2,1)}, bf16[384,512]{0,1:T(8,128)(2,1)S(1)}, u32[]{:S(2)}) copy-start(bf16[384,512]{0,1:T(8,128)(2,1)S(1)} %get-tuple-element.32) | copy-start | bytes 1179652
  35.3 4.8 %copy-start.14 = (bf16[384,512]{0,1:T(8,128)(2,1)}, bf16[384,512]{0,1:T(8,128)(2,1)S(1)}, u32[]{:S(2)}) copy-start(bf16[384,512]{0,1:T(8,128)(2,1)S(1)} %get-tuple-element.27) | copy-start | bytes 1179652
  35.4 4.8 %copy-start.16 = (bf16[384,512]{0,1:T(8,128)(2,1)}, bf16[384,512]{0,1:T(8,128)(2,1)S(1)}, u32[]{:S(2)}) copy-start(bf16[384,512]{0,1:T(8,128)(2,1)S(1)} %get-tuple-element.28) | copy-start | bytes 1179652
  35.4 4.8 %copy-start.18 = (bf16[384,512]{0,1:T(8,128)(2,1)}, bf16[384,512]{0,1:T(8,128)(2,1)S(1)}, u32[]{:S(2)}) copy-start(bf16[384,512]{0,1:T(8,128)(2,1)S(1)} %get-tuple-element.29) | copy-start | bytes 1179652
  38.0 2.1 %copy-start.1 = (f32[3,8,128,384]{3,2,1,0:T(8,128)}, f32[3,8,128,384]{3,2,1,0:T(8,128)S(1)}, u32[]{:S(2)}) copy-start(f32[3,8,128,384]{3,2,1,0:T(8,128)S(1)} %get-tuple-element.45) | copy-start | bytes 14155780
  41.3 5.3 %copy-start.7 = (f32[3,128,8,64]{1,3,2,0:T(8,128)}, f32[3,128,8,64]{1,3,2,0:T(8,128)S(1)}, u32[]{:S(2)}) copy-start(f32[3,128,8,64]{1,3,2,0:T(8,128)S(1)} %get-tuple-element.46) | copy-start | bytes 2359300
  41.4 3.7 %collective-permute-start.3 = (f32[2,384]{1,0:T(2,128)S(1)}, f32[2,384]{1,0:T(2,128)S(1)}, u32[]{:S(2)}, u32[]{:S(2)}) collective-permute-start(f32[2,384]{1,0:T(2,128)S(1)} %pad_maximum_fusion.11), channel_id=1, source_target_pairs={{0,16},{16,0},{1,17},{17,1},{2,18},{18,2},{3,19},{19,3},{4,20},{20... | collective-permute-start | bytes 9224 | tf_op jit(solution)/shard_map/ppermute | solution.py:34
  45.1 3.7 %collective-permute-start.4 = (f32[2,384]{1,0:T(2,128)S(1)}, f32[2,384]{1,0:T(2,128)S(1)}, u32[]{:S(2)}, u32[]{:S(2)}) collective-permute-start(f32[2,384]{1,0:T(2,128)S(1)} %fusion.35), channel_id=1, source_target_pairs={{0,1},{1,0},{2,3},{3,2},{4,5},{5,4},{6,7},{7,6},{8,9},{9,8},{10,11... | collective-permute-start | bytes 9224 | tf_op jit(solution)/shard_map/ppermute | solution.py:143
  50.5 2.3 %copy-start.2 = (f32[3,8,128,384]{3,2,1,0:T(8,128)S(1)}, f32[3,8,128,384]{3,2,1,0:T(8,128)}, u32[]{:S(2)}) copy-start(f32[3,8,128,384]{3,2,1,0:T(8,128)} %copy-done.1) | copy-start | bytes 14155780
  50.5 2.4 %copy-start.15 = (bf16[384,512]{0,1:T(8,128)(2,1)S(1)}, bf16[384,512]{0,1:T(8,128)(2,1)}, u32[]{:S(2)}) copy-start(bf16[384,512]{0,1:T(8,128)(2,1)} %copy-done.14) | copy-start | bytes 1179652
  50.5 2.5 %copy-start.17 = (bf16[384,512]{0,1:T(8,128)(2,1)S(1)}, bf16[384,512]{0,1:T(8,128)(2,1)}, u32[]{:S(2)}) copy-start(bf16[384,512]{0,1:T(8,128)(2,1)} %copy-done.16) | copy-start | bytes 1179652
  50.5 2.6 %copy-start.19 = (bf16[384,512]{0,1:T(8,128)(2,1)S(1)}, bf16[384,512]{0,1:T(8,128)(2,1)}, u32[]{:S(2)}) copy-start(bf16[384,512]{0,1:T(8,128)(2,1)} %copy-done.18) | copy-start | bytes 1179652
  53.1 1.9 %copy-start.5 = (bf16[3,128,8,64]{1,0,3,2:T(4,128)(2,1)S(1)}, bf16[3,128,8,64]{1,0,3,2:T(4,128)(2,1)}, u32[]{:S(2)}) copy-start(bf16[3,128,8,64]{1,0,3,2:T(4,128)(2,1)} %copy-done.4) | copy-start | bytes 1179652
  56.5 1.8 %copy-start = (f32[896,1024]{0,1:T(8,128)}, f32[896,1024]{0,1:T(8,128)S(1)}, u32[]{:S(2)}) copy-start(f32[896,1024]{0,1:T(8,128)S(1)} %fusion.17) | copy-start | bytes 11010052
  56.5 6.5 %copy-start.9 = (bf16[384,512]{0,1:T(8,128)(2,1)S(1)}, bf16[384,512]{0,1:T(8,128)(2,1)}, u32[]{:S(2)}) copy-start(bf16[384,512]{0,1:T(8,128)(2,1)} %copy-done.8) | copy-start | bytes 1179652
  56.6 6.5 %copy-start.11 = (bf16[384,512]{0,1:T(8,128)(2,1)S(1)}, bf16[384,512]{0,1:T(8,128)(2,1)}, u32[]{:S(2)}) copy-start(bf16[384,512]{0,1:T(8,128)(2,1)} %copy-done.10) | copy-start | bytes 1179652
  56.6 6.5 %copy-start.13 = (bf16[384,512]{0,1:T(8,128)(2,1)S(1)}, bf16[384,512]{0,1:T(8,128)(2,1)}, u32[]{:S(2)}) copy-start(bf16[384,512]{0,1:T(8,128)(2,1)} %copy-done.12) | copy-start | bytes 1179652
  59.2 10.7 %collective-permute-start.5 = (bf16[256,1024]{0,1:T(8,128)(2,1)}, bf16[256,1024]{0,1:T(8,128)(2,1)S(1)}, u32[]{:S(2)}, u32[]{:S(2)}) collective-permute-start(bf16[256,1024]{0,1:T(8,128)(2,1)} %get-tuple-element.13), channel_id=1, source_target_pairs={{2,4},{6,8},{10,12},{4,2},{8,6},{12,10},{3,5},{7,9},{11,13},{5,3},... | collective-permute-start | bytes 1572872 | tf_op jit(solution)/shard_map/ppermute | solution.py:27
  61.3 3.6 %copy-start.6 = (f32[1,384,512]{1,2,0:T(8,128)S(1)}, f32[1,384,512]{1,2,0:T(8,128)}, u32[]{:S(2)}) copy-start(f32[1,384,512]{1,2,0:T(8,128)} %reshape.302) | copy-start | bytes 2359300
  61.3 8.6 %collective-permute-start.6 = (bf16[256,1024]{0,1:T(8,128)(2,1)S(1)}, bf16[256,1024]{0,1:T(8,128)(2,1)S(1)}, u32[]{:S(2)}, u32[]{:S(2)}) collective-permute-start(bf16[256,1024]{0,1:T(8,128)(2,1)S(1)} %get-tuple-element.14), channel_id=1, source_target_pairs={{0,2},{2,0},{4,6},{6,4},{8,10},{10,8},{12,14},{14,12},{1,3},{3,1},... | collective-permute-start | bytes 1572872 | tf_op jit(solution)/shard_map/ppermute | solution.py:26
  71.9 19.6 %collective-permute-start.7 = (bf16[2,384,512]{1,2,0:T(8,128)(2,1)S(1)}, bf16[2,384,512]{1,2,0:T(8,128)(2,1)S(1)}, u32[]{:S(2)}, u32[]{:S(2)}) collective-permute-start(bf16[2,384,512]{1,2,0:T(8,128)(2,1)S(1)} %get-tuple-element.18), channel_id=1, source_target_pairs={{0,16},{16,0},{1,17},{17,1},{2,18},{18,2},{3,19},{19,3},{4,20},{20... | collective-permute-start | bytes 2359304 | tf_op jit(solution)/shard_map/ppermute | solution.py:34

commit v13 on v12

--- a/solution.py
+++ b/solution.py
@@ -166,12 +166,11 @@
 
     kv_pair = jnp.stack([grad_k, grad_v])
     qn_pair = jnp.stack([grad_q.astype(jnp.bfloat16), normed.astype(jnp.bfloat16)])
-    keep_pair = jnp.where(is_first, kv_pair, qn_pair)
     back = sec_swap(jnp.where(is_first, qn_pair, kv_pair))
     result = jnp.where(
         is_first,
-        jnp.concatenate([keep_pair, back], axis=2),
-        jnp.concatenate([back, keep_pair], axis=2),
+        jnp.concatenate([kv_pair, back], axis=2),
+        jnp.concatenate([back, qn_pair], axis=2),
     )
     return result[None]
 

time: 93.9 us -> 93.9 us (level)
  no operation moved by 1% of the time
where the time goes in v13:
time: 93.9 us; the launch traced here: 93.6 us
  waiting for transfers between devices  46.5 us (50%)
  local copies, waits for them, and re-layouts  15.1 us (16%)
  other arithmetic  12.6 us (13%)
  starting transfers between devices  10.9 us (12%)
  matrix products  6.2 us (7%)
  between operations  2.34 us (2%)
    ppermute x3, waiting for transfers between devices, sec_swap(): return lax.ppermute(value, 'sec', [(0, 1), (1, 0)])  39.6 us
    ppermute x2, waiting for transfers between devices, halo_swap(): across = lax.ppermute(jnp.where(even, top, bottom), 'seq', between)  6.71 us
    unnamed x46, local copies, waits for them, and re-layouts  5.29 us
    ppermute x2, starting transfers between devices, halo_swap(): across = lax.ppermute(jnp.where(even, top, bottom), 'seq', between)  4 us
    ppermute x2, starting transfers between devices, halo_swap(): within = lax.ppermute(jnp.where(even, bottom, top), 'seq', inside)  3.49 us
    select_n x2, other arithmetic, halo_swap(): across = lax.ppermute(jnp.where(even, top, bottom), 'seq', between)  2.04 us
    another operation x3, other arithmetic  2.02 us
  transfers between devices with their start and end apart: 8, of which 6 were waited for; matrix products, arithmetic and copies ran while one was open for 9% of the time, Pallas kernels for 0%

profile of v13, /device:TPU:18, one launch (start us, length us, event | category | flops | bytes accessed | tf_op | source)
XLA Modules:
  0.0 93.6 jit_solution(1332919913829050216)
XLA Ops:
  0.0 1.5 %constant_dynamic-slice_fusion.6 = (bf16[1,2,384,512]{3,2,1,0:T(8,128)(2,1)S(1)}, bf16[1,2,384,512]{3,2,1,0:T(8,128)(2,1)S(1)}) fusion(bf16[1,2,384,1024]{3,2,1,0:T(8,128)(2,1)} %param.2, s32[]{:T(128)S(6)} %select_n.123, s32[]{:T(128)S(6)} %select_n.122), kind=kLoop, calls=%fused_computation.76 | loop fusion | bytes 3145736 | tf_op jit(solution)/shard_map/dynamic_slice | solution.py:129
  1.5 0.4 copy.20
  1.9 0.6 collective-permute-start
  2.5 0.4 copy.21
  3.7 17.5 %collective-permute-done = bf16[2,384,512]{1,2,0:T(8,128)(2,1)S(1)} collective-permute-done((bf16[2,384,512]{1,2,0:T(8,128)(2,1)S(1)}, bf16[2,384,512]{1,2,0:T(8,128)(2,1)S(1)}, u32[]{:S(2)}, u32[]{:S(2)}) %collective-permute-start) | collective-permute-done | bytes 786464 | tf_op jit(solution)/shard_map/ppermute | solution.py:34
  21.4 1.2 %broadcast_select_fusion.8 = (bf16[256,1024]{0,1:T(8,128)(2,1)}, bf16[256,1024]{0,1:T(8,128)(2,1)}) fusion(pred[]{:T(512)S(6)} %eq.21, bf16[384,512]{0,1:T(8,128)(2,1)S(1)} %get-tuple-element.41, bf16[384,512]{0,1:T(8,128)(2,1)S(1)} %get-tuple-element.40), kind=kLoop, calls=%fused_computation.56 | loop fusion | flops 3670016 | bytes 1835009 | tf_op jit(solution)/shard_map/jit(_where)/select_n | solution.py:27
  22.6 1.9 %collective-permute-start.1 = (bf16[256,1024]{0,1:T(8,128)(2,1)}, bf16[256,1024]{0,1:T(8,128)(2,1)}, u32[]{:S(2)}, u32[]{:S(2)}) collective-permute-start(bf16[256,1024]{0,1:T(8,128)(2,1)} %get-tuple-element.38), channel_id=1, source_target_pairs={{2,4},{6,8},{10,12},{4,2},{8,6},{12,10},{3,5},{7,9},{11,13},{5,3},... | collective-permute-start | bytes 1572872 | tf_op jit(solution)/shard_map/ppermute | solution.py:27
  24.5 1.7 %collective-permute-start.2 = (bf16[256,1024]{0,1:T(8,128)(2,1)}, bf16[256,1024]{0,1:T(8,128)(2,1)}, u32[]{:S(2)}, u32[]{:S(2)}) collective-permute-start(bf16[256,1024]{0,1:T(8,128)(2,1)} %get-tuple-element.39), channel_id=1, source_target_pairs={{0,2},{2,0},{4,6},{6,4},{8,10},{10,8},{12,14},{14,12},{1,3},{3,1},... | collective-permute-start | bytes 1572872 | tf_op jit(solution)/shard_map/ppermute | solution.py:26
  26.3 0.6 fusion.39
  28.8 0.8 slice_convert_fusion
  29.6 0.3 reshape.249
  30.0 1.6 %reshape_squeeze.3 = bf16[3,128,8,64]{1,0,3,2:T(4,128)(2,1)S(1)} reshape(bf16[1,384,512]{1,2,0:T(8,128)(2,1)} %get-tuple-element.37) | data formatting | bytes 786432 | tf_op jit(solution)/shard_map/reshape;squeeze | solution.py:69
  31.6 1.8 %collective-permute-done.1 = bf16[256,1024]{0,1:T(8,128)(2,1)} collective-permute-done((bf16[256,1024]{0,1:T(8,128)(2,1)}, bf16[256,1024]{0,1:T(8,128)(2,1)}, u32[]{:S(2)}, u32[]{:S(2)}) %collective-permute-start.1) | collective-permute-done | bytes 524320 | tf_op jit(solution)/shard_map/ppermute | solution.py:27
  33.4 1.3 %broadcast_select_fusion.6 = (bf16[256,1024]{0,1:T(8,128)(2,1)S(1)}, bf16[256,1024]{0,1:T(8,128)(2,1)S(1)}) fusion(bf16[256,1024]{0,1:T(8,128)(2,1)} %collective-permute-done.1, bf16[256,1024]{0,1:T(8,128)(2,1)} %collective-permute-done.2, pred[]{:T(512)S(6)} %eq.21), kind=kLoop, calls=%fused_computation.54 | loop fusion | flops 524288 | bytes 2097153 | tf_op jit(solution)/shard_map/jit(_where)/select_n | solution.py:28
  35.4 0.8 fusion.22
  36.2 1.7 %fusion.40 = (f32[3,8,128]{2,1,0:T(8,128)S(1)}, f32[3,8,128,384]{3,2,1,0:T(8,128)S(1)}) fusion(f32[3,8,128,384]{3,2,1,0:T(8,128)S(1)} %fusion.22, pred[3,384]{1,0:T(4,128)(4,1)S(1)} %bitcast.117), kind=kOutput, calls=%fused_computation.106 | output fusion | flops 7078271 | bytes 9450624 | tf_op jit(solution)/shard_map/sub | solution.py:78
  38.0 0.6 fusion.5
  38.6 1.5 %copy-done.1 = f32[3,8,128,384]{3,2,1,0:T(8,128)} copy-done((f32[3,8,128,384]{3,2,1,0:T(8,128)}, f32[3,8,128,384]{3,2,1,0:T(8,128)S(1)}, u32[]{:S(2)}) %copy-start.1) | copy-done | bytes 4718616
  40.1 1.2 %multiply_reduce_fusion.2 = (f32[3,128]{1,0:T(4,128)S(1)}, f32[3,128]{1,0:T(4,128)S(1)}, f32[3,128,8,64]{1,3,2,0:T(8,128)S(1)}) fusion(f32[3,128,8,64]{1,0,3,2:T(4,128)S(1)} %reshape.249, bf16[3,8,128,384]{3,2,1,0:T(8,128)(2,1)S(1)} %fusion.5, bf16[1,384,8,64]{1,3,2,0:T(8,128)(2,1)S(1)} %bitcast.102, bf16[1,384,8,64]{1,3,2,0:T(8,128)(2,1)S(1)} %bitcast.104, ...), kind=kOutput, calls=%fused_computation.45 | convolution fusion | flops 152960256 | bytes 5114880 | tf_op jit(solution)/shard_map/jhqk,jkhd->jqhd/dot_general | solution.py:81
  41.4 0.6 collective-permute-start.3
  42.0 3.1 %collective-permute-done.3 = f32[2,384]{1,0:T(2,128)S(1)} collective-permute-done((f32[2,384]{1,0:T(2,128)S(1)}, f32[2,384]{1,0:T(2,128)S(1)}, u32[]{:S(2)}, u32[]{:S(2)}) %collective-permute-start.3) | collective-permute-done | bytes 3104 | tf_op jit(solution)/shard_map/ppermute | solution.py:34
  45.1 1.6 %collective-permute-start.4 = (f32[2,384]{1,0:T(2,128)S(1)}, f32[2,384]{1,0:T(2,128)S(1)}, u32[]{:S(2)}, u32[]{:S(2)}) collective-permute-start(f32[2,384]{1,0:T(2,128)S(1)} %fusion.37), channel_id=1, source_target_pairs={{0,1},{1,0},{2,3},{3,2},{4,5},{5,4},{6,7},{7,6},{8,9},{9,8},{10,11... | collective-permute-start | bytes 9224 | tf_op jit(solution)/shard_map/ppermute | solution.py:143
  46.6 0.5 copy.27
  47.2 1.3 %reshape.248 = f32[1,384,512]{1,2,0:T(8,128)} reshape(f32[3,128,8,64]{1,0,3,2:T(4,128)S(1)} %copy.27) | data formatting | bytes 1572864 | tf_op jit(solution)/shard_map/reshape | solution.py:82
  48.5 0.2 collective-permute-done.4
  48.8 1.7 %multiply_reduce_fusion = (f32[3,128,8]{1,2,0:T(8,128)S(1)}, bf16[3,128,8,64]{1,3,2,0:T(8,128)(2,1)S(1)}) fusion(f32[3,128,8,64]{1,3,2,0:T(8,128)} %copy-done.7, f32[3,128]{1,0:T(4,128)S(1)} %bitcast.114, f32[3,128]{1,0:T(4,128)S(1)} %bitcast.112, f32[3,128,8,64]{1,0,3,2:T(4,128)} %copy-done.3), kind=kLoop, calls=%fused_computation.42 | loop fusion | flops 1569792 | bytes 1981440 | tf_op jit(solution)/shard_map/reduce_sum | solution.py:93
  50.5 0.6 fusion.41
  51.0 1.7 %copy-done.2 = f32[3,8,128,384]{3,2,1,0:T(8,128)S(1)} copy-done((f32[3,8,128,384]{3,2,1,0:T(8,128)S(1)}, f32[3,8,128,384]{3,2,1,0:T(8,128)}, u32[]{:S(2)}) %copy-start.2) | copy-done | bytes 4718616
  53.1 1.9 %multiply_convert_fusion = bf16[3,8,128,384]{3,2,1,0:T(8,128)(2,1)S(1)} fusion(f32[3,8,128]{2,1,0:T(8,128)S(1)} %bitcast.113, bf16[3,128,8,64]{1,3,2,0:T(8,128)(2,1)S(1)} %get-tuple-element.12, f32[3,8,128,384]{3,2,1,0:T(8,128)S(1)} %copy-done.2, f32[3,8,128]{2,1,0:T(8,128)S(1)} %get-tuple-element.45, bf16[1,384,8,64]{1,3,2,0:T(8,128)(2,1)S(1)} %bitcast.103, ...), kind=kOutput, calls=%fused_computation.5 | convolution fusion | flops 158072832 | bytes 8675328 | tf_op jit(solution)/shard_map/jqhd,jkhd->jhqk/dot_general | solution.py:95
  55.0 0.6 fusion.24
  55.5 0.2 broadcast_in_dim.36
  55.9 0.3 fusion.9
  56.2 0.3 fusion.17
  56.6 0.2 convert.13
  56.8 1.6 %copy-done = f32[896,1024]{0,1:T(8,128)} copy-done((f32[896,1024]{0,1:T(8,128)}, f32[896,1024]{0,1:T(8,128)S(1)}, u32[]{:S(2)}) %copy-start) | copy-done | bytes 3670040
  58.3 0.9 broadcast_select_fusion.4
  59.2 2.1 %collective-permute-start.5 = (bf16[256,1024]{0,1:T(8,128)(2,1)}, bf16[256,1024]{0,1:T(8,128)(2,1)S(1)}, u32[]{:S(2)}, u32[]{:S(2)}) collective-permute-start(bf16[256,1024]{0,1:T(8,128)(2,1)} %get-tuple-element.13), channel_id=1, source_target_pairs={{2,4},{6,8},{10,12},{4,2},{8,6},{12,10},{3,5},{7,9},{11,13},{5,3},... | collective-permute-start | bytes 1572872 | tf_op jit(solution)/shard_map/ppermute | solution.py:27
  61.3 1.7 %collective-permute-start.6 = (bf16[256,1024]{0,1:T(8,128)(2,1)S(1)}, bf16[256,1024]{0,1:T(8,128)(2,1)S(1)}, u32[]{:S(2)}, u32[]{:S(2)}) collective-permute-start(bf16[256,1024]{0,1:T(8,128)(2,1)S(1)} %get-tuple-element.14), channel_id=1, source_target_pairs={{0,2},{2,0},{4,6},{6,4},{8,10},{10,8},{12,14},{14,12},{1,3},{3,1},... | collective-permute-start | bytes 1572872 | tf_op jit(solution)/shard_map/ppermute | solution.py:26
  63.0 1.2 %fusion.18 = bf16[3,128,8,64]{1,3,2,0:T(8,128)(2,1)S(1)} fusion(bf16[3,8,128,384]{3,2,1,0:T(8,128)(2,1)S(1)} %multiply_convert_fusion, bf16[1,384,8,64]{1,3,2,0:T(8,128)(2,1)S(1)} %bitcast.95, bf16[1,384,8,64]{1,3,2,0:T(8,128)(2,1)S(1)} %bitcast.97, bf16[1,384,8,64]{1,3,2,0:T(8,128)(2,1)S(1)} %bitcast.93), kind=kOutput, calls=%fused_computation.32 | convolution fusion | flops 152371200 | bytes 3932160 | tf_op jit(solution)/shard_map/jhqk,jkhd->jqhd/dot_general | solution.py:97
  64.2 0.3 copy.26
  64.6 0.3 convert_element_type.73
  65.0 4.9 %collective-permute-done.5 = bf16[256,1024]{0,1:T(8,128)(2,1)S(1)} collective-permute-done((bf16[256,1024]{0,1:T(8,128)(2,1)}, bf16[256,1024]{0,1:T(8,128)(2,1)S(1)}, u32[]{:S(2)}, u32[]{:S(2)}) %collective-permute-start.5) | collective-permute-done | bytes 524320 | tf_op jit(solution)/shard_map/ppermute | solution.py:27
  70.0 1.6 %fusion.14 = bf16[384,1024]{0,1:T(8,128)(2,1)S(1)} fusion(f32[896,1024]{0,1:T(8,128)} %copy-done, bf16[256,1024]{0,1:T(8,128)(2,1)S(1)} %get-tuple-element.22, bf16[256,1024]{0,1:T(8,128)(2,1)S(1)} %get-tuple-element.21), kind=kLoop, calls=%fused_computation.24 | loop fusion | flops 1966080 | bytes 3407872 | tf_op jit(solution)/shard_map/convert.6
  71.7 0.2 fusion.20
  72.0 0.6 collective-permute-start.7
  72.6 19.0 %collective-permute-done.7 = bf16[2,384,512]{1,2,0:T(8,128)(2,1)S(1)} collective-permute-done((bf16[2,384,512]{1,2,0:T(8,128)(2,1)S(1)}, bf16[2,384,512]{1,2,0:T(8,128)(2,1)S(1)}, u32[]{:S(2)}, u32[]{:S(2)}) %collective-permute-start.7) | collective-permute-done | bytes 786464 | tf_op jit(solution)/shard_map/ppermute | solution.py:34
  91.6 0.4 maximum_select_fusion
  92.0 1.6 %copy.28 = bf16[1,2,384,1024]{3,2,1,0:T(8,128)(2,1)} copy(bf16[1,2,384,1024]{2,3,1,0:T(8,128)(2,1)S(1)} %maximum_select_fusion) | data formatting | bytes 3145728 | tf_op jit(solution)/shard_map/jit(_where)/select_n | solution.py:170
  (68 shorter events, 2.6 us)
Async XLA Ops:
  1.5 1.3 %copy-start.20 = (s32[12]{0:T(128)S(1)}, s32[12]{0:T(128)}, u32[]{:S(2)}) copy-start(s32[12]{0:T(128)} %param.3) | copy-start | bytes 148
  1.9 19.3 %collective-permute-start = (bf16[2,384,512]{1,2,0:T(8,128)(2,1)S(1)}, bf16[2,384,512]{1,2,0:T(8,128)(2,1)S(1)}, u32[]{:S(2)}, u32[]{:S(2)}) collective-permute-start(bf16[2,384,512]{1,2,0:T(8,128)(2,1)S(1)} %bitcast.98), channel_id=1, source_target_pairs={{0,16},{16,0},{1,17},{17,1},{2,18},{18,2},{3,19},{19,3},{4,20},{20... | collective-permute-start | bytes 2359304 | tf_op jit(solution)/shard_map/ppermute | solution.py:34
  22.6 10.8 %collective-permute-start.1 = (bf16[256,1024]{0,1:T(8,128)(2,1)}, bf16[256,1024]{0,1:T(8,128)(2,1)}, u32[]{:S(2)}, u32[]{:S(2)}) collective-permute-start(bf16[256,1024]{0,1:T(8,128)(2,1)} %get-tuple-element.38), channel_id=1, source_target_pairs={{2,4},{6,8},{10,12},{4,2},{8,6},{12,10},{3,5},{7,9},{11,13},{5,3},... | collective-permute-start | bytes 1572872 | tf_op jit(solution)/shard_map/ppermute | solution.py:27
  24.5 8.9 %collective-permute-start.2 = (bf16[256,1024]{0,1:T(8,128)(2,1)}, bf16[256,1024]{0,1:T(8,128)(2,1)}, u32[]{:S(2)}, u32[]{:S(2)}) collective-permute-start(bf16[256,1024]{0,1:T(8,128)(2,1)} %get-tuple-element.39), channel_id=1, source_target_pairs={{0,2},{2,0},{4,6},{6,4},{8,10},{10,8},{12,14},{14,12},{1,3},{3,1},... | collective-permute-start | bytes 1572872 | tf_op jit(solution)/shard_map/ppermute | solution.py:26
  30.0 10.1 %copy-start.3 = (f32[3,128,8,64]{1,0,3,2:T(4,128)}, f32[3,128,8,64]{1,0,3,2:T(4,128)S(1)}, u32[]{:S(2)}) copy-start(f32[3,128,8,64]{1,0,3,2:T(4,128)S(1)} %reshape.249) | copy-start | bytes 2359300
  31.6 3.8 %copy-start.4 = (bf16[3,128,8,64]{1,0,3,2:T(4,128)(2,1)}, bf16[3,128,8,64]{1,0,3,2:T(4,128)(2,1)S(1)}, u32[]{:S(2)}) copy-start(bf16[3,128,8,64]{1,0,3,2:T(4,128)(2,1)S(1)} %reshape_squeeze.3) | copy-start | bytes 1179652
  35.2 1.0 %copy-start.8 = (bf16[384,512]{0,1:T(8,128)(2,1)}, bf16[384,512]{0,1:T(8,128)(2,1)S(1)}, u32[]{:S(2)}) copy-start(bf16[384,512]{0,1:T(8,128)(2,1)S(1)} %get-tuple-element.28) | copy-start | bytes 1179652
  35.2 1.0 %copy-start.10 = (bf16[384,512]{0,1:T(8,128)(2,1)}, bf16[384,512]{0,1:T(8,128)(2,1)S(1)}, u32[]{:S(2)}) copy-start(bf16[384,512]{0,1:T(8,128)(2,1)S(1)} %get-tuple-element.29) | copy-start | bytes 1179652
  35.2 1.0 %copy-start.12 = (bf16[384,512]{0,1:T(8,128)(2,1)}, bf16[384,512]{0,1:T(8,128)(2,1)S(1)}, u32[]{:S(2)}) copy-start(bf16[384,512]{0,1:T(8,128)(2,1)S(1)} %get-tuple-element.30) | copy-start | bytes 1179652
  35.3 4.8 %copy-start.14 = (bf16[384,512]{0,1:T(8,128)(2,1)}, bf16[384,512]{0,1:T(8,128)(2,1)S(1)}, u32[]{:S(2)}) copy-start(bf16[384,512]{0,1:T(8,128)(2,1)S(1)} %get-tuple-element.25) | copy-start | bytes 1179652
  35.3 4.8 %copy-start.16 = (bf16[384,512]{0,1:T(8,128)(2,1)}, bf16[384,512]{0,1:T(8,128)(2,1)S(1)}, u32[]{:S(2)}) copy-start(bf16[384,512]{0,1:T(8,128)(2,1)S(1)} %get-tuple-element.26) | copy-start | bytes 1179652
  35.4 4.8 %copy-start.18 = (bf16[384,512]{0,1:T(8,128)(2,1)}, bf16[384,512]{0,1:T(8,128)(2,1)S(1)}, u32[]{:S(2)}) copy-start(bf16[384,512]{0,1:T(8,128)(2,1)S(1)} %get-tuple-element.27) | copy-start | bytes 1179652
  38.0 2.1 %copy-start.1 = (f32[3,8,128,384]{3,2,1,0:T(8,128)}, f32[3,8,128,384]{3,2,1,0:T(8,128)S(1)}, u32[]{:S(2)}) copy-start(f32[3,8,128,384]{3,2,1,0:T(8,128)S(1)} %get-tuple-element.46) | copy-start | bytes 14155780
  41.3 5.3 %copy-start.7 = (f32[3,128,8,64]{1,3,2,0:T(8,128)}, f32[3,128,8,64]{1,3,2,0:T(8,128)S(1)}, u32[]{:S(2)}) copy-start(f32[3,128,8,64]{1,3,2,0:T(8,128)S(1)} %get-tuple-element.47) | copy-start | bytes 2359300
  41.4 3.7 %collective-permute-start.3 = (f32[2,384]{1,0:T(2,128)S(1)}, f32[2,384]{1,0:T(2,128)S(1)}, u32[]{:S(2)}, u32[]{:S(2)}) collective-permute-start(f32[2,384]{1,0:T(2,128)S(1)} %pad_maximum_fusion.11), channel_id=1, source_target_pairs={{0,16},{16,0},{1,17},{17,1},{2,18},{18,2},{3,19},{19,3},{4,20},{20... | collective-permute-start | bytes 9224 | tf_op jit(solution)/shard_map/ppermute | solution.py:34
  45.1 3.7 %collective-permute-start.4 = (f32[2,384]{1,0:T(2,128)S(1)}, f32[2,384]{1,0:T(2,128)S(1)}, u32[]{:S(2)}, u32[]{:S(2)}) collective-permute-start(f32[2,384]{1,0:T(2,128)S(1)} %fusion.37), channel_id=1, source_target_pairs={{0,1},{1,0},{2,3},{3,2},{4,5},{5,4},{6,7},{7,6},{8,9},{9,8},{10,11... | collective-permute-start | bytes 9224 | tf_op jit(solution)/shard_map/ppermute | solution.py:143
  50.5 2.3 %copy-start.2 = (f32[3,8,128,384]{3,2,1,0:T(8,128)S(1)}, f32[3,8,128,384]{3,2,1,0:T(8,128)}, u32[]{:S(2)}) copy-start(f32[3,8,128,384]{3,2,1,0:T(8,128)} %copy-done.1) | copy-start | bytes 14155780
  50.5 2.4 %copy-start.15 = (bf16[384,512]{0,1:T(8,128)(2,1)S(1)}, bf16[384,512]{0,1:T(8,128)(2,1)}, u32[]{:S(2)}) copy-start(bf16[384,512]{0,1:T(8,128)(2,1)} %copy-done.14) | copy-start | bytes 1179652
  50.5 2.5 %copy-start.17 = (bf16[384,512]{0,1:T(8,128)(2,1)S(1)}, bf16[384,512]{0,1:T(8,128)(2,1)}, u32[]{:S(2)}) copy-start(bf16[384,512]{0,1:T(8,128)(2,1)} %copy-done.16) | copy-start | bytes 1179652
  50.5 2.6 %copy-start.19 = (bf16[384,512]{0,1:T(8,128)(2,1)S(1)}, bf16[384,512]{0,1:T(8,128)(2,1)}, u32[]{:S(2)}) copy-start(bf16[384,512]{0,1:T(8,128)(2,1)} %copy-done.18) | copy-start | bytes 1179652
  53.1 1.9 %copy-start.5 = (bf16[3,128,8,64]{1,0,3,2:T(4,128)(2,1)S(1)}, bf16[3,128,8,64]{1,0,3,2:T(4,128)(2,1)}, u32[]{:S(2)}) copy-start(bf16[3,128,8,64]{1,0,3,2:T(4,128)(2,1)} %copy-done.4) | copy-start | bytes 1179652
  56.5 1.8 %copy-start = (f32[896,1024]{0,1:T(8,128)}, f32[896,1024]{0,1:T(8,128)S(1)}, u32[]{:S(2)}) copy-start(f32[896,1024]{0,1:T(8,128)S(1)} %fusion.17) | copy-start | bytes 11010052
  56.5 6.5 %copy-start.9 = (bf16[384,512]{0,1:T(8,128)(2,1)S(1)}, bf16[384,512]{0,1:T(8,128)(2,1)}, u32[]{:S(2)}) copy-start(bf16[384,512]{0,1:T(8,128)(2,1)} %copy-done.8) | copy-start | bytes 1179652
  56.5 6.5 %copy-start.11 = (bf16[384,512]{0,1:T(8,128)(2,1)S(1)}, bf16[384,512]{0,1:T(8,128)(2,1)}, u32[]{:S(2)}) copy-start(bf16[384,512]{0,1:T(8,128)(2,1)} %copy-done.10) | copy-start | bytes 1179652
  56.6 6.5 %copy-start.13 = (bf16[384,512]{0,1:T(8,128)(2,1)S(1)}, bf16[384,512]{0,1:T(8,128)(2,1)}, u32[]{:S(2)}) copy-start(bf16[384,512]{0,1:T(8,128)(2,1)} %copy-done.12) | copy-start | bytes 1179652
  59.2 10.7 %collective-permute-start.5 = (bf16[256,1024]{0,1:T(8,128)(2,1)}, bf16[256,1024]{0,1:T(8,128)(2,1)S(1)}, u32[]{:S(2)}, u32[]{:S(2)}) collective-permute-start(bf16[256,1024]{0,1:T(8,128)(2,1)} %get-tuple-element.13), channel_id=1, source_target_pairs={{2,4},{6,8},{10,12},{4,2},{8,6},{12,10},{3,5},{7,9},{11,13},{5,3},... | collective-permute-start | bytes 1572872 | tf_op jit(solution)/shard_map/ppermute | solution.py:27
  61.3 3.6 %copy-start.6 = (f32[1,384,512]{1,2,0:T(8,128)S(1)}, f32[1,384,512]{1,2,0:T(8,128)}, u32[]{:S(2)}) copy-start(f32[1,384,512]{1,2,0:T(8,128)} %reshape.248) | copy-start | bytes 2359300
  61.3 8.6 %collective-permute-start.6 = (bf16[256,1024]{0,1:T(8,128)(2,1)S(1)}, bf16[256,1024]{0,1:T(8,128)(2,1)S(1)}, u32[]{:S(2)}, u32[]{:S(2)}) collective-permute-start(bf16[256,1024]{0,1:T(8,128)(2,1)S(1)} %get-tuple-element.14), channel_id=1, source_target_pairs={{0,2},{2,0},{4,6},{6,4},{8,10},{10,8},{12,14},{14,12},{1,3},{3,1},... | collective-permute-start | bytes 1572872 | tf_op jit(solution)/shard_map/ppermute | solution.py:26
  72.0 19.6 %collective-permute-start.7 = (bf16[2,384,512]{1,2,0:T(8,128)(2,1)S(1)}, bf16[2,384,512]{1,2,0:T(8,128)(2,1)S(1)}, u32[]{:S(2)}, u32[]{:S(2)}) collective-permute-start(bf16[2,384,512]{1,2,0:T(8,128)(2,1)S(1)} %get-tuple-element.32), channel_id=1, source_target_pairs={{0,16},{16,0},{1,17},{17,1},{2,18},{18,2},{3,19},{19,3},{4,20},{20... | collective-permute-start | bytes 2359304 | tf_op jit(solution)/shard_map/ppermute | solution.py:34

commit v14 on v13

--- a/solution.py
+++ b/solution.py
@@ -89,6 +89,15 @@
     shared = crosses / total_cols / spread
     upstream = ((cot_float - normed * shared[:, None]) / spread[:, None]).astype(jnp.bfloat16)
     up4 = upstream.reshape(unit_count, UNIT, heads, DH)
+    q_again, keys_again, up4 = lax.optimization_barrier((q4, keys_w, up4))
+    scores = (
+        jnp.einsum("jqhd,jkhd->jhqk", q_again, keys_again, preferred_element_type=jnp.float32)
+        * score_scale
+    )
+    scores = jnp.where(mask, scores, -jnp.inf)
+    expven = jnp.exp(scores - jnp.max(scores, axis=3, keepdims=True))
+    weights = expven / jnp.sum(expven, axis=3, keepdims=True)
+    rounded = weights.astype(jnp.bfloat16)
 
     delta = jnp.sum(up4.astype(jnp.float32) * attended4, axis=3)
     delta = jnp.transpose(delta, (0, 2, 1))[..., None]

time: 93.9 us -> 99.6 us (1.061)
  matrix products: 6.2 us -> 13 us
  local copies, waits for them, and re-layouts: 15.1 us -> 12.9 us
  other arithmetic: 12.6 us -> 13.7 us
    sub x0 -> x1, matrix products: none -> 3.65 us  [attention_grads(): expven = jnp.exp(scores - row_max)]
    unnamed x46 -> x36, local copies, waits for them, and re-layouts: 5.29 us -> 2 us
    dot_general x1, matrix products: 1.23 us -> 4 us  [attention_grads(): jnp.einsum('jhqk,jkhd->jqhd', rounded, values_w, preferred_element_type=j...]
    reduce_sum x1, other arithmetic: 1.68 us -> 0.11 us  [attention_grads(): delta = jnp.sum(up4.astype(jnp.float32) * attended4, axis=3)]
    select_n x1, other arithmetic: 0.15 us -> 1.28 us  [per_device(): key_value = jnp.where(is_first, kept, arrived)]
    dynamic_slice x2, local copies, waits for them, and re-layouts: 0.26 us -> 1.28 us  [windows(): lax.dynamic_slice_in_dim(near, rel_starts[j] * UNIT, window, 0)]
    another operation x3 -> x4, other arithmetic: 2.02 us -> 2.18 us
where the time goes in v14:
time: 99.6 us; the launch traced here: 99.3 us
  waiting for transfers between devices  46.4 us (47%)
  other arithmetic  13.7 us (14%)
  matrix products  13 us (13%)
  local copies, waits for them, and re-layouts  12.9 us (13%)
  starting transfers between devices  10.8 us (11%)
  between operations  2.45 us (2%)
    ppermute x3, waiting for transfers between devices, sec_swap(): return lax.ppermute(value, 'sec', [(0, 1), (1, 0)])  39.7 us
    ppermute x2, waiting for transfers between devices, halo_swap(): across = lax.ppermute(jnp.where(even, top, bottom), 'seq', between)  6.48 us
    dot_general x1, matrix products, attention_grads(): jnp.einsum('jhqk,jkhd->jqhd', rounded, values_w, preferred_element_type=j...  4 us
    ppermute x2, starting transfers between devices, halo_swap(): across = lax.ppermute(jnp.where(even, top, bottom), 'seq', between)  4 us
    sub x1, matrix products, attention_grads(): expven = jnp.exp(scores - row_max)  3.65 us
    ppermute x2, starting transfers between devices, halo_swap(): within = lax.ppermute(jnp.where(even, bottom, top), 'seq', inside)  3.49 us
    select_n x2, other arithmetic, halo_swap(): across = lax.ppermute(jnp.where(even, top, bottom), 'seq', between)  2.04 us
    another operation x3, other arithmetic  2.02 us
  transfers between devices with their start and end apart: 8, of which 6 were waited for; matrix products, arithmetic and copies ran while one was open for 9% of the time, Pallas kernels for 0%

profile of v14, /device:TPU:18, one launch (start us, length us, event | category | flops | bytes accessed | tf_op | source)
XLA Modules:
  0.0 99.3 jit_solution(14623029661566866544)
XLA Ops:
  0.0 1.5 %constant_dynamic-slice_fusion.6 = (bf16[1,2,384,512]{3,2,1,0:T(8,128)(2,1)S(1)}, bf16[1,2,384,512]{3,2,1,0:T(8,128)(2,1)S(1)}) fusion(bf16[1,2,384,1024]{3,2,1,0:T(8,128)(2,1)} %param.2, s32[]{:T(128)S(6)} %select_n.126, s32[]{:T(128)S(6)} %select_n.125), kind=kLoop, calls=%fused_computation.90 | loop fusion | bytes 3145736 | tf_op jit(solution)/shard_map/dynamic_slice | solution.py:138
  1.5 0.4 copy.21
  1.9 0.6 collective-permute-start
  2.5 0.4 copy.22
  3.7 17.6 %collective-permute-done = bf16[2,384,512]{1,2,0:T(8,128)(2,1)} collective-permute-done((bf16[2,384,512]{1,2,0:T(8,128)(2,1)S(1)}, bf16[2,384,512]{1,2,0:T(8,128)(2,1)}, u32[]{:S(2)}, u32[]{:S(2)}) %collective-permute-start) | collective-permute-done | bytes 786464 | tf_op jit(solution)/shard_map/ppermute | solution.py:34
  21.3 1.3 %bitcast_select_fusion = (bf16[2,384,512]{1,2,0:T(8,128)(2,1)S(1)}, bf16[2,384,512]{1,2,0:T(8,128)(2,1)S(1)}) fusion(bf16[2,384,512]{1,2,0:T(8,128)(2,1)} %collective-permute-done, bf16[1,2,384,512]{2,3,1,0:T(8,128)(2,1)S(1)} %copy.22, pred[]{:T(512)S(6)} %eq.18), kind=kLoop, calls=%fused_computation.49 | loop fusion | flops 786432 | bytes 3145729 | tf_op jit(solution)/shard_map/jit(_where)/select_n | solution.py:140
  22.7 1.2 %broadcast_select_fusion.8 = (bf16[256,1024]{0,1:T(8,128)(2,1)}, bf16[256,1024]{0,1:T(8,128)(2,1)}) fusion(pred[]{:T(512)S(6)} %eq.21, bf16[384,512]{0,1:T(8,128)(2,1)S(1)} %get-tuple-element.45, bf16[384,512]{0,1:T(8,128)(2,1)S(1)} %get-tuple-element.44), kind=kLoop, calls=%fused_computation.66 | loop fusion | flops 3670016 | bytes 1835009 | tf_op jit(solution)/shard_map/jit(_where)/select_n | solution.py:27
  23.8 1.9 %collective-permute-start.1 = (bf16[256,1024]{0,1:T(8,128)(2,1)}, bf16[256,1024]{0,1:T(8,128)(2,1)}, u32[]{:S(2)}, u32[]{:S(2)}) collective-permute-start(bf16[256,1024]{0,1:T(8,128)(2,1)} %get-tuple-element.42), channel_id=1, source_target_pairs={{2,4},{6,8},{10,12},{4,2},{8,6},{12,10},{3,5},{7,9},{11,13},{5,3},... | collective-permute-start | bytes 1572872 | tf_op jit(solution)/shard_map/ppermute | solution.py:27
  25.8 1.7 %collective-permute-start.2 = (bf16[256,1024]{0,1:T(8,128)(2,1)}, bf16[256,1024]{0,1:T(8,128)(2,1)}, u32[]{:S(2)}, u32[]{:S(2)}) collective-permute-start(bf16[256,1024]{0,1:T(8,128)(2,1)} %get-tuple-element.43), channel_id=1, source_target_pairs={{0,2},{2,0},{4,6},{6,4},{8,10},{10,8},{12,14},{14,12},{1,3},{3,1},... | collective-permute-start | bytes 1572872 | tf_op jit(solution)/shard_map/ppermute | solution.py:26
  27.5 0.7 fusion.56
  30.3 0.8 slice_convert_fusion
  31.1 0.3 reshape.251
  31.4 1.6 %reshape_squeeze.3 = bf16[3,128,8,64]{1,0,3,2:T(4,128)(2,1)S(1)} reshape(bf16[1,384,512]{1,2,0:T(8,128)(2,1)} %get-tuple-element.41) | data formatting | bytes 786432 | tf_op jit(solution)/shard_map/reshape;squeeze | solution.py:69
  33.1 1.6 %collective-permute-done.1 = bf16[256,1024]{0,1:T(8,128)(2,1)} collective-permute-done((bf16[256,1024]{0,1:T(8,128)(2,1)}, bf16[256,1024]{0,1:T(8,128)(2,1)}, u32[]{:S(2)}, u32[]{:S(2)}) %collective-permute-start.1) | collective-permute-done | bytes 524320 | tf_op jit(solution)/shard_map/ppermute | solution.py:27
  34.7 1.3 %broadcast_select_fusion.6 = (bf16[256,1024]{0,1:T(8,128)(2,1)S(1)}, bf16[256,1024]{0,1:T(8,128)(2,1)S(1)}) fusion(bf16[256,1024]{0,1:T(8,128)(2,1)} %collective-permute-done.1, bf16[256,1024]{0,1:T(8,128)(2,1)} %collective-permute-done.2, pred[]{:T(512)S(6)} %eq.21), kind=kLoop, calls=%fused_computation.64 | loop fusion | flops 524288 | bytes 2097153 | tf_op jit(solution)/shard_map/jit(_where)/select_n | solution.py:28
  36.4 1.2 %constant_dynamic-slice_fusion.2 = (bf16[384,512]{0,1:T(8,128)(2,1)}, bf16[384,512]{0,1:T(8,128)(2,1)}, bf16[384,512]{0,1:T(8,128)(2,1)}) fusion(bf16[896,512]{0,1:T(8,128)(2,1)S(1)} %get-tuple-element.19, s32[]{:T(128)S(6)} %select_n.138, s32[]{:T(128)S(6)} %select_n.140, s32[]{:T(128)S(6)} %select_n.139), kind=kLoop, calls=%fused_computation.86 | loop fusion | bytes 2359308 | tf_op jit(solution)/shard_map/dynamic_slice | solution.py:63
  37.6 3.7 %fusion.57 = (f32[3,8,128]{2,1,0:T(8,128)S(1)}, f32[3,8,128,384]{3,2,1,0:T(8,128)}) fusion(pred[3,384]{1,0:T(4,128)(4,1)S(1)} %bitcast.119, bf16[3,128,8,64]{1,0,3,2:T(4,128)(2,1)S(1)} %reshape_squeeze.3, bf16[1,384,8,64]{1,3,2,0:T(8,128)(2,1)S(1)} %bitcast.94, bf16[1,384,8,64]{1,3,2,0:T(8,128)(2,1)S(1)} %bitcast.97, bf16[1,384,8,64]{1,3,2,0:T(8,128)(2,1)S(1)} %bitcast.91), kind=kOutput, calls=%fused_computation.120 | convolution fusion | flops 156893568 | bytes 6304896 | tf_op jit(solution)/shard_map/sub | solution.py:78
  41.3 4.0 %multiply_reduce_fusion.2 = (f32[3,128]{1,0:T(4,128)S(1)}, f32[3,128]{1,0:T(4,128)S(1)}, f32[3,128,8,64]{1,3,2,0:T(8,128)S(1)}) fusion(f32[3,128,8,64]{1,0,3,2:T(4,128)S(1)} %reshape.251, f32[3,8,128,384]{3,2,1,0:T(8,128)} %get-tuple-element.50, f32[3,8,128]{2,1,0:T(8,128)S(1)} %get-tuple-element.49, bf16[1,384,8,64]{1,3,2,0:T(8,128)(2,1)} %bitcast.104, ...), kind=kOutput, calls=%fused_computation.55 | convolution fusion | flops 155319552 | bytes 7486464 | tf_op jit(solution)/shard_map/jhqk,jkhd->jqhd/dot_general | solution.py:81
  45.3 0.6 collective-permute-start.3
  45.9 3.1 %collective-permute-done.3 = f32[2,384]{1,0:T(2,128)S(1)} collective-permute-done((f32[2,384]{1,0:T(2,128)S(1)}, f32[2,384]{1,0:T(2,128)S(1)}, u32[]{:S(2)}, u32[]{:S(2)}) %collective-permute-start.3) | collective-permute-done | bytes 3104 | tf_op jit(solution)/shard_map/ppermute | solution.py:34
  49.0 0.6 fusion.54
  49.6 1.5 %collective-permute-start.4 = (f32[2,384]{1,0:T(2,128)}, f32[2,384]{1,0:T(2,128)S(1)}, u32[]{:S(2)}, u32[]{:S(2)}) collective-permute-start(f32[2,384]{1,0:T(2,128)} %fusion.54), channel_id=1, source_target_pairs={{0,1},{1,0},{2,3},{3,2},{4,5},{5,4},{6,7},{7,6},{8,9},{9,8},{10,11... | collective-permute-start | bytes 9224 | tf_op jit(solution)/shard_map/ppermute | solution.py:152
  51.3 0.5 copy.29
  51.8 1.3 %reshape.250 = f32[1,384,512]{1,2,0:T(8,128)} reshape(f32[3,128,8,64]{1,0,3,2:T(4,128)S(1)} %copy.29) | data formatting | bytes 1572864 | tf_op jit(solution)/shard_map/reshape | solution.py:82
  53.1 0.3 collective-permute-done.4
  53.4 1.4 %divide_convert_fusion.5 = bf16[3,128,8,64]{1,3,2,0:T(8,128)(2,1)S(1)} fusion(f32[3,128,8,64]{1,3,2,0:T(8,128)S(1)} %get-tuple-element.51, f32[3,128,8,64]{1,0,3,2:T(4,128)} %copy-done.1, f32[3,128]{1,0:T(4,128)S(1)} %bitcast.116, f32[3,128]{1,0:T(4,128)S(1)} %bitcast.114), kind=kLoop, calls=%fused_computation.53 | loop fusion | flops 983040 | bytes 1969152 | tf_op jit(solution)/shard_map/convert_element_type | solution.py:90
  54.9 0.8 fusion.30
  55.8 1.8 %fusion.62 = (f32[3,8,128]{2,1,0:T(8,128)S(1)}, f32[3,8,128,384]{3,2,1,0:T(8,128)S(1)}) fusion(f32[3,8,128,384]{3,2,1,0:T(8,128)S(1)} %fusion.30, pred[3,384]{1,0:T(4,128)(4,1)S(1)} %bitcast.120), kind=kOutput, calls=%fused_computation.121 | output fusion | flops 7078271 | bytes 9450624 | tf_op jit(solution)/shard_map/sub | solution.py:98
  57.5 0.9 fusion.4
  58.8 1.9 %multiply_convert_fusion = bf16[3,8,128,384]{3,2,1,0:T(8,128)(2,1)S(1)} fusion(f32[3,8,128]{2,1,0:T(8,128)S(1)} %bitcast.115, bf16[3,128,8,64]{1,3,2,0:T(8,128)(2,1)S(1)} %divide_convert_fusion.5, f32[3,8,128,384]{3,2,1,0:T(8,128)S(1)} %get-tuple-element.53, f32[3,8,128]{2,1,0:T(8,128)S(1)} %get-tuple-element.52, bf16[1,384,8,64]{1,3,2,0:T(8,128)(2,1)S(1)} %bitcast.105, ...), kind=kOutput, calls=%fused_computation.6 | convolution fusion | flops 158072832 | bytes 8675328 | tf_op jit(solution)/shard_map/jqhd,jkhd->jhqk/dot_general | solution.py:104
  60.6 0.6 fusion.39
  61.2 0.2 broadcast_in_dim.60
  61.5 0.3 fusion.16
  61.8 0.3 fusion.24
  62.4 1.6 %copy-done = f32[896,1024]{0,1:T(8,128)} copy-done((f32[896,1024]{0,1:T(8,128)}, f32[896,1024]{0,1:T(8,128)S(1)}, u32[]{:S(2)}) %copy-start) | copy-done | bytes 3670040
  63.9 0.9 broadcast_select_fusion.4
  64.8 2.1 %collective-permute-start.5 = (bf16[256,1024]{0,1:T(8,128)(2,1)}, bf16[256,1024]{0,1:T(8,128)(2,1)S(1)}, u32[]{:S(2)}, u32[]{:S(2)}) collective-permute-start(bf16[256,1024]{0,1:T(8,128)(2,1)} %get-tuple-element.17), channel_id=1, source_target_pairs={{2,4},{6,8},{10,12},{4,2},{8,6},{12,10},{3,5},{7,9},{11,13},{5,3},... | collective-permute-start | bytes 1572872 | tf_op jit(solution)/shard_map/ppermute | solution.py:27
  66.9 1.7 %collective-permute-start.6 = (bf16[256,1024]{0,1:T(8,128)(2,1)S(1)}, bf16[256,1024]{0,1:T(8,128)(2,1)S(1)}, u32[]{:S(2)}, u32[]{:S(2)}) collective-permute-start(bf16[256,1024]{0,1:T(8,128)(2,1)S(1)} %get-tuple-element.18), channel_id=1, source_target_pairs={{0,2},{2,0},{4,6},{6,4},{8,10},{10,8},{12,14},{14,12},{1,3},{3,1},... | collective-permute-start | bytes 1572872 | tf_op jit(solution)/shard_map/ppermute | solution.py:26
  68.7 1.2 %fusion.26 = bf16[3,128,8,64]{1,3,2,0:T(8,128)(2,1)S(1)} fusion(bf16[3,8,128,384]{3,2,1,0:T(8,128)(2,1)S(1)} %multiply_convert_fusion, bf16[1,384,8,64]{1,3,2,0:T(8,128)(2,1)S(1)} %bitcast.96, bf16[1,384,8,64]{1,3,2,0:T(8,128)(2,1)S(1)} %bitcast.99, bf16[1,384,8,64]{1,3,2,0:T(8,128)(2,1)S(1)} %bitcast.93), kind=kOutput, calls=%fused_computation.42 | convolution fusion | flops 152371200 | bytes 3932160 | tf_op jit(solution)/shard_map/jhqk,jkhd->jqhd/dot_general | solution.py:106
  69.8 0.3 copy.28
  70.2 0.3 convert_element_type.77
  70.6 4.9 %collective-permute-done.5 = bf16[256,1024]{0,1:T(8,128)(2,1)S(1)} collective-permute-done((bf16[256,1024]{0,1:T(8,128)(2,1)}, bf16[256,1024]{0,1:T(8,128)(2,1)S(1)}, u32[]{:S(2)}, u32[]{:S(2)}) %collective-permute-start.5) | collective-permute-done | bytes 524320 | tf_op jit(solution)/shard_map/ppermute | solution.py:27
  75.6 1.6 %fusion.21 = bf16[384,1024]{0,1:T(8,128)(2,1)S(1)} fusion(f32[896,1024]{0,1:T(8,128)} %copy-done, bf16[256,1024]{0,1:T(8,128)(2,1)S(1)} %get-tuple-element.26, bf16[256,1024]{0,1:T(8,128)(2,1)S(1)} %get-tuple-element.25), kind=kLoop, calls=%fused_computation.34 | loop fusion | flops 1966080 | bytes 3407872 | tf_op jit(solution)/shard_map/convert.6
  77.3 0.2 fusion.28
  77.6 0.6 collective-permute-start.7
  78.2 19.0 %collective-permute-done.7 = bf16[2,384,512]{1,2,0:T(8,128)(2,1)S(1)} collective-permute-done((bf16[2,384,512]{1,2,0:T(8,128)(2,1)S(1)}, bf16[2,384,512]{1,2,0:T(8,128)(2,1)S(1)}, u32[]{:S(2)}, u32[]{:S(2)}) %collective-permute-start.7) | collective-permute-done | bytes 786464 | tf_op jit(solution)/shard_map/ppermute | solution.py:34
  97.2 0.4 maximum_select_fusion
  97.6 1.6 %copy.30 = bf16[1,2,384,1024]{3,2,1,0:T(8,128)(2,1)} copy(bf16[1,2,384,1024]{2,3,1,0:T(8,128)(2,1)S(1)} %maximum_select_fusion) | data formatting | bytes 3145728 | tf_op jit(solution)/shard_map/jit(_where)/select_n | solution.py:179
  (60 shorter events, 2.7 us)
Async XLA Ops:
  1.5 1.3 %copy-start.15 = (s32[12]{0:T(128)S(1)}, s32[12]{0:T(128)}, u32[]{:S(2)}) copy-start(s32[12]{0:T(128)} %param.3) | copy-start | bytes 148
  1.9 19.5 %collective-permute-start = (bf16[2,384,512]{1,2,0:T(8,128)(2,1)S(1)}, bf16[2,384,512]{1,2,0:T(8,128)(2,1)}, u32[]{:S(2)}, u32[]{:S(2)}) collective-permute-start(bf16[2,384,512]{1,2,0:T(8,128)(2,1)S(1)} %bitcast.100), channel_id=1, source_target_pairs={{0,16},{16,0},{1,17},{17,1},{2,18},{18,2},{3,19},{19,3},{4,20},{20... | collective-permute-start | bytes 2359304 | tf_op jit(solution)/shard_map/ppermute | solution.py:34
  23.8 10.8 %collective-permute-start.1 = (bf16[256,1024]{0,1:T(8,128)(2,1)}, bf16[256,1024]{0,1:T(8,128)(2,1)}, u32[]{:S(2)}, u32[]{:S(2)}) collective-permute-start(bf16[256,1024]{0,1:T(8,128)(2,1)} %get-tuple-element.42), channel_id=1, source_target_pairs={{2,4},{6,8},{10,12},{4,2},{8,6},{12,10},{3,5},{7,9},{11,13},{5,3},... | collective-permute-start | bytes 1572872 | tf_op jit(solution)/shard_map/ppermute | solution.py:27
  25.8 8.9 %collective-permute-start.2 = (bf16[256,1024]{0,1:T(8,128)(2,1)}, bf16[256,1024]{0,1:T(8,128)(2,1)}, u32[]{:S(2)}, u32[]{:S(2)}) collective-permute-start(bf16[256,1024]{0,1:T(8,128)(2,1)} %get-tuple-element.43), channel_id=1, source_target_pairs={{0,2},{2,0},{4,6},{6,4},{8,10},{10,8},{12,14},{14,12},{1,3},{3,1},... | collective-permute-start | bytes 1572872 | tf_op jit(solution)/shard_map/ppermute | solution.py:26
  30.3 7.3 %copy-start.13 = (pred[1,3,3,128]{3,1,2,0:T(4,128)(4,1)}, pred[1,3,3,128]{3,1,2,0:T(4,128)(4,1)S(1)}, u32[]{:S(2)}) copy-start(pred[1,3,3,128]{3,1,2,0:T(4,128)(4,1)S(1)} %copy.55) | copy-start | bytes 3460
  31.4 9.8 %copy-start.1 = (f32[3,128,8,64]{1,0,3,2:T(4,128)}, f32[3,128,8,64]{1,0,3,2:T(4,128)S(1)}, u32[]{:S(2)}) copy-start(f32[3,128,8,64]{1,0,3,2:T(4,128)S(1)} %reshape.251) | copy-start | bytes 2359300
  36.4 4.8 %copy-start.7 = (bf16[384,512]{0,1:T(8,128)(2,1)}, bf16[384,512]{0,1:T(8,128)(2,1)S(1)}, u32[]{:S(2)}) copy-start(bf16[384,512]{0,1:T(8,128)(2,1)S(1)} %get-tuple-element.34) | copy-start | bytes 1179652
  36.4 14.7 %copy-start.3 = (bf16[384,512]{0,1:T(8,128)(2,1)}, bf16[384,512]{0,1:T(8,128)(2,1)S(1)}, u32[]{:S(2)}) copy-start(bf16[384,512]{0,1:T(8,128)(2,1)S(1)} %get-tuple-element.32) | copy-start | bytes 1179652
  36.4 14.7 %copy-start.5 = (bf16[384,512]{0,1:T(8,128)(2,1)}, bf16[384,512]{0,1:T(8,128)(2,1)S(1)}, u32[]{:S(2)}) copy-start(bf16[384,512]{0,1:T(8,128)(2,1)S(1)} %get-tuple-element.33) | copy-start | bytes 1179652
  41.3 9.8 %copy-start.8 = (bf16[384,512]{0,1:T(8,128)(2,1)S(1)}, bf16[384,512]{0,1:T(8,128)(2,1)}, u32[]{:S(2)}) copy-start(bf16[384,512]{0,1:T(8,128)(2,1)} %copy-done.7) | copy-start | bytes 1179652
  45.3 3.7 %collective-permute-start.3 = (f32[2,384]{1,0:T(2,128)S(1)}, f32[2,384]{1,0:T(2,128)S(1)}, u32[]{:S(2)}, u32[]{:S(2)}) collective-permute-start(f32[2,384]{1,0:T(2,128)S(1)} %pad_maximum_fusion.9), channel_id=1, source_target_pairs={{0,16},{16,0},{1,17},{17,1},{2,18},{18,2},{3,19},{19,3},{4,20},{20... | collective-permute-start | bytes 9224 | tf_op jit(solution)/shard_map/ppermute | solution.py:34
  49.6 3.8 %collective-permute-start.4 = (f32[2,384]{1,0:T(2,128)}, f32[2,384]{1,0:T(2,128)S(1)}, u32[]{:S(2)}, u32[]{:S(2)}) collective-permute-start(f32[2,384]{1,0:T(2,128)} %fusion.54), channel_id=1, source_target_pairs={{0,1},{1,0},{2,3},{3,2},{4,5},{5,4},{6,7},{7,6},{8,9},{9,8},{10,11... | collective-permute-start | bytes 9224 | tf_op jit(solution)/shard_map/ppermute | solution.py:152
  54.9 0.8 copy-start.14
  57.5 1.0 %copy-start.10 = (bf16[384,512]{0,1:T(8,128)(2,1)S(1)}, bf16[384,512]{0,1:T(8,128)(2,1)}, u32[]{:S(2)}) copy-start(bf16[384,512]{0,1:T(8,128)(2,1)} %get-tuple-element.29) | copy-start | bytes 1179652
  57.5 1.1 %copy-start.11 = (bf16[384,512]{0,1:T(8,128)(2,1)S(1)}, bf16[384,512]{0,1:T(8,128)(2,1)}, u32[]{:S(2)}) copy-start(bf16[384,512]{0,1:T(8,128)(2,1)} %get-tuple-element.30) | copy-start | bytes 1179652
  57.5 1.2 %copy-start.12 = (bf16[384,512]{0,1:T(8,128)(2,1)S(1)}, bf16[384,512]{0,1:T(8,128)(2,1)}, u32[]{:S(2)}) copy-start(bf16[384,512]{0,1:T(8,128)(2,1)} %get-tuple-element.31) | copy-start | bytes 1179652
  62.1 1.8 %copy-start = (f32[896,1024]{0,1:T(8,128)}, f32[896,1024]{0,1:T(8,128)S(1)}, u32[]{:S(2)}) copy-start(f32[896,1024]{0,1:T(8,128)S(1)} %fusion.24) | copy-start | bytes 11010052
  62.2 6.5 %copy-start.4 = (bf16[384,512]{0,1:T(8,128)(2,1)S(1)}, bf16[384,512]{0,1:T(8,128)(2,1)}, u32[]{:S(2)}) copy-start(bf16[384,512]{0,1:T(8,128)(2,1)} %copy-done.3) | copy-start | bytes 1179652
  62.2 6.5 %copy-start.6 = (bf16[384,512]{0,1:T(8,128)(2,1)S(1)}, bf16[384,512]{0,1:T(8,128)(2,1)}, u32[]{:S(2)}) copy-start(bf16[384,512]{0,1:T(8,128)(2,1)} %copy-done.5) | copy-start | bytes 1179652
  62.2 6.5 %copy-start.9 = (bf16[384,512]{0,1:T(8,128)(2,1)S(1)}, bf16[384,512]{0,1:T(8,128)(2,1)}, u32[]{:S(2)}) copy-start(bf16[384,512]{0,1:T(8,128)(2,1)} %copy-done.7) | copy-start | bytes 1179652
  64.8 10.7 %collective-permute-start.5 = (bf16[256,1024]{0,1:T(8,128)(2,1)}, bf16[256,1024]{0,1:T(8,128)(2,1)S(1)}, u32[]{:S(2)}, u32[]{:S(2)}) collective-permute-start(bf16[256,1024]{0,1:T(8,128)(2,1)} %get-tuple-element.17), channel_id=1, source_target_pairs={{2,4},{6,8},{10,12},{4,2},{8,6},{12,10},{3,5},{7,9},{11,13},{5,3},... | collective-permute-start | bytes 1572872 | tf_op jit(solution)/shard_map/ppermute | solution.py:27
  66.9 3.6 %copy-start.2 = (f32[1,384,512]{1,2,0:T(8,128)S(1)}, f32[1,384,512]{1,2,0:T(8,128)}, u32[]{:S(2)}) copy-start(f32[1,384,512]{1,2,0:T(8,128)} %reshape.250) | copy-start | bytes 2359300
  66.9 8.6 %collective-permute-start.6 = (bf16[256,1024]{0,1:T(8,128)(2,1)S(1)}, bf16[256,1024]{0,1:T(8,128)(2,1)S(1)}, u32[]{:S(2)}, u32[]{:S(2)}) collective-permute-start(bf16[256,1024]{0,1:T(8,128)(2,1)S(1)} %get-tuple-element.18), channel_id=1, source_target_pairs={{0,2},{2,0},{4,6},{6,4},{8,10},{10,8},{12,14},{14,12},{1,3},{3,1},... | collective-permute-start | bytes 1572872 | tf_op jit(solution)/shard_map/ppermute | solution.py:26
  77.6 19.6 %collective-permute-start.7 = (bf16[2,384,512]{1,2,0:T(8,128)(2,1)S(1)}, bf16[2,384,512]{1,2,0:T(8,128)(2,1)S(1)}, u32[]{:S(2)}, u32[]{:S(2)}) collective-permute-start(bf16[2,384,512]{1,2,0:T(8,128)(2,1)S(1)} %get-tuple-element.36), channel_id=1, source_target_pairs={{0,16},{16,0},{1,17},{17,1},{2,18},{18,2},{3,19},{19,3},{4,20},{20... | collective-permute-start | bytes 2359304 | tf_op jit(solution)/shard_map/ppermute | solution.py:34

commit v15 on v13

--- a/solution.py
+++ b/solution.py
@@ -153,20 +153,43 @@
         row_total,
         total_cols,
     )
-    from_left, from_right = halo_swap(
-        total[:halo].astype(jnp.bfloat16), total[near.shape[0] - halo :].astype(jnp.bfloat16)
-    )
+    count = lax.axis_size("seq")
+    even = seq_place % 2 == 0
+    top = total[:halo].astype(jnp.bfloat16)
+    bottom = total[near.shape[0] - halo :].astype(jnp.bfloat16)
+    inside = [(i, i ^ 1) for i in range(count) if (i ^ 1) < count]
+    between = [(i, i + 1) for i in range(1, count - 1, 2)] + [(i + 1, i) for i in range(1, count - 1, 2)]
+    within = lax.ppermute(jnp.where(even, bottom, top), "seq", inside)
+    across = lax.ppermute(jnp.where(even, top, bottom), "seq", between)
+    middle = total[halo : halo + rows]
+    early = rows - halo
+    early_even = middle[rows - early :] + within[halo - early :].astype(jnp.float32)
+    early_odd = middle[:early] + within[:early].astype(jnp.float32)
+    early_own = jnp.where(even, early_even, early_odd).astype(jnp.bfloat16)
+    qn_pair = jnp.stack([grad_q.astype(jnp.bfloat16), normed.astype(jnp.bfloat16)])
+    early_kv = jnp.stack([early_own[:, :half], early_own[:, half:]])
+    early_qn = jnp.where(even, qn_pair[:, rows - early :], qn_pair[:, :early])
+    back_early = sec_swap(jnp.where(is_first, early_qn, early_kv))
+    back_early, across = lax.optimization_barrier((back_early, across))
+    from_left = jnp.where(even, across, within)
+    from_right = jnp.where(even, within, across)
     own = (
-        total[halo : halo + rows]
+        middle
         + jnp.pad(from_left.astype(jnp.float32), ((0, rows - halo), (0, 0)))
         + jnp.pad(from_right.astype(jnp.float32), ((rows - halo, 0), (0, 0)))
     )
+    late_own = jnp.where(even, own[: rows - early], own[early:]).astype(jnp.bfloat16)
     grad_k = own[:, :half].astype(jnp.bfloat16)
     grad_v = own[:, half:].astype(jnp.bfloat16)
-
     kv_pair = jnp.stack([grad_k, grad_v])
-    qn_pair = jnp.stack([grad_q.astype(jnp.bfloat16), normed.astype(jnp.bfloat16)])
-    back = sec_swap(jnp.where(is_first, qn_pair, kv_pair))
+    late_kv = jnp.stack([late_own[:, :half], late_own[:, half:]])
+    late_qn = jnp.where(even, qn_pair[:, : rows - early], qn_pair[:, early:])
+    back_late = sec_swap(jnp.where(is_first, late_qn, late_kv))
+    back = jnp.where(
+        even,
+        jnp.concatenate([back_late, back_early], axis=1),
+        jnp.concatenate([back_early, back_late], axis=1),
+    )
     result = jnp.where(
         is_first,
         jnp.concatenate([kv_pair, back], axis=2),

time: 93.9 us -> 92 us (0.980)
  waiting for transfers between devices: 46.5 us -> 44.1 us
  other arithmetic: 12.6 us -> 13.7 us
    ppermute x0 -> x2, waiting for transfers between devices: none -> 6.06 us  [the longest x1 6.06 us: per_device(): across = lax.ppermute(jnp.where(even, top, bottom), 'seq', between)]
    ppermute x2 -> x1, waiting for transfers between devices: 6.71 us -> 1.9 us  [halo_swap(): across = lax.ppermute(jnp.where(even, top, bottom), 'seq', between)]
    ppermute x3 -> x4, waiting for transfers between devices: 39.6 us -> 36 us  [sec_swap(): return lax.ppermute(value, 'sec', [(0, 1), (1, 0)])]
    ppermute x0 -> x2, starting transfers between devices: none -> 2.38 us  [the longest x1 2.31 us: per_device(): across = lax.ppermute(jnp.where(even, top, bottom), 'seq', between)]
    ppermute x2 -> x1, starting transfers between devices: 4 us -> 1.91 us  [halo_swap(): across = lax.ppermute(jnp.where(even, top, bottom), 'seq', between)]
    ppermute x2 -> x1, starting transfers between devices: 3.49 us -> 1.74 us  [halo_swap(): within = lax.ppermute(jnp.where(even, bottom, top), 'seq', inside)]
    another operation x3 -> x2, other arithmetic: 2.02 us -> 0.38 us
    add x0 -> x1, other arithmetic: none -> 1.65 us  [per_device(): middle + jnp.pad(from_left.astype(jnp.float32), ((0, rows - halo), (0, 0)))]
  transfers between devices with their start and end apart: 8 -> 9, of which waited for: 6 -> 7; matrix products, arithmetic and copies ran while one was open for 9% -> 11% of each run, Pallas kernels for 0% -> 0%
where the time goes in v15:
time: 92 us; the launch traced here: 91.6 us
  waiting for transfers between devices  44.1 us (48%)
  local copies, waits for them, and re-layouts  15.3 us (17%)
  other arithmetic  13.7 us (15%)
  starting transfers between devices  10 us (11%)
  matrix products  6.16 us (7%)
  between operations  2.36 us (3%)
    ppermute x4, waiting for transfers between devices, sec_swap(): return lax.ppermute(value, 'sec', [(0, 1), (1, 0)])  36 us
    ppermute x1, waiting for transfers between devices, per_device(): across = lax.ppermute(jnp.where(even, top, bottom), 'seq', between)  6.06 us
    unnamed x46, local copies, waits for them, and re-layouts  5.41 us
    ppermute x4, starting transfers between devices, sec_swap(): return lax.ppermute(value, 'sec', [(0, 1), (1, 0)])  2.41 us
    ppermute x1, starting transfers between devices, per_device(): across = lax.ppermute(jnp.where(even, top, bottom), 'seq', between)  2.31 us
    ppermute x1, starting transfers between devices, halo_swap(): across = lax.ppermute(jnp.where(even, top, bottom), 'seq', between)  1.91 us
    ppermute x1, waiting for transfers between devices, halo_swap(): across = lax.ppermute(jnp.where(even, top, bottom), 'seq', between)  1.9 us
    dot_general x1, matrix products, attention_grads(): jnp.einsum('jqhd,jkhd->jhqk', up4, values_w, preferred_element_type=jnp.f...  1.86 us
  transfers between devices with their start and end apart: 9, of which 7 were waited for; matrix products, arithmetic and copies ran while one was open for 11% of the time, Pallas kernels for 0%

profile of v15, /device:TPU:18, one launch (start us, length us, event | category | flops | bytes accessed | tf_op | source)
XLA Modules:
  0.0 91.6 jit_solution(14471233836076343671)
XLA Ops:
  0.0 1.5 %constant_dynamic-slice_fusion.6 = (bf16[1,2,384,512]{3,2,1,0:T(8,128)(2,1)S(1)}, bf16[1,2,384,512]{3,2,1,0:T(8,128)(2,1)S(1)}) fusion(bf16[1,2,384,1024]{3,2,1,0:T(8,128)(2,1)} %param.2, s32[]{:T(128)S(6)} %select_n.176, s32[]{:T(128)S(6)} %select_n.175), kind=kLoop, calls=%fused_computation.101 | loop fusion | bytes 3145736 | tf_op jit(solution)/shard_map/dynamic_slice | solution.py:129
  1.5 0.4 copy.20
  1.9 0.6 collective-permute-start
  2.5 0.4 copy.21
  3.7 17.5 %collective-permute-done = bf16[2,384,512]{1,2,0:T(8,128)(2,1)S(1)} collective-permute-done((bf16[2,384,512]{1,2,0:T(8,128)(2,1)S(1)}, bf16[2,384,512]{1,2,0:T(8,128)(2,1)S(1)}, u32[]{:S(2)}, u32[]{:S(2)}) %collective-permute-start) | collective-permute-done | bytes 786464 | tf_op jit(solution)/shard_map/ppermute | solution.py:34
  21.4 1.2 %broadcast_select_fusion.7 = (bf16[256,1024]{0,1:T(8,128)(2,1)}, bf16[256,1024]{0,1:T(8,128)(2,1)}) fusion(pred[]{:T(512)S(6)} %eq.21, bf16[384,512]{0,1:T(8,128)(2,1)S(1)} %get-tuple-element.42, bf16[384,512]{0,1:T(8,128)(2,1)S(1)} %get-tuple-element.41), kind=kLoop, calls=%fused_computation.75 | loop fusion | flops 3670016 | bytes 1835009 | tf_op jit(solution)/shard_map/jit(_where)/select_n | solution.py:27
  22.6 1.9 %collective-permute-start.1 = (bf16[256,1024]{0,1:T(8,128)(2,1)}, bf16[256,1024]{0,1:T(8,128)(2,1)}, u32[]{:S(2)}, u32[]{:S(2)}) collective-permute-start(bf16[256,1024]{0,1:T(8,128)(2,1)} %get-tuple-element.39), channel_id=1, source_target_pairs={{2,4},{6,8},{10,12},{4,2},{8,6},{12,10},{3,5},{7,9},{11,13},{5,3},... | collective-permute-start | bytes 1572872 | tf_op jit(solution)/shard_map/ppermute | solution.py:27
  24.5 1.7 %collective-permute-start.2 = (bf16[256,1024]{0,1:T(8,128)(2,1)}, bf16[256,1024]{0,1:T(8,128)(2,1)}, u32[]{:S(2)}, u32[]{:S(2)}) collective-permute-start(bf16[256,1024]{0,1:T(8,128)(2,1)} %get-tuple-element.40), channel_id=1, source_target_pairs={{0,2},{2,0},{4,6},{6,4},{8,10},{10,8},{12,14},{14,12},{1,3},{3,1},... | collective-permute-start | bytes 1572872 | tf_op jit(solution)/shard_map/ppermute | solution.py:26
  26.3 0.6 fusion.49
  28.7 0.8 slice_convert_fusion
  29.6 0.3 reshape.297
  29.9 1.6 %reshape_squeeze.3 = bf16[3,128,8,64]{1,0,3,2:T(4,128)(2,1)S(1)} reshape(bf16[1,384,512]{1,2,0:T(8,128)(2,1)} %get-tuple-element.38) | data formatting | bytes 786432 | tf_op jit(solution)/shard_map/reshape;squeeze | solution.py:69
  31.5 1.9 %collective-permute-done.1 = bf16[256,1024]{0,1:T(8,128)(2,1)} collective-permute-done((bf16[256,1024]{0,1:T(8,128)(2,1)}, bf16[256,1024]{0,1:T(8,128)(2,1)}, u32[]{:S(2)}, u32[]{:S(2)}) %collective-permute-start.1) | collective-permute-done | bytes 524320 | tf_op jit(solution)/shard_map/ppermute | solution.py:27
  33.4 1.3 %broadcast_select_fusion.5 = (bf16[256,1024]{0,1:T(8,128)(2,1)S(1)}, bf16[256,1024]{0,1:T(8,128)(2,1)S(1)}) fusion(bf16[256,1024]{0,1:T(8,128)(2,1)} %collective-permute-done.1, bf16[256,1024]{0,1:T(8,128)(2,1)} %collective-permute-done.2, pred[]{:T(512)S(6)} %eq.21), kind=kLoop, calls=%fused_computation.73 | loop fusion | flops 524288 | bytes 2097153 | tf_op jit(solution)/shard_map/jit(_where)/select_n | solution.py:28
  35.4 0.8 fusion.28
  36.2 1.7 %fusion.50 = (f32[3,8,128]{2,1,0:T(8,128)S(1)}, f32[3,8,128,384]{3,2,1,0:T(8,128)S(1)}) fusion(f32[3,8,128,384]{3,2,1,0:T(8,128)S(1)} %fusion.28, pred[3,384]{1,0:T(4,128)(4,1)S(1)} %bitcast.125), kind=kOutput, calls=%fused_computation.131 | output fusion | flops 7078271 | bytes 9450624 | tf_op jit(solution)/shard_map/sub | solution.py:78
  38.0 0.6 fusion.5
  38.6 1.5 %copy-done.1 = f32[3,8,128,384]{3,2,1,0:T(8,128)} copy-done((f32[3,8,128,384]{3,2,1,0:T(8,128)}, f32[3,8,128,384]{3,2,1,0:T(8,128)S(1)}, u32[]{:S(2)}) %copy-start.1) | copy-done | bytes 4718616
  40.1 1.2 %multiply_reduce_fusion.2 = (f32[3,128]{1,0:T(4,128)S(1)}, f32[3,128]{1,0:T(4,128)S(1)}, f32[3,128,8,64]{1,3,2,0:T(8,128)S(1)}) fusion(f32[3,128,8,64]{1,0,3,2:T(4,128)S(1)} %reshape.297, bf16[3,8,128,384]{3,2,1,0:T(8,128)(2,1)S(1)} %fusion.5, bf16[1,384,8,64]{1,3,2,0:T(8,128)(2,1)S(1)} %bitcast.110, bf16[1,384,8,64]{1,3,2,0:T(8,128)(2,1)S(1)} %bitcast.112, ...), kind=kOutput, calls=%fused_computation.57 | convolution fusion | flops 152960256 | bytes 5114880 | tf_op jit(solution)/shard_map/jhqk,jkhd->jqhd/dot_general | solution.py:81
  41.4 0.6 collective-permute-start.3
  42.0 3.1 %collective-permute-done.3 = f32[2,384]{1,0:T(2,128)S(1)} collective-permute-done((f32[2,384]{1,0:T(2,128)S(1)}, f32[2,384]{1,0:T(2,128)S(1)}, u32[]{:S(2)}, u32[]{:S(2)}) %collective-permute-start.3) | collective-permute-done | bytes 3104 | tf_op jit(solution)/shard_map/ppermute | solution.py:34
  45.1 1.6 %collective-permute-start.4 = (f32[2,384]{1,0:T(2,128)S(1)}, f32[2,384]{1,0:T(2,128)S(1)}, u32[]{:S(2)}, u32[]{:S(2)}) collective-permute-start(f32[2,384]{1,0:T(2,128)S(1)} %fusion.47), channel_id=1, source_target_pairs={{0,1},{1,0},{2,3},{3,2},{4,5},{5,4},{6,7},{7,6},{8,9},{9,8},{10,11... | collective-permute-start | bytes 9224 | tf_op jit(solution)/shard_map/ppermute | solution.py:143
  46.6 0.5 copy.27
  47.2 1.3 %reshape.296 = f32[1,384,512]{1,2,0:T(8,128)} reshape(f32[3,128,8,64]{1,0,3,2:T(4,128)S(1)} %copy.27) | data formatting | bytes 1572864 | tf_op jit(solution)/shard_map/reshape | solution.py:82
  48.8 1.7 %multiply_reduce_fusion = (f32[3,128,8]{1,2,0:T(8,128)S(1)}, bf16[3,128,8,64]{1,3,2,0:T(8,128)(2,1)S(1)}) fusion(f32[3,128,8,64]{1,3,2,0:T(8,128)} %copy-done.7, f32[3,128]{1,0:T(4,128)S(1)} %bitcast.122, f32[3,128]{1,0:T(4,128)S(1)} %bitcast.120, f32[3,128,8,64]{1,0,3,2:T(4,128)} %copy-done.3), kind=kLoop, calls=%fused_computation.54 | loop fusion | flops 1569792 | bytes 1981440 | tf_op jit(solution)/shard_map/reduce_sum | solution.py:93
  50.5 0.6 fusion.51
  51.0 1.7 %copy-done.2 = f32[3,8,128,384]{3,2,1,0:T(8,128)S(1)} copy-done((f32[3,8,128,384]{3,2,1,0:T(8,128)S(1)}, f32[3,8,128,384]{3,2,1,0:T(8,128)}, u32[]{:S(2)}) %copy-start.2) | copy-done | bytes 4718616
  53.1 1.9 %multiply_convert_fusion = bf16[3,8,128,384]{3,2,1,0:T(8,128)(2,1)S(1)} fusion(f32[3,8,128]{2,1,0:T(8,128)S(1)} %bitcast.121, bf16[3,128,8,64]{1,3,2,0:T(8,128)(2,1)S(1)} %get-tuple-element.16, f32[3,8,128,384]{3,2,1,0:T(8,128)S(1)} %copy-done.2, f32[3,8,128]{2,1,0:T(8,128)S(1)} %get-tuple-element.50, bf16[1,384,8,64]{1,3,2,0:T(8,128)(2,1)S(1)} %bitcast.111, ...), kind=kOutput, calls=%fused_computation.5 | convolution fusion | flops 158072832 | bytes 8675328 | tf_op jit(solution)/shard_map/jqhd,jkhd->jhqk/dot_general | solution.py:95
  55.0 0.6 fusion.30
  55.5 0.2 broadcast_in_dim.36
  55.9 0.3 fusion.9
  56.2 0.3 fusion.16
  56.8 1.5 %copy-done = f32[896,1024]{0,1:T(8,128)} copy-done((f32[896,1024]{0,1:T(8,128)}, f32[896,1024]{0,1:T(8,128)S(1)}, u32[]{:S(2)}) %copy-start) | copy-done | bytes 3670040
  58.6 1.1 %fusion.17 = bf16[3,128,8,64]{1,3,2,0:T(8,128)(2,1)S(1)} fusion(bf16[3,8,128,384]{3,2,1,0:T(8,128)(2,1)S(1)} %multiply_convert_fusion, bf16[1,384,8,64]{1,3,2,0:T(8,128)(2,1)S(1)} %bitcast.104, bf16[1,384,8,64]{1,3,2,0:T(8,128)(2,1)S(1)} %bitcast.106, bf16[1,384,8,64]{1,3,2,0:T(8,128)(2,1)S(1)} %bitcast.102), kind=kOutput, calls=%fused_computation.31 | convolution fusion | flops 152371200 | bytes 3932160 | tf_op jit(solution)/shard_map/jhqk,jkhd->jqhd/dot_general | solution.py:97
  59.8 0.3 copy.26
  60.1 0.3 convert_element_type.85
  60.5 2.3 %collective-permute-start.7 = (bf16[256,1024]{0,1:T(8,128)(2,1)S(1)}, bf16[256,1024]{0,1:T(8,128)(2,1)S(1)}, u32[]{:S(2)}, u32[]{:S(2)}) collective-permute-start(bf16[256,1024]{0,1:T(8,128)(2,1)S(1)} %get-tuple-element.17), channel_id=1, source_target_pairs={{2,4},{6,8},{10,12},{4,2},{8,6},{12,10},{3,5},{7,9},{11,13},{5,3},... | collective-permute-start | bytes 1572872 | tf_op jit(solution)/shard_map/ppermute | solution.py:163
  62.9 1.3 %fusion.27 = bf16[128,1024]{0,1:T(8,128)(2,1)S(1)} fusion(f32[896,1024]{0,1:T(8,128)} %copy-done, bf16[256,1024]{0,1:T(8,128)(2,1)S(1)} %collective-permute-done.5, pred[]{:T(512)S(6)} %eq.21), kind=kLoop, calls=%fused_computation.65 | loop fusion | flops 786432 | bytes 1835009 | tf_op jit(solution)/shard_map/convert_element_type | solution.py:168
  64.3 0.6 collective-permute-start.6
  64.9 6.1 %collective-permute-done.7 = bf16[256,1024]{0,1:T(8,128)(2,1)S(1)} collective-permute-done((bf16[256,1024]{0,1:T(8,128)(2,1)S(1)}, bf16[256,1024]{0,1:T(8,128)(2,1)S(1)}, u32[]{:S(2)}, u32[]{:S(2)}) %collective-permute-start.7) | collective-permute-done | bytes 524320 | tf_op jit(solution)/shard_map/ppermute | solution.py:163
  71.0 2.3 %collective-permute-done.6 = bf16[2,128,512]{1,2,0:T(8,128)(2,1)S(1)} collective-permute-done((bf16[2,128,512]{1,2,0:T(8,128)(2,1)S(1)}, bf16[2,128,512]{1,2,0:T(8,128)(2,1)S(1)}, u32[]{:S(2)}, u32[]{:S(2)}) %collective-permute-start.6) | collective-permute-done | bytes 262176 | tf_op jit(solution)/shard_map/ppermute | solution.py:34
  73.3 1.6 %fusion.13 = bf16[384,1024]{0,1:T(8,128)(2,1)S(1)} fusion(f32[896,1024]{0,1:T(8,128)} %copy-done, bf16[256,1024]{0,1:T(8,128)(2,1)S(1)} %get-tuple-element.26, bf16[256,1024]{0,1:T(8,128)(2,1)S(1)} %get-tuple-element.25), kind=kLoop, calls=%fused_computation.23 | loop fusion | flops 1966080 | bytes 3407872 | tf_op jit(solution)/shard_map/add | solution.py:177
  75.1 0.2 fusion.24
  75.3 0.6 collective-permute-start.8
  76.2 13.2 %collective-permute-done.8 = bf16[2,256,512]{1,2,0:T(8,128)(2,1)S(1)} collective-permute-done((bf16[2,256,512]{1,2,0:T(8,128)(2,1)S(1)}, bf16[2,256,512]{1,2,0:T(8,128)(2,1)S(1)}, u32[]{:S(2)}, u32[]{:S(2)}) %collective-permute-start.8) | collective-permute-done | bytes 524320 | tf_op jit(solution)/shard_map/ppermute | solution.py:34
  89.3 0.2 fusion.20
  89.6 0.4 maximum_select_fusion
  90.0 1.6 %copy.28 = bf16[1,2,384,1024]{3,2,1,0:T(8,128)(2,1)} copy(bf16[1,2,384,1024]{2,3,1,0:T(8,128)(2,1)S(1)} %maximum_select_fusion) | data formatting | bytes 3145728 | tf_op jit(solution)/shard_map/jit(_where)/select_n | solution.py:193
  (78 shorter events, 3.6 us)
Async XLA Ops:
  1.5 1.3 %copy-start.20 = (s32[12]{0:T(128)S(1)}, s32[12]{0:T(128)}, u32[]{:S(2)}) copy-start(s32[12]{0:T(128)} %param.3) | copy-start | bytes 148
  1.9 19.3 %collective-permute-start = (bf16[2,384,512]{1,2,0:T(8,128)(2,1)S(1)}, bf16[2,384,512]{1,2,0:T(8,128)(2,1)S(1)}, u32[]{:S(2)}, u32[]{:S(2)}) collective-permute-start(bf16[2,384,512]{1,2,0:T(8,128)(2,1)S(1)} %bitcast.107), channel_id=1, source_target_pairs={{0,16},{16,0},{1,17},{17,1},{2,18},{18,2},{3,19},{19,3},{4,20},{20... | collective-permute-start | bytes 2359304 | tf_op jit(solution)/shard_map/ppermute | solution.py:34
  22.6 10.8 %collective-permute-start.1 = (bf16[256,1024]{0,1:T(8,128)(2,1)}, bf16[256,1024]{0,1:T(8,128)(2,1)}, u32[]{:S(2)}, u32[]{:S(2)}) collective-permute-start(bf16[256,1024]{0,1:T(8,128)(2,1)} %get-tuple-element.39), channel_id=1, source_target_pairs={{2,4},{6,8},{10,12},{4,2},{8,6},{12,10},{3,5},{7,9},{11,13},{5,3},... | collective-permute-start | bytes 1572872 | tf_op jit(solution)/shard_map/ppermute | solution.py:27
  24.5 8.9 %collective-permute-start.2 = (bf16[256,1024]{0,1:T(8,128)(2,1)}, bf16[256,1024]{0,1:T(8,128)(2,1)}, u32[]{:S(2)}, u32[]{:S(2)}) collective-permute-start(bf16[256,1024]{0,1:T(8,128)(2,1)} %get-tuple-element.40), channel_id=1, source_target_pairs={{0,2},{2,0},{4,6},{6,4},{8,10},{10,8},{12,14},{14,12},{1,3},{3,1},... | collective-permute-start | bytes 1572872 | tf_op jit(solution)/shard_map/ppermute | solution.py:26
  29.9 10.2 %copy-start.3 = (f32[3,128,8,64]{1,0,3,2:T(4,128)}, f32[3,128,8,64]{1,0,3,2:T(4,128)S(1)}, u32[]{:S(2)}) copy-start(f32[3,128,8,64]{1,0,3,2:T(4,128)S(1)} %reshape.297) | copy-start | bytes 2359300
  31.5 3.9 %copy-start.4 = (bf16[3,128,8,64]{1,0,3,2:T(4,128)(2,1)}, bf16[3,128,8,64]{1,0,3,2:T(4,128)(2,1)S(1)}, u32[]{:S(2)}) copy-start(bf16[3,128,8,64]{1,0,3,2:T(4,128)(2,1)S(1)} %reshape_squeeze.3) | copy-start | bytes 1179652
  35.2 1.0 %copy-start.8 = (bf16[384,512]{0,1:T(8,128)(2,1)}, bf16[384,512]{0,1:T(8,128)(2,1)S(1)}, u32[]{:S(2)}) copy-start(bf16[384,512]{0,1:T(8,128)(2,1)S(1)} %get-tuple-element.32) | copy-start | bytes 1179652
  35.2 1.0 %copy-start.10 = (bf16[384,512]{0,1:T(8,128)(2,1)}, bf16[384,512]{0,1:T(8,128)(2,1)S(1)}, u32[]{:S(2)}) copy-start(bf16[384,512]{0,1:T(8,128)(2,1)S(1)} %get-tuple-element.33) | copy-start | bytes 1179652
  35.2 1.0 %copy-start.12 = (bf16[384,512]{0,1:T(8,128)(2,1)}, bf16[384,512]{0,1:T(8,128)(2,1)S(1)}, u32[]{:S(2)}) copy-start(bf16[384,512]{0,1:T(8,128)(2,1)S(1)} %get-tuple-element.34) | copy-start | bytes 1179652
  35.3 4.8 %copy-start.14 = (bf16[384,512]{0,1:T(8,128)(2,1)}, bf16[384,512]{0,1:T(8,128)(2,1)S(1)}, u32[]{:S(2)}) copy-start(bf16[384,512]{0,1:T(8,128)(2,1)S(1)} %get-tuple-element.29) | copy-start | bytes 1179652
  35.4 4.7 %copy-start.16 = (bf16[384,512]{0,1:T(8,128)(2,1)}, bf16[384,512]{0,1:T(8,128)(2,1)S(1)}, u32[]{:S(2)}) copy-start(bf16[384,512]{0,1:T(8,128)(2,1)S(1)} %get-tuple-element.30) | copy-start | bytes 1179652
  35.4 4.7 %copy-start.18 = (bf16[384,512]{0,1:T(8,128)(2,1)}, bf16[384,512]{0,1:T(8,128)(2,1)S(1)}, u32[]{:S(2)}) copy-start(bf16[384,512]{0,1:T(8,128)(2,1)S(1)} %get-tuple-element.31) | copy-start | bytes 1179652
  38.0 2.1 %copy-start.1 = (f32[3,8,128,384]{3,2,1,0:T(8,128)}, f32[3,8,128,384]{3,2,1,0:T(8,128)S(1)}, u32[]{:S(2)}) copy-start(f32[3,8,128,384]{3,2,1,0:T(8,128)S(1)} %get-tuple-element.51) | copy-start | bytes 14155780
  41.3 5.3 %copy-start.7 = (f32[3,128,8,64]{1,3,2,0:T(8,128)}, f32[3,128,8,64]{1,3,2,0:T(8,128)S(1)}, u32[]{:S(2)}) copy-start(f32[3,128,8,64]{1,3,2,0:T(8,128)S(1)} %get-tuple-element.52) | copy-start | bytes 2359300
  41.4 3.7 %collective-permute-start.3 = (f32[2,384]{1,0:T(2,128)S(1)}, f32[2,384]{1,0:T(2,128)S(1)}, u32[]{:S(2)}, u32[]{:S(2)}) collective-permute-start(f32[2,384]{1,0:T(2,128)S(1)} %pad_maximum_fusion.10), channel_id=1, source_target_pairs={{0,16},{16,0},{1,17},{17,1},{2,18},{18,2},{3,19},{19,3},{4,20},{20... | collective-permute-start | bytes 9224 | tf_op jit(solution)/shard_map/ppermute | solution.py:34
  45.1 3.7 %collective-permute-start.4 = (f32[2,384]{1,0:T(2,128)S(1)}, f32[2,384]{1,0:T(2,128)S(1)}, u32[]{:S(2)}, u32[]{:S(2)}) collective-permute-start(f32[2,384]{1,0:T(2,128)S(1)} %fusion.47), channel_id=1, source_target_pairs={{0,1},{1,0},{2,3},{3,2},{4,5},{5,4},{6,7},{7,6},{8,9},{9,8},{10,11... | collective-permute-start | bytes 9224 | tf_op jit(solution)/shard_map/ppermute | solution.py:143
  50.4 2.3 %copy-start.2 = (f32[3,8,128,384]{3,2,1,0:T(8,128)S(1)}, f32[3,8,128,384]{3,2,1,0:T(8,128)}, u32[]{:S(2)}) copy-start(f32[3,8,128,384]{3,2,1,0:T(8,128)} %copy-done.1) | copy-start | bytes 14155780
  50.5 2.4 %copy-start.15 = (bf16[384,512]{0,1:T(8,128)(2,1)S(1)}, bf16[384,512]{0,1:T(8,128)(2,1)}, u32[]{:S(2)}) copy-start(bf16[384,512]{0,1:T(8,128)(2,1)} %copy-done.14) | copy-start | bytes 1179652
  50.5 2.5 %copy-start.17 = (bf16[384,512]{0,1:T(8,128)(2,1)S(1)}, bf16[384,512]{0,1:T(8,128)(2,1)}, u32[]{:S(2)}) copy-start(bf16[384,512]{0,1:T(8,128)(2,1)} %copy-done.16) | copy-start | bytes 1179652
  50.5 2.6 %copy-start.19 = (bf16[384,512]{0,1:T(8,128)(2,1)S(1)}, bf16[384,512]{0,1:T(8,128)(2,1)}, u32[]{:S(2)}) copy-start(bf16[384,512]{0,1:T(8,128)(2,1)} %copy-done.18) | copy-start | bytes 1179652
  53.1 1.9 %copy-start.5 = (bf16[3,128,8,64]{1,0,3,2:T(4,128)(2,1)S(1)}, bf16[3,128,8,64]{1,0,3,2:T(4,128)(2,1)}, u32[]{:S(2)}) copy-start(bf16[3,128,8,64]{1,0,3,2:T(4,128)(2,1)} %copy-done.4) | copy-start | bytes 1179652
  56.5 1.8 %copy-start = (f32[896,1024]{0,1:T(8,128)}, f32[896,1024]{0,1:T(8,128)S(1)}, u32[]{:S(2)}) copy-start(f32[896,1024]{0,1:T(8,128)S(1)} %fusion.16) | copy-start | bytes 11010052
  56.5 1.9 %copy-start.9 = (bf16[384,512]{0,1:T(8,128)(2,1)S(1)}, bf16[384,512]{0,1:T(8,128)(2,1)}, u32[]{:S(2)}) copy-start(bf16[384,512]{0,1:T(8,128)(2,1)} %copy-done.8) | copy-start | bytes 1179652
  56.5 1.9 %copy-start.11 = (bf16[384,512]{0,1:T(8,128)(2,1)S(1)}, bf16[384,512]{0,1:T(8,128)(2,1)}, u32[]{:S(2)}) copy-start(bf16[384,512]{0,1:T(8,128)(2,1)} %copy-done.10) | copy-start | bytes 1179652
  56.5 2.1 %copy-start.13 = (bf16[384,512]{0,1:T(8,128)(2,1)S(1)}, bf16[384,512]{0,1:T(8,128)(2,1)}, u32[]{:S(2)}) copy-start(bf16[384,512]{0,1:T(8,128)(2,1)} %copy-done.12) | copy-start | bytes 1179652
  58.4 4.4 %copy-start.6 = (f32[1,384,512]{1,2,0:T(8,128)S(1)}, f32[1,384,512]{1,2,0:T(8,128)}, u32[]{:S(2)}) copy-start(f32[1,384,512]{1,2,0:T(8,128)} %reshape.296) | copy-start | bytes 2359300
  58.4 4.5 %collective-permute-start.5 = (bf16[256,1024]{0,1:T(8,128)(2,1)S(1)}, bf16[256,1024]{0,1:T(8,128)(2,1)S(1)}, u32[]{:S(2)}, u32[]{:S(2)}) collective-permute-start(bf16[256,1024]{0,1:T(8,128)(2,1)S(1)} %get-tuple-element.18), channel_id=1, source_target_pairs={{0,2},{2,0},{4,6},{6,4},{8,10},{10,8},{12,14},{14,12},{1,3},{3,1},... | collective-permute-start | bytes 1572872 | tf_op jit(solution)/shard_map/ppermute | solution.py:162
  60.5 10.5 %collective-permute-start.7 = (bf16[256,1024]{0,1:T(8,128)(2,1)S(1)}, bf16[256,1024]{0,1:T(8,128)(2,1)S(1)}, u32[]{:S(2)}, u32[]{:S(2)}) collective-permute-start(bf16[256,1024]{0,1:T(8,128)(2,1)S(1)} %get-tuple-element.17), channel_id=1, source_target_pairs={{2,4},{6,8},{10,12},{4,2},{8,6},{12,10},{3,5},{7,9},{11,13},{5,3},... | collective-permute-start | bytes 1572872 | tf_op jit(solution)/shard_map/ppermute | solution.py:163
  64.3 8.9 %collective-permute-start.6 = (bf16[2,128,512]{1,2,0:T(8,128)(2,1)S(1)}, bf16[2,128,512]{1,2,0:T(8,128)(2,1)S(1)}, u32[]{:S(2)}, u32[]{:S(2)}) collective-permute-start(bf16[2,128,512]{1,2,0:T(8,128)(2,1)S(1)} %fusion.34), channel_id=1, source_target_pairs={{0,16},{16,0},{1,17},{17,1},{2,18},{18,2},{3,19},{19,3},{4,20},{20... | collective-permute-start | bytes 786440 | tf_op jit(solution)/shard_map/ppermute | solution.py:34
  75.3 14.0 %collective-permute-start.8 = (bf16[2,256,512]{1,2,0:T(8,128)(2,1)S(1)}, bf16[2,256,512]{1,2,0:T(8,128)(2,1)S(1)}, u32[]{:S(2)}, u32[]{:S(2)}) collective-permute-start(bf16[2,256,512]{1,2,0:T(8,128)(2,1)S(1)} %fusion.24), channel_id=1, source_target_pairs={{0,16},{16,0},{1,17},{17,1},{2,18},{18,2},{3,19},{19,3},{4,20},{20... | collective-permute-start | bytes 1572872 | tf_op jit(solution)/shard_map/ppermute | solution.py:34

commit v16 on v15

--- a/solution.py
+++ b/solution.py
@@ -125,14 +125,32 @@
 
     keep_offset = section * half
     send_offset = (1 - section) * half
+    even = seq_place % 2 == 0
+    count = lax.axis_size("seq")
+    inside = [(i, i ^ 1) for i in range(count) if (i ^ 1) < count]
+    between = [(i, i + 1) for i in range(1, count - 1, 2)] + [(i + 1, i) for i in range(1, count - 1, 2)]
     sent = lax.dynamic_slice_in_dim(local_heads, send_offset, half, 2)
     kept = lax.dynamic_slice_in_dim(local_heads, keep_offset, half, 2)
-    arrived = sec_swap(sent)
+    first_rows = jnp.where(even, sent[:, :halo], sent[:, rows - halo :])
+    rest_rows = jnp.where(even, sent[:, halo:], sent[:, : rows - halo])
+    arrived_first = sec_swap(first_rows)
+    kept_first = jnp.where(even, kept[:, :halo], kept[:, rows - halo :])
+    pair_first = jnp.where(is_first, kept_first, arrived_first)
+    across = lax.ppermute(jnp.concatenate([pair_first[0], pair_first[1]], axis=1), "seq", between)
+    arrived_rest = sec_swap(rest_rows)
+    arrived_rest, across = lax.optimization_barrier((arrived_rest, across))
+    arrived = jnp.where(
+        even,
+        jnp.concatenate([arrived_first, arrived_rest], axis=1),
+        jnp.concatenate([arrived_rest, arrived_first], axis=1),
+    )
     key_value = jnp.where(is_first, kept, arrived)
     query_cot = jnp.where(is_first, arrived, kept)
 
     joined = jnp.concatenate([key_value[0], key_value[1]], axis=1)
-    low, high = halo_swap(joined[:halo], joined[rows - halo :])
+    within = lax.ppermute(jnp.where(even, joined[rows - halo :], joined[:halo]), "seq", inside)
+    low = jnp.where(even, across, within)
+    high = jnp.where(even, within, across)
     near = jnp.concatenate([low, joined, high], axis=0)
 
     rel_starts, allowed = window_plan(doc_units, seq_place, unit_count, halo_units)

time: 92 us -> 93.6 us (1.017)
    ppermute x2, waiting for transfers between devices: 1.9 us -> 6.32 us  [the longest x1 6.32 us: per_device(): lax.ppermute(jnp.concatenate([pair_first[0], pair_first[1]], axis=1), 'se...]
    ppermute x4 -> x5, waiting for transfers between devices: 36 us -> 32.4 us  [sec_swap(): return lax.ppermute(value, 'sec', [(0, 1), (1, 0)])]
    ppermute x2, starting transfers between devices: 3.65 us -> 2.04 us  [the longest x1 1.92 us: per_device(): lax.ppermute(jnp.concatenate([pair_first[0], pair_first[1]], axis=1), 'se...]
    ppermute x4 -> x5, starting transfers between devices: 2.41 us -> 3.9 us  [sec_swap(): return lax.ppermute(value, 'sec', [(0, 1), (1, 0)])]
    select_n x2 -> x5, other arithmetic: 2.45 us -> 2.61 us  [the longest x1 1.46 us: per_device(): low = jnp.where(even, across, within)]
  transfers between devices with their start and end apart: 9 -> 10, of which waited for: 7 -> 8; matrix products, arithmetic and copies ran while one was open for 11% -> 11% of each run, Pallas kernels for 0% -> 0%
where the time goes in v16:
time: 93.6 us; the launch traced here: 93.2 us
  waiting for transfers between devices  45 us (48%)
  local copies, waits for them, and re-layouts  15.4 us (16%)
  other arithmetic  14.1 us (15%)
  starting transfers between devices  9.96 us (11%)
  matrix products  6.17 us (7%)
  between operations  2.57 us (3%)
    ppermute x5, waiting for transfers between devices, sec_swap(): return lax.ppermute(value, 'sec', [(0, 1), (1, 0)])  32.4 us
    ppermute x1, waiting for transfers between devices, per_device(): lax.ppermute(jnp.concatenate([pair_first[0], pair_first[1]], axis=1), 'se...  6.32 us
    ppermute x1, waiting for transfers between devices, per_device(): across = lax.ppermute(jnp.where(even, top, bottom), 'seq', between)  6.07 us
    unnamed x46, local copies, waits for them, and re-layouts  5.41 us
    ppermute x5, starting transfers between devices, sec_swap(): return lax.ppermute(value, 'sec', [(0, 1), (1, 0)])  3.9 us
    ppermute x1, starting transfers between devices, per_device(): across = lax.ppermute(jnp.where(even, top, bottom), 'seq', between)  2.33 us
    ppermute x1, starting transfers between devices, per_device(): lax.ppermute(jnp.concatenate([pair_first[0], pair_first[1]], axis=1), 'se...  1.92 us
  transfers between devices with their start and end apart: 10, of which 8 were waited for; matrix products, arithmetic and copies ran while one was open for 11% of the time, Pallas kernels for 0%

profile of v16, /device:TPU:18, one launch (start us, length us, event | category | flops | bytes accessed | tf_op | source)
XLA Modules:
  0.0 93.2 jit_solution(14133406618254123986)
XLA Ops:
  0.0 1.5 %constant_dynamic-slice_fusion.6 = (bf16[1,2,384,512]{3,2,1,0:T(8,128)(2,1)S(1)}, bf16[1,2,384,512]{3,2,1,0:T(8,128)(2,1)S(1)}) fusion(bf16[1,2,384,1024]{3,2,1,0:T(8,128)(2,1)} %param.2, s32[]{:T(128)S(6)} %select_n.199, s32[]{:T(128)S(6)} %select_n.194), kind=kLoop, calls=%fused_computation.108 | loop fusion | bytes 3145736 | tf_op jit(solution)/shard_map/dynamic_slice | solution.py:133
  1.5 0.4 copy.20
  2.0 0.6 collective-permute-start
  2.6 1.6 %collective-permute-start.1 = (bf16[2,128,512]{1,2,0:T(8,128)(2,1)S(1)}, bf16[2,128,512]{1,2,0:T(8,128)(2,1)S(1)}, u32[]{:S(2)}, u32[]{:S(2)}) collective-permute-start(bf16[2,128,512]{1,2,0:T(8,128)(2,1)S(1)} %slice_select_fusion.3), channel_id=1, source_target_pairs={{0,16},{16,0},{1,17},{17,1},{2,18},{18,2},{3,19},{19,3},{4,20},{20... | collective-permute-start | bytes 786440 | tf_op jit(solution)/shard_map/ppermute | solution.py:34
  4.2 0.4 copy.21
  5.1 11.8 %collective-permute-done = bf16[2,256,512]{1,2,0:T(8,128)(2,1)S(1)} collective-permute-done((bf16[2,256,512]{1,2,0:T(8,128)(2,1)S(1)}, bf16[2,256,512]{1,2,0:T(8,128)(2,1)S(1)}, u32[]{:S(2)}, u32[]{:S(2)}) %collective-permute-start) | collective-permute-done | bytes 524320 | tf_op jit(solution)/shard_map/ppermute | solution.py:34
  17.0 1.9 %collective-permute-start.2 = (bf16[256,1024]{0,1:T(8,128)(2,1)S(1)}, bf16[256,1024]{0,1:T(8,128)(2,1)}, u32[]{:S(2)}, u32[]{:S(2)}) collective-permute-start(bf16[256,1024]{0,1:T(8,128)(2,1)S(1)} %pad_maximum_fusion.6), channel_id=1, source_target_pairs={{2,4},{6,8},{10,12},{4,2},{8,6},{12,10},{3,5},{7,9},{11,13},{5,3},... | collective-permute-start | bytes 1572872 | tf_op jit(solution)/shard_map/ppermute | solution.py:139
  19.3 2.0 %collective-permute-done.1 = bf16[2,128,512]{1,2,0:T(8,128)(2,1)S(1)} collective-permute-done((bf16[2,128,512]{1,2,0:T(8,128)(2,1)S(1)}, bf16[2,128,512]{1,2,0:T(8,128)(2,1)S(1)}, u32[]{:S(2)}, u32[]{:S(2)}) %collective-permute-start.1) | collective-permute-done | bytes 262176 | tf_op jit(solution)/shard_map/ppermute | solution.py:34
  21.3 6.3 %collective-permute-done.2 = bf16[256,1024]{0,1:T(8,128)(2,1)} collective-permute-done((bf16[256,1024]{0,1:T(8,128)(2,1)S(1)}, bf16[256,1024]{0,1:T(8,128)(2,1)}, u32[]{:S(2)}, u32[]{:S(2)}) %collective-permute-start.2) | collective-permute-done | bytes 524320 | tf_op jit(solution)/shard_map/ppermute | solution.py:139
  27.6 0.4 broadcast_select_fusion.1
  28.1 0.9 %fusion.22 = bf16[256,1024]{0,1:T(8,128)(2,1)} fusion(bf16[384,512]{0,1:T(8,128)(2,1)S(1)} %get-tuple-element.44, bf16[384,512]{0,1:T(8,128)(2,1)S(1)} %get-tuple-element.43, pred[]{:T(512)S(6)} %eq.19), kind=kLoop, calls=%fused_computation.60 | loop fusion | flops 2359296 | bytes 1310721 | tf_op jit(solution)/shard_map/jit(_where)/select_n | solution.py:151
  29.2 0.7 fusion.51
  31.9 0.8 slice_convert_fusion
  32.7 0.3 reshape.297
  33.0 1.6 %reshape_squeeze.3 = bf16[3,128,8,64]{1,0,3,2:T(4,128)(2,1)S(1)} reshape(bf16[1,384,512]{1,2,0:T(8,128)(2,1)} %get-tuple-element.42) | data formatting | bytes 786432 | tf_op jit(solution)/shard_map/reshape;squeeze | solution.py:69
  34.7 1.5 %broadcast_select_fusion.7 = (bf16[256,1024]{0,1:T(8,128)(2,1)S(1)}, bf16[256,1024]{0,1:T(8,128)(2,1)S(1)}) fusion(bf16[256,1024]{0,1:T(8,128)(2,1)} %collective-permute-done.2, bf16[256,1024]{0,1:T(8,128)(2,1)} %collective-permute-done.3, pred[]{:T(512)S(6)} %eq.19), kind=kLoop, calls=%fused_computation.79 | loop fusion | flops 524288 | bytes 2097153 | tf_op jit(solution)/shard_map/jit(_where)/select_n | solution.py:152
  36.8 0.8 fusion.30
  37.7 1.7 %fusion.52 = (f32[3,8,128]{2,1,0:T(8,128)S(1)}, f32[3,8,128,384]{3,2,1,0:T(8,128)S(1)}) fusion(f32[3,8,128,384]{3,2,1,0:T(8,128)S(1)} %fusion.30, pred[3,384]{1,0:T(4,128)(4,1)S(1)} %bitcast.131), kind=kOutput, calls=%fused_computation.138 | output fusion | flops 7078271 | bytes 9450624 | tf_op jit(solution)/shard_map/sub | solution.py:78
  39.4 0.6 fusion.5
  40.0 1.5 %copy-done.1 = f32[3,8,128,384]{3,2,1,0:T(8,128)} copy-done((f32[3,8,128,384]{3,2,1,0:T(8,128)}, f32[3,8,128,384]{3,2,1,0:T(8,128)S(1)}, u32[]{:S(2)}) %copy-start.1) | copy-done | bytes 4718616
  41.5 1.2 %multiply_reduce_fusion.2 = (f32[3,128]{1,0:T(4,128)S(1)}, f32[3,128]{1,0:T(4,128)S(1)}, f32[3,128,8,64]{1,3,2,0:T(8,128)S(1)}) fusion(f32[3,128,8,64]{1,0,3,2:T(4,128)S(1)} %reshape.297, bf16[3,8,128,384]{3,2,1,0:T(8,128)(2,1)S(1)} %fusion.5, bf16[1,384,8,64]{1,3,2,0:T(8,128)(2,1)S(1)} %bitcast.116, bf16[1,384,8,64]{1,3,2,0:T(8,128)(2,1)S(1)} %bitcast.118, ...), kind=kOutput, calls=%fused_computation.56 | convolution fusion | flops 152960256 | bytes 5114880 | tf_op jit(solution)/shard_map/jhqk,jkhd->jqhd/dot_general | solution.py:81
  42.8 0.6 collective-permute-start.4
  43.4 3.0 %collective-permute-done.4 = f32[2,384]{1,0:T(2,128)S(1)} collective-permute-done((f32[2,384]{1,0:T(2,128)S(1)}, f32[2,384]{1,0:T(2,128)S(1)}, u32[]{:S(2)}, u32[]{:S(2)}) %collective-permute-start.4) | collective-permute-done | bytes 3104 | tf_op jit(solution)/shard_map/ppermute | solution.py:34
  46.5 1.6 %collective-permute-start.5 = (f32[2,384]{1,0:T(2,128)S(1)}, f32[2,384]{1,0:T(2,128)S(1)}, u32[]{:S(2)}, u32[]{:S(2)}) collective-permute-start(f32[2,384]{1,0:T(2,128)S(1)} %fusion.49), channel_id=1, source_target_pairs={{0,1},{1,0},{2,3},{3,2},{4,5},{5,4},{6,7},{7,6},{8,9},{9,8},{10,11... | collective-permute-start | bytes 9224 | tf_op jit(solution)/shard_map/ppermute | solution.py:161
  48.1 0.5 copy.27
  48.7 1.3 %reshape.296 = f32[1,384,512]{1,2,0:T(8,128)} reshape(f32[3,128,8,64]{1,0,3,2:T(4,128)S(1)} %copy.27) | data formatting | bytes 1572864 | tf_op jit(solution)/shard_map/reshape | solution.py:82
  50.2 1.7 %multiply_reduce_fusion = (f32[3,128,8]{1,2,0:T(8,128)S(1)}, bf16[3,128,8,64]{1,3,2,0:T(8,128)(2,1)S(1)}) fusion(f32[3,128,8,64]{1,3,2,0:T(8,128)} %copy-done.7, f32[3,128]{1,0:T(4,128)S(1)} %bitcast.128, f32[3,128]{1,0:T(4,128)S(1)} %bitcast.126, f32[3,128,8,64]{1,0,3,2:T(4,128)} %copy-done.3), kind=kLoop, calls=%fused_computation.53 | loop fusion | flops 1569792 | bytes 1981440 | tf_op jit(solution)/shard_map/reduce_sum | solution.py:93
  51.9 0.6 fusion.53
  52.5 1.7 %copy-done.2 = f32[3,8,128,384]{3,2,1,0:T(8,128)S(1)} copy-done((f32[3,8,128,384]{3,2,1,0:T(8,128)S(1)}, f32[3,8,128,384]{3,2,1,0:T(8,128)}, u32[]{:S(2)}) %copy-start.2) | copy-done | bytes 4718616
  54.5 1.9 %multiply_convert_fusion = bf16[3,8,128,384]{3,2,1,0:T(8,128)(2,1)S(1)} fusion(f32[3,8,128]{2,1,0:T(8,128)S(1)} %bitcast.127, bf16[3,128,8,64]{1,3,2,0:T(8,128)(2,1)S(1)} %get-tuple-element.20, f32[3,8,128,384]{3,2,1,0:T(8,128)S(1)} %copy-done.2, f32[3,8,128]{2,1,0:T(8,128)S(1)} %get-tuple-element.54, bf16[1,384,8,64]{1,3,2,0:T(8,128)(2,1)S(1)} %bitcast.117, ...), kind=kOutput, calls=%fused_computation.5 | convolution fusion | flops 158072832 | bytes 8675328 | tf_op jit(solution)/shard_map/jqhd,jkhd->jhqk/dot_general | solution.py:95
  56.4 0.6 fusion.32
  57.0 0.2 broadcast_in_dim.36
  57.3 0.3 fusion.9
  57.6 0.3 fusion.16
  58.2 1.5 %copy-done = f32[896,1024]{0,1:T(8,128)} copy-done((f32[896,1024]{0,1:T(8,128)}, f32[896,1024]{0,1:T(8,128)S(1)}, u32[]{:S(2)}) %copy-start) | copy-done | bytes 3670040
  60.1 1.2 %fusion.17 = bf16[3,128,8,64]{1,3,2,0:T(8,128)(2,1)S(1)} fusion(bf16[3,8,128,384]{3,2,1,0:T(8,128)(2,1)S(1)} %multiply_convert_fusion, bf16[1,384,8,64]{1,3,2,0:T(8,128)(2,1)S(1)} %bitcast.111, bf16[1,384,8,64]{1,3,2,0:T(8,128)(2,1)S(1)} %bitcast.113, bf16[1,384,8,64]{1,3,2,0:T(8,128)(2,1)S(1)} %bitcast.109), kind=kOutput, calls=%fused_computation.31 | convolution fusion | flops 152371200 | bytes 3932160 | tf_op jit(solution)/shard_map/jhqk,jkhd->jqhd/dot_general | solution.py:97
  61.2 0.3 copy.26
  61.6 0.3 convert_element_type.85
  61.9 2.3 %collective-permute-start.8 = (bf16[256,1024]{0,1:T(8,128)(2,1)S(1)}, bf16[256,1024]{0,1:T(8,128)(2,1)S(1)}, u32[]{:S(2)}, u32[]{:S(2)}) collective-permute-start(bf16[256,1024]{0,1:T(8,128)(2,1)S(1)} %get-tuple-element.21), channel_id=1, source_target_pairs={{2,4},{6,8},{10,12},{4,2},{8,6},{12,10},{3,5},{7,9},{11,13},{5,3},... | collective-permute-start | bytes 1572872 | tf_op jit(solution)/shard_map/ppermute | solution.py:181
  64.4 1.3 %fusion.28 = bf16[128,1024]{0,1:T(8,128)(2,1)S(1)} fusion(f32[896,1024]{0,1:T(8,128)} %copy-done, bf16[256,1024]{0,1:T(8,128)(2,1)S(1)} %collective-permute-done.6, pred[]{:T(512)S(6)} %eq.19), kind=kLoop, calls=%fused_computation.67 | loop fusion | flops 786432 | bytes 1835009 | tf_op jit(solution)/shard_map/convert_element_type | solution.py:186
  65.8 0.6 collective-permute-start.7
  66.3 6.1 %collective-permute-done.8 = bf16[256,1024]{0,1:T(8,128)(2,1)S(1)} collective-permute-done((bf16[256,1024]{0,1:T(8,128)(2,1)S(1)}, bf16[256,1024]{0,1:T(8,128)(2,1)S(1)}, u32[]{:S(2)}, u32[]{:S(2)}) %collective-permute-start.8) | collective-permute-done | bytes 524320 | tf_op jit(solution)/shard_map/ppermute | solution.py:181
  72.4 2.4 %collective-permute-done.7 = bf16[2,128,512]{1,2,0:T(8,128)(2,1)S(1)} collective-permute-done((bf16[2,128,512]{1,2,0:T(8,128)(2,1)S(1)}, bf16[2,128,512]{1,2,0:T(8,128)(2,1)S(1)}, u32[]{:S(2)}, u32[]{:S(2)}) %collective-permute-start.7) | collective-permute-done | bytes 262176 | tf_op jit(solution)/shard_map/ppermute | solution.py:34
  74.9 1.6 %fusion.13 = bf16[384,1024]{0,1:T(8,128)(2,1)S(1)} fusion(f32[896,1024]{0,1:T(8,128)} %copy-done, bf16[256,1024]{0,1:T(8,128)(2,1)S(1)} %get-tuple-element.30, bf16[256,1024]{0,1:T(8,128)(2,1)S(1)} %get-tuple-element.29), kind=kLoop, calls=%fused_computation.23 | loop fusion | flops 1966080 | bytes 3407872 | tf_op jit(solution)/shard_map/add | solution.py:195
  76.9 0.5 collective-permute-start.9
  77.7 13.2 %collective-permute-done.9 = bf16[2,256,512]{1,2,0:T(8,128)(2,1)S(1)} collective-permute-done((bf16[2,256,512]{1,2,0:T(8,128)(2,1)S(1)}, bf16[2,256,512]{1,2,0:T(8,128)(2,1)S(1)}, u32[]{:S(2)}, u32[]{:S(2)}) %collective-permute-start.9) | collective-permute-done | bytes 524320 | tf_op jit(solution)/shard_map/ppermute | solution.py:34
  91.2 0.4 maximum_select_fusion
  91.6 1.6 %copy.28 = bf16[1,2,384,1024]{3,2,1,0:T(8,128)(2,1)} copy(bf16[1,2,384,1024]{2,3,1,0:T(8,128)(2,1)S(1)} %maximum_select_fusion) | data formatting | bytes 3145728 | tf_op jit(solution)/shard_map/jit(_where)/select_n | solution.py:211
  (85 shorter events, 4.3 us)
Async XLA Ops:
  1.8 2.7 %copy-start.20 = (s32[12]{0:T(128)S(1)}, s32[12]{0:T(128)}, u32[]{:S(2)}) copy-start(s32[12]{0:T(128)} %param.3) | copy-start | bytes 148
  2.0 14.9 %collective-permute-start = (bf16[2,256,512]{1,2,0:T(8,128)(2,1)S(1)}, bf16[2,256,512]{1,2,0:T(8,128)(2,1)S(1)}, u32[]{:S(2)}, u32[]{:S(2)}) collective-permute-start(bf16[2,256,512]{1,2,0:T(8,128)(2,1)S(1)} %slice_select_fusion.2), channel_id=1, source_target_pairs={{0,16},{16,0},{1,17},{17,1},{2,18},{18,2},{3,19},{19,3},{4,20},{20... | collective-permute-start | bytes 1572872 | tf_op jit(solution)/shard_map/ppermute | solution.py:34
  2.6 18.7 %collective-permute-start.1 = (bf16[2,128,512]{1,2,0:T(8,128)(2,1)S(1)}, bf16[2,128,512]{1,2,0:T(8,128)(2,1)S(1)}, u32[]{:S(2)}, u32[]{:S(2)}) collective-permute-start(bf16[2,128,512]{1,2,0:T(8,128)(2,1)S(1)} %slice_select_fusion.3), channel_id=1, source_target_pairs={{0,16},{16,0},{1,17},{17,1},{2,18},{18,2},{3,19},{19,3},{4,20},{20... | collective-permute-start | bytes 786440 | tf_op jit(solution)/shard_map/ppermute | solution.py:34
  17.0 10.6 %collective-permute-start.2 = (bf16[256,1024]{0,1:T(8,128)(2,1)S(1)}, bf16[256,1024]{0,1:T(8,128)(2,1)}, u32[]{:S(2)}, u32[]{:S(2)}) collective-permute-start(bf16[256,1024]{0,1:T(8,128)(2,1)S(1)} %pad_maximum_fusion.6), channel_id=1, source_target_pairs={{2,4},{6,8},{10,12},{4,2},{8,6},{12,10},{3,5},{7,9},{11,13},{5,3},... | collective-permute-start | bytes 1572872 | tf_op jit(solution)/shard_map/ppermute | solution.py:139
  29.0 5.6 %collective-permute-start.3 = (bf16[256,1024]{0,1:T(8,128)(2,1)}, bf16[256,1024]{0,1:T(8,128)(2,1)}, u32[]{:S(2)}, u32[]{:S(2)}) collective-permute-start(bf16[256,1024]{0,1:T(8,128)(2,1)} %fusion.22), channel_id=1, source_target_pairs={{0,2},{2,0},{4,6},{6,4},{8,10},{10,8},{12,14},{14,12},{1,3},{3,1},... | collective-permute-start | bytes 1572872 | tf_op jit(solution)/shard_map/ppermute | solution.py:151
  33.0 8.5 %copy-start.3 = (f32[3,128,8,64]{1,0,3,2:T(4,128)}, f32[3,128,8,64]{1,0,3,2:T(4,128)S(1)}, u32[]{:S(2)}) copy-start(f32[3,128,8,64]{1,0,3,2:T(4,128)S(1)} %reshape.297) | copy-start | bytes 2359300
  34.6 2.2 %copy-start.4 = (bf16[3,128,8,64]{1,0,3,2:T(4,128)(2,1)}, bf16[3,128,8,64]{1,0,3,2:T(4,128)(2,1)S(1)}, u32[]{:S(2)}) copy-start(bf16[3,128,8,64]{1,0,3,2:T(4,128)(2,1)S(1)} %reshape_squeeze.3) | copy-start | bytes 1179652
  36.6 1.0 %copy-start.8 = (bf16[384,512]{0,1:T(8,128)(2,1)}, bf16[384,512]{0,1:T(8,128)(2,1)S(1)}, u32[]{:S(2)}) copy-start(bf16[384,512]{0,1:T(8,128)(2,1)S(1)} %get-tuple-element.36) | copy-start | bytes 1179652
  36.6 1.0 %copy-start.10 = (bf16[384,512]{0,1:T(8,128)(2,1)}, bf16[384,512]{0,1:T(8,128)(2,1)S(1)}, u32[]{:S(2)}) copy-start(bf16[384,512]{0,1:T(8,128)(2,1)S(1)} %get-tuple-element.37) | copy-start | bytes 1179652
  36.6 1.0 %copy-start.12 = (bf16[384,512]{0,1:T(8,128)(2,1)}, bf16[384,512]{0,1:T(8,128)(2,1)S(1)}, u32[]{:S(2)}) copy-start(bf16[384,512]{0,1:T(8,128)(2,1)S(1)} %get-tuple-element.38) | copy-start | bytes 1179652
  36.8 4.8 %copy-start.14 = (bf16[384,512]{0,1:T(8,128)(2,1)}, bf16[384,512]{0,1:T(8,128)(2,1)S(1)}, u32[]{:S(2)}) copy-start(bf16[384,512]{0,1:T(8,128)(2,1)S(1)} %get-tuple-element.33) | copy-start | bytes 1179652
  36.8 4.8 %copy-start.16 = (bf16[384,512]{0,1:T(8,128)(2,1)}, bf16[384,512]{0,1:T(8,128)(2,1)S(1)}, u32[]{:S(2)}) copy-start(bf16[384,512]{0,1:T(8,128)(2,1)S(1)} %get-tuple-element.34) | copy-start | bytes 1179652
  36.8 4.7 %copy-start.18 = (bf16[384,512]{0,1:T(8,128)(2,1)}, bf16[384,512]{0,1:T(8,128)(2,1)S(1)}, u32[]{:S(2)}) copy-start(bf16[384,512]{0,1:T(8,128)(2,1)S(1)} %get-tuple-element.35) | copy-start | bytes 1179652
  39.4 2.1 %copy-start.1 = (f32[3,8,128,384]{3,2,1,0:T(8,128)}, f32[3,8,128,384]{3,2,1,0:T(8,128)S(1)}, u32[]{:S(2)}) copy-start(f32[3,8,128,384]{3,2,1,0:T(8,128)S(1)} %get-tuple-element.55) | copy-start | bytes 14155780
  42.8 5.3 %copy-start.7 = (f32[3,128,8,64]{1,3,2,0:T(8,128)}, f32[3,128,8,64]{1,3,2,0:T(8,128)S(1)}, u32[]{:S(2)}) copy-start(f32[3,128,8,64]{1,3,2,0:T(8,128)S(1)} %get-tuple-element.56) | copy-start | bytes 2359300
  42.8 3.7 %collective-permute-start.4 = (f32[2,384]{1,0:T(2,128)S(1)}, f32[2,384]{1,0:T(2,128)S(1)}, u32[]{:S(2)}, u32[]{:S(2)}) collective-permute-start(f32[2,384]{1,0:T(2,128)S(1)} %pad_maximum_fusion.11), channel_id=1, source_target_pairs={{0,16},{16,0},{1,17},{17,1},{2,18},{18,2},{3,19},{19,3},{4,20},{20... | collective-permute-start | bytes 9224 | tf_op jit(solution)/shard_map/ppermute | solution.py:34
  46.5 3.7 %collective-permute-start.5 = (f32[2,384]{1,0:T(2,128)S(1)}, f32[2,384]{1,0:T(2,128)S(1)}, u32[]{:S(2)}, u32[]{:S(2)}) collective-permute-start(f32[2,384]{1,0:T(2,128)S(1)} %fusion.49), channel_id=1, source_target_pairs={{0,1},{1,0},{2,3},{3,2},{4,5},{5,4},{6,7},{7,6},{8,9},{9,8},{10,11... | collective-permute-start | bytes 9224 | tf_op jit(solution)/shard_map/ppermute | solution.py:161
  51.9 2.3 %copy-start.2 = (f32[3,8,128,384]{3,2,1,0:T(8,128)S(1)}, f32[3,8,128,384]{3,2,1,0:T(8,128)}, u32[]{:S(2)}) copy-start(f32[3,8,128,384]{3,2,1,0:T(8,128)} %copy-done.1) | copy-start | bytes 14155780
  51.9 2.4 %copy-start.15 = (bf16[384,512]{0,1:T(8,128)(2,1)S(1)}, bf16[384,512]{0,1:T(8,128)(2,1)}, u32[]{:S(2)}) copy-start(bf16[384,512]{0,1:T(8,128)(2,1)} %copy-done.14) | copy-start | bytes 1179652
  51.9 2.5 %copy-start.17 = (bf16[384,512]{0,1:T(8,128)(2,1)S(1)}, bf16[384,512]{0,1:T(8,128)(2,1)}, u32[]{:S(2)}) copy-start(bf16[384,512]{0,1:T(8,128)(2,1)} %copy-done.16) | copy-start | bytes 1179652
  51.9 2.6 %copy-start.19 = (bf16[384,512]{0,1:T(8,128)(2,1)S(1)}, bf16[384,512]{0,1:T(8,128)(2,1)}, u32[]{:S(2)}) copy-start(bf16[384,512]{0,1:T(8,128)(2,1)} %copy-done.18) | copy-start | bytes 1179652
  54.5 1.9 %copy-start.5 = (bf16[3,128,8,64]{1,0,3,2:T(4,128)(2,1)S(1)}, bf16[3,128,8,64]{1,0,3,2:T(4,128)(2,1)}, u32[]{:S(2)}) copy-start(bf16[3,128,8,64]{1,0,3,2:T(4,128)(2,1)} %copy-done.4) | copy-start | bytes 1179652
  57.9 1.8 %copy-start = (f32[896,1024]{0,1:T(8,128)}, f32[896,1024]{0,1:T(8,128)S(1)}, u32[]{:S(2)}) copy-start(f32[896,1024]{0,1:T(8,128)S(1)} %fusion.16) | copy-start | bytes 11010052
  58.0 1.9 %copy-start.9 = (bf16[384,512]{0,1:T(8,128)(2,1)S(1)}, bf16[384,512]{0,1:T(8,128)(2,1)}, u32[]{:S(2)}) copy-start(bf16[384,512]{0,1:T(8,128)(2,1)} %copy-done.8) | copy-start | bytes 1179652
  58.0 1.9 %copy-start.11 = (bf16[384,512]{0,1:T(8,128)(2,1)S(1)}, bf16[384,512]{0,1:T(8,128)(2,1)}, u32[]{:S(2)}) copy-start(bf16[384,512]{0,1:T(8,128)(2,1)} %copy-done.10) | copy-start | bytes 1179652
  58.0 2.1 %copy-start.13 = (bf16[384,512]{0,1:T(8,128)(2,1)S(1)}, bf16[384,512]{0,1:T(8,128)(2,1)}, u32[]{:S(2)}) copy-start(bf16[384,512]{0,1:T(8,128)(2,1)} %copy-done.12) | copy-start | bytes 1179652
  59.8 4.5 %copy-start.6 = (f32[1,384,512]{1,2,0:T(8,128)S(1)}, f32[1,384,512]{1,2,0:T(8,128)}, u32[]{:S(2)}) copy-start(f32[1,384,512]{1,2,0:T(8,128)} %reshape.296) | copy-start | bytes 2359300
  59.8 4.5 %collective-permute-start.6 = (bf16[256,1024]{0,1:T(8,128)(2,1)S(1)}, bf16[256,1024]{0,1:T(8,128)(2,1)S(1)}, u32[]{:S(2)}, u32[]{:S(2)}) collective-permute-start(bf16[256,1024]{0,1:T(8,128)(2,1)S(1)} %get-tuple-element.22), channel_id=1, source_target_pairs={{0,2},{2,0},{4,6},{6,4},{8,10},{10,8},{12,14},{14,12},{1,3},{3,1},... | collective-permute-start | bytes 1572872 | tf_op jit(solution)/shard_map/ppermute | solution.py:180
  61.9 10.5 %collective-permute-start.8 = (bf16[256,1024]{0,1:T(8,128)(2,1)S(1)}, bf16[256,1024]{0,1:T(8,128)(2,1)S(1)}, u32[]{:S(2)}, u32[]{:S(2)}) collective-permute-start(bf16[256,1024]{0,1:T(8,128)(2,1)S(1)} %get-tuple-element.21), channel_id=1, source_target_pairs={{2,4},{6,8},{10,12},{4,2},{8,6},{12,10},{3,5},{7,9},{11,13},{5,3},... | collective-permute-start | bytes 1572872 | tf_op jit(solution)/shard_map/ppermute | solution.py:181
  65.8 9.1 %collective-permute-start.7 = (bf16[2,128,512]{1,2,0:T(8,128)(2,1)S(1)}, bf16[2,128,512]{1,2,0:T(8,128)(2,1)S(1)}, u32[]{:S(2)}, u32[]{:S(2)}) collective-permute-start(bf16[2,128,512]{1,2,0:T(8,128)(2,1)S(1)} %fusion.36), channel_id=1, source_target_pairs={{0,16},{16,0},{1,17},{17,1},{2,18},{18,2},{3,19},{19,3},{4,20},{20... | collective-permute-start | bytes 786440 | tf_op jit(solution)/shard_map/ppermute | solution.py:34
  76.9 14.0 %collective-permute-start.9 = (bf16[2,256,512]{1,2,0:T(8,128)(2,1)S(1)}, bf16[2,256,512]{1,2,0:T(8,128)(2,1)S(1)}, u32[]{:S(2)}, u32[]{:S(2)}) collective-permute-start(bf16[2,256,512]{1,2,0:T(8,128)(2,1)S(1)} %fusion.25), channel_id=1, source_target_pairs={{0,16},{16,0},{1,17},{17,1},{2,18},{18,2},{3,19},{19,3},{4,20},{20... | collective-permute-start | bytes 1572872 | tf_op jit(solution)/shard_map/ppermute | solution.py:34

commit v17 on v16

--- a/solution.py
+++ b/solution.py
@@ -134,6 +134,7 @@
     first_rows = jnp.where(even, sent[:, :halo], sent[:, rows - halo :])
     rest_rows = jnp.where(even, sent[:, halo:], sent[:, : rows - halo])
     arrived_first = sec_swap(first_rows)
+    rest_rows, arrived_first = lax.optimization_barrier((rest_rows, arrived_first))
     kept_first = jnp.where(even, kept[:, :halo], kept[:, rows - halo :])
     pair_first = jnp.where(is_first, kept_first, arrived_first)
     across = lax.ppermute(jnp.concatenate([pair_first[0], pair_first[1]], axis=1), "seq", between)

time: 93.6 us -> 93.7 us (level)
    ppermute x1, waiting for transfers between devices: 6.32 us -> 0.08 us  [per_device(): lax.ppermute(jnp.concatenate([pair_first[0], pair_first[1]], axis=1), 'se...]
    ppermute x5, waiting for transfers between devices: 32.4 us -> 38.6 us  [sec_swap(): return lax.ppermute(value, 'sec', [(0, 1), (1, 0)])]
    ppermute x5, starting transfers between devices: 3.9 us -> 2.95 us  [sec_swap(): return lax.ppermute(value, 'sec', [(0, 1), (1, 0)])]
where the time goes in v17:
time: 93.7 us; the launch traced here: 93.3 us
  waiting for transfers between devices  45 us (48%)
  local copies, waits for them, and re-layouts  15.4 us (16%)
  other arithmetic  14.9 us (16%)
  starting transfers between devices  9.24 us (10%)
  matrix products  6.16 us (7%)
  between operations  2.58 us (3%)
    ppermute x5, waiting for transfers between devices, sec_swap(): return lax.ppermute(value, 'sec', [(0, 1), (1, 0)])  38.6 us
    ppermute x1, waiting for transfers between devices, per_device(): across = lax.ppermute(jnp.where(even, top, bottom), 'seq', between)  6.06 us
    unnamed x46, local copies, waits for them, and re-layouts  5.41 us
    ppermute x5, starting transfers between devices, sec_swap(): return lax.ppermute(value, 'sec', [(0, 1), (1, 0)])  2.95 us
    ppermute x1, starting transfers between devices, per_device(): across = lax.ppermute(jnp.where(even, top, bottom), 'seq', between)  2.3 us
    ppermute x1, starting transfers between devices, per_device(): lax.ppermute(jnp.concatenate([pair_first[0], pair_first[1]], axis=1), 'se...  1.92 us
  transfers between devices with their start and end apart: 10, of which 8 were waited for; matrix products, arithmetic and copies ran while one was open for 11% of the time, Pallas kernels for 0%

profile of v17, /device:TPU:18, one launch (start us, length us, event | category | flops | bytes accessed | tf_op | source)
XLA Modules:
  0.0 93.3 jit_solution(4189365460405297138)
XLA Ops:
  0.0 1.5 %constant_dynamic-slice_fusion.6 = (bf16[1,2,384,512]{3,2,1,0:T(8,128)(2,1)S(1)}, bf16[1,2,384,512]{3,2,1,0:T(8,128)(2,1)S(1)}) fusion(bf16[1,2,384,1024]{3,2,1,0:T(8,128)(2,1)} %param.2, s32[]{:T(128)S(6)} %select_n.199, s32[]{:T(128)S(6)} %select_n.194), kind=kLoop, calls=%fused_computation.108 | loop fusion | bytes 3145736 | tf_op jit(solution)/shard_map/dynamic_slice | solution.py:133
  1.5 0.4 copy.20
  1.9 0.9 slice_select_fusion.2
  2.7 0.5 collective-permute-start
  3.3 0.4 copy.21
  4.2 12.4 %collective-permute-done = bf16[2,256,512]{1,2,0:T(8,128)(2,1)S(1)} collective-permute-done((bf16[2,256,512]{1,2,0:T(8,128)(2,1)}, bf16[2,256,512]{1,2,0:T(8,128)(2,1)S(1)}, u32[]{:S(2)}, u32[]{:S(2)}) %collective-permute-start) | collective-permute-done | bytes 524320 | tf_op jit(solution)/shard_map/ppermute | solution.py:34
  16.8 1.9 %collective-permute-start.2 = (bf16[256,1024]{0,1:T(8,128)(2,1)S(1)}, bf16[256,1024]{0,1:T(8,128)(2,1)}, u32[]{:S(2)}, u32[]{:S(2)}) collective-permute-start(bf16[256,1024]{0,1:T(8,128)(2,1)S(1)} %pad_maximum_fusion.6), channel_id=1, source_target_pairs={{2,4},{6,8},{10,12},{4,2},{8,6},{12,10},{3,5},{7,9},{11,13},{5,3},... | collective-permute-start | bytes 1572872 | tf_op jit(solution)/shard_map/ppermute | solution.py:140
  18.8 0.6 collective-permute-start.1
  19.7 7.6 %collective-permute-done.1 = bf16[2,128,512]{1,2,0:T(8,128)(2,1)S(1)} collective-permute-done((bf16[2,128,512]{1,2,0:T(8,128)(2,1)S(1)}, bf16[2,128,512]{1,2,0:T(8,128)(2,1)S(1)}, u32[]{:S(2)}, u32[]{:S(2)}) %collective-permute-start.1) | collective-permute-done | bytes 262176 | tf_op jit(solution)/shard_map/ppermute | solution.py:34
  27.4 0.4 broadcast_select_fusion.1
  27.9 0.9 %fusion.22 = bf16[256,1024]{0,1:T(8,128)(2,1)} fusion(bf16[384,512]{0,1:T(8,128)(2,1)S(1)} %get-tuple-element.48, bf16[384,512]{0,1:T(8,128)(2,1)S(1)} %get-tuple-element.47, pred[]{:T(512)S(6)} %eq.19), kind=kLoop, calls=%fused_computation.60 | loop fusion | flops 2359296 | bytes 1310721 | tf_op jit(solution)/shard_map/jit(_where)/select_n | solution.py:152
  28.8 0.4 collective-permute-start.3
  29.2 0.7 fusion.51
  31.9 0.8 slice_convert_fusion
  32.8 0.3 reshape.297
  33.1 1.6 %reshape_squeeze.3 = bf16[3,128,8,64]{1,0,3,2:T(4,128)(2,1)S(1)} reshape(bf16[1,384,512]{1,2,0:T(8,128)(2,1)} %get-tuple-element.46) | data formatting | bytes 786432 | tf_op jit(solution)/shard_map/reshape;squeeze | solution.py:69
  34.7 1.5 %broadcast_select_fusion.7 = (bf16[256,1024]{0,1:T(8,128)(2,1)S(1)}, bf16[256,1024]{0,1:T(8,128)(2,1)S(1)}) fusion(bf16[256,1024]{0,1:T(8,128)(2,1)} %collective-permute-done.2, bf16[256,1024]{0,1:T(8,128)(2,1)} %collective-permute-done.3, pred[]{:T(512)S(6)} %eq.19), kind=kLoop, calls=%fused_computation.79 | loop fusion | flops 524288 | bytes 2097153 | tf_op jit(solution)/shard_map/jit(_where)/select_n | solution.py:153
  36.9 0.8 fusion.30
  37.7 1.7 %fusion.52 = (f32[3,8,128]{2,1,0:T(8,128)S(1)}, f32[3,8,128,384]{3,2,1,0:T(8,128)S(1)}) fusion(f32[3,8,128,384]{3,2,1,0:T(8,128)S(1)} %fusion.30, pred[3,384]{1,0:T(4,128)(4,1)S(1)} %bitcast.131), kind=kOutput, calls=%fused_computation.138 | output fusion | flops 7078271 | bytes 9450624 | tf_op jit(solution)/shard_map/sub | solution.py:78
  39.5 0.6 fusion.5
  40.1 1.5 %copy-done.1 = f32[3,8,128,384]{3,2,1,0:T(8,128)} copy-done((f32[3,8,128,384]{3,2,1,0:T(8,128)}, f32[3,8,128,384]{3,2,1,0:T(8,128)S(1)}, u32[]{:S(2)}) %copy-start.1) | copy-done | bytes 4718616
  41.6 1.2 %multiply_reduce_fusion.2 = (f32[3,128]{1,0:T(4,128)S(1)}, f32[3,128]{1,0:T(4,128)S(1)}, f32[3,128,8,64]{1,3,2,0:T(8,128)S(1)}) fusion(f32[3,128,8,64]{1,0,3,2:T(4,128)S(1)} %reshape.297, bf16[3,8,128,384]{3,2,1,0:T(8,128)(2,1)S(1)} %fusion.5, bf16[1,384,8,64]{1,3,2,0:T(8,128)(2,1)S(1)} %bitcast.116, bf16[1,384,8,64]{1,3,2,0:T(8,128)(2,1)S(1)} %bitcast.118, ...), kind=kOutput, calls=%fused_computation.56 | convolution fusion | flops 152960256 | bytes 5114880 | tf_op jit(solution)/shard_map/jhqk,jkhd->jqhd/dot_general | solution.py:81
  42.9 0.6 collective-permute-start.4
  43.5 3.1 %collective-permute-done.4 = f32[2,384]{1,0:T(2,128)S(1)} collective-permute-done((f32[2,384]{1,0:T(2,128)S(1)}, f32[2,384]{1,0:T(2,128)S(1)}, u32[]{:S(2)}, u32[]{:S(2)}) %collective-permute-start.4) | collective-permute-done | bytes 3104 | tf_op jit(solution)/shard_map/ppermute | solution.py:34
  46.6 1.6 %collective-permute-start.5 = (f32[2,384]{1,0:T(2,128)S(1)}, f32[2,384]{1,0:T(2,128)S(1)}, u32[]{:S(2)}, u32[]{:S(2)}) collective-permute-start(f32[2,384]{1,0:T(2,128)S(1)} %fusion.49), channel_id=1, source_target_pairs={{0,1},{1,0},{2,3},{3,2},{4,5},{5,4},{6,7},{7,6},{8,9},{9,8},{10,11... | collective-permute-start | bytes 9224 | tf_op jit(solution)/shard_map/ppermute | solution.py:162
  48.1 0.5 copy.27
  48.7 1.3 %reshape.296 = f32[1,384,512]{1,2,0:T(8,128)} reshape(f32[3,128,8,64]{1,0,3,2:T(4,128)S(1)} %copy.27) | data formatting | bytes 1572864 | tf_op jit(solution)/shard_map/reshape | solution.py:82
  50.3 1.7 %multiply_reduce_fusion = (f32[3,128,8]{1,2,0:T(8,128)S(1)}, bf16[3,128,8,64]{1,3,2,0:T(8,128)(2,1)S(1)}) fusion(f32[3,128,8,64]{1,3,2,0:T(8,128)} %copy-done.7, f32[3,128]{1,0:T(4,128)S(1)} %bitcast.128, f32[3,128]{1,0:T(4,128)S(1)} %bitcast.126, f32[3,128,8,64]{1,0,3,2:T(4,128)} %copy-done.3), kind=kLoop, calls=%fused_computation.53 | loop fusion | flops 1569792 | bytes 1981440 | tf_op jit(solution)/shard_map/reduce_sum | solution.py:93
  52.0 0.6 fusion.53
  52.5 1.7 %copy-done.2 = f32[3,8,128,384]{3,2,1,0:T(8,128)S(1)} copy-done((f32[3,8,128,384]{3,2,1,0:T(8,128)S(1)}, f32[3,8,128,384]{3,2,1,0:T(8,128)}, u32[]{:S(2)}) %copy-start.2) | copy-done | bytes 4718616
  54.6 1.9 %multiply_convert_fusion = bf16[3,8,128,384]{3,2,1,0:T(8,128)(2,1)S(1)} fusion(f32[3,8,128]{2,1,0:T(8,128)S(1)} %bitcast.127, bf16[3,128,8,64]{1,3,2,0:T(8,128)(2,1)S(1)} %get-tuple-element.24, f32[3,8,128,384]{3,2,1,0:T(8,128)S(1)} %copy-done.2, f32[3,8,128]{2,1,0:T(8,128)S(1)} %get-tuple-element.58, bf16[1,384,8,64]{1,3,2,0:T(8,128)(2,1)S(1)} %bitcast.117, ...), kind=kOutput, calls=%fused_computation.5 | convolution fusion | flops 158072832 | bytes 8675328 | tf_op jit(solution)/shard_map/jqhd,jkhd->jhqk/dot_general | solution.py:95
  56.5 0.6 fusion.32
  57.4 0.3 fusion.9
  57.7 0.3 fusion.16
  58.3 1.5 %copy-done = f32[896,1024]{0,1:T(8,128)} copy-done((f32[896,1024]{0,1:T(8,128)}, f32[896,1024]{0,1:T(8,128)S(1)}, u32[]{:S(2)}) %copy-start) | copy-done | bytes 3670040
  60.1 1.1 %fusion.17 = bf16[3,128,8,64]{1,3,2,0:T(8,128)(2,1)S(1)} fusion(bf16[3,8,128,384]{3,2,1,0:T(8,128)(2,1)S(1)} %multiply_convert_fusion, bf16[1,384,8,64]{1,3,2,0:T(8,128)(2,1)S(1)} %bitcast.111, bf16[1,384,8,64]{1,3,2,0:T(8,128)(2,1)S(1)} %bitcast.113, bf16[1,384,8,64]{1,3,2,0:T(8,128)(2,1)S(1)} %bitcast.109), kind=kOutput, calls=%fused_computation.31 | convolution fusion | flops 152371200 | bytes 3932160 | tf_op jit(solution)/shard_map/jhqk,jkhd->jqhd/dot_general | solution.py:97
  61.3 0.3 copy.26
  61.6 0.3 convert_element_type.85
  62.0 2.3 %collective-permute-start.8 = (bf16[256,1024]{0,1:T(8,128)(2,1)S(1)}, bf16[256,1024]{0,1:T(8,128)(2,1)S(1)}, u32[]{:S(2)}, u32[]{:S(2)}) collective-permute-start(bf16[256,1024]{0,1:T(8,128)(2,1)S(1)} %get-tuple-element.25), channel_id=1, source_target_pairs={{2,4},{6,8},{10,12},{4,2},{8,6},{12,10},{3,5},{7,9},{11,13},{5,3},... | collective-permute-start | bytes 1572872 | tf_op jit(solution)/shard_map/ppermute | solution.py:182
  64.4 1.3 %fusion.28 = bf16[128,1024]{0,1:T(8,128)(2,1)S(1)} fusion(f32[896,1024]{0,1:T(8,128)} %copy-done, bf16[256,1024]{0,1:T(8,128)(2,1)S(1)} %collective-permute-done.6, pred[]{:T(512)S(6)} %eq.19), kind=kLoop, calls=%fused_computation.67 | loop fusion | flops 786432 | bytes 1835009 | tf_op jit(solution)/shard_map/convert_element_type | solution.py:187
  65.8 0.6 collective-permute-start.7
  66.4 6.1 %collective-permute-done.8 = bf16[256,1024]{0,1:T(8,128)(2,1)S(1)} collective-permute-done((bf16[256,1024]{0,1:T(8,128)(2,1)S(1)}, bf16[256,1024]{0,1:T(8,128)(2,1)S(1)}, u32[]{:S(2)}, u32[]{:S(2)}) %collective-permute-start.8) | collective-permute-done | bytes 524320 | tf_op jit(solution)/shard_map/ppermute | solution.py:182
  72.5 2.5 %collective-permute-done.7 = bf16[2,128,512]{1,2,0:T(8,128)(2,1)S(1)} collective-permute-done((bf16[2,128,512]{1,2,0:T(8,128)(2,1)S(1)}, bf16[2,128,512]{1,2,0:T(8,128)(2,1)S(1)}, u32[]{:S(2)}, u32[]{:S(2)}) %collective-permute-start.7) | collective-permute-done | bytes 262176 | tf_op jit(solution)/shard_map/ppermute | solution.py:34
  75.1 1.6 %fusion.13 = bf16[384,1024]{0,1:T(8,128)(2,1)S(1)} fusion(f32[896,1024]{0,1:T(8,128)} %copy-done, bf16[256,1024]{0,1:T(8,128)(2,1)S(1)} %get-tuple-element.34, bf16[256,1024]{0,1:T(8,128)(2,1)S(1)} %get-tuple-element.33), kind=kLoop, calls=%fused_computation.23 | loop fusion | flops 1966080 | bytes 3407872 | tf_op jit(solution)/shard_map/add | solution.py:196
  77.1 0.6 collective-permute-start.9
  78.0 13.1 %collective-permute-done.9 = bf16[2,256,512]{1,2,0:T(8,128)(2,1)S(1)} collective-permute-done((bf16[2,256,512]{1,2,0:T(8,128)(2,1)S(1)}, bf16[2,256,512]{1,2,0:T(8,128)(2,1)S(1)}, u32[]{:S(2)}, u32[]{:S(2)}) %collective-permute-start.9) | collective-permute-done | bytes 524320 | tf_op jit(solution)/shard_map/ppermute | solution.py:34
  91.2 0.4 maximum_select_fusion
  91.7 1.6 %copy.28 = bf16[1,2,384,1024]{3,2,1,0:T(8,128)(2,1)} copy(bf16[1,2,384,1024]{2,3,1,0:T(8,128)(2,1)S(1)} %maximum_select_fusion) | data formatting | bytes 3145728 | tf_op jit(solution)/shard_map/jit(_where)/select_n | solution.py:212
  (85 shorter events, 4.4 us)
Async XLA Ops:
  1.5 2.2 %copy-start.20 = (s32[12]{0:T(128)S(1)}, s32[12]{0:T(128)}, u32[]{:S(2)}) copy-start(s32[12]{0:T(128)} %param.3) | copy-start | bytes 148
  2.7 13.9 %collective-permute-start = (bf16[2,256,512]{1,2,0:T(8,128)(2,1)}, bf16[2,256,512]{1,2,0:T(8,128)(2,1)S(1)}, u32[]{:S(2)}, u32[]{:S(2)}) collective-permute-start(bf16[2,256,512]{1,2,0:T(8,128)(2,1)} %slice_select_fusion.2), channel_id=1, source_target_pairs={{0,16},{16,0},{1,17},{17,1},{2,18},{18,2},{3,19},{19,3},{4,20},{20... | collective-permute-start | bytes 1572872 | tf_op jit(solution)/shard_map/ppermute | solution.py:34
  16.8 10.6 %collective-permute-start.2 = (bf16[256,1024]{0,1:T(8,128)(2,1)S(1)}, bf16[256,1024]{0,1:T(8,128)(2,1)}, u32[]{:S(2)}, u32[]{:S(2)}) collective-permute-start(bf16[256,1024]{0,1:T(8,128)(2,1)S(1)} %pad_maximum_fusion.6), channel_id=1, source_target_pairs={{2,4},{6,8},{10,12},{4,2},{8,6},{12,10},{3,5},{7,9},{11,13},{5,3},... | collective-permute-start | bytes 1572872 | tf_op jit(solution)/shard_map/ppermute | solution.py:140
  18.8 8.6 %collective-permute-start.1 = (bf16[2,128,512]{1,2,0:T(8,128)(2,1)S(1)}, bf16[2,128,512]{1,2,0:T(8,128)(2,1)S(1)}, u32[]{:S(2)}, u32[]{:S(2)}) collective-permute-start(bf16[2,128,512]{1,2,0:T(8,128)(2,1)S(1)} %slice_select_fusion.3), channel_id=1, source_target_pairs={{0,16},{16,0},{1,17},{17,1},{2,18},{18,2},{3,19},{19,3},{4,20},{20... | collective-permute-start | bytes 786440 | tf_op jit(solution)/shard_map/ppermute | solution.py:34
  28.8 5.9 %collective-permute-start.3 = (bf16[256,1024]{0,1:T(8,128)(2,1)}, bf16[256,1024]{0,1:T(8,128)(2,1)}, u32[]{:S(2)}, u32[]{:S(2)}) collective-permute-start(bf16[256,1024]{0,1:T(8,128)(2,1)} %fusion.22), channel_id=1, source_target_pairs={{0,2},{2,0},{4,6},{6,4},{8,10},{10,8},{12,14},{14,12},{1,3},{3,1},... | collective-permute-start | bytes 1572872 | tf_op jit(solution)/shard_map/ppermute | solution.py:152
  33.1 8.5 %copy-start.3 = (f32[3,128,8,64]{1,0,3,2:T(4,128)}, f32[3,128,8,64]{1,0,3,2:T(4,128)S(1)}, u32[]{:S(2)}) copy-start(f32[3,128,8,64]{1,0,3,2:T(4,128)S(1)} %reshape.297) | copy-start | bytes 2359300
  34.7 2.2 %copy-start.4 = (bf16[3,128,8,64]{1,0,3,2:T(4,128)(2,1)}, bf16[3,128,8,64]{1,0,3,2:T(4,128)(2,1)S(1)}, u32[]{:S(2)}) copy-start(bf16[3,128,8,64]{1,0,3,2:T(4,128)(2,1)S(1)} %reshape_squeeze.3) | copy-start | bytes 1179652
  36.7 1.0 %copy-start.8 = (bf16[384,512]{0,1:T(8,128)(2,1)}, bf16[384,512]{0,1:T(8,128)(2,1)S(1)}, u32[]{:S(2)}) copy-start(bf16[384,512]{0,1:T(8,128)(2,1)S(1)} %get-tuple-element.40) | copy-start | bytes 1179652
  36.7 1.0 %copy-start.10 = (bf16[384,512]{0,1:T(8,128)(2,1)}, bf16[384,512]{0,1:T(8,128)(2,1)S(1)}, u32[]{:S(2)}) copy-start(bf16[384,512]{0,1:T(8,128)(2,1)S(1)} %get-tuple-element.41) | copy-start | bytes 1179652
  36.7 1.0 %copy-start.12 = (bf16[384,512]{0,1:T(8,128)(2,1)}, bf16[384,512]{0,1:T(8,128)(2,1)S(1)}, u32[]{:S(2)}) copy-start(bf16[384,512]{0,1:T(8,128)(2,1)S(1)} %get-tuple-element.42) | copy-start | bytes 1179652
  36.9 4.8 %copy-start.14 = (bf16[384,512]{0,1:T(8,128)(2,1)}, bf16[384,512]{0,1:T(8,128)(2,1)S(1)}, u32[]{:S(2)}) copy-start(bf16[384,512]{0,1:T(8,128)(2,1)S(1)} %get-tuple-element.37) | copy-start | bytes 1179652
  36.9 4.8 %copy-start.16 = (bf16[384,512]{0,1:T(8,128)(2,1)}, bf16[384,512]{0,1:T(8,128)(2,1)S(1)}, u32[]{:S(2)}) copy-start(bf16[384,512]{0,1:T(8,128)(2,1)S(1)} %get-tuple-element.38) | copy-start | bytes 1179652
  36.9 4.7 %copy-start.18 = (bf16[384,512]{0,1:T(8,128)(2,1)}, bf16[384,512]{0,1:T(8,128)(2,1)S(1)}, u32[]{:S(2)}) copy-start(bf16[384,512]{0,1:T(8,128)(2,1)S(1)} %get-tuple-element.39) | copy-start | bytes 1179652
  39.5 2.1 %copy-start.1 = (f32[3,8,128,384]{3,2,1,0:T(8,128)}, f32[3,8,128,384]{3,2,1,0:T(8,128)S(1)}, u32[]{:S(2)}) copy-start(f32[3,8,128,384]{3,2,1,0:T(8,128)S(1)} %get-tuple-element.59) | copy-start | bytes 14155780
  42.8 5.3 %copy-start.7 = (f32[3,128,8,64]{1,3,2,0:T(8,128)}, f32[3,128,8,64]{1,3,2,0:T(8,128)S(1)}, u32[]{:S(2)}) copy-start(f32[3,128,8,64]{1,3,2,0:T(8,128)S(1)} %get-tuple-element.60) | copy-start | bytes 2359300
  42.9 3.7 %collective-permute-start.4 = (f32[2,384]{1,0:T(2,128)S(1)}, f32[2,384]{1,0:T(2,128)S(1)}, u32[]{:S(2)}, u32[]{:S(2)}) collective-permute-start(f32[2,384]{1,0:T(2,128)S(1)} %pad_maximum_fusion.11), channel_id=1, source_target_pairs={{0,16},{16,0},{1,17},{17,1},{2,18},{18,2},{3,19},{19,3},{4,20},{20... | collective-permute-start | bytes 9224 | tf_op jit(solution)/shard_map/ppermute | solution.py:34
  46.6 3.7 %collective-permute-start.5 = (f32[2,384]{1,0:T(2,128)S(1)}, f32[2,384]{1,0:T(2,128)S(1)}, u32[]{:S(2)}, u32[]{:S(2)}) collective-permute-start(f32[2,384]{1,0:T(2,128)S(1)} %fusion.49), channel_id=1, source_target_pairs={{0,1},{1,0},{2,3},{3,2},{4,5},{5,4},{6,7},{7,6},{8,9},{9,8},{10,11... | collective-permute-start | bytes 9224 | tf_op jit(solution)/shard_map/ppermute | solution.py:162
  52.0 2.3 %copy-start.2 = (f32[3,8,128,384]{3,2,1,0:T(8,128)S(1)}, f32[3,8,128,384]{3,2,1,0:T(8,128)}, u32[]{:S(2)}) copy-start(f32[3,8,128,384]{3,2,1,0:T(8,128)} %copy-done.1) | copy-start | bytes 14155780
  52.0 2.4 %copy-start.15 = (bf16[384,512]{0,1:T(8,128)(2,1)S(1)}, bf16[384,512]{0,1:T(8,128)(2,1)}, u32[]{:S(2)}) copy-start(bf16[384,512]{0,1:T(8,128)(2,1)} %copy-done.14) | copy-start | bytes 1179652
  52.0 2.5 %copy-start.17 = (bf16[384,512]{0,1:T(8,128)(2,1)S(1)}, bf16[384,512]{0,1:T(8,128)(2,1)}, u32[]{:S(2)}) copy-start(bf16[384,512]{0,1:T(8,128)(2,1)} %copy-done.16) | copy-start | bytes 1179652
  52.0 2.6 %copy-start.19 = (bf16[384,512]{0,1:T(8,128)(2,1)S(1)}, bf16[384,512]{0,1:T(8,128)(2,1)}, u32[]{:S(2)}) copy-start(bf16[384,512]{0,1:T(8,128)(2,1)} %copy-done.18) | copy-start | bytes 1179652
  54.6 1.9 %copy-start.5 = (bf16[3,128,8,64]{1,0,3,2:T(4,128)(2,1)S(1)}, bf16[3,128,8,64]{1,0,3,2:T(4,128)(2,1)}, u32[]{:S(2)}) copy-start(bf16[3,128,8,64]{1,0,3,2:T(4,128)(2,1)} %copy-done.4) | copy-start | bytes 1179652
  58.0 1.8 %copy-start = (f32[896,1024]{0,1:T(8,128)}, f32[896,1024]{0,1:T(8,128)S(1)}, u32[]{:S(2)}) copy-start(f32[896,1024]{0,1:T(8,128)S(1)} %fusion.16) | copy-start | bytes 11010052
  58.0 1.9 %copy-start.9 = (bf16[384,512]{0,1:T(8,128)(2,1)S(1)}, bf16[384,512]{0,1:T(8,128)(2,1)}, u32[]{:S(2)}) copy-start(bf16[384,512]{0,1:T(8,128)(2,1)} %copy-done.8) | copy-start | bytes 1179652
  58.0 1.9 %copy-start.11 = (bf16[384,512]{0,1:T(8,128)(2,1)S(1)}, bf16[384,512]{0,1:T(8,128)(2,1)}, u32[]{:S(2)}) copy-start(bf16[384,512]{0,1:T(8,128)(2,1)} %copy-done.10) | copy-start | bytes 1179652
  58.1 2.1 %copy-start.13 = (bf16[384,512]{0,1:T(8,128)(2,1)S(1)}, bf16[384,512]{0,1:T(8,128)(2,1)}, u32[]{:S(2)}) copy-start(bf16[384,512]{0,1:T(8,128)(2,1)} %copy-done.12) | copy-start | bytes 1179652
  59.9 4.4 %copy-start.6 = (f32[1,384,512]{1,2,0:T(8,128)S(1)}, f32[1,384,512]{1,2,0:T(8,128)}, u32[]{:S(2)}) copy-start(f32[1,384,512]{1,2,0:T(8,128)} %reshape.296) | copy-start | bytes 2359300
  59.9 4.5 %collective-permute-start.6 = (bf16[256,1024]{0,1:T(8,128)(2,1)S(1)}, bf16[256,1024]{0,1:T(8,128)(2,1)S(1)}, u32[]{:S(2)}, u32[]{:S(2)}) collective-permute-start(bf16[256,1024]{0,1:T(8,128)(2,1)S(1)} %get-tuple-element.26), channel_id=1, source_target_pairs={{0,2},{2,0},{4,6},{6,4},{8,10},{10,8},{12,14},{14,12},{1,3},{3,1},... | collective-permute-start | bytes 1572872 | tf_op jit(solution)/shard_map/ppermute | solution.py:181
  62.0 10.5 %collective-permute-start.8 = (bf16[256,1024]{0,1:T(8,128)(2,1)S(1)}, bf16[256,1024]{0,1:T(8,128)(2,1)S(1)}, u32[]{:S(2)}, u32[]{:S(2)}) collective-permute-start(bf16[256,1024]{0,1:T(8,128)(2,1)S(1)} %get-tuple-element.25), channel_id=1, source_target_pairs={{2,4},{6,8},{10,12},{4,2},{8,6},{12,10},{3,5},{7,9},{11,13},{5,3},... | collective-permute-start | bytes 1572872 | tf_op jit(solution)/shard_map/ppermute | solution.py:182
  65.8 9.2 %collective-permute-start.7 = (bf16[2,128,512]{1,2,0:T(8,128)(2,1)S(1)}, bf16[2,128,512]{1,2,0:T(8,128)(2,1)S(1)}, u32[]{:S(2)}, u32[]{:S(2)}) collective-permute-start(bf16[2,128,512]{1,2,0:T(8,128)(2,1)S(1)} %fusion.36), channel_id=1, source_target_pairs={{0,16},{16,0},{1,17},{17,1},{2,18},{18,2},{3,19},{19,3},{4,20},{20... | collective-permute-start | bytes 786440 | tf_op jit(solution)/shard_map/ppermute | solution.py:34
  77.1 13.9 %collective-permute-start.9 = (bf16[2,256,512]{1,2,0:T(8,128)(2,1)S(1)}, bf16[2,256,512]{1,2,0:T(8,128)(2,1)S(1)}, u32[]{:S(2)}, u32[]{:S(2)}) collective-permute-start(bf16[2,256,512]{1,2,0:T(8,128)(2,1)S(1)} %fusion.25), channel_id=1, source_target_pairs={{0,16},{16,0},{1,17},{17,1},{2,18},{18,2},{3,19},{19,3},{4,20},{20... | collective-permute-start | bytes 1572872 | tf_op jit(solution)/shard_map/ppermute | solution.py:34

commit v18 on v15

--- a/solution.py
+++ b/solution.py
@@ -123,10 +123,10 @@
     halo = halo_units * UNIT
     total_cols = cols * lax.axis_size("mp")
 
-    keep_offset = section * half
-    send_offset = (1 - section) * half
-    sent = lax.dynamic_slice_in_dim(local_heads, send_offset, half, 2)
-    kept = lax.dynamic_slice_in_dim(local_heads, keep_offset, half, 2)
+    first_half = local_heads[:, :, :half]
+    second_half = local_heads[:, :, half:]
+    sent = jnp.where(is_first, second_half, first_half)
+    kept = jnp.where(is_first, first_half, second_half)
     arrived = sec_swap(sent)
     key_value = jnp.where(is_first, kept, arrived)
     query_cot = jnp.where(is_first, arrived, kept)

time: 92 us -> 92.2 us (level)
    dynamic_slice x3 -> x0, local copies, waits for them, and re-layouts: 2.18 us -> none  [the longest x2 1.83 us: per_device(): kept = lax.dynamic_slice_in_dim(local_heads, keep_offset, half, 2)]
    unnamed x46 -> x47, local copies, waits for them, and re-layouts: 5.41 us -> 7.3 us
where the time goes in v18:
time: 92.2 us; the launch traced here: 91.8 us
  waiting for transfers between devices  44.2 us (48%)
  local copies, waits for them, and re-layouts  15.1 us (16%)
  other arithmetic  13.8 us (15%)
  starting transfers between devices  10 us (11%)
  matrix products  6.18 us (7%)
  between operations  2.57 us (3%)
    ppermute x4, waiting for transfers between devices, sec_swap(): return lax.ppermute(value, 'sec', [(0, 1), (1, 0)])  36.3 us
    unnamed x47, local copies, waits for them, and re-layouts  7.3 us
    ppermute x1, waiting for transfers between devices, per_device(): across = lax.ppermute(jnp.where(even, top, bottom), 'seq', between)  6.07 us
    ppermute x4, starting transfers between devices, sec_swap(): return lax.ppermute(value, 'sec', [(0, 1), (1, 0)])  2.42 us
    ppermute x1, starting transfers between devices, per_device(): across = lax.ppermute(jnp.where(even, top, bottom), 'seq', between)  2.3 us
    ppermute x1, starting transfers between devices, halo_swap(): across = lax.ppermute(jnp.where(even, top, bottom), 'seq', between)  1.91 us
    dot_general x1, matrix products, attention_grads(): jnp.einsum('jqhd,jkhd->jhqk', up4, values_w, preferred_element_type=jnp.f...  1.86 us
  transfers between devices with their start and end apart: 9, of which 7 were waited for; matrix products, arithmetic and copies ran while one was open for 11% of the time, Pallas kernels for 0%

profile of v18, /device:TPU:18, one launch (start us, length us, event | category | flops | bytes accessed | tf_op | source)
XLA Modules:
  0.0 91.8 jit_solution(9030790937490298310)
XLA Ops:
  0.0 1.9 %copy.19 = bf16[1,2,384,1024]{2,3,1,0:T(8,128)(2,1)S(1)} copy(bf16[1,2,384,1024]{3,2,1,0:T(8,128)(2,1)} %param.2) | data formatting | bytes 3145728 | tf_op args[0]
  2.0 0.6 collective-permute-start
  3.5 17.9 %collective-permute-done = bf16[2,384,512]{1,2,0:T(8,128)(2,1)S(1)} collective-permute-done((bf16[2,384,512]{1,2,0:T(8,128)(2,1)S(1)}, bf16[2,384,512]{1,2,0:T(8,128)(2,1)S(1)}, u32[]{:S(2)}, u32[]{:S(2)}) %collective-permute-start) | collective-permute-done | bytes 786464 | tf_op jit(solution)/shard_map/ppermute | solution.py:34
  21.6 1.2 %broadcast_select_fusion.11 = (bf16[256,1024]{0,1:T(8,128)(2,1)}, bf16[256,1024]{0,1:T(8,128)(2,1)}) fusion(pred[]{:T(512)S(6)} %eq.21, bf16[384,512]{0,1:T(8,128)(2,1)S(1)} %get-tuple-element.40, bf16[384,512]{0,1:T(8,128)(2,1)S(1)} %get-tuple-element.39), kind=kLoop, calls=%fused_computation.77 | loop fusion | flops 3670016 | bytes 1835009 | tf_op jit(solution)/shard_map/jit(_where)/select_n | solution.py:27
  22.8 1.9 %collective-permute-start.1 = (bf16[256,1024]{0,1:T(8,128)(2,1)}, bf16[256,1024]{0,1:T(8,128)(2,1)}, u32[]{:S(2)}, u32[]{:S(2)}) collective-permute-start(bf16[256,1024]{0,1:T(8,128)(2,1)} %get-tuple-element.37), channel_id=1, source_target_pairs={{2,4},{6,8},{10,12},{4,2},{8,6},{12,10},{3,5},{7,9},{11,13},{5,3},... | collective-permute-start | bytes 1572872 | tf_op jit(solution)/shard_map/ppermute | solution.py:27
  24.7 1.7 %collective-permute-start.2 = (bf16[256,1024]{0,1:T(8,128)(2,1)}, bf16[256,1024]{0,1:T(8,128)(2,1)}, u32[]{:S(2)}, u32[]{:S(2)}) collective-permute-start(bf16[256,1024]{0,1:T(8,128)(2,1)} %get-tuple-element.38), channel_id=1, source_target_pairs={{0,2},{2,0},{4,6},{6,4},{8,10},{10,8},{12,14},{14,12},{1,3},{3,1},... | collective-permute-start | bytes 1572872 | tf_op jit(solution)/shard_map/ppermute | solution.py:26
  26.5 0.7 fusion.49
  29.2 0.8 slice_convert_fusion
  30.1 0.3 reshape.295
  30.4 1.6 %reshape_squeeze.3 = bf16[3,128,8,64]{1,0,3,2:T(4,128)(2,1)S(1)} reshape(bf16[1,384,512]{1,2,0:T(8,128)(2,1)} %get-tuple-element.36) | data formatting | bytes 786432 | tf_op jit(solution)/shard_map/reshape;squeeze | solution.py:69
  32.0 1.6 %collective-permute-done.1 = bf16[256,1024]{0,1:T(8,128)(2,1)} collective-permute-done((bf16[256,1024]{0,1:T(8,128)(2,1)}, bf16[256,1024]{0,1:T(8,128)(2,1)}, u32[]{:S(2)}, u32[]{:S(2)}) %collective-permute-start.1) | collective-permute-done | bytes 524320 | tf_op jit(solution)/shard_map/ppermute | solution.py:27
  33.6 1.3 %broadcast_select_fusion.9 = (bf16[256,1024]{0,1:T(8,128)(2,1)S(1)}, bf16[256,1024]{0,1:T(8,128)(2,1)S(1)}) fusion(bf16[256,1024]{0,1:T(8,128)(2,1)} %collective-permute-done.1, bf16[256,1024]{0,1:T(8,128)(2,1)} %collective-permute-done.2, pred[]{:T(512)S(6)} %eq.21), kind=kLoop, calls=%fused_computation.75 | loop fusion | flops 524288 | bytes 2097153 | tf_op jit(solution)/shard_map/jit(_where)/select_n | solution.py:28
  35.6 0.8 fusion.28
  36.4 1.7 %fusion.50 = (f32[3,8,128]{2,1,0:T(8,128)S(1)}, f32[3,8,128,384]{3,2,1,0:T(8,128)S(1)}) fusion(f32[3,8,128,384]{3,2,1,0:T(8,128)S(1)} %fusion.28, pred[3,384]{1,0:T(4,128)(4,1)S(1)} %bitcast.123), kind=kOutput, calls=%fused_computation.131 | output fusion | flops 7078271 | bytes 9450624 | tf_op jit(solution)/shard_map/sub | solution.py:78
  38.2 0.6 fusion.5
  38.8 1.5 %copy-done.1 = f32[3,8,128,384]{3,2,1,0:T(8,128)} copy-done((f32[3,8,128,384]{3,2,1,0:T(8,128)}, f32[3,8,128,384]{3,2,1,0:T(8,128)S(1)}, u32[]{:S(2)}) %copy-start.1) | copy-done | bytes 4718616
  40.3 1.2 %multiply_reduce_fusion.2 = (f32[3,128]{1,0:T(4,128)S(1)}, f32[3,128]{1,0:T(4,128)S(1)}, f32[3,128,8,64]{1,3,2,0:T(8,128)S(1)}) fusion(f32[3,128,8,64]{1,0,3,2:T(4,128)S(1)} %reshape.295, bf16[3,8,128,384]{3,2,1,0:T(8,128)(2,1)S(1)} %fusion.5, bf16[1,384,8,64]{1,3,2,0:T(8,128)(2,1)S(1)} %bitcast.108, bf16[1,384,8,64]{1,3,2,0:T(8,128)(2,1)S(1)} %bitcast.110, ...), kind=kOutput, calls=%fused_computation.55 | convolution fusion | flops 152960256 | bytes 5114880 | tf_op jit(solution)/shard_map/jhqk,jkhd->jqhd/dot_general | solution.py:81
  41.6 0.6 collective-permute-start.3
  42.2 3.1 %collective-permute-done.3 = f32[2,384]{1,0:T(2,128)S(1)} collective-permute-done((f32[2,384]{1,0:T(2,128)S(1)}, f32[2,384]{1,0:T(2,128)S(1)}, u32[]{:S(2)}, u32[]{:S(2)}) %collective-permute-start.3) | collective-permute-done | bytes 3104 | tf_op jit(solution)/shard_map/ppermute | solution.py:34
  45.2 1.6 %collective-permute-start.4 = (f32[2,384]{1,0:T(2,128)S(1)}, f32[2,384]{1,0:T(2,128)S(1)}, u32[]{:S(2)}, u32[]{:S(2)}) collective-permute-start(f32[2,384]{1,0:T(2,128)S(1)} %fusion.47), channel_id=1, source_target_pairs={{0,1},{1,0},{2,3},{3,2},{4,5},{5,4},{6,7},{7,6},{8,9},{9,8},{10,11... | collective-permute-start | bytes 9224 | tf_op jit(solution)/shard_map/ppermute | solution.py:143
  46.8 0.5 copy.25
  47.4 1.3 %reshape.294 = f32[1,384,512]{1,2,0:T(8,128)} reshape(f32[3,128,8,64]{1,0,3,2:T(4,128)S(1)} %copy.25) | data formatting | bytes 1572864 | tf_op jit(solution)/shard_map/reshape | solution.py:82
  48.7 0.2 collective-permute-done.4
  49.0 1.7 %multiply_reduce_fusion = (f32[3,128,8]{1,2,0:T(8,128)S(1)}, bf16[3,128,8,64]{1,3,2,0:T(8,128)(2,1)S(1)}) fusion(f32[3,128,8,64]{1,3,2,0:T(8,128)} %copy-done.7, f32[3,128]{1,0:T(4,128)S(1)} %bitcast.120, f32[3,128]{1,0:T(4,128)S(1)} %bitcast.118, f32[3,128,8,64]{1,0,3,2:T(4,128)} %copy-done.3), kind=kLoop, calls=%fused_computation.52 | loop fusion | flops 1569792 | bytes 1981440 | tf_op jit(solution)/shard_map/reduce_sum | solution.py:93
  50.7 0.6 fusion.51
  51.2 1.7 %copy-done.2 = f32[3,8,128,384]{3,2,1,0:T(8,128)S(1)} copy-done((f32[3,8,128,384]{3,2,1,0:T(8,128)S(1)}, f32[3,8,128,384]{3,2,1,0:T(8,128)}, u32[]{:S(2)}) %copy-start.2) | copy-done | bytes 4718616
  53.3 1.9 %multiply_convert_fusion = bf16[3,8,128,384]{3,2,1,0:T(8,128)(2,1)S(1)} fusion(f32[3,8,128]{2,1,0:T(8,128)S(1)} %bitcast.119, bf16[3,128,8,64]{1,3,2,0:T(8,128)(2,1)S(1)} %get-tuple-element.16, f32[3,8,128,384]{3,2,1,0:T(8,128)S(1)} %copy-done.2, f32[3,8,128]{2,1,0:T(8,128)S(1)} %get-tuple-element.48, bf16[1,384,8,64]{1,3,2,0:T(8,128)(2,1)S(1)} %bitcast.109, ...), kind=kOutput, calls=%fused_computation.5 | convolution fusion | flops 158072832 | bytes 8675328 | tf_op jit(solution)/shard_map/jqhd,jkhd->jhqk/dot_general | solution.py:95
  55.2 0.6 fusion.30
  55.7 0.2 broadcast_in_dim.36
  56.1 0.3 fusion.9
  56.4 0.3 fusion.16
  56.7 0.2 convert.13
  56.9 1.6 %copy-done = f32[896,1024]{0,1:T(8,128)} copy-done((f32[896,1024]{0,1:T(8,128)}, f32[896,1024]{0,1:T(8,128)S(1)}, u32[]{:S(2)}) %copy-start) | copy-done | bytes 3670040
  58.8 1.2 %fusion.17 = bf16[3,128,8,64]{1,3,2,0:T(8,128)(2,1)S(1)} fusion(bf16[3,8,128,384]{3,2,1,0:T(8,128)(2,1)S(1)} %multiply_convert_fusion, bf16[1,384,8,64]{1,3,2,0:T(8,128)(2,1)S(1)} %bitcast.103, bf16[1,384,8,64]{1,3,2,0:T(8,128)(2,1)S(1)} %bitcast.105, bf16[1,384,8,64]{1,3,2,0:T(8,128)(2,1)S(1)} %bitcast.101), kind=kOutput, calls=%fused_computation.31 | convolution fusion | flops 152371200 | bytes 3932160 | tf_op jit(solution)/shard_map/jhqk,jkhd->jqhd/dot_general | solution.py:97
  60.0 0.3 copy.24
  60.3 0.3 convert_element_type.85
  60.7 2.3 %collective-permute-start.7 = (bf16[256,1024]{0,1:T(8,128)(2,1)S(1)}, bf16[256,1024]{0,1:T(8,128)(2,1)S(1)}, u32[]{:S(2)}, u32[]{:S(2)}) collective-permute-start(bf16[256,1024]{0,1:T(8,128)(2,1)S(1)} %get-tuple-element.19), channel_id=1, source_target_pairs={{2,4},{6,8},{10,12},{4,2},{8,6},{12,10},{3,5},{7,9},{11,13},{5,3},... | collective-permute-start | bytes 1572872 | tf_op jit(solution)/shard_map/ppermute | solution.py:163
  63.1 1.3 %fusion.27 = bf16[128,1024]{0,1:T(8,128)(2,1)S(1)} fusion(f32[896,1024]{0,1:T(8,128)} %copy-done, bf16[256,1024]{0,1:T(8,128)(2,1)S(1)} %collective-permute-done.5, pred[]{:T(512)S(6)} %eq.21), kind=kLoop, calls=%fused_computation.67 | loop fusion | flops 786432 | bytes 1835009 | tf_op jit(solution)/shard_map/convert_element_type | solution.py:168
  64.5 0.6 collective-permute-start.6
  65.1 6.1 %collective-permute-done.7 = bf16[256,1024]{0,1:T(8,128)(2,1)S(1)} collective-permute-done((bf16[256,1024]{0,1:T(8,128)(2,1)S(1)}, bf16[256,1024]{0,1:T(8,128)(2,1)S(1)}, u32[]{:S(2)}, u32[]{:S(2)}) %collective-permute-start.7) | collective-permute-done | bytes 524320 | tf_op jit(solution)/shard_map/ppermute | solution.py:163
  71.2 2.2 %collective-permute-done.6 = bf16[2,128,512]{1,2,0:T(8,128)(2,1)S(1)} collective-permute-done((bf16[2,128,512]{1,2,0:T(8,128)(2,1)S(1)}, bf16[2,128,512]{1,2,0:T(8,128)(2,1)S(1)}, u32[]{:S(2)}, u32[]{:S(2)}) %collective-permute-start.6) | collective-permute-done | bytes 262176 | tf_op jit(solution)/shard_map/ppermute | solution.py:34
  73.5 1.6 %fusion.13 = bf16[384,1024]{0,1:T(8,128)(2,1)S(1)} fusion(f32[896,1024]{0,1:T(8,128)} %copy-done, bf16[256,1024]{0,1:T(8,128)(2,1)S(1)} %get-tuple-element.24, bf16[256,1024]{0,1:T(8,128)(2,1)S(1)} %get-tuple-element.23), kind=kLoop, calls=%fused_computation.23 | loop fusion | flops 1966080 | bytes 3407872 | tf_op jit(solution)/shard_map/add | solution.py:177
  75.3 0.2 fusion.24
  75.5 0.6 collective-permute-start.8
  76.4 13.1 %collective-permute-done.8 = bf16[2,256,512]{1,2,0:T(8,128)(2,1)S(1)} collective-permute-done((bf16[2,256,512]{1,2,0:T(8,128)(2,1)S(1)}, bf16[2,256,512]{1,2,0:T(8,128)(2,1)S(1)}, u32[]{:S(2)}, u32[]{:S(2)}) %collective-permute-start.8) | collective-permute-done | bytes 524320 | tf_op jit(solution)/shard_map/ppermute | solution.py:34
  89.5 0.2 fusion.20
  89.8 0.4 maximum_select_fusion
  90.2 1.6 %copy.26 = bf16[1,2,384,1024]{3,2,1,0:T(8,128)(2,1)} copy(bf16[1,2,384,1024]{2,3,1,0:T(8,128)(2,1)S(1)} %maximum_select_fusion) | data formatting | bytes 3145728 | tf_op jit(solution)/shard_map/jit(_where)/select_n | solution.py:193
  (77 shorter events, 3.4 us)
Async XLA Ops:
  0.0 2.6 %copy-start.20 = (s32[12]{0:T(128)S(1)}, s32[12]{0:T(128)}, u32[]{:S(2)}) copy-start(s32[12]{0:T(128)} %param.3) | copy-start | bytes 148
  2.0 19.3 %collective-permute-start = (bf16[2,384,512]{1,2,0:T(8,128)(2,1)S(1)}, bf16[2,384,512]{1,2,0:T(8,128)(2,1)S(1)}, u32[]{:S(2)}, u32[]{:S(2)}) collective-permute-start(bf16[2,384,512]{1,2,0:T(8,128)(2,1)S(1)} %broadcast_select_fusion.3), channel_id=1, source_target_pairs={{0,16},{16,0},{1,17},{17,1},{2,18},{18,2},{3,19},{19,3},{4,20},{20... | collective-permute-start | bytes 2359304 | tf_op jit(solution)/shard_map/ppermute | solution.py:34
  22.8 10.8 %collective-permute-start.1 = (bf16[256,1024]{0,1:T(8,128)(2,1)}, bf16[256,1024]{0,1:T(8,128)(2,1)}, u32[]{:S(2)}, u32[]{:S(2)}) collective-permute-start(bf16[256,1024]{0,1:T(8,128)(2,1)} %get-tuple-element.37), channel_id=1, source_target_pairs={{2,4},{6,8},{10,12},{4,2},{8,6},{12,10},{3,5},{7,9},{11,13},{5,3},... | collective-permute-start | bytes 1572872 | tf_op jit(solution)/shard_map/ppermute | solution.py:27
  24.7 8.9 %collective-permute-start.2 = (bf16[256,1024]{0,1:T(8,128)(2,1)}, bf16[256,1024]{0,1:T(8,128)(2,1)}, u32[]{:S(2)}, u32[]{:S(2)}) collective-permute-start(bf16[256,1024]{0,1:T(8,128)(2,1)} %get-tuple-element.38), channel_id=1, source_target_pairs={{0,2},{2,0},{4,6},{6,4},{8,10},{10,8},{12,14},{14,12},{1,3},{3,1},... | collective-permute-start | bytes 1572872 | tf_op jit(solution)/shard_map/ppermute | solution.py:26
  30.4 9.9 %copy-start.3 = (f32[3,128,8,64]{1,0,3,2:T(4,128)}, f32[3,128,8,64]{1,0,3,2:T(4,128)S(1)}, u32[]{:S(2)}) copy-start(f32[3,128,8,64]{1,0,3,2:T(4,128)S(1)} %reshape.295) | copy-start | bytes 2359300
  32.0 3.6 %copy-start.4 = (bf16[3,128,8,64]{1,0,3,2:T(4,128)(2,1)}, bf16[3,128,8,64]{1,0,3,2:T(4,128)(2,1)S(1)}, u32[]{:S(2)}) copy-start(bf16[3,128,8,64]{1,0,3,2:T(4,128)(2,1)S(1)} %reshape_squeeze.3) | copy-start | bytes 1179652
  35.4 1.0 %copy-start.8 = (bf16[384,512]{0,1:T(8,128)(2,1)}, bf16[384,512]{0,1:T(8,128)(2,1)S(1)}, u32[]{:S(2)}) copy-start(bf16[384,512]{0,1:T(8,128)(2,1)S(1)} %get-tuple-element.30) | copy-start | bytes 1179652
  35.4 1.0 %copy-start.10 = (bf16[384,512]{0,1:T(8,128)(2,1)}, bf16[384,512]{0,1:T(8,128)(2,1)S(1)}, u32[]{:S(2)}) copy-start(bf16[384,512]{0,1:T(8,128)(2,1)S(1)} %get-tuple-element.31) | copy-start | bytes 1179652
  35.4 1.0 %copy-start.12 = (bf16[384,512]{0,1:T(8,128)(2,1)}, bf16[384,512]{0,1:T(8,128)(2,1)S(1)}, u32[]{:S(2)}) copy-start(bf16[384,512]{0,1:T(8,128)(2,1)S(1)} %get-tuple-element.32) | copy-start | bytes 1179652
  35.5 4.8 %copy-start.14 = (bf16[384,512]{0,1:T(8,128)(2,1)}, bf16[384,512]{0,1:T(8,128)(2,1)S(1)}, u32[]{:S(2)}) copy-start(bf16[384,512]{0,1:T(8,128)(2,1)S(1)} %get-tuple-element.27) | copy-start | bytes 1179652
  35.5 4.8 %copy-start.16 = (bf16[384,512]{0,1:T(8,128)(2,1)}, bf16[384,512]{0,1:T(8,128)(2,1)S(1)}, u32[]{:S(2)}) copy-start(bf16[384,512]{0,1:T(8,128)(2,1)S(1)} %get-tuple-element.28) | copy-start | bytes 1179652
  35.6 4.7 %copy-start.18 = (bf16[384,512]{0,1:T(8,128)(2,1)}, bf16[384,512]{0,1:T(8,128)(2,1)S(1)}, u32[]{:S(2)}) copy-start(bf16[384,512]{0,1:T(8,128)(2,1)S(1)} %get-tuple-element.29) | copy-start | bytes 1179652
  38.2 2.1 %copy-start.1 = (f32[3,8,128,384]{3,2,1,0:T(8,128)}, f32[3,8,128,384]{3,2,1,0:T(8,128)S(1)}, u32[]{:S(2)}) copy-start(f32[3,8,128,384]{3,2,1,0:T(8,128)S(1)} %get-tuple-element.49) | copy-start | bytes 14155780
  41.5 5.3 %copy-start.7 = (f32[3,128,8,64]{1,3,2,0:T(8,128)}, f32[3,128,8,64]{1,3,2,0:T(8,128)S(1)}, u32[]{:S(2)}) copy-start(f32[3,128,8,64]{1,3,2,0:T(8,128)S(1)} %get-tuple-element.50) | copy-start | bytes 2359300
  41.6 3.7 %collective-permute-start.3 = (f32[2,384]{1,0:T(2,128)S(1)}, f32[2,384]{1,0:T(2,128)S(1)}, u32[]{:S(2)}, u32[]{:S(2)}) collective-permute-start(f32[2,384]{1,0:T(2,128)S(1)} %pad_maximum_fusion.10), channel_id=1, source_target_pairs={{0,16},{16,0},{1,17},{17,1},{2,18},{18,2},{3,19},{19,3},{4,20},{20... | collective-permute-start | bytes 9224 | tf_op jit(solution)/shard_map/ppermute | solution.py:34
  45.2 3.7 %collective-permute-start.4 = (f32[2,384]{1,0:T(2,128)S(1)}, f32[2,384]{1,0:T(2,128)S(1)}, u32[]{:S(2)}, u32[]{:S(2)}) collective-permute-start(f32[2,384]{1,0:T(2,128)S(1)} %fusion.47), channel_id=1, source_target_pairs={{0,1},{1,0},{2,3},{3,2},{4,5},{5,4},{6,7},{7,6},{8,9},{9,8},{10,11... | collective-permute-start | bytes 9224 | tf_op jit(solution)/shard_map/ppermute | solution.py:143
  50.6 2.3 %copy-start.2 = (f32[3,8,128,384]{3,2,1,0:T(8,128)S(1)}, f32[3,8,128,384]{3,2,1,0:T(8,128)}, u32[]{:S(2)}) copy-start(f32[3,8,128,384]{3,2,1,0:T(8,128)} %copy-done.1) | copy-start | bytes 14155780
  50.6 2.4 %copy-start.15 = (bf16[384,512]{0,1:T(8,128)(2,1)S(1)}, bf16[384,512]{0,1:T(8,128)(2,1)}, u32[]{:S(2)}) copy-start(bf16[384,512]{0,1:T(8,128)(2,1)} %copy-done.14) | copy-start | bytes 1179652
  50.7 2.5 %copy-start.17 = (bf16[384,512]{0,1:T(8,128)(2,1)S(1)}, bf16[384,512]{0,1:T(8,128)(2,1)}, u32[]{:S(2)}) copy-start(bf16[384,512]{0,1:T(8,128)(2,1)} %copy-done.16) | copy-start | bytes 1179652
  50.7 2.6 %copy-start.19 = (bf16[384,512]{0,1:T(8,128)(2,1)S(1)}, bf16[384,512]{0,1:T(8,128)(2,1)}, u32[]{:S(2)}) copy-start(bf16[384,512]{0,1:T(8,128)(2,1)} %copy-done.18) | copy-start | bytes 1179652
  53.3 1.9 %copy-start.5 = (bf16[3,128,8,64]{1,0,3,2:T(4,128)(2,1)S(1)}, bf16[3,128,8,64]{1,0,3,2:T(4,128)(2,1)}, u32[]{:S(2)}) copy-start(bf16[3,128,8,64]{1,0,3,2:T(4,128)(2,1)} %copy-done.4) | copy-start | bytes 1179652
  56.7 1.8 %copy-start = (f32[896,1024]{0,1:T(8,128)}, f32[896,1024]{0,1:T(8,128)S(1)}, u32[]{:S(2)}) copy-start(f32[896,1024]{0,1:T(8,128)S(1)} %fusion.16) | copy-start | bytes 11010052
  56.7 1.9 %copy-start.9 = (bf16[384,512]{0,1:T(8,128)(2,1)S(1)}, bf16[384,512]{0,1:T(8,128)(2,1)}, u32[]{:S(2)}) copy-start(bf16[384,512]{0,1:T(8,128)(2,1)} %copy-done.8) | copy-start | bytes 1179652
  56.7 1.9 %copy-start.11 = (bf16[384,512]{0,1:T(8,128)(2,1)S(1)}, bf16[384,512]{0,1:T(8,128)(2,1)}, u32[]{:S(2)}) copy-start(bf16[384,512]{0,1:T(8,128)(2,1)} %copy-done.10) | copy-start | bytes 1179652
  56.7 2.1 %copy-start.13 = (bf16[384,512]{0,1:T(8,128)(2,1)S(1)}, bf16[384,512]{0,1:T(8,128)(2,1)}, u32[]{:S(2)}) copy-start(bf16[384,512]{0,1:T(8,128)(2,1)} %copy-done.12) | copy-start | bytes 1179652
  58.6 4.4 %copy-start.6 = (f32[1,384,512]{1,2,0:T(8,128)S(1)}, f32[1,384,512]{1,2,0:T(8,128)}, u32[]{:S(2)}) copy-start(f32[1,384,512]{1,2,0:T(8,128)} %reshape.294) | copy-start | bytes 2359300
  58.6 4.5 %collective-permute-start.5 = (bf16[256,1024]{0,1:T(8,128)(2,1)S(1)}, bf16[256,1024]{0,1:T(8,128)(2,1)S(1)}, u32[]{:S(2)}, u32[]{:S(2)}) collective-permute-start(bf16[256,1024]{0,1:T(8,128)(2,1)S(1)} %get-tuple-element.20), channel_id=1, source_target_pairs={{0,2},{2,0},{4,6},{6,4},{8,10},{10,8},{12,14},{14,12},{1,3},{3,1},... | collective-permute-start | bytes 1572872 | tf_op jit(solution)/shard_map/ppermute | solution.py:162
  60.7 10.5 %collective-permute-start.7 = (bf16[256,1024]{0,1:T(8,128)(2,1)S(1)}, bf16[256,1024]{0,1:T(8,128)(2,1)S(1)}, u32[]{:S(2)}, u32[]{:S(2)}) collective-permute-start(bf16[256,1024]{0,1:T(8,128)(2,1)S(1)} %get-tuple-element.19), channel_id=1, source_target_pairs={{2,4},{6,8},{10,12},{4,2},{8,6},{12,10},{3,5},{7,9},{11,13},{5,3},... | collective-permute-start | bytes 1572872 | tf_op jit(solution)/shard_map/ppermute | solution.py:163
  64.5 8.9 %collective-permute-start.6 = (bf16[2,128,512]{1,2,0:T(8,128)(2,1)S(1)}, bf16[2,128,512]{1,2,0:T(8,128)(2,1)S(1)}, u32[]{:S(2)}, u32[]{:S(2)}) collective-permute-start(bf16[2,128,512]{1,2,0:T(8,128)(2,1)S(1)} %fusion.34), channel_id=1, source_target_pairs={{0,16},{16,0},{1,17},{17,1},{2,18},{18,2},{3,19},{19,3},{4,20},{20... | collective-permute-start | bytes 786440 | tf_op jit(solution)/shard_map/ppermute | solution.py:34
  75.5 14.0 %collective-permute-start.8 = (bf16[2,256,512]{1,2,0:T(8,128)(2,1)S(1)}, bf16[2,256,512]{1,2,0:T(8,128)(2,1)S(1)}, u32[]{:S(2)}, u32[]{:S(2)}) collective-permute-start(bf16[2,256,512]{1,2,0:T(8,128)(2,1)S(1)} %fusion.24), channel_id=1, source_target_pairs={{0,16},{16,0},{1,17},{17,1},{2,18},{18,2},{3,19},{19,3},{4,20},{20... | collective-permute-start | bytes 1572872 | tf_op jit(solution)/shard_map/ppermute | solution.py:34

commit v19 on v15

--- a/solution.py
+++ b/solution.py
@@ -139,8 +139,8 @@
 
     def row_total(sums_pair):
         sums = jnp.stack(sums_pair)
+        sums = sums + lax.ppermute(sums, "mp", [(0, 1), (1, 0)])
         sums = sums + sec_swap(sums)
-        sums = sums + lax.ppermute(sums, "mp", [(0, 1), (1, 0)])
         return sums[0], sums[1]
 
     grad_q, normed, total = attention_grads(

time: 92 us -> 92 us (level)
    ppermute x1, waiting for transfers between devices: 0.18 us -> 2.08 us  [row_total(): sums = sums + lax.ppermute(sums, 'mp', [(0, 1), (1, 0)])]
    ppermute x4, waiting for transfers between devices: 36 us -> 34.1 us  [sec_swap(): return lax.ppermute(value, 'sec', [(0, 1), (1, 0)])]
where the time goes in v19:
time: 92 us; the launch traced here: 91.6 us
  waiting for transfers between devices  44.1 us (48%)
  local copies, waits for them, and re-layouts  15.3 us (17%)
  other arithmetic  13.6 us (15%)
  starting transfers between devices  10 us (11%)
  matrix products  6.18 us (7%)
  between operations  2.35 us (3%)
    ppermute x4, waiting for transfers between devices, sec_swap(): return lax.ppermute(value, 'sec', [(0, 1), (1, 0)])  34.1 us
    ppermute x1, waiting for transfers between devices, per_device(): across = lax.ppermute(jnp.where(even, top, bottom), 'seq', between)  6.06 us
    unnamed x46, local copies, waits for them, and re-layouts  5.41 us
    ppermute x4, starting transfers between devices, sec_swap(): return lax.ppermute(value, 'sec', [(0, 1), (1, 0)])  2.41 us
    ppermute x1, starting transfers between devices, per_device(): across = lax.ppermute(jnp.where(even, top, bottom), 'seq', between)  2.31 us
    ppermute x1, waiting for transfers between devices, row_total(): sums = sums + lax.ppermute(sums, 'mp', [(0, 1), (1, 0)])  2.08 us
    ppermute x1, starting transfers between devices, halo_swap(): across = lax.ppermute(jnp.where(even, top, bottom), 'seq', between)  1.91 us
    ppermute x1, waiting for transfers between devices, halo_swap(): across = lax.ppermute(jnp.where(even, top, bottom), 'seq', between)  1.9 us
  transfers between devices with their start and end apart: 9, of which 7 were waited for; matrix products, arithmetic and copies ran while one was open for 11% of the time, Pallas kernels for 0%

profile of v19, /device:TPU:18, one launch (start us, length us, event | category | flops | bytes accessed | tf_op | source)
XLA Modules:
  0.0 91.6 jit_solution(5986219988572807127)
XLA Ops:
  0.0 1.5 %constant_dynamic-slice_fusion.6 = (bf16[1,2,384,512]{3,2,1,0:T(8,128)(2,1)S(1)}, bf16[1,2,384,512]{3,2,1,0:T(8,128)(2,1)S(1)}) fusion(bf16[1,2,384,1024]{3,2,1,0:T(8,128)(2,1)} %param.2, s32[]{:T(128)S(6)} %select_n.176, s32[]{:T(128)S(6)} %select_n.175), kind=kLoop, calls=%fused_computation.101 | loop fusion | bytes 3145736 | tf_op jit(solution)/shard_map/dynamic_slice | solution.py:129
  1.5 0.4 copy.20
  1.9 0.6 collective-permute-start
  2.5 0.4 copy.21
  3.7 17.5 %collective-permute-done = bf16[2,384,512]{1,2,0:T(8,128)(2,1)S(1)} collective-permute-done((bf16[2,384,512]{1,2,0:T(8,128)(2,1)S(1)}, bf16[2,384,512]{1,2,0:T(8,128)(2,1)S(1)}, u32[]{:S(2)}, u32[]{:S(2)}) %collective-permute-start) | collective-permute-done | bytes 786464 | tf_op jit(solution)/shard_map/ppermute | solution.py:34
  21.4 1.2 %broadcast_select_fusion.7 = (bf16[256,1024]{0,1:T(8,128)(2,1)}, bf16[256,1024]{0,1:T(8,128)(2,1)}) fusion(pred[]{:T(512)S(6)} %eq.21, bf16[384,512]{0,1:T(8,128)(2,1)S(1)} %get-tuple-element.42, bf16[384,512]{0,1:T(8,128)(2,1)S(1)} %get-tuple-element.41), kind=kLoop, calls=%fused_computation.75 | loop fusion | flops 3670016 | bytes 1835009 | tf_op jit(solution)/shard_map/jit(_where)/select_n | solution.py:27
  22.6 1.9 %collective-permute-start.1 = (bf16[256,1024]{0,1:T(8,128)(2,1)}, bf16[256,1024]{0,1:T(8,128)(2,1)}, u32[]{:S(2)}, u32[]{:S(2)}) collective-permute-start(bf16[256,1024]{0,1:T(8,128)(2,1)} %get-tuple-element.39), channel_id=1, source_target_pairs={{2,4},{6,8},{10,12},{4,2},{8,6},{12,10},{3,5},{7,9},{11,13},{5,3},... | collective-permute-start | bytes 1572872 | tf_op jit(solution)/shard_map/ppermute | solution.py:27
  24.5 1.7 %collective-permute-start.2 = (bf16[256,1024]{0,1:T(8,128)(2,1)}, bf16[256,1024]{0,1:T(8,128)(2,1)}, u32[]{:S(2)}, u32[]{:S(2)}) collective-permute-start(bf16[256,1024]{0,1:T(8,128)(2,1)} %get-tuple-element.40), channel_id=1, source_target_pairs={{0,2},{2,0},{4,6},{6,4},{8,10},{10,8},{12,14},{14,12},{1,3},{3,1},... | collective-permute-start | bytes 1572872 | tf_op jit(solution)/shard_map/ppermute | solution.py:26
  26.3 0.6 fusion.49
  28.7 0.8 slice_convert_fusion
  29.6 0.3 reshape.297
  29.9 1.6 %reshape_squeeze.3 = bf16[3,128,8,64]{1,0,3,2:T(4,128)(2,1)S(1)} reshape(bf16[1,384,512]{1,2,0:T(8,128)(2,1)} %get-tuple-element.38) | data formatting | bytes 786432 | tf_op jit(solution)/shard_map/reshape;squeeze | solution.py:69
  31.5 1.9 %collective-permute-done.1 = bf16[256,1024]{0,1:T(8,128)(2,1)} collective-permute-done((bf16[256,1024]{0,1:T(8,128)(2,1)}, bf16[256,1024]{0,1:T(8,128)(2,1)}, u32[]{:S(2)}, u32[]{:S(2)}) %collective-permute-start.1) | collective-permute-done | bytes 524320 | tf_op jit(solution)/shard_map/ppermute | solution.py:27
  33.4 1.3 %broadcast_select_fusion.5 = (bf16[256,1024]{0,1:T(8,128)(2,1)S(1)}, bf16[256,1024]{0,1:T(8,128)(2,1)S(1)}) fusion(bf16[256,1024]{0,1:T(8,128)(2,1)} %collective-permute-done.1, bf16[256,1024]{0,1:T(8,128)(2,1)} %collective-permute-done.2, pred[]{:T(512)S(6)} %eq.21), kind=kLoop, calls=%fused_computation.73 | loop fusion | flops 524288 | bytes 2097153 | tf_op jit(solution)/shard_map/jit(_where)/select_n | solution.py:28
  35.4 0.8 fusion.28
  36.2 1.7 %fusion.50 = (f32[3,8,128]{2,1,0:T(8,128)S(1)}, f32[3,8,128,384]{3,2,1,0:T(8,128)S(1)}) fusion(f32[3,8,128,384]{3,2,1,0:T(8,128)S(1)} %fusion.28, pred[3,384]{1,0:T(4,128)(4,1)S(1)} %bitcast.125), kind=kOutput, calls=%fused_computation.131 | output fusion | flops 7078271 | bytes 9450624 | tf_op jit(solution)/shard_map/sub | solution.py:78
  38.0 0.6 fusion.5
  38.6 1.5 %copy-done.1 = f32[3,8,128,384]{3,2,1,0:T(8,128)} copy-done((f32[3,8,128,384]{3,2,1,0:T(8,128)}, f32[3,8,128,384]{3,2,1,0:T(8,128)S(1)}, u32[]{:S(2)}) %copy-start.1) | copy-done | bytes 4718616
  40.1 1.2 %multiply_reduce_fusion.2 = (f32[3,128]{1,0:T(4,128)S(1)}, f32[3,128]{1,0:T(4,128)S(1)}, f32[3,128,8,64]{1,3,2,0:T(8,128)S(1)}) fusion(f32[3,128,8,64]{1,0,3,2:T(4,128)S(1)} %reshape.297, bf16[3,8,128,384]{3,2,1,0:T(8,128)(2,1)S(1)} %fusion.5, bf16[1,384,8,64]{1,3,2,0:T(8,128)(2,1)S(1)} %bitcast.110, bf16[1,384,8,64]{1,3,2,0:T(8,128)(2,1)S(1)} %bitcast.112, ...), kind=kOutput, calls=%fused_computation.57 | convolution fusion | flops 152960256 | bytes 5114880 | tf_op jit(solution)/shard_map/jhqk,jkhd->jqhd/dot_general | solution.py:81
  41.4 1.6 %collective-permute-start.3 = (f32[2,384]{1,0:T(2,128)S(1)}, f32[2,384]{1,0:T(2,128)S(1)}, u32[]{:S(2)}, u32[]{:S(2)}) collective-permute-start(f32[2,384]{1,0:T(2,128)S(1)} %pad_maximum_fusion.10), channel_id=1, source_target_pairs={{0,1},{1,0},{2,3},{3,2},{4,5},{5,4},{6,7},{7,6},{8,9},{9,8},{10,11... | collective-permute-start | bytes 9224 | tf_op jit(solution)/shard_map/ppermute | solution.py:142
  43.0 2.1 %collective-permute-done.3 = f32[2,384]{1,0:T(2,128)S(1)} collective-permute-done((f32[2,384]{1,0:T(2,128)S(1)}, f32[2,384]{1,0:T(2,128)S(1)}, u32[]{:S(2)}, u32[]{:S(2)}) %collective-permute-start.3) | collective-permute-done | bytes 3104 | tf_op jit(solution)/shard_map/ppermute | solution.py:142
  45.1 0.6 collective-permute-start.4
  45.7 0.5 copy.27
  46.2 1.3 %reshape.296 = f32[1,384,512]{1,2,0:T(8,128)} reshape(f32[3,128,8,64]{1,0,3,2:T(4,128)S(1)} %copy.27) | data formatting | bytes 1572864 | tf_op jit(solution)/shard_map/reshape | solution.py:82
  47.5 1.2 %collective-permute-done.4 = f32[2,384]{1,0:T(2,128)S(1)} collective-permute-done((f32[2,384]{1,0:T(2,128)S(1)}, f32[2,384]{1,0:T(2,128)S(1)}, u32[]{:S(2)}, u32[]{:S(2)}) %collective-permute-start.4) | collective-permute-done | bytes 3104 | tf_op jit(solution)/shard_map/ppermute | solution.py:34
  48.8 1.7 %multiply_reduce_fusion = (f32[3,128,8]{1,2,0:T(8,128)S(1)}, bf16[3,128,8,64]{1,3,2,0:T(8,128)(2,1)S(1)}) fusion(f32[3,128,8,64]{1,3,2,0:T(8,128)} %copy-done.7, f32[3,128]{1,0:T(4,128)S(1)} %bitcast.122, f32[3,128]{1,0:T(4,128)S(1)} %bitcast.120, f32[3,128,8,64]{1,0,3,2:T(4,128)} %copy-done.3), kind=kLoop, calls=%fused_computation.54 | loop fusion | flops 1569792 | bytes 1981440 | tf_op jit(solution)/shard_map/reduce_sum | solution.py:93
  50.5 0.6 fusion.51
  51.0 1.7 %copy-done.2 = f32[3,8,128,384]{3,2,1,0:T(8,128)S(1)} copy-done((f32[3,8,128,384]{3,2,1,0:T(8,128)S(1)}, f32[3,8,128,384]{3,2,1,0:T(8,128)}, u32[]{:S(2)}) %copy-start.2) | copy-done | bytes 4718616
  53.1 1.9 %multiply_convert_fusion = bf16[3,8,128,384]{3,2,1,0:T(8,128)(2,1)S(1)} fusion(f32[3,8,128]{2,1,0:T(8,128)S(1)} %bitcast.121, bf16[3,128,8,64]{1,3,2,0:T(8,128)(2,1)S(1)} %get-tuple-element.16, f32[3,8,128,384]{3,2,1,0:T(8,128)S(1)} %copy-done.2, f32[3,8,128]{2,1,0:T(8,128)S(1)} %get-tuple-element.50, bf16[1,384,8,64]{1,3,2,0:T(8,128)(2,1)S(1)} %bitcast.111, ...), kind=kOutput, calls=%fused_computation.5 | convolution fusion | flops 158072832 | bytes 8675328 | tf_op jit(solution)/shard_map/jqhd,jkhd->jhqk/dot_general | solution.py:95
  55.0 0.6 fusion.30
  55.5 0.2 broadcast_in_dim.36
  55.9 0.3 fusion.9
  56.2 0.3 fusion.16
  56.7 1.5 %copy-done = f32[896,1024]{0,1:T(8,128)} copy-done((f32[896,1024]{0,1:T(8,128)}, f32[896,1024]{0,1:T(8,128)S(1)}, u32[]{:S(2)}) %copy-start) | copy-done | bytes 3670040
  58.6 1.2 %fusion.17 = bf16[3,128,8,64]{1,3,2,0:T(8,128)(2,1)S(1)} fusion(bf16[3,8,128,384]{3,2,1,0:T(8,128)(2,1)S(1)} %multiply_convert_fusion, bf16[1,384,8,64]{1,3,2,0:T(8,128)(2,1)S(1)} %bitcast.104, bf16[1,384,8,64]{1,3,2,0:T(8,128)(2,1)S(1)} %bitcast.106, bf16[1,384,8,64]{1,3,2,0:T(8,128)(2,1)S(1)} %bitcast.102), kind=kOutput, calls=%fused_computation.31 | convolution fusion | flops 152371200 | bytes 3932160 | tf_op jit(solution)/shard_map/jhqk,jkhd->jqhd/dot_general | solution.py:97
  59.8 0.3 copy.26
  60.1 0.3 convert_element_type.85
  60.5 2.3 %collective-permute-start.7 = (bf16[256,1024]{0,1:T(8,128)(2,1)S(1)}, bf16[256,1024]{0,1:T(8,128)(2,1)S(1)}, u32[]{:S(2)}, u32[]{:S(2)}) collective-permute-start(bf16[256,1024]{0,1:T(8,128)(2,1)S(1)} %get-tuple-element.17), channel_id=1, source_target_pairs={{2,4},{6,8},{10,12},{4,2},{8,6},{12,10},{3,5},{7,9},{11,13},{5,3},... | collective-permute-start | bytes 1572872 | tf_op jit(solution)/shard_map/ppermute | solution.py:163
  62.9 1.3 %fusion.27 = bf16[128,1024]{0,1:T(8,128)(2,1)S(1)} fusion(f32[896,1024]{0,1:T(8,128)} %copy-done, bf16[256,1024]{0,1:T(8,128)(2,1)S(1)} %collective-permute-done.5, pred[]{:T(512)S(6)} %eq.21), kind=kLoop, calls=%fused_computation.65 | loop fusion | flops 786432 | bytes 1835009 | tf_op jit(solution)/shard_map/convert_element_type | solution.py:168
  64.3 0.6 collective-permute-start.6
  64.9 6.1 %collective-permute-done.7 = bf16[256,1024]{0,1:T(8,128)(2,1)S(1)} collective-permute-done((bf16[256,1024]{0,1:T(8,128)(2,1)S(1)}, bf16[256,1024]{0,1:T(8,128)(2,1)S(1)}, u32[]{:S(2)}, u32[]{:S(2)}) %collective-permute-start.7) | collective-permute-done | bytes 524320 | tf_op jit(solution)/shard_map/ppermute | solution.py:163
  71.0 2.3 %collective-permute-done.6 = bf16[2,128,512]{1,2,0:T(8,128)(2,1)S(1)} collective-permute-done((bf16[2,128,512]{1,2,0:T(8,128)(2,1)S(1)}, bf16[2,128,512]{1,2,0:T(8,128)(2,1)S(1)}, u32[]{:S(2)}, u32[]{:S(2)}) %collective-permute-start.6) | collective-permute-done | bytes 262176 | tf_op jit(solution)/shard_map/ppermute | solution.py:34
  73.3 1.6 %fusion.13 = bf16[384,1024]{0,1:T(8,128)(2,1)S(1)} fusion(f32[896,1024]{0,1:T(8,128)} %copy-done, bf16[256,1024]{0,1:T(8,128)(2,1)S(1)} %get-tuple-element.26, bf16[256,1024]{0,1:T(8,128)(2,1)S(1)} %get-tuple-element.25), kind=kLoop, calls=%fused_computation.23 | loop fusion | flops 1966080 | bytes 3407872 | tf_op jit(solution)/shard_map/add | solution.py:177
  75.3 0.6 collective-permute-start.8
  76.2 13.2 %collective-permute-done.8 = bf16[2,256,512]{1,2,0:T(8,128)(2,1)S(1)} collective-permute-done((bf16[2,256,512]{1,2,0:T(8,128)(2,1)S(1)}, bf16[2,256,512]{1,2,0:T(8,128)(2,1)S(1)}, u32[]{:S(2)}, u32[]{:S(2)}) %collective-permute-start.8) | collective-permute-done | bytes 524320 | tf_op jit(solution)/shard_map/ppermute | solution.py:34
  89.3 0.2 fusion.20
  89.6 0.4 maximum_select_fusion
  90.0 1.6 %copy.28 = bf16[1,2,384,1024]{3,2,1,0:T(8,128)(2,1)} copy(bf16[1,2,384,1024]{2,3,1,0:T(8,128)(2,1)S(1)} %maximum_select_fusion) | data formatting | bytes 3145728 | tf_op jit(solution)/shard_map/jit(_where)/select_n | solution.py:193
  (78 shorter events, 3.6 us)
Async XLA Ops:
  1.5 1.3 %copy-start.20 = (s32[12]{0:T(128)S(1)}, s32[12]{0:T(128)}, u32[]{:S(2)}) copy-start(s32[12]{0:T(128)} %param.3) | copy-start | bytes 148
  1.9 19.3 %collective-permute-start = (bf16[2,384,512]{1,2,0:T(8,128)(2,1)S(1)}, bf16[2,384,512]{1,2,0:T(8,128)(2,1)S(1)}, u32[]{:S(2)}, u32[]{:S(2)}) collective-permute-start(bf16[2,384,512]{1,2,0:T(8,128)(2,1)S(1)} %bitcast.107), channel_id=1, source_target_pairs={{0,16},{16,0},{1,17},{17,1},{2,18},{18,2},{3,19},{19,3},{4,20},{20... | collective-permute-start | bytes 2359304 | tf_op jit(solution)/shard_map/ppermute | solution.py:34
  22.6 10.8 %collective-permute-start.1 = (bf16[256,1024]{0,1:T(8,128)(2,1)}, bf16[256,1024]{0,1:T(8,128)(2,1)}, u32[]{:S(2)}, u32[]{:S(2)}) collective-permute-start(bf16[256,1024]{0,1:T(8,128)(2,1)} %get-tuple-element.39), channel_id=1, source_target_pairs={{2,4},{6,8},{10,12},{4,2},{8,6},{12,10},{3,5},{7,9},{11,13},{5,3},... | collective-permute-start | bytes 1572872 | tf_op jit(solution)/shard_map/ppermute | solution.py:27
  24.5 8.9 %collective-permute-start.2 = (bf16[256,1024]{0,1:T(8,128)(2,1)}, bf16[256,1024]{0,1:T(8,128)(2,1)}, u32[]{:S(2)}, u32[]{:S(2)}) collective-permute-start(bf16[256,1024]{0,1:T(8,128)(2,1)} %get-tuple-element.40), channel_id=1, source_target_pairs={{0,2},{2,0},{4,6},{6,4},{8,10},{10,8},{12,14},{14,12},{1,3},{3,1},... | collective-permute-start | bytes 1572872 | tf_op jit(solution)/shard_map/ppermute | solution.py:26
  29.9 10.2 %copy-start.3 = (f32[3,128,8,64]{1,0,3,2:T(4,128)}, f32[3,128,8,64]{1,0,3,2:T(4,128)S(1)}, u32[]{:S(2)}) copy-start(f32[3,128,8,64]{1,0,3,2:T(4,128)S(1)} %reshape.297) | copy-start | bytes 2359300
  31.5 3.9 %copy-start.4 = (bf16[3,128,8,64]{1,0,3,2:T(4,128)(2,1)}, bf16[3,128,8,64]{1,0,3,2:T(4,128)(2,1)S(1)}, u32[]{:S(2)}) copy-start(bf16[3,128,8,64]{1,0,3,2:T(4,128)(2,1)S(1)} %reshape_squeeze.3) | copy-start | bytes 1179652
  35.2 1.0 %copy-start.8 = (bf16[384,512]{0,1:T(8,128)(2,1)}, bf16[384,512]{0,1:T(8,128)(2,1)S(1)}, u32[]{:S(2)}) copy-start(bf16[384,512]{0,1:T(8,128)(2,1)S(1)} %get-tuple-element.32) | copy-start | bytes 1179652
  35.2 1.0 %copy-start.10 = (bf16[384,512]{0,1:T(8,128)(2,1)}, bf16[384,512]{0,1:T(8,128)(2,1)S(1)}, u32[]{:S(2)}) copy-start(bf16[384,512]{0,1:T(8,128)(2,1)S(1)} %get-tuple-element.33) | copy-start | bytes 1179652
  35.2 1.0 %copy-start.12 = (bf16[384,512]{0,1:T(8,128)(2,1)}, bf16[384,512]{0,1:T(8,128)(2,1)S(1)}, u32[]{:S(2)}) copy-start(bf16[384,512]{0,1:T(8,128)(2,1)S(1)} %get-tuple-element.34) | copy-start | bytes 1179652
  35.3 4.8 %copy-start.14 = (bf16[384,512]{0,1:T(8,128)(2,1)}, bf16[384,512]{0,1:T(8,128)(2,1)S(1)}, u32[]{:S(2)}) copy-start(bf16[384,512]{0,1:T(8,128)(2,1)S(1)} %get-tuple-element.29) | copy-start | bytes 1179652
  35.4 4.7 %copy-start.16 = (bf16[384,512]{0,1:T(8,128)(2,1)}, bf16[384,512]{0,1:T(8,128)(2,1)S(1)}, u32[]{:S(2)}) copy-start(bf16[384,512]{0,1:T(8,128)(2,1)S(1)} %get-tuple-element.30) | copy-start | bytes 1179652
  35.4 4.7 %copy-start.18 = (bf16[384,512]{0,1:T(8,128)(2,1)}, bf16[384,512]{0,1:T(8,128)(2,1)S(1)}, u32[]{:S(2)}) copy-start(bf16[384,512]{0,1:T(8,128)(2,1)S(1)} %get-tuple-element.31) | copy-start | bytes 1179652
  38.0 2.1 %copy-start.1 = (f32[3,8,128,384]{3,2,1,0:T(8,128)}, f32[3,8,128,384]{3,2,1,0:T(8,128)S(1)}, u32[]{:S(2)}) copy-start(f32[3,8,128,384]{3,2,1,0:T(8,128)S(1)} %get-tuple-element.51) | copy-start | bytes 14155780
  41.3 4.3 %copy-start.7 = (f32[3,128,8,64]{1,3,2,0:T(8,128)}, f32[3,128,8,64]{1,3,2,0:T(8,128)S(1)}, u32[]{:S(2)}) copy-start(f32[3,128,8,64]{1,3,2,0:T(8,128)S(1)} %get-tuple-element.52) | copy-start | bytes 2359300
  41.4 3.7 %collective-permute-start.3 = (f32[2,384]{1,0:T(2,128)S(1)}, f32[2,384]{1,0:T(2,128)S(1)}, u32[]{:S(2)}, u32[]{:S(2)}) collective-permute-start(f32[2,384]{1,0:T(2,128)S(1)} %pad_maximum_fusion.10), channel_id=1, source_target_pairs={{0,1},{1,0},{2,3},{3,2},{4,5},{5,4},{6,7},{7,6},{8,9},{9,8},{10,11... | collective-permute-start | bytes 9224 | tf_op jit(solution)/shard_map/ppermute | solution.py:142
  45.1 3.7 %collective-permute-start.4 = (f32[2,384]{1,0:T(2,128)S(1)}, f32[2,384]{1,0:T(2,128)S(1)}, u32[]{:S(2)}, u32[]{:S(2)}) collective-permute-start(f32[2,384]{1,0:T(2,128)S(1)} %fusion.47), channel_id=1, source_target_pairs={{0,16},{16,0},{1,17},{17,1},{2,18},{18,2},{3,19},{19,3},{4,20},{20... | collective-permute-start | bytes 9224 | tf_op jit(solution)/shard_map/ppermute | solution.py:34
  50.4 2.3 %copy-start.2 = (f32[3,8,128,384]{3,2,1,0:T(8,128)S(1)}, f32[3,8,128,384]{3,2,1,0:T(8,128)}, u32[]{:S(2)}) copy-start(f32[3,8,128,384]{3,2,1,0:T(8,128)} %copy-done.1) | copy-start | bytes 14155780
  50.5 2.4 %copy-start.15 = (bf16[384,512]{0,1:T(8,128)(2,1)S(1)}, bf16[384,512]{0,1:T(8,128)(2,1)}, u32[]{:S(2)}) copy-start(bf16[384,512]{0,1:T(8,128)(2,1)} %copy-done.14) | copy-start | bytes 1179652
  50.5 2.5 %copy-start.17 = (bf16[384,512]{0,1:T(8,128)(2,1)S(1)}, bf16[384,512]{0,1:T(8,128)(2,1)}, u32[]{:S(2)}) copy-start(bf16[384,512]{0,1:T(8,128)(2,1)} %copy-done.16) | copy-start | bytes 1179652
  50.5 2.6 %copy-start.19 = (bf16[384,512]{0,1:T(8,128)(2,1)S(1)}, bf16[384,512]{0,1:T(8,128)(2,1)}, u32[]{:S(2)}) copy-start(bf16[384,512]{0,1:T(8,128)(2,1)} %copy-done.18) | copy-start | bytes 1179652
  53.1 1.9 %copy-start.5 = (bf16[3,128,8,64]{1,0,3,2:T(4,128)(2,1)S(1)}, bf16[3,128,8,64]{1,0,3,2:T(4,128)(2,1)}, u32[]{:S(2)}) copy-start(bf16[3,128,8,64]{1,0,3,2:T(4,128)(2,1)} %copy-done.4) | copy-start | bytes 1179652
  56.5 1.8 %copy-start = (f32[896,1024]{0,1:T(8,128)}, f32[896,1024]{0,1:T(8,128)S(1)}, u32[]{:S(2)}) copy-start(f32[896,1024]{0,1:T(8,128)S(1)} %fusion.16) | copy-start | bytes 11010052
  56.5 1.9 %copy-start.9 = (bf16[384,512]{0,1:T(8,128)(2,1)S(1)}, bf16[384,512]{0,1:T(8,128)(2,1)}, u32[]{:S(2)}) copy-start(bf16[384,512]{0,1:T(8,128)(2,1)} %copy-done.8) | copy-start | bytes 1179652
  56.5 1.9 %copy-start.11 = (bf16[384,512]{0,1:T(8,128)(2,1)S(1)}, bf16[384,512]{0,1:T(8,128)(2,1)}, u32[]{:S(2)}) copy-start(bf16[384,512]{0,1:T(8,128)(2,1)} %copy-done.10) | copy-start | bytes 1179652
  56.5 2.1 %copy-start.13 = (bf16[384,512]{0,1:T(8,128)(2,1)S(1)}, bf16[384,512]{0,1:T(8,128)(2,1)}, u32[]{:S(2)}) copy-start(bf16[384,512]{0,1:T(8,128)(2,1)} %copy-done.12) | copy-start | bytes 1179652
  58.4 4.4 %copy-start.6 = (f32[1,384,512]{1,2,0:T(8,128)S(1)}, f32[1,384,512]{1,2,0:T(8,128)}, u32[]{:S(2)}) copy-start(f32[1,384,512]{1,2,0:T(8,128)} %reshape.296) | copy-start | bytes 2359300
  58.4 4.5 %collective-permute-start.5 = (bf16[256,1024]{0,1:T(8,128)(2,1)S(1)}, bf16[256,1024]{0,1:T(8,128)(2,1)S(1)}, u32[]{:S(2)}, u32[]{:S(2)}) collective-permute-start(bf16[256,1024]{0,1:T(8,128)(2,1)S(1)} %get-tuple-element.18), channel_id=1, source_target_pairs={{0,2},{2,0},{4,6},{6,4},{8,10},{10,8},{12,14},{14,12},{1,3},{3,1},... | collective-permute-start | bytes 1572872 | tf_op jit(solution)/shard_map/ppermute | solution.py:162
  60.5 10.5 %collective-permute-start.7 = (bf16[256,1024]{0,1:T(8,128)(2,1)S(1)}, bf16[256,1024]{0,1:T(8,128)(2,1)S(1)}, u32[]{:S(2)}, u32[]{:S(2)}) collective-permute-start(bf16[256,1024]{0,1:T(8,128)(2,1)S(1)} %get-tuple-element.17), channel_id=1, source_target_pairs={{2,4},{6,8},{10,12},{4,2},{8,6},{12,10},{3,5},{7,9},{11,13},{5,3},... | collective-permute-start | bytes 1572872 | tf_op jit(solution)/shard_map/ppermute | solution.py:163
  64.3 8.9 %collective-permute-start.6 = (bf16[2,128,512]{1,2,0:T(8,128)(2,1)S(1)}, bf16[2,128,512]{1,2,0:T(8,128)(2,1)S(1)}, u32[]{:S(2)}, u32[]{:S(2)}) collective-permute-start(bf16[2,128,512]{1,2,0:T(8,128)(2,1)S(1)} %fusion.34), channel_id=1, source_target_pairs={{0,16},{16,0},{1,17},{17,1},{2,18},{18,2},{3,19},{19,3},{4,20},{20... | collective-permute-start | bytes 786440 | tf_op jit(solution)/shard_map/ppermute | solution.py:34
  75.3 14.0 %collective-permute-start.8 = (bf16[2,256,512]{1,2,0:T(8,128)(2,1)S(1)}, bf16[2,256,512]{1,2,0:T(8,128)(2,1)S(1)}, u32[]{:S(2)}, u32[]{:S(2)}) collective-permute-start(bf16[2,256,512]{1,2,0:T(8,128)(2,1)S(1)} %fusion.24), channel_id=1, source_target_pairs={{0,16},{16,0},{1,17},{17,1},{2,18},{18,2},{3,19},{19,3},{4,20},{20... | collective-permute-start | bytes 1572872 | tf_op jit(solution)/shard_map/ppermute | solution.py:34

commit v20 on v15

--- a/solution.py
+++ b/solution.py
@@ -190,11 +190,13 @@
         jnp.concatenate([back_late, back_early], axis=1),
         jnp.concatenate([back_early, back_late], axis=1),
     )
-    result = jnp.where(
+    empty = jnp.zeros_like(kv_pair)
+    base = jnp.where(
         is_first,
-        jnp.concatenate([kv_pair, back], axis=2),
-        jnp.concatenate([back, qn_pair], axis=2),
-    )
+        jnp.concatenate([kv_pair, empty], axis=2),
+        jnp.concatenate([empty, qn_pair], axis=2),
+    )
+    result = lax.dynamic_update_slice(base, back, (0, 0, jnp.where(is_first, half, 0)))
     return result[None]
 
 

time: 92 us -> 93.7 us (1.018)
  waiting for transfers between devices: 44.1 us -> 46.4 us
  local copies, waits for them, and re-layouts: 15.3 us -> 13.7 us
  other arithmetic: 13.7 us -> 14.7 us
    ppermute x1, waiting for transfers between devices: 1.9 us -> 4.13 us  [halo_swap(): across = lax.ppermute(jnp.where(even, top, bottom), 'seq', between)]
    select_n x1 -> x0, local copies, waits for them, and re-layouts: 1.63 us -> none  [per_device(): jnp.where(is_first, jnp.concatenate([kv_pair, back], axis=2), jnp.concate...]
    dynamic_update_slice x0 -> x1, local copies, waits for them, and re-layouts: none -> 1.63 us  [per_device(): lax.dynamic_update_slice(base, back, (0, 0, jnp.where(is_first, half, 0)))]
    another operation x1, local copies, waits for them, and re-layouts: 1.61 us -> 0.11 us  [attention_grads(): q4 = queries.reshape(unit_count, UNIT, heads, DH)]
    select_n x1, other arithmetic: 0.15 us -> 1.28 us  [per_device(): query_cot = jnp.where(is_first, arrived, kept)]
  transfers between devices with their start and end apart: 9 -> 9, of which waited for: 7 -> 7; matrix products, arithmetic and copies ran while one was open for 11% -> 9% of each run, Pallas kernels for 0% -> 0%
where the time goes in v20:
time: 93.7 us; the launch traced here: 93.4 us
  waiting for transfers between devices  46.4 us (50%)
  other arithmetic  14.7 us (16%)
  local copies, waits for them, and re-layouts  13.7 us (15%)
  starting transfers between devices  10.1 us (11%)
  matrix products  6.18 us (7%)
  between operations  2.32 us (2%)
    ppermute x4, waiting for transfers between devices, sec_swap(): return lax.ppermute(value, 'sec', [(0, 1), (1, 0)])  36.2 us
    ppermute x1, waiting for transfers between devices, per_device(): across = lax.ppermute(jnp.where(even, top, bottom), 'seq', between)  5.89 us
    unnamed x46, local copies, waits for them, and re-layouts  5.26 us
    ppermute x1, waiting for transfers between devices, halo_swap(): across = lax.ppermute(jnp.where(even, top, bottom), 'seq', between)  4.13 us
    ppermute x1, starting transfers between devices, per_device(): across = lax.ppermute(jnp.where(even, top, bottom), 'seq', between)  2.48 us
    ppermute x4, starting transfers between devices, sec_swap(): return lax.ppermute(value, 'sec', [(0, 1), (1, 0)])  2.41 us
    ppermute x1, starting transfers between devices, halo_swap(): across = lax.ppermute(jnp.where(even, top, bottom), 'seq', between)  1.91 us
  transfers between devices with their start and end apart: 9, of which 7 were waited for; matrix products, arithmetic and copies ran while one was open for 9% of the time, Pallas kernels for 0%

profile of v20, /device:TPU:18, one launch (start us, length us, event | category | flops | bytes accessed | tf_op | source)
XLA Modules:
  0.0 93.4 jit_solution(14303675385303478240)
XLA Ops:
  0.0 1.5 %constant_dynamic-slice_fusion.6 = (bf16[1,2,384,512]{3,2,1,0:T(8,128)(2,1)S(1)}, bf16[1,2,384,512]{3,2,1,0:T(8,128)(2,1)S(1)}) fusion(bf16[1,2,384,1024]{3,2,1,0:T(8,128)(2,1)} %param.2, s32[]{:T(128)S(6)} %select_n.172, s32[]{:T(128)S(6)} %select_n.171), kind=kLoop, calls=%fused_computation.104 | loop fusion | bytes 3145736 | tf_op jit(solution)/shard_map/dynamic_slice | solution.py:129
  1.5 0.4 copy.20
  1.9 0.6 collective-permute-start
  2.8 0.4 copy.21
  3.7 17.6 %collective-permute-done = bf16[2,384,512]{1,2,0:T(8,128)(2,1)} collective-permute-done((bf16[2,384,512]{1,2,0:T(8,128)(2,1)S(1)}, bf16[2,384,512]{1,2,0:T(8,128)(2,1)}, u32[]{:S(2)}, u32[]{:S(2)}) %collective-permute-start) | collective-permute-done | bytes 786464 | tf_op jit(solution)/shard_map/ppermute | solution.py:34
  21.3 1.3 %bitcast_select_fusion.1 = (bf16[2,384,512]{1,2,0:T(8,128)(2,1)S(1)}, bf16[2,384,512]{1,2,0:T(8,128)(2,1)S(1)}) fusion(bf16[2,384,512]{1,2,0:T(8,128)(2,1)} %collective-permute-done, bf16[1,2,384,512]{2,3,1,0:T(8,128)(2,1)S(1)} %copy.21, pred[]{:T(512)S(6)} %eq.18), kind=kLoop, calls=%fused_computation.55 | loop fusion | flops 786432 | bytes 3145729 | tf_op jit(solution)/shard_map/jit(_where)/select_n | solution.py:132
  22.7 1.2 %broadcast_select_fusion.7 = (bf16[256,1024]{0,1:T(8,128)(2,1)}, bf16[256,1024]{0,1:T(8,128)(2,1)}) fusion(pred[]{:T(512)S(6)} %eq.21, bf16[384,512]{0,1:T(8,128)(2,1)S(1)} %get-tuple-element.42, bf16[384,512]{0,1:T(8,128)(2,1)S(1)} %get-tuple-element.41), kind=kLoop, calls=%fused_computation.78 | loop fusion | flops 3670016 | bytes 1835009 | tf_op jit(solution)/shard_map/jit(_where)/select_n | solution.py:27
  23.9 1.9 %collective-permute-start.1 = (bf16[256,1024]{0,1:T(8,128)(2,1)}, bf16[256,1024]{0,1:T(8,128)(2,1)}, u32[]{:S(2)}, u32[]{:S(2)}) collective-permute-start(bf16[256,1024]{0,1:T(8,128)(2,1)} %get-tuple-element.39), channel_id=1, source_target_pairs={{2,4},{6,8},{10,12},{4,2},{8,6},{12,10},{3,5},{7,9},{11,13},{5,3},... | collective-permute-start | bytes 1572872 | tf_op jit(solution)/shard_map/ppermute | solution.py:27
  25.8 1.7 %collective-permute-start.2 = (bf16[256,1024]{0,1:T(8,128)(2,1)}, bf16[256,1024]{0,1:T(8,128)(2,1)}, u32[]{:S(2)}, u32[]{:S(2)}) collective-permute-start(bf16[256,1024]{0,1:T(8,128)(2,1)} %get-tuple-element.40), channel_id=1, source_target_pairs={{0,2},{2,0},{4,6},{6,4},{8,10},{10,8},{12,14},{14,12},{1,3},{3,1},... | collective-permute-start | bytes 1572872 | tf_op jit(solution)/shard_map/ppermute | solution.py:26
  27.5 0.6 fusion.53
  30.2 0.3 reshape.251
  30.5 4.1 %collective-permute-done.1 = bf16[256,1024]{0,1:T(8,128)(2,1)} collective-permute-done((bf16[256,1024]{0,1:T(8,128)(2,1)}, bf16[256,1024]{0,1:T(8,128)(2,1)}, u32[]{:S(2)}, u32[]{:S(2)}) %collective-permute-start.1) | collective-permute-done | bytes 524320 | tf_op jit(solution)/shard_map/ppermute | solution.py:27
  34.7 1.3 %broadcast_select_fusion.5 = (bf16[256,1024]{0,1:T(8,128)(2,1)S(1)}, bf16[256,1024]{0,1:T(8,128)(2,1)S(1)}) fusion(bf16[256,1024]{0,1:T(8,128)(2,1)} %collective-permute-done.1, bf16[256,1024]{0,1:T(8,128)(2,1)} %collective-permute-done.2, pred[]{:T(512)S(6)} %eq.21), kind=kLoop, calls=%fused_computation.76 | loop fusion | flops 524288 | bytes 2097153 | tf_op jit(solution)/shard_map/jit(_where)/select_n | solution.py:28
  36.6 0.8 fusion.32
  37.5 1.7 %fusion.54 = (f32[3,8,128]{2,1,0:T(8,128)S(1)}, f32[3,8,128,384]{3,2,1,0:T(8,128)S(1)}) fusion(f32[3,8,128,384]{3,2,1,0:T(8,128)S(1)} %fusion.32, pred[3,384]{1,0:T(4,128)(4,1)S(1)} %bitcast.125), kind=kOutput, calls=%fused_computation.134 | output fusion | flops 7078271 | bytes 9450624 | tf_op jit(solution)/shard_map/sub | solution.py:78
  39.2 0.6 fusion.7
  39.8 1.5 %copy-done.1 = f32[3,8,128,384]{3,2,1,0:T(8,128)} copy-done((f32[3,8,128,384]{3,2,1,0:T(8,128)}, f32[3,8,128,384]{3,2,1,0:T(8,128)S(1)}, u32[]{:S(2)}) %copy-start.1) | copy-done | bytes 4718616
  41.4 1.2 %multiply_reduce_fusion.2 = (f32[3,128]{1,0:T(4,128)S(1)}, f32[3,128]{1,0:T(4,128)S(1)}, f32[3,128,8,64]{1,3,2,0:T(8,128)S(1)}) fusion(f32[3,128,8,64]{1,0,3,2:T(4,128)S(1)} %reshape.251, bf16[3,8,128,384]{3,2,1,0:T(8,128)(2,1)S(1)} %fusion.7, bf16[1,384,8,64]{1,3,2,0:T(8,128)(2,1)S(1)} %bitcast.109, bf16[1,384,8,64]{1,3,2,0:T(8,128)(2,1)S(1)} %bitcast.111, ...), kind=kOutput, calls=%fused_computation.60 | convolution fusion | flops 152960256 | bytes 5114880 | tf_op jit(solution)/shard_map/jhqk,jkhd->jqhd/dot_general | solution.py:81
  42.6 0.6 collective-permute-start.3
  43.2 3.1 %collective-permute-done.3 = f32[2,384]{1,0:T(2,128)S(1)} collective-permute-done((f32[2,384]{1,0:T(2,128)S(1)}, f32[2,384]{1,0:T(2,128)S(1)}, u32[]{:S(2)}, u32[]{:S(2)}) %collective-permute-start.3) | collective-permute-done | bytes 3104 | tf_op jit(solution)/shard_map/ppermute | solution.py:34
  46.3 1.6 %collective-permute-start.4 = (f32[2,384]{1,0:T(2,128)S(1)}, f32[2,384]{1,0:T(2,128)S(1)}, u32[]{:S(2)}, u32[]{:S(2)}) collective-permute-start(f32[2,384]{1,0:T(2,128)S(1)} %fusion.51), channel_id=1, source_target_pairs={{0,1},{1,0},{2,3},{3,2},{4,5},{5,4},{6,7},{7,6},{8,9},{9,8},{10,11... | collective-permute-start | bytes 9224 | tf_op jit(solution)/shard_map/ppermute | solution.py:143
  47.9 0.5 copy.27
  48.4 1.3 %reshape.250 = f32[1,384,512]{1,2,0:T(8,128)} reshape(f32[3,128,8,64]{1,0,3,2:T(4,128)S(1)} %copy.27) | data formatting | bytes 1572864 | tf_op jit(solution)/shard_map/reshape | solution.py:82
  50.0 1.7 %multiply_reduce_fusion = (f32[3,128,8]{1,2,0:T(8,128)S(1)}, bf16[3,128,8,64]{1,3,2,0:T(8,128)(2,1)S(1)}) fusion(f32[3,128,8,64]{1,3,2,0:T(8,128)} %copy-done.7, f32[3,128]{1,0:T(4,128)S(1)} %bitcast.122, f32[3,128]{1,0:T(4,128)S(1)} %bitcast.120, f32[3,128,8,64]{1,0,3,2:T(4,128)} %copy-done.3), kind=kLoop, calls=%fused_computation.57 | loop fusion | flops 1569792 | bytes 1981440 | tf_op jit(solution)/shard_map/reduce_sum | solution.py:93
  51.7 0.6 fusion.55
  52.3 1.7 %copy-done.2 = f32[3,8,128,384]{3,2,1,0:T(8,128)S(1)} copy-done((f32[3,8,128,384]{3,2,1,0:T(8,128)S(1)}, f32[3,8,128,384]{3,2,1,0:T(8,128)}, u32[]{:S(2)}) %copy-start.2) | copy-done | bytes 4718616
  54.3 1.9 %multiply_convert_fusion = bf16[3,8,128,384]{3,2,1,0:T(8,128)(2,1)S(1)} fusion(f32[3,8,128]{2,1,0:T(8,128)S(1)} %bitcast.121, bf16[3,128,8,64]{1,3,2,0:T(8,128)(2,1)S(1)} %get-tuple-element.16, f32[3,8,128,384]{3,2,1,0:T(8,128)S(1)} %copy-done.2, f32[3,8,128]{2,1,0:T(8,128)S(1)} %get-tuple-element.50, bf16[1,384,8,64]{1,3,2,0:T(8,128)(2,1)S(1)} %bitcast.110, ...), kind=kOutput, calls=%fused_computation.5 | convolution fusion | flops 158072832 | bytes 8675328 | tf_op jit(solution)/shard_map/jqhd,jkhd->jhqk/dot_general | solution.py:95
  56.2 0.6 fusion.34
  56.8 0.2 broadcast_in_dim.38
  57.1 0.3 fusion.14
  57.4 0.3 fusion.21
  58.0 1.5 %copy-done = f32[896,1024]{0,1:T(8,128)} copy-done((f32[896,1024]{0,1:T(8,128)}, f32[896,1024]{0,1:T(8,128)S(1)}, u32[]{:S(2)}) %copy-start) | copy-done | bytes 3670040
  59.5 0.9 broadcast_select_fusion.2
  60.4 1.2 %fusion.22 = bf16[3,128,8,64]{1,3,2,0:T(8,128)(2,1)S(1)} fusion(bf16[3,8,128,384]{3,2,1,0:T(8,128)(2,1)S(1)} %multiply_convert_fusion, bf16[1,384,8,64]{1,3,2,0:T(8,128)(2,1)S(1)} %bitcast.102, bf16[1,384,8,64]{1,3,2,0:T(8,128)(2,1)S(1)} %bitcast.104, bf16[1,384,8,64]{1,3,2,0:T(8,128)(2,1)S(1)} %bitcast.100), kind=kOutput, calls=%fused_computation.36 | convolution fusion | flops 152371200 | bytes 3932160 | tf_op jit(solution)/shard_map/jhqk,jkhd->jqhd/dot_general | solution.py:97
  61.6 0.3 copy.26
  61.9 0.3 convert_element_type.85
  62.3 2.5 %collective-permute-start.7 = (bf16[256,1024]{0,1:T(8,128)(2,1)S(1)}, bf16[256,1024]{0,1:T(8,128)(2,1)S(1)}, u32[]{:S(2)}, u32[]{:S(2)}) collective-permute-start(bf16[256,1024]{0,1:T(8,128)(2,1)S(1)} %get-tuple-element.17), channel_id=1, source_target_pairs={{2,4},{6,8},{10,12},{4,2},{8,6},{12,10},{3,5},{7,9},{11,13},{5,3},... | collective-permute-start | bytes 1572872 | tf_op jit(solution)/shard_map/ppermute | solution.py:163
  64.8 1.3 %fusion.31 = bf16[128,1024]{0,1:T(8,128)(2,1)S(1)} fusion(f32[896,1024]{0,1:T(8,128)} %copy-done, bf16[256,1024]{0,1:T(8,128)(2,1)S(1)} %collective-permute-done.5, pred[]{:T(512)S(6)} %eq.21), kind=kLoop, calls=%fused_computation.68 | loop fusion | flops 786432 | bytes 1835009 | tf_op jit(solution)/shard_map/convert_element_type | solution.py:168
  66.3 0.6 collective-permute-start.6
  66.9 5.9 %collective-permute-done.7 = bf16[256,1024]{0,1:T(8,128)(2,1)S(1)} collective-permute-done((bf16[256,1024]{0,1:T(8,128)(2,1)S(1)}, bf16[256,1024]{0,1:T(8,128)(2,1)S(1)}, u32[]{:S(2)}, u32[]{:S(2)}) %collective-permute-start.7) | collective-permute-done | bytes 524320 | tf_op jit(solution)/shard_map/ppermute | solution.py:163
  72.8 2.6 %collective-permute-done.6 = bf16[2,128,512]{1,2,0:T(8,128)(2,1)S(1)} collective-permute-done((bf16[2,128,512]{1,2,0:T(8,128)(2,1)S(1)}, bf16[2,128,512]{1,2,0:T(8,128)(2,1)S(1)}, u32[]{:S(2)}, u32[]{:S(2)}) %collective-permute-start.6) | collective-permute-done | bytes 262176 | tf_op jit(solution)/shard_map/ppermute | solution.py:34
  75.4 1.6 %fusion.18 = bf16[384,1024]{0,1:T(8,128)(2,1)S(1)} fusion(f32[896,1024]{0,1:T(8,128)} %copy-done, bf16[256,1024]{0,1:T(8,128)(2,1)S(1)} %get-tuple-element.26, bf16[256,1024]{0,1:T(8,128)(2,1)S(1)} %get-tuple-element.25), kind=kLoop, calls=%fused_computation.29 | loop fusion | flops 1966080 | bytes 3407872 | tf_op jit(solution)/shard_map/add | solution.py:177
  77.2 0.2 fusion.28
  77.4 0.6 collective-permute-start.8
  78.2 0.3 fusion.10
  78.5 12.9 %collective-permute-done.8 = bf16[2,256,512]{1,2,0:T(8,128)(2,1)S(1)} collective-permute-done((bf16[2,256,512]{1,2,0:T(8,128)(2,1)S(1)}, bf16[2,256,512]{1,2,0:T(8,128)(2,1)S(1)}, u32[]{:S(2)}, u32[]{:S(2)}) %collective-permute-start.8) | collective-permute-done | bytes 524320 | tf_op jit(solution)/shard_map/ppermute | solution.py:34
  91.4 0.3 fusion.24
  91.7 1.6 %copy.28 = bf16[1,2,384,1024]{3,2,1,0:T(8,128)(2,1)} copy(bf16[1,2,384,1024]{2,3,1,0:T(8,128)(2,1)S(1)} %fusion.24) | data formatting | bytes 3145728 | tf_op jit(solution)/shard_map/dynamic_update_slice | solution.py:199
  (77 shorter events, 3.3 us)
Async XLA Ops:
  0.0 2.5 %copy-start.20 = (s32[12]{0:T(128)S(1)}, s32[12]{0:T(128)}, u32[]{:S(2)}) copy-start(s32[12]{0:T(128)} %param.3) | copy-start | bytes 148
  1.9 19.5 %collective-permute-start = (bf16[2,384,512]{1,2,0:T(8,128)(2,1)S(1)}, bf16[2,384,512]{1,2,0:T(8,128)(2,1)}, u32[]{:S(2)}, u32[]{:S(2)}) collective-permute-start(bf16[2,384,512]{1,2,0:T(8,128)(2,1)S(1)} %bitcast.105), channel_id=1, source_target_pairs={{0,16},{16,0},{1,17},{17,1},{2,18},{18,2},{3,19},{19,3},{4,20},{20... | collective-permute-start | bytes 2359304 | tf_op jit(solution)/shard_map/ppermute | solution.py:34
  23.9 10.8 %collective-permute-start.1 = (bf16[256,1024]{0,1:T(8,128)(2,1)}, bf16[256,1024]{0,1:T(8,128)(2,1)}, u32[]{:S(2)}, u32[]{:S(2)}) collective-permute-start(bf16[256,1024]{0,1:T(8,128)(2,1)} %get-tuple-element.39), channel_id=1, source_target_pairs={{2,4},{6,8},{10,12},{4,2},{8,6},{12,10},{3,5},{7,9},{11,13},{5,3},... | collective-permute-start | bytes 1572872 | tf_op jit(solution)/shard_map/ppermute | solution.py:27
  25.8 8.9 %collective-permute-start.2 = (bf16[256,1024]{0,1:T(8,128)(2,1)}, bf16[256,1024]{0,1:T(8,128)(2,1)}, u32[]{:S(2)}, u32[]{:S(2)}) collective-permute-start(bf16[256,1024]{0,1:T(8,128)(2,1)} %get-tuple-element.40), channel_id=1, source_target_pairs={{0,2},{2,0},{4,6},{6,4},{8,10},{10,8},{12,14},{14,12},{1,3},{3,1},... | collective-permute-start | bytes 1572872 | tf_op jit(solution)/shard_map/ppermute | solution.py:26
  30.2 6.4 %copy-start.4 = (bf16[3,128,8,64]{1,0,3,2:T(4,128)(2,1)}, bf16[3,128,8,64]{1,0,3,2:T(4,128)(2,1)S(1)}, u32[]{:S(2)}) copy-start(bf16[3,128,8,64]{1,0,3,2:T(4,128)(2,1)S(1)} %reshape_squeeze.3) | copy-start | bytes 1179652
  30.5 10.8 %copy-start.3 = (f32[3,128,8,64]{1,0,3,2:T(4,128)}, f32[3,128,8,64]{1,0,3,2:T(4,128)S(1)}, u32[]{:S(2)}) copy-start(f32[3,128,8,64]{1,0,3,2:T(4,128)S(1)} %reshape.251) | copy-start | bytes 2359300
  36.4 1.0 %copy-start.8 = (bf16[384,512]{0,1:T(8,128)(2,1)}, bf16[384,512]{0,1:T(8,128)(2,1)S(1)}, u32[]{:S(2)}) copy-start(bf16[384,512]{0,1:T(8,128)(2,1)S(1)} %get-tuple-element.32) | copy-start | bytes 1179652
  36.4 1.0 %copy-start.10 = (bf16[384,512]{0,1:T(8,128)(2,1)}, bf16[384,512]{0,1:T(8,128)(2,1)S(1)}, u32[]{:S(2)}) copy-start(bf16[384,512]{0,1:T(8,128)(2,1)S(1)} %get-tuple-element.33) | copy-start | bytes 1179652
  36.4 1.0 %copy-start.12 = (bf16[384,512]{0,1:T(8,128)(2,1)}, bf16[384,512]{0,1:T(8,128)(2,1)S(1)}, u32[]{:S(2)}) copy-start(bf16[384,512]{0,1:T(8,128)(2,1)S(1)} %get-tuple-element.34) | copy-start | bytes 1179652
  36.6 4.8 %copy-start.14 = (bf16[384,512]{0,1:T(8,128)(2,1)}, bf16[384,512]{0,1:T(8,128)(2,1)S(1)}, u32[]{:S(2)}) copy-start(bf16[384,512]{0,1:T(8,128)(2,1)S(1)} %get-tuple-element.29) | copy-start | bytes 1179652
  36.6 4.8 %copy-start.16 = (bf16[384,512]{0,1:T(8,128)(2,1)}, bf16[384,512]{0,1:T(8,128)(2,1)S(1)}, u32[]{:S(2)}) copy-start(bf16[384,512]{0,1:T(8,128)(2,1)S(1)} %get-tuple-element.30) | copy-start | bytes 1179652
  36.6 4.7 %copy-start.18 = (bf16[384,512]{0,1:T(8,128)(2,1)}, bf16[384,512]{0,1:T(8,128)(2,1)S(1)}, u32[]{:S(2)}) copy-start(bf16[384,512]{0,1:T(8,128)(2,1)S(1)} %get-tuple-element.31) | copy-start | bytes 1179652
  39.2 2.1 %copy-start.1 = (f32[3,8,128,384]{3,2,1,0:T(8,128)}, f32[3,8,128,384]{3,2,1,0:T(8,128)S(1)}, u32[]{:S(2)}) copy-start(f32[3,8,128,384]{3,2,1,0:T(8,128)S(1)} %get-tuple-element.51) | copy-start | bytes 14155780
  42.6 5.3 %copy-start.7 = (f32[3,128,8,64]{1,3,2,0:T(8,128)}, f32[3,128,8,64]{1,3,2,0:T(8,128)S(1)}, u32[]{:S(2)}) copy-start(f32[3,128,8,64]{1,3,2,0:T(8,128)S(1)} %get-tuple-element.52) | copy-start | bytes 2359300
  42.6 3.7 %collective-permute-start.3 = (f32[2,384]{1,0:T(2,128)S(1)}, f32[2,384]{1,0:T(2,128)S(1)}, u32[]{:S(2)}, u32[]{:S(2)}) collective-permute-start(f32[2,384]{1,0:T(2,128)S(1)} %pad_maximum_fusion.10), channel_id=1, source_target_pairs={{0,16},{16,0},{1,17},{17,1},{2,18},{18,2},{3,19},{19,3},{4,20},{20... | collective-permute-start | bytes 9224 | tf_op jit(solution)/shard_map/ppermute | solution.py:34
  46.3 3.7 %collective-permute-start.4 = (f32[2,384]{1,0:T(2,128)S(1)}, f32[2,384]{1,0:T(2,128)S(1)}, u32[]{:S(2)}, u32[]{:S(2)}) collective-permute-start(f32[2,384]{1,0:T(2,128)S(1)} %fusion.51), channel_id=1, source_target_pairs={{0,1},{1,0},{2,3},{3,2},{4,5},{5,4},{6,7},{7,6},{8,9},{9,8},{10,11... | collective-permute-start | bytes 9224 | tf_op jit(solution)/shard_map/ppermute | solution.py:143
  51.7 2.3 %copy-start.2 = (f32[3,8,128,384]{3,2,1,0:T(8,128)S(1)}, f32[3,8,128,384]{3,2,1,0:T(8,128)}, u32[]{:S(2)}) copy-start(f32[3,8,128,384]{3,2,1,0:T(8,128)} %copy-done.1) | copy-start | bytes 14155780
  51.7 2.4 %copy-start.15 = (bf16[384,512]{0,1:T(8,128)(2,1)S(1)}, bf16[384,512]{0,1:T(8,128)(2,1)}, u32[]{:S(2)}) copy-start(bf16[384,512]{0,1:T(8,128)(2,1)} %copy-done.14) | copy-start | bytes 1179652
  51.7 2.5 %copy-start.17 = (bf16[384,512]{0,1:T(8,128)(2,1)S(1)}, bf16[384,512]{0,1:T(8,128)(2,1)}, u32[]{:S(2)}) copy-start(bf16[384,512]{0,1:T(8,128)(2,1)} %copy-done.16) | copy-start | bytes 1179652
  51.7 2.6 %copy-start.19 = (bf16[384,512]{0,1:T(8,128)(2,1)S(1)}, bf16[384,512]{0,1:T(8,128)(2,1)}, u32[]{:S(2)}) copy-start(bf16[384,512]{0,1:T(8,128)(2,1)} %copy-done.18) | copy-start | bytes 1179652
  54.3 1.9 %copy-start.5 = (bf16[3,128,8,64]{1,0,3,2:T(4,128)(2,1)S(1)}, bf16[3,128,8,64]{1,0,3,2:T(4,128)(2,1)}, u32[]{:S(2)}) copy-start(bf16[3,128,8,64]{1,0,3,2:T(4,128)(2,1)} %copy-done.4) | copy-start | bytes 1179652
  57.7 1.8 %copy-start = (f32[896,1024]{0,1:T(8,128)}, f32[896,1024]{0,1:T(8,128)S(1)}, u32[]{:S(2)}) copy-start(f32[896,1024]{0,1:T(8,128)S(1)} %fusion.21) | copy-start | bytes 11010052
  57.7 2.6 %copy-start.9 = (bf16[384,512]{0,1:T(8,128)(2,1)S(1)}, bf16[384,512]{0,1:T(8,128)(2,1)}, u32[]{:S(2)}) copy-start(bf16[384,512]{0,1:T(8,128)(2,1)} %copy-done.8) | copy-start | bytes 1179652
  57.8 2.6 %copy-start.11 = (bf16[384,512]{0,1:T(8,128)(2,1)S(1)}, bf16[384,512]{0,1:T(8,128)(2,1)}, u32[]{:S(2)}) copy-start(bf16[384,512]{0,1:T(8,128)(2,1)} %copy-done.10) | copy-start | bytes 1179652
  57.8 2.6 %copy-start.13 = (bf16[384,512]{0,1:T(8,128)(2,1)S(1)}, bf16[384,512]{0,1:T(8,128)(2,1)}, u32[]{:S(2)}) copy-start(bf16[384,512]{0,1:T(8,128)(2,1)} %copy-done.12) | copy-start | bytes 1179652
  60.4 4.4 %copy-start.6 = (f32[1,384,512]{1,2,0:T(8,128)S(1)}, f32[1,384,512]{1,2,0:T(8,128)}, u32[]{:S(2)}) copy-start(f32[1,384,512]{1,2,0:T(8,128)} %reshape.250) | copy-start | bytes 2359300
  60.4 4.5 %collective-permute-start.5 = (bf16[256,1024]{0,1:T(8,128)(2,1)}, bf16[256,1024]{0,1:T(8,128)(2,1)S(1)}, u32[]{:S(2)}, u32[]{:S(2)}) collective-permute-start(bf16[256,1024]{0,1:T(8,128)(2,1)} %get-tuple-element.18), channel_id=1, source_target_pairs={{0,2},{2,0},{4,6},{6,4},{8,10},{10,8},{12,14},{14,12},{1,3},{3,1},... | collective-permute-start | bytes 1572872 | tf_op jit(solution)/shard_map/ppermute | solution.py:162
  62.3 10.5 %collective-permute-start.7 = (bf16[256,1024]{0,1:T(8,128)(2,1)S(1)}, bf16[256,1024]{0,1:T(8,128)(2,1)S(1)}, u32[]{:S(2)}, u32[]{:S(2)}) collective-permute-start(bf16[256,1024]{0,1:T(8,128)(2,1)S(1)} %get-tuple-element.17), channel_id=1, source_target_pairs={{2,4},{6,8},{10,12},{4,2},{8,6},{12,10},{3,5},{7,9},{11,13},{5,3},... | collective-permute-start | bytes 1572872 | tf_op jit(solution)/shard_map/ppermute | solution.py:163
  66.3 9.1 %collective-permute-start.6 = (bf16[2,128,512]{1,2,0:T(8,128)(2,1)S(1)}, bf16[2,128,512]{1,2,0:T(8,128)(2,1)S(1)}, u32[]{:S(2)}, u32[]{:S(2)}) collective-permute-start(bf16[2,128,512]{1,2,0:T(8,128)(2,1)S(1)} %fusion.38), channel_id=1, source_target_pairs={{0,16},{16,0},{1,17},{17,1},{2,18},{18,2},{3,19},{19,3},{4,20},{20... | collective-permute-start | bytes 786440 | tf_op jit(solution)/shard_map/ppermute | solution.py:34
  77.4 14.0 %collective-permute-start.8 = (bf16[2,256,512]{1,2,0:T(8,128)(2,1)S(1)}, bf16[2,256,512]{1,2,0:T(8,128)(2,1)S(1)}, u32[]{:S(2)}, u32[]{:S(2)}) collective-permute-start(bf16[2,256,512]{1,2,0:T(8,128)(2,1)S(1)} %fusion.28), channel_id=1, source_target_pairs={{0,16},{16,0},{1,17},{17,1},{2,18},{18,2},{3,19},{19,3},{4,20},{20... | collective-permute-start | bytes 1572872 | tf_op jit(solution)/shard_map/ppermute | solution.py:34

commit v21 on v15

--- a/solution.py
+++ b/solution.py
@@ -178,7 +178,13 @@
         + jnp.pad(from_left.astype(jnp.float32), ((0, rows - halo), (0, 0)))
         + jnp.pad(from_right.astype(jnp.float32), ((rows - halo, 0), (0, 0)))
     )
-    late_own = jnp.where(even, own[: rows - early], own[early:]).astype(jnp.bfloat16)
+    late_even = (middle[: rows - early] + across.astype(jnp.float32)) + jnp.pad(
+        within[: halo - early].astype(jnp.float32), ((early, 0), (0, 0))
+    )
+    late_odd = (
+        middle[early:] + jnp.pad(within[early:].astype(jnp.float32), ((0, rows - halo), (0, 0)))
+    ) + across.astype(jnp.float32)
+    late_own = jnp.where(even, late_even, late_odd).astype(jnp.bfloat16)
     grad_k = own[:, :half].astype(jnp.bfloat16)
     grad_v = own[:, half:].astype(jnp.bfloat16)
     kv_pair = jnp.stack([grad_k, grad_v])

time: 92 us -> 90.6 us (0.985)
  other arithmetic: 13.7 us -> 12.5 us
    add x1 -> x0, other arithmetic: 1.65 us -> none  [per_device(): middle + jnp.pad(from_left.astype(jnp.float32), ((0, rows - halo), (0, 0)))]
    unnamed x46 -> x48, local copies, waits for them, and re-layouts: 5.41 us -> 5.41 us
  transfers between devices with their start and end apart: 9 -> 9, of which waited for: 7 -> 7; matrix products, arithmetic and copies ran while one was open for 11% -> 12% of each run, Pallas kernels for 0% -> 0%
where the time goes in v21:
time: 90.6 us; the launch traced here: 90.3 us
  waiting for transfers between devices  43.7 us (48%)
  local copies, waits for them, and re-layouts  15.3 us (17%)
  other arithmetic  12.5 us (14%)
  starting transfers between devices  10.1 us (11%)
  matrix products  6.17 us (7%)
  between operations  2.43 us (3%)
    ppermute x4, waiting for transfers between devices, sec_swap(): return lax.ppermute(value, 'sec', [(0, 1), (1, 0)])  35.9 us
    ppermute x1, waiting for transfers between devices, per_device(): across = lax.ppermute(jnp.where(even, top, bottom), 'seq', between)  5.74 us
    unnamed x48, local copies, waits for them, and re-layouts  5.41 us
    ppermute x1, starting transfers between devices, per_device(): across = lax.ppermute(jnp.where(even, top, bottom), 'seq', between)  2.46 us
    ppermute x4, starting transfers between devices, sec_swap(): return lax.ppermute(value, 'sec', [(0, 1), (1, 0)])  2.38 us
    ppermute x1, starting transfers between devices, halo_swap(): across = lax.ppermute(jnp.where(even, top, bottom), 'seq', between)  1.91 us
    dot_general x1, matrix products, attention_grads(): jnp.einsum('jqhd,jkhd->jhqk', up4, values_w, preferred_element_type=jnp.f...  1.87 us
    dynamic_slice x2, local copies, waits for them, and re-layouts, per_device(): kept = lax.dynamic_slice_in_dim(local_heads, keep_offset, half, 2)  1.83 us
  transfers between devices with their start and end apart: 9, of which 7 were waited for; matrix products, arithmetic and copies ran while one was open for 12% of the time, Pallas kernels for 0%

profile of v21, /device:TPU:18, one launch (start us, length us, event | category | flops | bytes accessed | tf_op | source)
XLA Modules:
  0.0 90.3 jit_solution(4227672280558295760)
XLA Ops:
  0.0 1.5 %constant_dynamic-slice_fusion.6 = (bf16[1,2,384,512]{3,2,1,0:T(8,128)(2,1)S(1)}, bf16[1,2,384,512]{3,2,1,0:T(8,128)(2,1)S(1)}) fusion(bf16[1,2,384,1024]{3,2,1,0:T(8,128)(2,1)} %param.2, s32[]{:T(128)S(6)} %select_n.176, s32[]{:T(128)S(6)} %select_n.175), kind=kLoop, calls=%fused_computation.108 | loop fusion | bytes 3145736 | tf_op jit(solution)/shard_map/dynamic_slice | solution.py:129
  1.5 0.4 copy.20
  1.9 0.6 collective-permute-start
  2.5 0.4 copy.21
  3.7 17.5 %collective-permute-done = bf16[2,384,512]{1,2,0:T(8,128)(2,1)S(1)} collective-permute-done((bf16[2,384,512]{1,2,0:T(8,128)(2,1)S(1)}, bf16[2,384,512]{1,2,0:T(8,128)(2,1)S(1)}, u32[]{:S(2)}, u32[]{:S(2)}) %collective-permute-start) | collective-permute-done | bytes 786464 | tf_op jit(solution)/shard_map/ppermute | solution.py:34
  21.4 1.2 %broadcast_select_fusion.7 = (bf16[256,1024]{0,1:T(8,128)(2,1)}, bf16[256,1024]{0,1:T(8,128)(2,1)}) fusion(pred[]{:T(512)S(6)} %eq.21, bf16[384,512]{0,1:T(8,128)(2,1)S(1)} %get-tuple-element.42, bf16[384,512]{0,1:T(8,128)(2,1)S(1)} %get-tuple-element.41), kind=kLoop, calls=%fused_computation.80 | loop fusion | flops 3670016 | bytes 1835009 | tf_op jit(solution)/shard_map/jit(_where)/select_n | solution.py:27
  22.6 1.9 %collective-permute-start.1 = (bf16[256,1024]{0,1:T(8,128)(2,1)}, bf16[256,1024]{0,1:T(8,128)(2,1)}, u32[]{:S(2)}, u32[]{:S(2)}) collective-permute-start(bf16[256,1024]{0,1:T(8,128)(2,1)} %get-tuple-element.39), channel_id=1, source_target_pairs={{2,4},{6,8},{10,12},{4,2},{8,6},{12,10},{3,5},{7,9},{11,13},{5,3},... | collective-permute-start | bytes 1572872 | tf_op jit(solution)/shard_map/ppermute | solution.py:27
  24.5 1.7 %collective-permute-start.2 = (bf16[256,1024]{0,1:T(8,128)(2,1)}, bf16[256,1024]{0,1:T(8,128)(2,1)}, u32[]{:S(2)}, u32[]{:S(2)}) collective-permute-start(bf16[256,1024]{0,1:T(8,128)(2,1)} %get-tuple-element.40), channel_id=1, source_target_pairs={{0,2},{2,0},{4,6},{6,4},{8,10},{10,8},{12,14},{14,12},{1,3},{3,1},... | collective-permute-start | bytes 1572872 | tf_op jit(solution)/shard_map/ppermute | solution.py:26
  26.3 0.6 fusion.52
  28.8 0.8 slice_convert_fusion
  29.7 0.3 reshape.297
  30.0 1.6 %reshape_squeeze.3 = bf16[3,128,8,64]{1,0,3,2:T(4,128)(2,1)S(1)} reshape(bf16[1,384,512]{1,2,0:T(8,128)(2,1)} %get-tuple-element.38) | data formatting | bytes 786432 | tf_op jit(solution)/shard_map/reshape;squeeze | solution.py:69
  31.6 1.8 %collective-permute-done.1 = bf16[256,1024]{0,1:T(8,128)(2,1)} collective-permute-done((bf16[256,1024]{0,1:T(8,128)(2,1)}, bf16[256,1024]{0,1:T(8,128)(2,1)}, u32[]{:S(2)}, u32[]{:S(2)}) %collective-permute-start.1) | collective-permute-done | bytes 524320 | tf_op jit(solution)/shard_map/ppermute | solution.py:27
  33.4 1.3 %broadcast_select_fusion.5 = (bf16[256,1024]{0,1:T(8,128)(2,1)S(1)}, bf16[256,1024]{0,1:T(8,128)(2,1)S(1)}) fusion(bf16[256,1024]{0,1:T(8,128)(2,1)} %collective-permute-done.1, bf16[256,1024]{0,1:T(8,128)(2,1)} %collective-permute-done.2, pred[]{:T(512)S(6)} %eq.21), kind=kLoop, calls=%fused_computation.78 | loop fusion | flops 524288 | bytes 2097153 | tf_op jit(solution)/shard_map/jit(_where)/select_n | solution.py:28
  35.4 0.8 fusion.31
  36.3 1.7 %fusion.53 = (f32[3,8,128]{2,1,0:T(8,128)S(1)}, f32[3,8,128,384]{3,2,1,0:T(8,128)S(1)}) fusion(f32[3,8,128,384]{3,2,1,0:T(8,128)S(1)} %fusion.31, pred[3,384]{1,0:T(4,128)(4,1)S(1)} %bitcast.125), kind=kOutput, calls=%fused_computation.138 | output fusion | flops 7078271 | bytes 9450624 | tf_op jit(solution)/shard_map/sub | solution.py:78
  38.0 0.6 fusion.5
  38.6 1.5 %copy-done.2 = f32[3,8,128,384]{3,2,1,0:T(8,128)} copy-done((f32[3,8,128,384]{3,2,1,0:T(8,128)}, f32[3,8,128,384]{3,2,1,0:T(8,128)S(1)}, u32[]{:S(2)}) %copy-start.2) | copy-done | bytes 4718616
  40.1 1.2 %multiply_reduce_fusion.2 = (f32[3,128]{1,0:T(4,128)S(1)}, f32[3,128]{1,0:T(4,128)S(1)}, f32[3,128,8,64]{1,3,2,0:T(8,128)S(1)}) fusion(f32[3,128,8,64]{1,0,3,2:T(4,128)S(1)} %reshape.297, bf16[3,8,128,384]{3,2,1,0:T(8,128)(2,1)S(1)} %fusion.5, bf16[1,384,8,64]{1,3,2,0:T(8,128)(2,1)S(1)} %bitcast.110, bf16[1,384,8,64]{1,3,2,0:T(8,128)(2,1)S(1)} %bitcast.112, ...), kind=kOutput, calls=%fused_computation.62 | convolution fusion | flops 152960256 | bytes 5114880 | tf_op jit(solution)/shard_map/jhqk,jkhd->jqhd/dot_general | solution.py:81
  41.4 0.6 collective-permute-start.3
  42.0 3.1 %collective-permute-done.3 = f32[2,384]{1,0:T(2,128)S(1)} collective-permute-done((f32[2,384]{1,0:T(2,128)S(1)}, f32[2,384]{1,0:T(2,128)S(1)}, u32[]{:S(2)}, u32[]{:S(2)}) %collective-permute-start.3) | collective-permute-done | bytes 3104 | tf_op jit(solution)/shard_map/ppermute | solution.py:34
  45.1 1.6 %collective-permute-start.4 = (f32[2,384]{1,0:T(2,128)S(1)}, f32[2,384]{1,0:T(2,128)S(1)}, u32[]{:S(2)}, u32[]{:S(2)}) collective-permute-start(f32[2,384]{1,0:T(2,128)S(1)} %fusion.50), channel_id=1, source_target_pairs={{0,1},{1,0},{2,3},{3,2},{4,5},{5,4},{6,7},{7,6},{8,9},{9,8},{10,11... | collective-permute-start | bytes 9224 | tf_op jit(solution)/shard_map/ppermute | solution.py:143
  46.6 0.5 copy.27
  47.2 1.3 %reshape.296 = f32[1,384,512]{1,2,0:T(8,128)} reshape(f32[3,128,8,64]{1,0,3,2:T(4,128)S(1)} %copy.27) | data formatting | bytes 1572864 | tf_op jit(solution)/shard_map/reshape | solution.py:82
  48.5 0.2 collective-permute-done.4
  48.8 1.7 %multiply_reduce_fusion = (f32[3,128,8]{1,2,0:T(8,128)S(1)}, bf16[3,128,8,64]{1,3,2,0:T(8,128)(2,1)S(1)}) fusion(f32[3,128,8,64]{1,3,2,0:T(8,128)} %copy-done.8, f32[3,128]{1,0:T(4,128)S(1)} %bitcast.122, f32[3,128]{1,0:T(4,128)S(1)} %bitcast.120, f32[3,128,8,64]{1,0,3,2:T(4,128)} %copy-done.4), kind=kLoop, calls=%fused_computation.59 | loop fusion | flops 1569792 | bytes 1981440 | tf_op jit(solution)/shard_map/reduce_sum | solution.py:93
  50.5 0.6 fusion.54
  51.0 1.7 %copy-done.3 = f32[3,8,128,384]{3,2,1,0:T(8,128)S(1)} copy-done((f32[3,8,128,384]{3,2,1,0:T(8,128)S(1)}, f32[3,8,128,384]{3,2,1,0:T(8,128)}, u32[]{:S(2)}) %copy-start.3) | copy-done | bytes 4718616
  53.1 1.9 %multiply_convert_fusion = bf16[3,8,128,384]{3,2,1,0:T(8,128)(2,1)S(1)} fusion(f32[3,8,128]{2,1,0:T(8,128)S(1)} %bitcast.121, bf16[3,128,8,64]{1,3,2,0:T(8,128)(2,1)S(1)} %get-tuple-element.16, f32[3,8,128,384]{3,2,1,0:T(8,128)S(1)} %copy-done.3, f32[3,8,128]{2,1,0:T(8,128)S(1)} %get-tuple-element.52, bf16[1,384,8,64]{1,3,2,0:T(8,128)(2,1)S(1)} %bitcast.111, ...), kind=kOutput, calls=%fused_computation.5 | convolution fusion | flops 158072832 | bytes 8675328 | tf_op jit(solution)/shard_map/jqhd,jkhd->jhqk/dot_general | solution.py:95
  55.0 0.6 fusion.33
  55.5 0.2 broadcast_in_dim.36
  55.9 0.3 fusion.9
  56.2 0.3 fusion.17
  56.8 1.5 %copy-done = f32[896,1024]{0,1:T(8,128)} copy-done((f32[896,1024]{0,1:T(8,128)}, f32[896,1024]{0,1:T(8,128)S(1)}, u32[]{:S(2)}) %copy-start) | copy-done | bytes 3670040
  58.6 1.2 %fusion.18 = bf16[3,128,8,64]{1,3,2,0:T(8,128)(2,1)S(1)} fusion(bf16[3,8,128,384]{3,2,1,0:T(8,128)(2,1)S(1)} %multiply_convert_fusion, bf16[1,384,8,64]{1,3,2,0:T(8,128)(2,1)S(1)} %bitcast.104, bf16[1,384,8,64]{1,3,2,0:T(8,128)(2,1)S(1)} %bitcast.106, bf16[1,384,8,64]{1,3,2,0:T(8,128)(2,1)S(1)} %bitcast.102), kind=kOutput, calls=%fused_computation.34 | convolution fusion | flops 152371200 | bytes 3932160 | tf_op jit(solution)/shard_map/jhqk,jkhd->jqhd/dot_general | solution.py:97
  59.8 0.3 copy.26
  60.2 0.3 convert_element_type.95
  60.5 2.5 %collective-permute-start.7 = (bf16[256,1024]{0,1:T(8,128)(2,1)S(1)}, bf16[256,1024]{0,1:T(8,128)(2,1)S(1)}, u32[]{:S(2)}, u32[]{:S(2)}) collective-permute-start(bf16[256,1024]{0,1:T(8,128)(2,1)S(1)} %get-tuple-element.17), channel_id=1, source_target_pairs={{2,4},{6,8},{10,12},{4,2},{8,6},{12,10},{3,5},{7,9},{11,13},{5,3},... | collective-permute-start | bytes 1572872 | tf_op jit(solution)/shard_map/ppermute | solution.py:163
  63.0 1.3 %fusion.30 = bf16[128,1024]{0,1:T(8,128)(2,1)S(1)} fusion(f32[896,1024]{0,1:T(8,128)} %copy-done, pred[]{:T(512)S(6)} %eq.21, bf16[256,1024]{0,1:T(8,128)(2,1)S(1)} %collective-permute-done.5), kind=kLoop, calls=%fused_computation.70 | loop fusion | flops 786432 | bytes 1835009 | tf_op jit(solution)/shard_map/convert_element_type | solution.py:168
  64.5 0.6 collective-permute-start.6
  65.3 5.7 %collective-permute-done.7 = bf16[256,1024]{0,1:T(8,128)(2,1)S(1)} collective-permute-done((bf16[256,1024]{0,1:T(8,128)(2,1)S(1)}, bf16[256,1024]{0,1:T(8,128)(2,1)S(1)}, u32[]{:S(2)}, u32[]{:S(2)}) %collective-permute-start.7) | collective-permute-done | bytes 524320 | tf_op jit(solution)/shard_map/ppermute | solution.py:163
  71.0 2.5 %collective-permute-done.6 = bf16[2,128,512]{1,2,0:T(8,128)(2,1)S(1)} collective-permute-done((bf16[2,128,512]{1,2,0:T(8,128)(2,1)S(1)}, bf16[2,128,512]{1,2,0:T(8,128)(2,1)S(1)}, u32[]{:S(2)}, u32[]{:S(2)}) %collective-permute-start.6) | collective-permute-done | bytes 262176 | tf_op jit(solution)/shard_map/ppermute | solution.py:34
  73.5 0.2 fusion.21
  74.0 0.6 collective-permute-start.8
  75.1 12.9 %collective-permute-done.8 = bf16[2,256,512]{1,2,0:T(8,128)(2,1)S(1)} collective-permute-done((bf16[2,256,512]{1,2,0:T(8,128)(2,1)S(1)}, bf16[2,256,512]{1,2,0:T(8,128)(2,1)S(1)}, u32[]{:S(2)}, u32[]{:S(2)}) %collective-permute-start.8) | collective-permute-done | bytes 524320 | tf_op jit(solution)/shard_map/ppermute | solution.py:34
  88.0 0.2 fusion.23
  88.2 0.4 maximum_select_fusion
  88.6 1.6 %copy.28 = bf16[1,2,384,1024]{3,2,1,0:T(8,128)(2,1)} copy(bf16[1,2,384,1024]{2,3,1,0:T(8,128)(2,1)S(1)} %maximum_select_fusion) | data formatting | bytes 3145728 | tf_op jit(solution)/shard_map/jit(_where)/select_n | solution.py:199
  (81 shorter events, 3.9 us)
Async XLA Ops:
  1.5 1.3 %copy-start.21 = (s32[12]{0:T(128)S(1)}, s32[12]{0:T(128)}, u32[]{:S(2)}) copy-start(s32[12]{0:T(128)} %param.3) | copy-start | bytes 148
  1.9 19.3 %collective-permute-start = (bf16[2,384,512]{1,2,0:T(8,128)(2,1)S(1)}, bf16[2,384,512]{1,2,0:T(8,128)(2,1)S(1)}, u32[]{:S(2)}, u32[]{:S(2)}) collective-permute-start(bf16[2,384,512]{1,2,0:T(8,128)(2,1)S(1)} %bitcast.107), channel_id=1, source_target_pairs={{0,16},{16,0},{1,17},{17,1},{2,18},{18,2},{3,19},{19,3},{4,20},{20... | collective-permute-start | bytes 2359304 | tf_op jit(solution)/shard_map/ppermute | solution.py:34
  22.6 10.8 %collective-permute-start.1 = (bf16[256,1024]{0,1:T(8,128)(2,1)}, bf16[256,1024]{0,1:T(8,128)(2,1)}, u32[]{:S(2)}, u32[]{:S(2)}) collective-permute-start(bf16[256,1024]{0,1:T(8,128)(2,1)} %get-tuple-element.39), channel_id=1, source_target_pairs={{2,4},{6,8},{10,12},{4,2},{8,6},{12,10},{3,5},{7,9},{11,13},{5,3},... | collective-permute-start | bytes 1572872 | tf_op jit(solution)/shard_map/ppermute | solution.py:27
  24.5 8.9 %collective-permute-start.2 = (bf16[256,1024]{0,1:T(8,128)(2,1)}, bf16[256,1024]{0,1:T(8,128)(2,1)}, u32[]{:S(2)}, u32[]{:S(2)}) collective-permute-start(bf16[256,1024]{0,1:T(8,128)(2,1)} %get-tuple-element.40), channel_id=1, source_target_pairs={{0,2},{2,0},{4,6},{6,4},{8,10},{10,8},{12,14},{14,12},{1,3},{3,1},... | collective-permute-start | bytes 1572872 | tf_op jit(solution)/shard_map/ppermute | solution.py:26
  30.0 10.1 %copy-start.4 = (f32[3,128,8,64]{1,0,3,2:T(4,128)}, f32[3,128,8,64]{1,0,3,2:T(4,128)S(1)}, u32[]{:S(2)}) copy-start(f32[3,128,8,64]{1,0,3,2:T(4,128)S(1)} %reshape.297) | copy-start | bytes 2359300
  31.6 3.8 %copy-start.5 = (bf16[3,128,8,64]{1,0,3,2:T(4,128)(2,1)}, bf16[3,128,8,64]{1,0,3,2:T(4,128)(2,1)S(1)}, u32[]{:S(2)}) copy-start(bf16[3,128,8,64]{1,0,3,2:T(4,128)(2,1)S(1)} %reshape_squeeze.3) | copy-start | bytes 1179652
  35.2 1.0 %copy-start.9 = (bf16[384,512]{0,1:T(8,128)(2,1)}, bf16[384,512]{0,1:T(8,128)(2,1)S(1)}, u32[]{:S(2)}) copy-start(bf16[384,512]{0,1:T(8,128)(2,1)S(1)} %get-tuple-element.32) | copy-start | bytes 1179652
  35.2 1.0 %copy-start.11 = (bf16[384,512]{0,1:T(8,128)(2,1)}, bf16[384,512]{0,1:T(8,128)(2,1)S(1)}, u32[]{:S(2)}) copy-start(bf16[384,512]{0,1:T(8,128)(2,1)S(1)} %get-tuple-element.33) | copy-start | bytes 1179652
  35.2 1.0 %copy-start.13 = (bf16[384,512]{0,1:T(8,128)(2,1)}, bf16[384,512]{0,1:T(8,128)(2,1)S(1)}, u32[]{:S(2)}) copy-start(bf16[384,512]{0,1:T(8,128)(2,1)S(1)} %get-tuple-element.34) | copy-start | bytes 1179652
  35.4 4.8 %copy-start.15 = (bf16[384,512]{0,1:T(8,128)(2,1)}, bf16[384,512]{0,1:T(8,128)(2,1)S(1)}, u32[]{:S(2)}) copy-start(bf16[384,512]{0,1:T(8,128)(2,1)S(1)} %get-tuple-element.29) | copy-start | bytes 1179652
  35.4 4.7 %copy-start.17 = (bf16[384,512]{0,1:T(8,128)(2,1)}, bf16[384,512]{0,1:T(8,128)(2,1)S(1)}, u32[]{:S(2)}) copy-start(bf16[384,512]{0,1:T(8,128)(2,1)S(1)} %get-tuple-element.30) | copy-start | bytes 1179652
  35.4 4.7 %copy-start.19 = (bf16[384,512]{0,1:T(8,128)(2,1)}, bf16[384,512]{0,1:T(8,128)(2,1)S(1)}, u32[]{:S(2)}) copy-start(bf16[384,512]{0,1:T(8,128)(2,1)S(1)} %get-tuple-element.31) | copy-start | bytes 1179652
  38.0 2.1 %copy-start.2 = (f32[3,8,128,384]{3,2,1,0:T(8,128)}, f32[3,8,128,384]{3,2,1,0:T(8,128)S(1)}, u32[]{:S(2)}) copy-start(f32[3,8,128,384]{3,2,1,0:T(8,128)S(1)} %get-tuple-element.53) | copy-start | bytes 14155780
  41.3 5.3 %copy-start.8 = (f32[3,128,8,64]{1,3,2,0:T(8,128)}, f32[3,128,8,64]{1,3,2,0:T(8,128)S(1)}, u32[]{:S(2)}) copy-start(f32[3,128,8,64]{1,3,2,0:T(8,128)S(1)} %get-tuple-element.54) | copy-start | bytes 2359300
  41.4 3.7 %collective-permute-start.3 = (f32[2,384]{1,0:T(2,128)S(1)}, f32[2,384]{1,0:T(2,128)S(1)}, u32[]{:S(2)}, u32[]{:S(2)}) collective-permute-start(f32[2,384]{1,0:T(2,128)S(1)} %pad_maximum_fusion.10), channel_id=1, source_target_pairs={{0,16},{16,0},{1,17},{17,1},{2,18},{18,2},{3,19},{19,3},{4,20},{20... | collective-permute-start | bytes 9224 | tf_op jit(solution)/shard_map/ppermute | solution.py:34
  45.1 3.7 %collective-permute-start.4 = (f32[2,384]{1,0:T(2,128)S(1)}, f32[2,384]{1,0:T(2,128)S(1)}, u32[]{:S(2)}, u32[]{:S(2)}) collective-permute-start(f32[2,384]{1,0:T(2,128)S(1)} %fusion.50), channel_id=1, source_target_pairs={{0,1},{1,0},{2,3},{3,2},{4,5},{5,4},{6,7},{7,6},{8,9},{9,8},{10,11... | collective-permute-start | bytes 9224 | tf_op jit(solution)/shard_map/ppermute | solution.py:143
  50.5 2.3 %copy-start.3 = (f32[3,8,128,384]{3,2,1,0:T(8,128)S(1)}, f32[3,8,128,384]{3,2,1,0:T(8,128)}, u32[]{:S(2)}) copy-start(f32[3,8,128,384]{3,2,1,0:T(8,128)} %copy-done.2) | copy-start | bytes 14155780
  50.5 2.4 %copy-start.16 = (bf16[384,512]{0,1:T(8,128)(2,1)S(1)}, bf16[384,512]{0,1:T(8,128)(2,1)}, u32[]{:S(2)}) copy-start(bf16[384,512]{0,1:T(8,128)(2,1)} %copy-done.15) | copy-start | bytes 1179652
  50.5 2.5 %copy-start.18 = (bf16[384,512]{0,1:T(8,128)(2,1)S(1)}, bf16[384,512]{0,1:T(8,128)(2,1)}, u32[]{:S(2)}) copy-start(bf16[384,512]{0,1:T(8,128)(2,1)} %copy-done.17) | copy-start | bytes 1179652
  50.5 2.6 %copy-start.20 = (bf16[384,512]{0,1:T(8,128)(2,1)S(1)}, bf16[384,512]{0,1:T(8,128)(2,1)}, u32[]{:S(2)}) copy-start(bf16[384,512]{0,1:T(8,128)(2,1)} %copy-done.19) | copy-start | bytes 1179652
  53.1 1.9 %copy-start.6 = (bf16[3,128,8,64]{1,0,3,2:T(4,128)(2,1)S(1)}, bf16[3,128,8,64]{1,0,3,2:T(4,128)(2,1)}, u32[]{:S(2)}) copy-start(bf16[3,128,8,64]{1,0,3,2:T(4,128)(2,1)} %copy-done.5) | copy-start | bytes 1179652
  56.5 1.8 %copy-start = (f32[896,1024]{0,1:T(8,128)}, f32[896,1024]{0,1:T(8,128)S(1)}, u32[]{:S(2)}) copy-start(f32[896,1024]{0,1:T(8,128)S(1)} %fusion.17) | copy-start | bytes 11010052
  56.5 1.9 %copy-start.10 = (bf16[384,512]{0,1:T(8,128)(2,1)S(1)}, bf16[384,512]{0,1:T(8,128)(2,1)}, u32[]{:S(2)}) copy-start(bf16[384,512]{0,1:T(8,128)(2,1)} %copy-done.9) | copy-start | bytes 1179652
  56.5 1.9 %copy-start.12 = (bf16[384,512]{0,1:T(8,128)(2,1)S(1)}, bf16[384,512]{0,1:T(8,128)(2,1)}, u32[]{:S(2)}) copy-start(bf16[384,512]{0,1:T(8,128)(2,1)} %copy-done.11) | copy-start | bytes 1179652
  56.6 2.1 %copy-start.14 = (bf16[384,512]{0,1:T(8,128)(2,1)S(1)}, bf16[384,512]{0,1:T(8,128)(2,1)}, u32[]{:S(2)}) copy-start(bf16[384,512]{0,1:T(8,128)(2,1)} %copy-done.13) | copy-start | bytes 1179652
  58.4 4.6 %copy-start.7 = (f32[1,384,512]{1,2,0:T(8,128)S(1)}, f32[1,384,512]{1,2,0:T(8,128)}, u32[]{:S(2)}) copy-start(f32[1,384,512]{1,2,0:T(8,128)} %reshape.296) | copy-start | bytes 2359300
  58.4 4.7 %collective-permute-start.5 = (bf16[256,1024]{0,1:T(8,128)(2,1)S(1)}, bf16[256,1024]{0,1:T(8,128)(2,1)S(1)}, u32[]{:S(2)}, u32[]{:S(2)}) collective-permute-start(bf16[256,1024]{0,1:T(8,128)(2,1)S(1)} %get-tuple-element.18), channel_id=1, source_target_pairs={{0,2},{2,0},{4,6},{6,4},{8,10},{10,8},{12,14},{14,12},{1,3},{3,1},... | collective-permute-start | bytes 1572872 | tf_op jit(solution)/shard_map/ppermute | solution.py:162
  60.5 10.5 %collective-permute-start.7 = (bf16[256,1024]{0,1:T(8,128)(2,1)S(1)}, bf16[256,1024]{0,1:T(8,128)(2,1)S(1)}, u32[]{:S(2)}, u32[]{:S(2)}) collective-permute-start(bf16[256,1024]{0,1:T(8,128)(2,1)S(1)} %get-tuple-element.17), channel_id=1, source_target_pairs={{2,4},{6,8},{10,12},{4,2},{8,6},{12,10},{3,5},{7,9},{11,13},{5,3},... | collective-permute-start | bytes 1572872 | tf_op jit(solution)/shard_map/ppermute | solution.py:163
  64.4 9.1 %copy-start.1 = (f32[896,1024]{0,1:T(8,128)S(1)}, f32[896,1024]{0,1:T(8,128)}, u32[]{:S(2)}) copy-start(f32[896,1024]{0,1:T(8,128)} %copy-done) | copy-start | bytes 11010052
  64.5 9.0 %collective-permute-start.6 = (bf16[2,128,512]{1,2,0:T(8,128)(2,1)S(1)}, bf16[2,128,512]{1,2,0:T(8,128)(2,1)S(1)}, u32[]{:S(2)}, u32[]{:S(2)}) collective-permute-start(bf16[2,128,512]{1,2,0:T(8,128)(2,1)S(1)} %fusion.37), channel_id=1, source_target_pairs={{0,16},{16,0},{1,17},{17,1},{2,18},{18,2},{3,19},{19,3},{4,20},{20... | collective-permute-start | bytes 786440 | tf_op jit(solution)/shard_map/ppermute | solution.py:34
  74.0 14.0 %collective-permute-start.8 = (bf16[2,256,512]{1,2,0:T(8,128)(2,1)S(1)}, bf16[2,256,512]{1,2,0:T(8,128)(2,1)S(1)}, u32[]{:S(2)}, u32[]{:S(2)}) collective-permute-start(bf16[2,256,512]{1,2,0:T(8,128)(2,1)S(1)} %fusion.27), channel_id=1, source_target_pairs={{0,16},{16,0},{1,17},{17,1},{2,18},{18,2},{3,19},{19,3},{4,20},{20... | collective-permute-start | bytes 1572872 | tf_op jit(solution)/shard_map/ppermute | solution.py:34
